TPU v7x, 32 devices: a whole 2x2x4 slice. The times are simulated.
32 devices in a mesh: slab: 4 (over y, x), rad: 8 (over z, core).
Axes of the slice: x: 2, y: 2, z: 4, core: 2. Of those that a mesh axis runs over, the one named last changes fastest.
Arguments:
- q_state: float32 [3, 524288], P(None, ('slab', 'rad')), may hold values from -6.71 to 6.71, as said below
- increments: float32 [3, 524288], P(None, ('slab', 'rad')), may hold values from -6 to 6
- velocity_grad: float32 [5, 12288], P(None, 'slab'), may hold values from -40 to 40
- element: int32 [524288], P(('slab', 'rad')), may hold values from 0 to 3071
- migration: int32 [524288], P(('slab', 'rad')), may hold values from -1 to 1, as said below
- volume: float32 [12288], P(('slab', 'rad')), may hold values from 14.222222 to 128
- div_map: float32 [192, 192], replicated, may hold values from -0.4375 to 0.4375
- stiffness: float32 [256, 4, 192, 192], P(('slab', 'rad')), may hold values from -0.06 to 1.06
- pattern: int32 [256, 4], P(('slab', 'rad')), may hold values from 0 to 191, as said below
- preconditioner: float32 [256, 192, 192], P(('slab', 'rad')), may hold values from -0.03 to 1.03
Outputs:
- q_out: float32 [3, 524288], P(None, ('slab', 'rad'))
- arrivals: float32 [2, 3, 32768], P(None, None, ('slab', 'rad'))
- element_stress: float32 [4, 12288], P(None, ('slab', 'rad'))
- velocity: float32 [256, 192], P(('slab', 'rad'))
Inputs may be any that keep to these rules, and one draw needn't show every extreme that they name: `q_state`: every dumbbell's stretch r^2 + z^2 + t^2 is below 45. Of the dumbbells of one device at most 1024 have migration 1 and at most 1024 have migration -1; some device has exactly 1024 with 1 and some device exactly 1024 with -1. pattern[b, 0] = 64 + b % 64; pattern[b, 1] lies in 0 .. 63, pattern[b, 2] in 64 .. 127, pattern[b, 3] in 128 .. 191.
All inputs are finite; a program needn't handle non-finite values.
Results may differ from a plain program's by a relative error of at most 0.0003.
Values sent between devices are 32-bit elements; how exact they have to be, the bound alone decides.
No kernel may reach another device: no remote copies, remote signals or barrier semaphores. Data moves between devices by JAX's collectives and lax.ppermute only.
A program may use at most 64 MiB of HBM per device.

v0:
```python
import math

import jax
import jax.numpy as jnp
from jax import lax
from jax.sharding import PartitionSpec as P

BLOCK = 192
ITERS = 6


extensibility = 50.0
time_step = 0.01
noise_scale = 0.1
damping = 0.6
highest = lax.Precision.HIGHEST


def passed_along(array, axis, by):
    size = lax.axis_size(axis)
    pairs = [(i, i + by) for i in range(size) if 0 <= i + by < size]
    return lax.ppermute(array, axis, pairs)


def extended(cells, sides, width):
    for axis, dim in sides:
        count = lax.axis_size(axis)
        ends = count - 1
        head = lax.slice_in_dim(cells, 0, width, axis=dim)
        tail = lax.slice_in_dim(cells, cells.shape[dim] - width, cells.shape[dim], axis=dim)
        cells = jnp.concatenate(
            [
                lax.ppermute(tail, axis, [(i, (i + 1) % count) for i in range(ends)]),
                cells,
                lax.ppermute(head, axis, [((i + 1) % count, i) for i in range(ends)]),
            ],
            axis=dim,
        )
    return cells


def update_dumbbells(q_here, inc_here, grads):
    radial = q_here[0]
    axial = q_here[1]
    azimuth = q_here[2]
    stretch = radial * radial + axial * axial + azimuth * azimuth
    spring = 1.0 / (1.0 - stretch / extensibility)
    drift = jnp.stack(
        [
            grads[0] * radial + grads[1] * axial,
            grads[2] * radial + grads[3] * axial,
            grads[4] * azimuth,
        ]
    )
    q_next = q_here + time_step * (drift - 0.5 * spring * q_here) + noise_scale * inc_here
    terms = jnp.stack(
        [
            spring * radial * radial - 1.0,
            spring * axial * axial - 1.0,
            spring * radial * axial,
            spring * azimuth * azimuth - 1.0,
        ]
    )
    return (q_next, terms)


def block_size(count):
    return math.gcd(count, 2048)


def split_onehots(index, count):
    upper_part = index // 128
    lower_part = index % 128
    hot_upper = (upper_part[None, :] == jnp.arange(count // 128, dtype=jnp.int32)[:, None]).astype(
        jnp.float32
    )
    hot_lower = (lower_part[None, :] == jnp.arange(128, dtype=jnp.int32)[:, None]).astype(
        jnp.float32
    )
    return (hot_upper, hot_lower)


def lookup_columns(table, index):
    rows, count = table.shape
    groups = count // 128
    arranged = table.reshape(rows, groups, 128).transpose(0, 2, 1).reshape(rows * 128, groups)
    size = block_size(index.shape[0])

    def one_block(indices):
        hot_upper, hot_lower = split_onehots(indices, count)
        picked = jnp.dot(arranged, hot_upper, precision=highest).reshape(rows, 128, size)
        return jnp.sum(picked * hot_lower[None], 1)

    result = lax.map(one_block, index.reshape(-1, size))
    return result.transpose(1, 0, 2).reshape(rows, -1)


def spread_block(values, indices, count):
    rows, size = values.shape
    hot_upper, hot_lower = split_onehots(indices, count)
    spread = (values[:, None, :] * hot_lower[None]).reshape(rows * 128, size)
    return lax.dot_general(spread, hot_upper, (((1,), (1,)), ((), ())), precision=highest)


def unarrange(total, rows, count):
    return total.reshape(rows, 128, count // 128).transpose(0, 2, 1).reshape(rows, count)


def accumulate_columns(values, index, count):
    rows = values.shape[0]
    size = block_size(index.shape[0])

    def accumulate_step(total, items):
        block_values, block_index = items
        return (total + spread_block(block_values, block_index, count), None)

    start = jnp.zeros((rows * 128, count // 128), jnp.float32)
    blocks = (values.reshape(rows, -1, size).transpose(1, 0, 2), index.reshape(-1, size))
    total, unused = lax.scan(accumulate_step, start, blocks)
    return unarrange(total, rows, count)


def pack_both(payload, migration, capacity):
    rows = payload.shape[0]
    padded_cap = -(-capacity // 128) * 128
    size = block_size(migration.shape[0])
    positions = jnp.arange(size, dtype=jnp.int32)
    earlier = (positions[:, None] < positions[None, :]).astype(jnp.bfloat16)

    def pack_step(carry, items):
        offsets, totals = carry
        block_values, block_moves = items
        chosen = jnp.stack([block_moves == 1, block_moves == -1])
        ranks = jnp.dot(
            chosen.astype(jnp.bfloat16), earlier, preferred_element_type=jnp.float32
        ).astype(jnp.int32)
        slots = jnp.where(chosen, offsets[:, None] + ranks, 0)
        filled = []
        for direction in range(2):
            masked = jnp.where(chosen[direction][None], block_values, 0.0)
            filled.append(spread_block(masked, slots[direction], padded_cap))
        offsets = offsets + jnp.sum(chosen.astype(jnp.int32), 1)
        return ((offsets, totals + jnp.stack(filled)), None)

    start = (jnp.zeros((2,), jnp.int32), jnp.zeros((2, rows * 128, padded_cap // 128), jnp.float32))
    blocks = (payload.reshape(rows, -1, size).transpose(1, 0, 2), migration.reshape(-1, size))
    (offsets, totals), unused = lax.scan(pack_step, start, blocks)
    upward = unarrange(totals[0], rows, padded_cap)
    downward = unarrange(totals[1], rows, padded_cap)
    return (upward, downward)


def body(
    q_state,
    increments,
    velocity_grad,
    element,
    migration,
    volume,
    div_map,
    stiffness,
    pattern,
    preconditioner,
):
    capacity = migration.shape[0] // 16
    slab_elems = velocity_grad.shape[1]
    grads = lookup_columns(velocity_grad, element)
    q_next, terms = update_dumbbells(q_state, increments, grads)
    payload = jnp.concatenate([q_next, terms, element.astype(jnp.float32)[None]], 0)
    upward, downward = pack_both(payload, migration, capacity)
    from_lower = passed_along(upward, "slab", 1)
    from_upper = passed_along(downward, "slab", -1)
    staying = jnp.where(migration == 0, terms, 0.0)
    all_terms = jnp.concatenate([staying, from_lower[3:7], from_upper[3:7]], 1)
    all_index = jnp.concatenate(
        [element, from_lower[7].astype(jnp.int32), from_upper[7].astype(jnp.int32)], 0
    )
    partial_value = accumulate_columns(all_terms, all_index, slab_elems)
    sums = lax.psum_scatter(partial_value, "rad", scatter_dimension=1, tiled=True)
    element_stress = sums / volume
    arrivals = jnp.stack([from_lower[0:3], from_upper[0:3]])
    own_blocks = stiffness.shape[0]
    groups = (
        element_stress.reshape(4, own_blocks, BLOCK // 4)
        .transpose(1, 0, 2)
        .reshape(own_blocks, BLOCK)
    )
    force = jnp.dot(groups, div_map, precision=highest)

    def precondition(vector):
        return jnp.einsum("bij,bj->bi", preconditioner, vector, precision=highest)

    window_rows = 3 * own_blocks * lax.axis_size("rad")
    selector = (
        pattern.reshape(-1)[:, None] == jnp.arange(window_rows, dtype=jnp.int32)[None, :]
    ).astype(jnp.float32)
    velocity = damping * precondition(force)
    for sweep_index in range(1, ITERS):
        gathered = lax.all_gather(velocity, "rad", axis=0, tiled=True)
        window = extended(gathered, (("slab", 0),), gathered.shape[0])
        neighbours = jnp.dot(selector, window, precision=highest).reshape(own_blocks, -1, BLOCK)
        image = jnp.einsum("bnij,bnj->bi", stiffness, neighbours, precision=highest)
        velocity = velocity + damping * precondition(force - image)
    return (q_next, arrivals, element_stress, velocity)


def solution(mesh):
    placed = (
        P(None, ("slab", "rad")),
        P(None, ("slab", "rad")),
        P(None, "slab"),
        P(("slab", "rad")),
        P(("slab", "rad")),
        P(("slab", "rad")),
        P(),
        P(("slab", "rad"), None, None, None),
        P(("slab", "rad"), None),
        P(("slab", "rad"), None, None),
    )
    return jax.shard_map(
        body,
        mesh=mesh,
        in_specs=placed,
        out_specs=(
            P(None, ("slab", "rad")),
            P(None, None, ("slab", "rad")),
            P(None, ("slab", "rad")),
            P(("slab", "rad"), None),
        ),
        check_vma=False,
    )
```

profile of v0, /device:TPU:0, one launch (start us, length us, event | category | flops | bytes accessed | tf_op | source)
XLA Modules:
  0.0 410.8 jit_solution(11150976871779817177)
XLA Ops:
  11.6 26.4 %while.41 = (s32[]{:T(128)}, f32[8,5,2048]{2,1,0:T(8,128)S(1)}, s32[8,2048]{1,0:T(8,128)S(1)}, f32[640,24]{0,1:T(8,128)S(1)}, s32[]{:T(128)}) while((s32[]{:T(128)}, f32[8,5,2048]{2,1,0:T(8,128)S(1)}, s32[8,2048]{1,0:T(8,128)S(1)}, f32[640,24]{0,1:T(8,128)S(1)}, s32[]{:T(128)}) %tuple.140), condition=%wide.region_2.3_spmd, body=%wide.region_0.2_spmd.sunk | while | flops 380719104 | bytes 12882001 | solution.py:94
  39.7 92.2 %while.42 = (s32[]{:T(128)}, s32[2]{0:T(128)S(1)}, f32[2,1024,8]{1,2,0:T(8,128)S(1)}, s32[8,2048]{1,0:T(8,128)S(1)}, f32[8,8,2048]{2,1,0:T(8,128)S(1)}, /*index=5*/s32[]{:T(128)}, s32[]{:T(128)}) while((s32[]{:T(128)}, s32[2]{0:T(128)S(1)}, f32[2,1024,8]{1,2,0:T(8,128)S(1)}, s32[8,2048]{1,0:T(8,128)S(1)}, ...), condition=%wide.region_5.6_spmd.clone, body=%wide.region_3.5_spmd.clone.sunk | while | flops 433287168 | bytes 38502552 | solution.py:147
  133.3 5.5 %collective-permute-start = (f32[8,1024]{1,0:T(8,128)S(1)}, f32[8,1024]{1,0:T(8,128)S(1)}, u32[]{:S(2)}, u32[]{:S(2)}) collective-permute-start(f32[8,1024]{1,0:T(8,128)S(1)} %bitcast.239), channel_id=1, source_target_pairs={{0,8},{8,16},{16,24},{1,9},{9,17},{17,25},{2,10},{10,18},{18,26},{... | collective-permute-start | bytes 98312 | tf_op jit(solution)/shard_map/ppermute | solution.py:22
  140.7 62.7 %while.43 = (s32[]{:T(128)}, f32[512,24]{0,1:T(8,128)S(1)}, f32[9,4,2048]{2,0,1:T(8,128)S(1)}, s32[9,2048]{1,0:T(8,128)S(1)}, s32[]{:T(128)}, /*index=5*/s32[]{:T(128)}) while((s32[]{:T(128)}, f32[512,24]{0,1:T(8,128)S(1)}, f32[9,4,2048]{2,0,1:T(8,128)S(1)}, s32[9,2048]{1,0:T(8,128)S(1)}, s32[]{:T(128)}, ...), condition=%wide.region_7.8_spmd.clone, body=%wide.region_6.7_spmd.clone.sunk | while | flops 303677440 | bytes 10805343 | solution.py:119
  157.6 4.2 %convolution_add_fusion.2 = f32[512,24]{0,1:T(8,128)S(1)} fusion(f32[512,2048]{1,0:T(8,128)} %bitcast.207, s32[2048]{0:T(1024)S(1)} %bitcast.214, f32[512,24]{0,1:T(8,128)S(1)} %get-tuple-element.504, pred[]{:T(512)S(6)} %compare.47), kind=kOutput, calls=%fused_computation.14.clone.1 | convolution fusion | flops 302063616 | bytes 4300801 | tf_op jit(solution)/shard_map/while/body/eval_jaxpr/dot_general | solution.py:102
  164.5 4.2 %convolution_add_fusion.2 = f32[512,24]{0,1:T(8,128)S(1)} fusion(f32[512,2048]{1,0:T(8,128)} %bitcast.207, s32[2048]{0:T(1024)S(1)} %bitcast.214, f32[512,24]{0,1:T(8,128)S(1)} %get-tuple-element.504, pred[]{:T(512)S(6)} %compare.47), kind=kOutput, calls=%fused_computation.14.clone.1 | convolution fusion | flops 302063616 | bytes 4300801 | tf_op jit(solution)/shard_map/while/body/eval_jaxpr/dot_general | solution.py:102
  171.4 4.2 %convolution_add_fusion.2 = f32[512,24]{0,1:T(8,128)S(1)} fusion(f32[512,2048]{1,0:T(8,128)} %bitcast.207, s32[2048]{0:T(1024)S(1)} %bitcast.214, f32[512,24]{0,1:T(8,128)S(1)} %get-tuple-element.504, pred[]{:T(512)S(6)} %compare.47), kind=kOutput, calls=%fused_computation.14.clone.1 | convolution fusion | flops 302063616 | bytes 4300801 | tf_op jit(solution)/shard_map/while/body/eval_jaxpr/dot_general | solution.py:102
  192.2 4.2 %convolution_add_fusion.2 = f32[512,24]{0,1:T(8,128)S(1)} fusion(f32[512,2048]{1,0:T(8,128)} %bitcast.207, s32[2048]{0:T(1024)S(1)} %bitcast.214, f32[512,24]{0,1:T(8,128)S(1)} %get-tuple-element.504, pred[]{:T(512)S(6)} %compare.47), kind=kOutput, calls=%fused_computation.14.clone.1 | convolution fusion | flops 302063616 | bytes 4300801 | tf_op jit(solution)/shard_map/while/body/eval_jaxpr/dot_general | solution.py:102
  205.1 37.6 %reduce-scatter.4.cloned.1.call-done = f32[384,4]{1,0:T(8,128)} async-done(((f32[3072,4]{1,0:T(8,128)}), f32[384,4]{1,0:T(8,128)}) %reduce-scatter.4.cloned.1.call-update) | async-done | bytes 6160
  245.6 14.0 %all_gather.15 = f32[64,192]{1,0:T(8,128)S(1)} all-gather(f32[8,192]{1,0:T(8,128)S(1)} %bitcast_multiply_fusion.5), channel_id=1, replica_groups=mesh['slab'=4,'rad'=8] {'rad'}, dimensions={0}, use_global_device_ids=true | all-gather | bytes 55296 | tf_op jit(solution)/shard_map/all_gather | solution.py:199
  260.9 4.5 %collective-permute-start.2 = (f32[64,192]{1,0:T(8,128)S(1)}, f32[64,192]{1,0:T(8,128)S(1)}, u32[]{:S(2)}, u32[]{:S(2)}) collective-permute-start(f32[64,192]{1,0:T(8,128)S(1)} %all_gather.15), channel_id=1, source_target_pairs={{0,8},{8,16},{16,24},{1,9},{9,17},{17,25},{2,10},{10,18},{18,26},{... | collective-permute-start | bytes 147464 | tf_op jit(solution)/shard_map/ppermute | solution.py:33
  267.6 7.2 %fusion.95 = f32[8,1,192,1]{2,1,3,0:T(1,128)S(1)} fusion(f32[8,4,192,1]{2,3,1,0:T(1,128)S(1)} %reshape.325, f32[8,4,192,192]{3,2,1,0:T(8,128)} %param.23), kind=kOutput, calls=%fused_computation.172 | convolution fusion | flops 14155776 | bytes 4749312 | tf_op jit(solution)/shard_map/bnij,bnj->bi/dot_general | solution.py:202
  276.2 14.0 %all_gather.16 = f32[64,192]{1,0:T(8,128)S(1)} all-gather(f32[8,192]{1,0:T(8,128)S(1)} %fusion.71), channel_id=1, replica_groups=mesh['slab'=4,'rad'=8] {'rad'}, dimensions={0}, use_global_device_ids=true | all-gather | bytes 55296 | tf_op jit(solution)/shard_map/all_gather | solution.py:199
  291.4 4.9 %collective-permute-start.4 = (f32[64,192]{1,0:T(8,128)S(1)}, f32[64,192]{1,0:T(8,128)S(1)}, u32[]{:S(2)}, u32[]{:S(2)}) collective-permute-start(f32[64,192]{1,0:T(8,128)S(1)} %all_gather.16), channel_id=1, source_target_pairs={{0,8},{8,16},{16,24},{1,9},{9,17},{17,25},{2,10},{10,18},{18,26},{... | collective-permute-start | bytes 147464 | tf_op jit(solution)/shard_map/ppermute | solution.py:33
  298.5 7.2 %fusion.96 = f32[8,1,192,1]{2,1,3,0:T(1,128)S(1)} fusion(f32[8,4,192,1]{2,3,1,0:T(1,128)S(1)} %reshape.327, f32[8,4,192,192]{3,2,1,0:T(8,128)} %param.23), kind=kOutput, calls=%fused_computation.173 | convolution fusion | flops 14155776 | bytes 4749312 | tf_op jit(solution)/shard_map/bnij,bnj->bi/dot_general | solution.py:202
  307.1 14.2 %all_gather.17 = f32[64,192]{1,0:T(8,128)S(1)} all-gather(f32[8,192]{1,0:T(8,128)S(1)} %fusion.69), channel_id=1, replica_groups=mesh['slab'=4,'rad'=8] {'rad'}, dimensions={0}, use_global_device_ids=true | all-gather | bytes 55296 | tf_op jit(solution)/shard_map/all_gather | solution.py:199
  322.6 5.8 %collective-permute-start.6 = (f32[64,192]{1,0:T(8,128)S(1)}, f32[64,192]{1,0:T(8,128)S(1)}, u32[]{:S(2)}, u32[]{:S(2)}) collective-permute-start(f32[64,192]{1,0:T(8,128)S(1)} %all_gather.17), channel_id=1, source_target_pairs={{0,8},{8,16},{16,24},{1,9},{9,17},{17,25},{2,10},{10,18},{18,26},{... | collective-permute-start | bytes 147464 | tf_op jit(solution)/shard_map/ppermute | solution.py:33
  330.6 7.2 %fusion.97 = f32[8,1,192,1]{2,1,3,0:T(1,128)S(1)} fusion(f32[8,4,192,1]{2,3,1,0:T(1,128)S(1)} %reshape.329, f32[8,4,192,192]{3,2,1,0:T(8,128)} %param.23), kind=kOutput, calls=%fused_computation.174 | convolution fusion | flops 14155776 | bytes 4749312 | tf_op jit(solution)/shard_map/bnij,bnj->bi/dot_general | solution.py:202
  339.2 14.0 %all_gather.18 = f32[64,192]{1,0:T(8,128)S(1)} all-gather(f32[8,192]{1,0:T(8,128)S(1)} %fusion.67), channel_id=1, replica_groups=mesh['slab'=4,'rad'=8] {'rad'}, dimensions={0}, use_global_device_ids=true | all-gather | bytes 55296 | tf_op jit(solution)/shard_map/all_gather | solution.py:199
  354.4 5.8 %collective-permute-start.8 = (f32[64,192]{1,0:T(8,128)S(1)}, f32[64,192]{1,0:T(8,128)S(1)}, u32[]{:S(2)}, u32[]{:S(2)}) collective-permute-start(f32[64,192]{1,0:T(8,128)S(1)} %all_gather.18), channel_id=1, source_target_pairs={{0,8},{8,16},{16,24},{1,9},{9,17},{17,25},{2,10},{10,18},{18,26},{... | collective-permute-start | bytes 147464 | tf_op jit(solution)/shard_map/ppermute | solution.py:33
  362.4 7.2 %fusion.98 = f32[8,1,192,1]{2,1,3,0:T(1,128)S(1)} fusion(f32[8,4,192,1]{2,3,1,0:T(1,128)S(1)} %reshape.331, f32[8,4,192,192]{3,2,1,0:T(8,128)} %param.23), kind=kOutput, calls=%fused_computation.175 | convolution fusion | flops 14155776 | bytes 4749312 | tf_op jit(solution)/shard_map/bnij,bnj->bi/dot_general | solution.py:202
  371.0 14.0 %all_gather.19 = f32[64,192]{1,0:T(8,128)S(1)} all-gather(f32[8,192]{1,0:T(8,128)S(1)} %fusion.65), channel_id=1, replica_groups=mesh['slab'=4,'rad'=8] {'rad'}, dimensions={0}, use_global_device_ids=true | all-gather | bytes 55296 | tf_op jit(solution)/shard_map/all_gather | solution.py:199
  386.3 5.8 %collective-permute-start.10 = (f32[64,192]{1,0:T(8,128)S(1)}, f32[64,192]{1,0:T(8,128)S(1)}, u32[]{:S(2)}, u32[]{:S(2)}) collective-permute-start(f32[64,192]{1,0:T(8,128)S(1)} %all_gather.19), channel_id=1, source_target_pairs={{0,8},{8,16},{16,24},{1,9},{9,17},{17,25},{2,10},{10,18},{18,26},{... | collective-permute-start | bytes 147464 | tf_op jit(solution)/shard_map/ppermute | solution.py:33
  394.3 7.2 %fusion.99 = f32[8,1,192,1]{2,1,3,0:T(1,128)S(1)} fusion(f32[8,4,192,1]{2,3,1,0:T(1,128)S(1)} %reshape.333, f32[8,4,192,192]{3,2,1,0:T(8,128)} %param.23), kind=kOutput, calls=%fused_computation.176 | convolution fusion | flops 14155776 | bytes 4749312 | tf_op jit(solution)/shard_map/bnij,bnj->bi/dot_general | solution.py:202
  (326 shorter events, 200.7 us)
Async XLA Ops:
  7.2 237.0 %copy-start = (f32[8,192,192]{2,1,0:T(8,128)S(1)}, f32[8,192,192]{2,1,0:T(8,128)}, u32[]{:S(2)}) copy-start(f32[8,192,192]{2,1,0:T(8,128)} %param.25) | copy-start | bytes 3538948
  7.2 235.6 %reduce-scatter.4.cloned.1.call-start = ((), (), s32[]{:S(2)}) async-start(), calls=%async_computation.1 | async-start | bytes 1769472
  11.5 26.7 %copy-start.4 = (s32[16384]{0:T(1024)S(1)}, s32[16384]{0:T(1024)}, u32[]{:S(2)}) copy-start(s32[16384]{0:T(1024)} %param.20) | copy-start | bytes 196612
  11.5 26.7 %copy-start.1 = (f32[3,16384]{1,0:T(4,128)S(1)}, f32[3,16384]{1,0:T(4,128)}, u32[]{:S(2)}) copy-start(f32[3,16384]{1,0:T(4,128)} %param.16) | copy-start | bytes 589828
  11.5 27.1 %copy-start.5 = (f32[3,16384]{1,0:T(4,128)S(1)}, f32[3,16384]{1,0:T(4,128)}, u32[]{:S(2)}) copy-start(f32[3,16384]{1,0:T(4,128)} %param.17) | copy-start | bytes 589828
  39.0 0.7 copy-start.2
  39.7 101.0 %copy-start.3 = (s32[16384]{0:T(1024)S(1)}, s32[16384]{0:T(1024)}, u32[]{:S(2)}) copy-start(s32[16384]{0:T(1024)} %param.19) | copy-start | bytes 196612
  131.9 7.1 %collective-permute-start.1 = (f32[8,1024]{1,0:T(8,128)S(1)}, f32[8,1024]{1,0:T(8,128)S(1)}, u32[]{:S(2)}, u32[]{:S(2)}) collective-permute-start(f32[8,1024]{1,0:T(8,128)S(1)} %bitcast.238), channel_id=1, source_target_pairs={{8,0},{16,8},{24,16},{9,1},{17,9},{25,17},{10,2},{18,10},{26,18},{... | collective-permute-start | bytes 98312 | tf_op jit(solution)/shard_map/ppermute | solution.py:22
  133.3 7.1 %collective-permute-start = (f32[8,1024]{1,0:T(8,128)S(1)}, f32[8,1024]{1,0:T(8,128)S(1)}, u32[]{:S(2)}, u32[]{:S(2)}) collective-permute-start(f32[8,1024]{1,0:T(8,128)S(1)} %bitcast.239), channel_id=1, source_target_pairs={{0,8},{8,16},{16,24},{1,9},{9,17},{17,25},{2,10},{10,18},{18,26},{... | collective-permute-start | bytes 98312 | tf_op jit(solution)/shard_map/ppermute | solution.py:22
  140.7 103.1 %copy-start.8 = (f32[384]{0:T(512)S(1)}, f32[384]{0:T(512)}, u32[]{:S(2)}) copy-start(f32[384]{0:T(512)} %param.21) | copy-start | bytes 4612
  140.7 103.3 %copy-start.6 = (f32[192,192]{1,0:T(8,128)S(1)}, f32[192,192]{1,0:T(8,128)}, u32[]{:S(2)}) copy-start(f32[192,192]{1,0:T(8,128)} %param.22) | copy-start | bytes 442372
  140.7 124.7 %copy-start.9 = (s32[8,4]{0,1:T(4,128)S(1)}, s32[8,4]{0,1:T(4,128)}, u32[]{:S(2)}) copy-start(s32[8,4]{0,1:T(4,128)} %param.24) | copy-start | bytes 388
  243.8 61.9 %copy-start.7 = (f32[4,384]{1,0:T(4,128)}, f32[4,384]{1,0:T(4,128)S(1)}, u32[]{:S(2)}) copy-start(f32[4,384]{1,0:T(4,128)S(1)} %broadcast_divide_fusion) | copy-start | bytes 18436
  259.6 6.2 %collective-permute-start.3 = (f32[64,192]{1,0:T(8,128)S(1)}, f32[64,192]{1,0:T(8,128)S(1)}, u32[]{:S(2)}, u32[]{:S(2)}) collective-permute-start(f32[64,192]{1,0:T(8,128)S(1)} %all_gather.15), channel_id=1, source_target_pairs={{8,0},{16,8},{24,16},{9,1},{17,9},{25,17},{10,2},{18,10},{26,18},{... | collective-permute-start | bytes 147464 | tf_op jit(solution)/shard_map/ppermute | solution.py:35
  260.9 6.4 %collective-permute-start.2 = (f32[64,192]{1,0:T(8,128)S(1)}, f32[64,192]{1,0:T(8,128)S(1)}, u32[]{:S(2)}, u32[]{:S(2)}) collective-permute-start(f32[64,192]{1,0:T(8,128)S(1)} %all_gather.15), channel_id=1, source_target_pairs={{0,8},{8,16},{16,24},{1,9},{9,17},{17,25},{2,10},{10,18},{18,26},{... | collective-permute-start | bytes 147464 | tf_op jit(solution)/shard_map/ppermute | solution.py:33
  290.1 6.8 %collective-permute-start.5 = (f32[64,192]{1,0:T(8,128)S(1)}, f32[64,192]{1,0:T(8,128)S(1)}, u32[]{:S(2)}, u32[]{:S(2)}) collective-permute-start(f32[64,192]{1,0:T(8,128)S(1)} %all_gather.16), channel_id=1, source_target_pairs={{8,0},{16,8},{24,16},{9,1},{17,9},{25,17},{10,2},{18,10},{26,18},{... | collective-permute-start | bytes 147464 | tf_op jit(solution)/shard_map/ppermute | solution.py:35
  291.4 6.8 %collective-permute-start.4 = (f32[64,192]{1,0:T(8,128)S(1)}, f32[64,192]{1,0:T(8,128)S(1)}, u32[]{:S(2)}, u32[]{:S(2)}) collective-permute-start(f32[64,192]{1,0:T(8,128)S(1)} %all_gather.16), channel_id=1, source_target_pairs={{0,8},{8,16},{16,24},{1,9},{9,17},{17,25},{2,10},{10,18},{18,26},{... | collective-permute-start | bytes 147464 | tf_op jit(solution)/shard_map/ppermute | solution.py:33
  321.3 7.7 %collective-permute-start.7 = (f32[64,192]{1,0:T(8,128)S(1)}, f32[64,192]{1,0:T(8,128)S(1)}, u32[]{:S(2)}, u32[]{:S(2)}) collective-permute-start(f32[64,192]{1,0:T(8,128)S(1)} %all_gather.17), channel_id=1, source_target_pairs={{8,0},{16,8},{24,16},{9,1},{17,9},{25,17},{10,2},{18,10},{26,18},{... | collective-permute-start | bytes 147464 | tf_op jit(solution)/shard_map/ppermute | solution.py:35
  322.6 7.7 %collective-permute-start.6 = (f32[64,192]{1,0:T(8,128)S(1)}, f32[64,192]{1,0:T(8,128)S(1)}, u32[]{:S(2)}, u32[]{:S(2)}) collective-permute-start(f32[64,192]{1,0:T(8,128)S(1)} %all_gather.17), channel_id=1, source_target_pairs={{0,8},{8,16},{16,24},{1,9},{9,17},{17,25},{2,10},{10,18},{18,26},{... | collective-permute-start | bytes 147464 | tf_op jit(solution)/shard_map/ppermute | solution.py:33
  353.1 7.8 %collective-permute-start.9 = (f32[64,192]{1,0:T(8,128)S(1)}, f32[64,192]{1,0:T(8,128)S(1)}, u32[]{:S(2)}, u32[]{:S(2)}) collective-permute-start(f32[64,192]{1,0:T(8,128)S(1)} %all_gather.18), channel_id=1, source_target_pairs={{8,0},{16,8},{24,16},{9,1},{17,9},{25,17},{10,2},{18,10},{26,18},{... | collective-permute-start | bytes 147464 | tf_op jit(solution)/shard_map/ppermute | solution.py:35
  354.4 7.7 %collective-permute-start.8 = (f32[64,192]{1,0:T(8,128)S(1)}, f32[64,192]{1,0:T(8,128)S(1)}, u32[]{:S(2)}, u32[]{:S(2)}) collective-permute-start(f32[64,192]{1,0:T(8,128)S(1)} %all_gather.18), channel_id=1, source_target_pairs={{0,8},{8,16},{16,24},{1,9},{9,17},{17,25},{2,10},{10,18},{18,26},{... | collective-permute-start | bytes 147464 | tf_op jit(solution)/shard_map/ppermute | solution.py:33
  385.0 7.8 %collective-permute-start.11 = (f32[64,192]{1,0:T(8,128)S(1)}, f32[64,192]{1,0:T(8,128)S(1)}, u32[]{:S(2)}, u32[]{:S(2)}) collective-permute-start(f32[64,192]{1,0:T(8,128)S(1)} %all_gather.19), channel_id=1, source_target_pairs={{8,0},{16,8},{24,16},{9,1},{17,9},{25,17},{10,2},{18,10},{26,18},{... | collective-permute-start | bytes 147464 | tf_op jit(solution)/shard_map/ppermute | solution.py:35
  386.3 7.7 %collective-permute-start.10 = (f32[64,192]{1,0:T(8,128)S(1)}, f32[64,192]{1,0:T(8,128)S(1)}, u32[]{:S(2)}, u32[]{:S(2)}) collective-permute-start(f32[64,192]{1,0:T(8,128)S(1)} %all_gather.19), channel_id=1, source_target_pairs={{0,8},{8,16},{16,24},{1,9},{9,17},{17,25},{2,10},{10,18},{18,26},{... | collective-permute-start | bytes 147464 | tf_op jit(solution)/shard_map/ppermute | solution.py:33
Sparse Core Ops, SparseCore 0:
  205.3 37.4 reduce-scatter.3
where the time goes:
time: 418 us; the launch traced here: 411 us
  matrix products  170 us (41%)
  blocking collectives  70.2 us (17%)
  other arithmetic  58 us (14%)
  waiting for transfers between devices  47.5 us (11%)
  starting transfers between devices  40.1 us (10%)
  between operations  15.1 us (4%)
  local copies, waits for them, and re-layouts  7.52 us (2%)
    dot_general x25, matrix products, spread_block(): lax.dot_general(spread, hot_upper, (((1,), (1,)), ((), ())), precision=hi...  100 us
    all_gather x5, blocking collectives, body(): gathered = lax.all_gather(velocity, 'rad', axis=0, tiled=True)  70.2 us
    mul x25, other arithmetic, spread_block(): spread = (values[:, None, :] * hot_lower[None]).reshape(rows * 128, size)  39.8 us
    unnamed x2, waiting for transfers between devices  37.7 us
    dot_general x5, matrix products, body(): image = jnp.einsum('bnij,bnj->bi', stiffness, neighbours, precision=highest)  35.9 us
    ppermute x5, starting transfers between devices, extended(): lax.ppermute(tail, axis, [(i, (i + 1) % count) for i in range(ends)])  26.9 us
    dot_general x8, matrix products, one_block(): jnp.dot(arranged, hot_upper, precision=highest).reshape(rows, 128, size)  18.2 us
  transfers between devices with their start and end apart: 13, of which 11 were waited for; matrix products, arithmetic and copies ran while one was open for 0% of the time, Pallas kernels for 0%

commit v1 on v0

v1 whole, which is shorter than its diff:
```python
import functools

import jax
import jax.numpy as jnp
from jax import lax
from jax.experimental import pallas as pl
from jax.experimental.pallas import tpu as pltpu
from jax.sharding import PartitionSpec as P

BLOCK = 192
ITERS = 6
CHUNK = 512

extensibility = 50.0
time_step = 0.01
noise_scale = 0.1
damping = 0.6
highest = lax.Precision.HIGHEST
nt_dims = (((1,), (1,)), ((), ()))


def round_up(value, step):
    return -(-value // step) * step


def bf16_pieces(x):
    hi = x.astype(jnp.bfloat16)
    rest = x - hi.astype(jnp.float32)
    mid = rest.astype(jnp.bfloat16)
    lo = (rest - mid.astype(jnp.float32)).astype(jnp.bfloat16)
    return (hi, mid, lo)


def spring_terms(q):
    radial = q[0:1]
    axial = q[1:2]
    azimuth = q[2:3]
    stretch = radial * radial + axial * axial + azimuth * azimuth
    spring = 1.0 / (1.0 - stretch / extensibility)
    terms = (
        spring * radial * radial - 1.0,
        spring * axial * axial - 1.0,
        spring * radial * axial,
        spring * azimuth * azimuth - 1.0,
    )
    return spring, terms


def stress_kernel(q_ref, e_ref, m_ref, out_ref, *, groups, rows):
    count = q_ref.shape[1]
    out_ref[...] = jnp.zeros_like(out_ref)
    low_iota = lax.broadcasted_iota(jnp.int32, (128, CHUNK), 0)
    row_iota = lax.broadcasted_iota(jnp.int32, (rows, CHUNK), 0)
    zero = jnp.zeros((), jnp.bfloat16)

    def body(step, carry):
        cols = pl.ds(pl.multiple_of(step * CHUNK, CHUNK), CHUNK)
        q = q_ref[:, cols]
        element = e_ref[:, cols]
        move = m_ref[:, cols]
        spring, terms = spring_terms(q)
        kind = jnp.where(move == 0, 1, jnp.where(move == 1, 2, 0))
        key = kind * groups + (element >> 7)
        low = (low_iota == (element & 127)).astype(jnp.bfloat16)
        mask = row_iota == key
        pieces = [bf16_pieces(term) for term in terms]
        for p in range(3):
            spread = jnp.concatenate(
                [jnp.where(mask, pieces[c][p], zero) for c in range(4)], axis=0
            )
            out_ref[p] += lax.dot_general(
                spread, low, nt_dims, preferred_element_type=jnp.float32
            )
        return carry

    lax.fori_loop(0, count // CHUNK, body, 0)


def update_kernel(
    q_ref, inc_ref, e_ref, m_ref, tab_ref, qn_ref, up_ref, dn_ref, tri_ref, *, groups16, slots16
):
    count = q_ref.shape[1]
    up_ref[...] = jnp.zeros_like(up_ref)
    dn_ref[...] = jnp.zeros_like(dn_ref)
    before = lax.broadcasted_iota(jnp.int32, (CHUNK, CHUNK), 0)
    after = lax.broadcasted_iota(jnp.int32, (CHUNK, CHUNK), 1)
    tri_ref[...] = (before < after).astype(jnp.bfloat16)
    low_iota = lax.broadcasted_iota(jnp.int32, (128, CHUNK), 0)
    group_iota = lax.broadcasted_iota(jnp.int32, (groups16, CHUNK), 0)
    slot_iota = lax.broadcasted_iota(jnp.int32, (slots16, CHUNK), 0)
    flag_row = lax.broadcasted_iota(jnp.int32, (8, CHUNK), 0)
    zero = jnp.zeros((), jnp.bfloat16)

    def body(step, offsets):
        cols = pl.ds(pl.multiple_of(step * CHUNK, CHUNK), CHUNK)
        q = q_ref[:, cols]
        inc = inc_ref[:, cols]
        element = e_ref[:, cols]
        move = m_ref[:, cols]
        low = (low_iota == (element & 127)).astype(jnp.bfloat16)
        picked = jnp.dot(tab_ref[0], low, preferred_element_type=jnp.float32)
        picked = picked + jnp.dot(tab_ref[1], low, preferred_element_type=jnp.float32)
        picked = picked + jnp.dot(tab_ref[2], low, preferred_element_type=jnp.float32)
        hit = group_iota == (element >> 7)
        grads = [
            jnp.sum(
                jnp.where(hit, picked[c * groups16 : (c + 1) * groups16], 0.0),
                axis=0,
                keepdims=True,
            )
            for c in range(5)
        ]
        radial = q[0:1]
        axial = q[1:2]
        azimuth = q[2:3]
        spring, terms = spring_terms(q)
        drift = (
            grads[0] * radial + grads[1] * axial,
            grads[2] * radial + grads[3] * axial,
            grads[4] * azimuth,
        )
        q_next = [
            q[k : k + 1] + time_step * (drift[k] - 0.5 * spring * q[k : k + 1]) + noise_scale * inc[k : k + 1]
            for k in range(3)
        ]
        qn_ref[:, cols] = jnp.concatenate(q_next, axis=0)
        going_up = move == 1
        going_down = move == -1
        flags = jnp.where(
            flag_row == 0,
            going_up.astype(jnp.float32),
            jnp.where(flag_row == 1, going_down.astype(jnp.float32), 0.0),
        )
        ranks = jnp.dot(flags.astype(jnp.bfloat16), tri_ref[...], preferred_element_type=jnp.float32)
        slots = (ranks + offsets).astype(jnp.int32)
        pieces = [bf16_pieces(value) for value in q_next]
        for direction, chosen, out_ref in ((0, going_up, up_ref), (1, going_down, dn_ref)):
            slot = slots[direction : direction + 1]
            place = ((low_iota == (slot & 127)) & chosen).astype(jnp.bfloat16)
            which = slot_iota == (slot >> 7)
            for p in range(3):
                spread = jnp.concatenate(
                    [jnp.where(which, pieces[k][p], zero) for k in range(3)], axis=0
                )
                out_ref[p] += lax.dot_general(
                    spread, place, nt_dims, preferred_element_type=jnp.float32
                )
        return offsets + jnp.sum(flags, axis=1, keepdims=True)

    lax.fori_loop(0, count // CHUNK, body, jnp.zeros((8, 1), jnp.float32))


def stress_partials(q_state, element, migration, slab_elems):
    groups = slab_elems // 128
    rows = round_up(3 * groups, 16)
    count = q_state.shape[1]
    out = pl.pallas_call(
        functools.partial(stress_kernel, groups=groups, rows=rows),
        out_shape=jax.ShapeDtypeStruct((3, 4 * rows, 128), jnp.float32),
        cost_estimate=pl.CostEstimate(
            flops=2 * 3 * 4 * rows * 128 * count, transcendentals=0, bytes_accessed=20 * count
        ),
    )(q_state, element.reshape(1, -1), migration.reshape(1, -1))
    total = out[0] + out[1] + out[2]
    total = total.reshape(4, rows, 128)[:, : 3 * groups].reshape(4, 3 * slab_elems)
    return total


def update_and_pack(q_state, increments, element, migration, table, capacity):
    rows, slab_elems = table.shape
    groups = slab_elems // 128
    groups16 = round_up(groups, 16)
    slots = capacity // 128
    slots16 = round_up(slots, 16)
    arranged = jnp.pad(table.reshape(rows, groups, 128), ((0, 0), (0, groups16 - groups), (0, 0)))
    arranged = arranged.reshape(rows * groups16, 128)
    hi = lax.reduce_precision(arranged, exponent_bits=8, mantissa_bits=7)
    rest = arranged - hi
    mid = lax.reduce_precision(rest, exponent_bits=8, mantissa_bits=7)
    lo = rest - mid
    pieces = jnp.stack([hi, mid, lo]).astype(jnp.bfloat16)
    count = q_state.shape[1]
    q_next, up, down = pl.pallas_call(
        functools.partial(update_kernel, groups16=groups16, slots16=slots16),
        out_shape=(
            jax.ShapeDtypeStruct((3, count), jnp.float32),
            jax.ShapeDtypeStruct((3, 3 * slots16, 128), jnp.float32),
            jax.ShapeDtypeStruct((3, 3 * slots16, 128), jnp.float32),
        ),
        scratch_shapes=[pltpu.VMEM((CHUNK, CHUNK), jnp.bfloat16)],
        cost_estimate=pl.CostEstimate(
            flops=2 * 3 * (5 * groups16 + 6 * slots16) * 128 * count,
            transcendentals=0,
            bytes_accessed=40 * count,
        ),
    )(q_state, increments, element.reshape(1, -1), migration.reshape(1, -1), pieces)

    def unpack(acc):
        whole = acc[0] + acc[1] + acc[2]
        return whole.reshape(3, slots16, 128)[:, :slots].reshape(3, slots * 128)

    return q_next, unpack(up), unpack(down)


def passed_along(array, axis, by):
    size = lax.axis_size(axis)
    pairs = [(i, i + by) for i in range(size) if 0 <= i + by < size]
    return lax.ppermute(array, axis, pairs)


def body(
    q_state,
    increments,
    velocity_grad,
    element,
    migration,
    volume,
    div_map,
    stiffness,
    pattern,
    preconditioner,
):
    capacity = migration.shape[0] // 16
    slab_elems = velocity_grad.shape[1]
    n_slab = lax.axis_size("slab")
    slab = lax.axis_index("slab")

    near = stress_partials(q_state, element, migration, slab_elems)
    spread = jnp.zeros((4, (n_slab + 2) * slab_elems), jnp.float32)
    spread = lax.dynamic_update_slice(spread, near, (0, slab * slab_elems))
    spread = spread[:, slab_elems : (n_slab + 1) * slab_elems]
    sums = lax.psum_scatter(spread, ("slab", "rad"), scatter_dimension=1, tiled=True)
    element_stress = sums / volume

    q_next, upward, downward = update_and_pack(
        q_state, increments, element, migration, velocity_grad, capacity
    )
    from_lower = passed_along(upward, "slab", 1)
    from_upper = passed_along(downward, "slab", -1)
    arrivals = jnp.stack([from_lower, from_upper])

    own_blocks = stiffness.shape[0]
    groups = (
        element_stress.reshape(4, own_blocks, BLOCK // 4)
        .transpose(1, 0, 2)
        .reshape(own_blocks, BLOCK)
    )
    force = jnp.dot(groups, div_map, precision=highest)

    def precondition(vector):
        return jnp.einsum("bij,bj->bi", preconditioner, vector, precision=highest)

    slab_blocks = own_blocks * lax.axis_size("rad")
    all_blocks = slab_blocks * n_slab
    where_read = (slab - 1) * slab_blocks + pattern.reshape(-1)
    selector = (
        where_read[:, None] == jnp.arange(all_blocks, dtype=jnp.int32)[None, :]
    ).astype(jnp.float32)
    velocity = damping * precondition(force)
    for sweep_index in range(1, ITERS):
        gathered = lax.all_gather(velocity, ("slab", "rad"), axis=0, tiled=True)
        neighbours = jnp.dot(selector, gathered, precision=highest).reshape(own_blocks, -1, BLOCK)
        image = jnp.einsum("bnij,bnj->bi", stiffness, neighbours, precision=highest)
        velocity = velocity + damping * precondition(force - image)
    return (q_next, arrivals, element_stress, velocity)


def solution(mesh):
    placed = (
        P(None, ("slab", "rad")),
        P(None, ("slab", "rad")),
        P(None, "slab"),
        P(("slab", "rad")),
        P(("slab", "rad")),
        P(("slab", "rad")),
        P(),
        P(("slab", "rad"), None, None, None),
        P(("slab", "rad"), None),
        P(("slab", "rad"), None, None),
    )
    return jax.shard_map(
        body,
        mesh=mesh,
        in_specs=placed,
        out_specs=(
            P(None, ("slab", "rad")),
            P(None, None, ("slab", "rad")),
            P(None, ("slab", "rad")),
            P(("slab", "rad"), None),
        ),
        check_vma=False,
    )
```

time: 418 us -> 395 us (0.945); the launches traced: 411 us -> 395 us
  matrix products: 170 us -> 45.4 us
  blocking collectives: 70.2 us -> 194 us
  other arithmetic: 58 us -> 3.4 us
  Pallas kernels: 0 us -> 40.9 us
  waiting for transfers between devices: 47.5 us -> 83.1 us
  starting transfers between devices: 40.1 us -> 6.18 us
    dot_general x46 -> x5, matrix products: 126 us -> 1.16 us  [body(): jnp.dot(selector, gathered, precision=highest)]
    all_gather x5, blocking collectives: 70.2 us -> 194 us  [body(): gathered = lax.all_gather(velocity, ('slab', 'rad'), axis=0, tiled=True)]
    unnamed x2, waiting for transfers between devices: 37.7 us -> 78.9 us
    pallas_call x0 -> x2, Pallas kernels: none -> 40.9 us  [the longest x1 24.9 us: update_and_pack(): pl.pallas_call(functools.partial(update_kernel, groups16=groups16, slots1...]
    mul x26 -> x0, other arithmetic: 40.2 us -> none  [the longest x25 39.8 us: spread_block(): spread = (values[:, None, :] * hot_lower[None]).reshape(rows * 128, size)]
    ppermute x10 -> x0, starting transfers between devices: 33.3 us -> none  [the longest x5 26.9 us: extended(): lax.ppermute(tail, axis, [(i, (i + 1) % count) for i in range(ends)])]
    ppermute x10 -> x0, waiting for transfers between devices: 8.58 us -> none  [the longest x5 6.51 us: extended(): lax.ppermute(tail, axis, [(i, (i + 1) % count) for i in range(ends)])]
    reduce_sum x16 -> x0, other arithmetic: 7.2 us -> none  [the longest x8 6.08 us: one_block(): return jnp.sum(picked * hot_lower[None], 1)]
  transfers between devices with their start and end apart: 13 -> 3, of which waited for: 11 -> 2; matrix products, arithmetic and copies ran while one was open for 0% -> 1% of each run, Pallas kernels for 0% -> 6%
where the time goes in v1:
time: 395 us
  blocking collectives  194 us (49%)
  waiting for transfers between devices  83.1 us (21%)
  matrix products  45.4 us (11%)
  Pallas kernels  40.9 us (10%)
  between operations  14.3 us (4%)
  local copies, waits for them, and re-layouts  7.18 us (2%)
  starting transfers between devices  6.18 us (2%)
    all_gather x5, blocking collectives, body(): gathered = lax.all_gather(velocity, ('slab', 'rad'), axis=0, tiled=True)  194 us
    unnamed x2, waiting for transfers between devices  78.9 us
    dot_general x5, matrix products, body(): image = jnp.einsum('bnij,bnj->bi', stiffness, neighbours, precision=highest)  35.9 us
    pallas_call x1, Pallas kernels, update_and_pack(): pl.pallas_call(functools.partial(update_kernel, groups16=groups16, slots1...  24.9 us
    pallas_call x1, Pallas kernels, stress_partials(): pl.pallas_call(functools.partial(stress_kernel, groups=groups, rows=rows)...  15.9 us
    dot_general x6, matrix products, precondition(): return jnp.einsum('bij,bj->bi', preconditioner, vector, precision=highest)  8.17 us
  transfers between devices with their start and end apart: 3, of which 2 were waited for; matrix products, arithmetic and copies ran while one was open for 1% of the time, Pallas kernels for 6%

profile of v1, /device:TPU:0, one launch (start us, length us, event | category | flops | bytes accessed | tf_op | source)
XLA Modules:
  0.0 394.9 jit_solution(16446476994175870893)
XLA Ops:
  7.2 15.9 %shard_map.130 = f32[3,320,128]{2,1,0:T(8,128)} custom-call(f32[3,16384]{1,0:T(4,128)} %q_ref.3, s32[1,16384]{1,0:T(1,128)} %bitcast.130, s32[1,16384]{1,0:T(1,128)} %bitcast.132), custom_call_target="tpu_custom_call" | custom-call | flops 4026531840 | bytes 327680 | tf_op jit(solution)/shard_map/pallas_call | solution.py:157
  23.2 1.1 slice_add_fusion
  24.4 4.0 %copy.43 = f32[4,12288]{0,1:T(8,128)} copy(f32[4,12288]{1,0:T(4,128)S(1)} %slice.58) | data formatting | bytes 393216
  30.0 24.9 %shard_map.129 = (f32[3,16384]{1,0:T(4,128)}, f32[3,48,128]{2,1,0:T(8,128)}, f32[3,48,128]{2,1,0:T(8,128)}) custom-call(f32[3,16384]{1,0:T(4,128)} %q_ref.3, f32[3,16384]{1,0:T(4,128)} %inc_ref.1, s32[1,16384]{1,0:T(1,128)} %bitcast.131, s32[1,16384]{1,0:T(1,128)} %bitcast.133, bf16[3,160,128]{2,1,0:T(8,128)(2,1)} %pad_maximum_fusion.tab_ref), custom_call_target="tpu_custom_call" | custom-call | flops 3221225472 | bytes 655360 | tf_op jit(solution)/shard_map/pallas_call | solution.py:183
  55.8 4.9 %collective-permute-start = (f32[3,1024]{1,0:T(4,128)S(1)}, f32[3,1024]{1,0:T(4,128)S(1)}, u32[]{:S(2)}, u32[]{:S(2)}) collective-permute-start(f32[3,1024]{1,0:T(4,128)S(1)} %bitcast.126), channel_id=1, source_target_pairs={{0,8},{8,16},{16,24},{1,9},{9,17},{17,25},{2,10},{10,18},{18,26},{... | collective-permute-start | bytes 36872 | tf_op jit(solution)/shard_map/ppermute | solution.py:208
  60.7 1.3 collective-permute-start.1
  62.2 4.1 %collective-permute-done.1 = f32[3,1024]{1,0:T(4,128)S(1)} collective-permute-done((f32[3,1024]{1,0:T(4,128)S(1)}, f32[3,1024]{1,0:T(4,128)S(1)}, u32[]{:S(2)}, u32[]{:S(2)}) %collective-permute-start.1) | collective-permute-done | bytes 12320 | tf_op jit(solution)/shard_map/ppermute | solution.py:208
  67.0 78.9 %reduce-scatter.4.cloned.1.call-done = f32[384,4]{1,0:T(8,128)} async-done(((f32[12288,4]{1,0:T(8,128)}), f32[384,4]{1,0:T(8,128)}) %reduce-scatter.4.cloned.1.call-update) | async-done | bytes 6160
  147.3 1.4 fusion.31
  148.7 40.7 %all_gather.15 = f32[256,192]{1,0:T(8,128)S(1)} all-gather(f32[8,192]{1,0:T(8,128)S(1)} %bitcast_multiply_fusion.5), channel_id=1, replica_groups=mesh['slab'=4,'rad'=8] {'slab','rad'}, dimensions={0}, use_global_device_ids=true | all-gather | bytes 202752 | tf_op jit(solution)/shard_map/all_gather | solution.py:261
  189.7 7.2 %fusion.34 = f32[8,1,192,1]{2,1,3,0:T(1,128)S(1)} fusion(f32[8,4,192,1]{2,3,1,0:T(1,128)S(1)} %reshape.152, f32[8,4,192,192]{3,2,1,0:T(8,128)} %param.17), kind=kOutput, calls=%fused_computation.66 | convolution fusion | flops 14155776 | bytes 4749312 | tf_op jit(solution)/shard_map/bnij,bnj->bi/dot_general | solution.py:263
  197.0 1.4 fusion.29
  198.3 37.7 %all_gather.16 = f32[256,192]{1,0:T(8,128)S(1)} all-gather(f32[8,192]{1,0:T(8,128)S(1)} %fusion.19), channel_id=1, replica_groups=mesh['slab'=4,'rad'=8] {'slab','rad'}, dimensions={0}, use_global_device_ids=true | all-gather | bytes 202752 | tf_op jit(solution)/shard_map/all_gather | solution.py:261
  236.3 7.2 %fusion.35 = f32[8,1,192,1]{2,1,3,0:T(1,128)S(1)} fusion(f32[8,4,192,1]{2,3,1,0:T(1,128)S(1)} %reshape.154, f32[8,4,192,192]{3,2,1,0:T(8,128)} %param.17), kind=kOutput, calls=%fused_computation.67 | convolution fusion | flops 14155776 | bytes 4749312 | tf_op jit(solution)/shard_map/bnij,bnj->bi/dot_general | solution.py:263
  243.5 1.4 fusion.27
  244.9 39.2 %all_gather.17 = f32[256,192]{1,0:T(8,128)S(1)} all-gather(f32[8,192]{1,0:T(8,128)S(1)} %fusion.17), channel_id=1, replica_groups=mesh['slab'=4,'rad'=8] {'slab','rad'}, dimensions={0}, use_global_device_ids=true | all-gather | bytes 202752 | tf_op jit(solution)/shard_map/all_gather | solution.py:261
  284.4 7.2 %fusion.36 = f32[8,1,192,1]{2,1,3,0:T(1,128)S(1)} fusion(f32[8,4,192,1]{2,3,1,0:T(1,128)S(1)} %reshape.156, f32[8,4,192,192]{3,2,1,0:T(8,128)} %param.17), kind=kOutput, calls=%fused_computation.68 | convolution fusion | flops 14155776 | bytes 4749312 | tf_op jit(solution)/shard_map/bnij,bnj->bi/dot_general | solution.py:263
  291.6 1.4 fusion.25
  293.0 37.7 %all_gather.18 = f32[256,192]{1,0:T(8,128)S(1)} all-gather(f32[8,192]{1,0:T(8,128)S(1)} %fusion.15), channel_id=1, replica_groups=mesh['slab'=4,'rad'=8] {'slab','rad'}, dimensions={0}, use_global_device_ids=true | all-gather | bytes 202752 | tf_op jit(solution)/shard_map/all_gather | solution.py:261
  330.9 7.2 %fusion.37 = f32[8,1,192,1]{2,1,3,0:T(1,128)S(1)} fusion(f32[8,4,192,1]{2,3,1,0:T(1,128)S(1)} %reshape.158, f32[8,4,192,192]{3,2,1,0:T(8,128)} %param.17), kind=kOutput, calls=%fused_computation.69 | convolution fusion | flops 14155776 | bytes 4749312 | tf_op jit(solution)/shard_map/bnij,bnj->bi/dot_general | solution.py:263
  338.1 1.4 fusion.23
  339.5 39.0 %all_gather.19 = f32[256,192]{1,0:T(8,128)S(1)} all-gather(f32[8,192]{1,0:T(8,128)S(1)} %fusion.13), channel_id=1, replica_groups=mesh['slab'=4,'rad'=8] {'slab','rad'}, dimensions={0}, use_global_device_ids=true | all-gather | bytes 202752 | tf_op jit(solution)/shard_map/all_gather | solution.py:261
  378.8 7.2 %fusion.38 = f32[8,1,192,1]{2,1,3,0:T(1,128)S(1)} fusion(f32[8,4,192,1]{2,3,1,0:T(1,128)S(1)} %reshape.160, f32[8,4,192,192]{3,2,1,0:T(8,128)} %param.17), kind=kOutput, calls=%fused_computation.70 | convolution fusion | flops 14155776 | bytes 4749312 | tf_op jit(solution)/shard_map/bnij,bnj->bi/dot_general | solution.py:263
  386.0 1.4 fusion.21
  (60 shorter events, 6.9 us)
Async XLA Ops:
  7.2 140.2 %copy-start = (f32[8,192,192]{2,1,0:T(8,128)S(1)}, f32[8,192,192]{2,1,0:T(8,128)}, u32[]{:S(2)}) copy-start(f32[8,192,192]{2,1,0:T(8,128)} %param.19) | copy-start | bytes 3538948
  7.2 138.7 %reduce-scatter.4.cloned.1.call-start = ((), (), s32[]{:S(2)}) async-start(), calls=%async_computation.1 | async-start | bytes 6488064
  28.4 0.9 copy-start.2
  30.0 32.0 %copy-start.5 = (s32[8,4]{0,1:T(4,128)S(1)}, s32[8,4]{0,1:T(4,128)}, u32[]{:S(2)}) copy-start(s32[8,4]{0,1:T(4,128)} %param.18) | copy-start | bytes 388
  30.0 116.9 %copy-start.4 = (f32[384]{0:T(512)S(1)}, f32[384]{0:T(512)}, u32[]{:S(2)}) copy-start(f32[384]{0:T(512)} %param.15) | copy-start | bytes 4612
  30.0 117.1 %copy-start.1 = (f32[192,192]{1,0:T(8,128)S(1)}, f32[192,192]{1,0:T(8,128)}, u32[]{:S(2)}) copy-start(f32[192,192]{1,0:T(8,128)} %param.16) | copy-start | bytes 442372
  55.8 6.4 %collective-permute-start = (f32[3,1024]{1,0:T(4,128)S(1)}, f32[3,1024]{1,0:T(4,128)S(1)}, u32[]{:S(2)}, u32[]{:S(2)}) collective-permute-start(f32[3,1024]{1,0:T(4,128)S(1)} %bitcast.126), channel_id=1, source_target_pairs={{0,8},{8,16},{16,24},{1,9},{9,17},{17,25},{2,10},{10,18},{18,26},{... | collective-permute-start | bytes 36872 | tf_op jit(solution)/shard_map/ppermute | solution.py:208
  60.7 5.6 %collective-permute-start.1 = (f32[3,1024]{1,0:T(4,128)S(1)}, f32[3,1024]{1,0:T(4,128)S(1)}, u32[]{:S(2)}, u32[]{:S(2)}) collective-permute-start(f32[3,1024]{1,0:T(4,128)S(1)} %bitcast.127), channel_id=1, source_target_pairs={{8,0},{16,8},{24,16},{9,1},{17,9},{25,17},{10,2},{18,10},{26,18},{... | collective-permute-start | bytes 36872 | tf_op jit(solution)/shard_map/ppermute | solution.py:208
  147.0 50.0 %copy-start.3 = (f32[4,384]{1,0:T(4,128)}, f32[4,384]{1,0:T(4,128)S(1)}, u32[]{:S(2)}) copy-start(f32[4,384]{1,0:T(4,128)S(1)} %broadcast_divide_fusion) | copy-start | bytes 18436
Sparse Core Ops, SparseCore 0:
  28.5 117.3 reduce-scatter.3

commit v2 on v1

--- a/solution.py
+++ b/solution.py
@@ -225,11 +225,14 @@
     n_slab = lax.axis_size("slab")
     slab = lax.axis_index("slab")
 
+    n_rad = lax.axis_size("rad")
     near = stress_partials(q_state, element, migration, slab_elems)
-    spread = jnp.zeros((4, (n_slab + 2) * slab_elems), jnp.float32)
-    spread = lax.dynamic_update_slice(spread, near, (0, slab * slab_elems))
-    spread = spread[:, slab_elems : (n_slab + 1) * slab_elems]
-    sums = lax.psum_scatter(spread, ("slab", "rad"), scatter_dimension=1, tiled=True)
+    near = near.reshape(4, 3, n_rad, slab_elems // n_rad).transpose(1, 2, 0, 3)
+    spread = jnp.zeros((n_slab + 2,) + near.shape[1:], jnp.float32)
+    spread = lax.dynamic_update_slice(spread, near, (slab, 0, 0, 0))
+    spread = spread[1 : n_slab + 1].reshape((n_slab * n_rad,) + near.shape[2:])
+    received = lax.all_to_all(spread, ("slab", "rad"), 0, 0, tiled=True)
+    sums = jnp.sum(received, axis=0)
     element_stress = sums / volume
 
     q_next, upward, downward = update_and_pack(
@@ -258,7 +261,9 @@
     ).astype(jnp.float32)
     velocity = damping * precondition(force)
     for sweep_index in range(1, ITERS):
-        gathered = lax.all_gather(velocity, ("slab", "rad"), axis=0, tiled=True)
+        gathered = lax.all_to_all(
+            jnp.tile(velocity, (n_slab * n_rad, 1)), ("slab", "rad"), 0, 0, tiled=True
+        )
         neighbours = jnp.dot(selector, gathered, precision=highest).reshape(own_blocks, -1, BLOCK)
         image = jnp.einsum("bnij,bnj->bi", stiffness, neighbours, precision=highest)
         velocity = velocity + damping * precondition(force - image)

time: 395 us -> 169 us (0.43)
  blocking collectives: 194 us -> 0 us
  waiting for transfers between devices: 83.1 us -> 43.7 us
  starting transfers between devices: 6.18 us -> 28.6 us
  between operations: 14.3 us -> 0.95 us
    all_gather x5 -> x0, blocking collectives: 194 us -> none  [body(): gathered = lax.all_gather(velocity, ('slab', 'rad'), axis=0, tiled=True)]
    unnamed x2 -> x0, waiting for transfers between devices: 78.9 us -> none
    all_to_all x0 -> x6, waiting for transfers between devices: none -> 39.3 us  [the longest x5 30.7 us: body(): lax.all_to_all(jnp.tile(velocity, (n_slab * n_rad, 1)), ('slab', 'rad'),...]
    all_to_all x0 -> x6, starting transfers between devices: none -> 23.6 us  [the longest x5 16.3 us: body(): lax.all_to_all(jnp.tile(velocity, (n_slab * n_rad, 1)), ('slab', 'rad'),...]
    unnamed x21 -> x20, local copies, waits for them, and re-layouts: 6.56 us -> 0.69 us
  transfers between devices with their start and end apart: 3 -> 8, of which waited for: 2 -> 6; matrix products, arithmetic and copies ran while one was open for 1% -> 7% of each run, Pallas kernels for 6% -> 15%
where the time goes in v2:
time: 169 us; the launch traced here: 168 us
  matrix products  45.4 us (27%)
  waiting for transfers between devices  43.7 us (26%)
  Pallas kernels  40.8 us (24%)
  starting transfers between devices  28.6 us (17%)
  local copies, waits for them, and re-layouts  5.54 us (3%)
  other arithmetic  3.31 us (2%)
    dot_general x5, matrix products, body(): image = jnp.einsum('bnij,bnj->bi', stiffness, neighbours, precision=highest)  36 us
    all_to_all x5, waiting for transfers between devices, body(): lax.all_to_all(jnp.tile(velocity, (n_slab * n_rad, 1)), ('slab', 'rad'),...  30.7 us
    pallas_call x1, Pallas kernels, update_and_pack(): pl.pallas_call(functools.partial(update_kernel, groups16=groups16, slots1...  24.9 us
    all_to_all x5, starting transfers between devices, body(): lax.all_to_all(jnp.tile(velocity, (n_slab * n_rad, 1)), ('slab', 'rad'),...  16.3 us
    pallas_call x1, Pallas kernels, stress_partials(): pl.pallas_call(functools.partial(stress_kernel, groups=groups, rows=rows)...  15.9 us
    all_to_all x1, waiting for transfers between devices, body(): received = lax.all_to_all(spread, ('slab', 'rad'), 0, 0, tiled=True)  8.66 us
    dot_general x6, matrix products, precondition(): return jnp.einsum('bij,bj->bi', preconditioner, vector, precision=highest)  8.17 us
    all_to_all x1, starting transfers between devices, body(): received = lax.all_to_all(spread, ('slab', 'rad'), 0, 0, tiled=True)  7.29 us
  transfers between devices with their start and end apart: 8, of which 6 were waited for; matrix products, arithmetic and copies ran while one was open for 7% of the time, Pallas kernels for 15%

profile of v2, /device:TPU:0, one launch (start us, length us, event | category | flops | bytes accessed | tf_op | source)
XLA Modules:
  0.0 168.3 jit_solution(8824841276132108092)
XLA Ops:
  0.6 15.9 %shard_map.130 = f32[3,320,128]{2,1,0:T(8,128)} custom-call(f32[3,16384]{1,0:T(4,128)} %q_ref.3, s32[1,16384]{1,0:T(1,128)} %bitcast.150, s32[1,16384]{1,0:T(1,128)} %bitcast.152), custom_call_target="tpu_custom_call" | custom-call | flops 4026531840 | bytes 327680 | tf_op jit(solution)/shard_map/pallas_call | solution.py:157
  18.6 7.3 %all-to-all-start = ((f32[32,4,384]{2,1,0:T(4,128)}), f32[32,4,384]{2,1,0:T(4,128)S(1)}, u32[]{:S(2)}, u32[]{:S(2)}) async-start(f32[32,4,384]{2,1,0:T(4,128)} %bitcast.9), calls=%async_computation | async-start | bytes 393216 | tf_op jit(solution)/shard_map/all_to_all | solution.py:234
  26.0 8.7 %all-to-all-done = f32[32,4,384]{2,1,0:T(4,128)S(1)} async-done(((f32[32,4,384]{2,1,0:T(4,128)}), f32[32,4,384]{2,1,0:T(4,128)S(1)}, u32[]{:S(2)}, u32[]{:S(2)}) %all-to-all-start) | async-done | bytes 196640 | tf_op jit(solution)/shard_map/all_to_all | solution.py:234
  35.1 1.4 fusion.38
  37.2 2.7 %all-to-all-start.1 = ((f32[32,8,192]{2,1,0:T(8,128)}), f32[32,8,192]{2,1,0:T(8,128)S(1)}, u32[]{:S(2)}, u32[]{:S(2)}) async-start(f32[32,8,192]{2,1,0:T(8,128)} %tile.10), calls=%async_computation.1 | async-start | bytes 524288 | tf_op jit(solution)/shard_map/all_to_all | solution.py:264
  40.0 10.3 %all-to-all-done.1 = f32[32,8,192]{2,1,0:T(8,128)S(1)} async-done(((f32[32,8,192]{2,1,0:T(8,128)}), f32[32,8,192]{2,1,0:T(8,128)S(1)}, u32[]{:S(2)}, u32[]{:S(2)}) %all-to-all-start.1) | async-done | bytes 196640 | tf_op jit(solution)/shard_map/all_to_all | solution.py:264
  50.5 7.2 %fusion.14 = f32[8,1,192,1]{2,1,3,0:T(1,128)S(1)} fusion(f32[8,4,192,192]{3,2,1,0:T(8,128)} %param.17, f32[8,4,192,1]{2,1,0,3:T(4,128)S(1)} %convolution_bitcast_fusion.4), kind=kOutput, calls=%fused_computation.29 | convolution fusion | flops 14155776 | bytes 4749312 | tf_op jit(solution)/shard_map/bnij,bnj->bi/dot_general | solution.py:268
  59.9 2.6 %all-to-all-start.2 = ((f32[32,8,192]{2,1,0:T(8,128)}), f32[32,8,192]{2,1,0:T(8,128)S(1)}, u32[]{:S(2)}, u32[]{:S(2)}) async-start(f32[32,8,192]{2,1,0:T(8,128)} %tile.11), calls=%async_computation.2 | async-start | bytes 524288 | tf_op jit(solution)/shard_map/all_to_all | solution.py:264
  62.5 10.3 %all-to-all-done.2 = f32[32,8,192]{2,1,0:T(8,128)S(1)} async-done(((f32[32,8,192]{2,1,0:T(8,128)}), f32[32,8,192]{2,1,0:T(8,128)S(1)}, u32[]{:S(2)}, u32[]{:S(2)}) %all-to-all-start.2) | async-done | bytes 196640 | tf_op jit(solution)/shard_map/all_to_all | solution.py:264
  73.1 7.2 %fusion.12 = f32[8,1,192,1]{2,1,3,0:T(1,128)S(1)} fusion(f32[8,4,192,192]{3,2,1,0:T(8,128)} %param.17, f32[8,4,192,1]{2,1,0,3:T(4,128)S(1)} %convolution_bitcast_fusion.3), kind=kOutput, calls=%fused_computation.27 | convolution fusion | flops 14155776 | bytes 4749312 | tf_op jit(solution)/shard_map/bnij,bnj->bi/dot_general | solution.py:268
  80.3 1.4 fusion.34
  82.4 2.8 %all-to-all-start.3 = ((f32[32,8,192]{2,1,0:T(8,128)}), f32[32,8,192]{2,1,0:T(8,128)S(1)}, u32[]{:S(2)}, u32[]{:S(2)}) async-start(f32[32,8,192]{2,1,0:T(8,128)} %tile.12), calls=%async_computation.3 | async-start | bytes 524288 | tf_op jit(solution)/shard_map/all_to_all | solution.py:264
  85.8 24.9 %shard_map.129 = (f32[3,16384]{1,0:T(4,128)}, f32[3,48,128]{2,1,0:T(8,128)}, f32[3,48,128]{2,1,0:T(8,128)}) custom-call(f32[3,16384]{1,0:T(4,128)} %q_ref.3, f32[3,16384]{1,0:T(4,128)} %inc_ref.1, s32[1,16384]{1,0:T(1,128)} %bitcast.151, s32[1,16384]{1,0:T(1,128)} %bitcast.153, bf16[3,160,128]{2,1,0:T(8,128)(2,1)} %pad_maximum_fusion.tab_ref), custom_call_target="tpu_custom_call" | custom-call | flops 3221225472 | bytes 655360 | tf_op jit(solution)/shard_map/pallas_call | solution.py:183
  110.9 7.2 %fusion.10 = f32[8,1,192,1]{2,1,3,0:T(1,128)S(1)} fusion(f32[8,4,192,192]{3,2,1,0:T(8,128)} %param.17, f32[8,4,192,1]{2,1,0,3:T(4,128)S(1)} %convolution_bitcast_fusion.2), kind=kOutput, calls=%fused_computation.25 | convolution fusion | flops 14155776 | bytes 4749312 | tf_op jit(solution)/shard_map/bnij,bnj->bi/dot_general | solution.py:268
  120.3 5.6 %all-to-all-start.4 = ((f32[32,8,192]{2,1,0:T(8,128)}), f32[32,8,192]{2,1,0:T(8,128)S(1)}, u32[]{:S(2)}, u32[]{:S(2)}) async-start(f32[32,8,192]{2,1,0:T(8,128)} %tile.13), calls=%async_computation.4 | async-start | bytes 524288 | tf_op jit(solution)/shard_map/all_to_all | solution.py:264
  126.0 3.7 %collective-permute-start = (f32[3,1024]{1,0:T(4,128)S(1)}, f32[3,1024]{1,0:T(4,128)S(1)}, u32[]{:S(2)}, u32[]{:S(2)}) collective-permute-start(f32[3,1024]{1,0:T(4,128)S(1)} %bitcast.146), channel_id=1, source_target_pairs={{0,8},{8,16},{16,24},{1,9},{9,17},{17,25},{2,10},{10,18},{18,26},{... | collective-permute-start | bytes 36872 | tf_op jit(solution)/shard_map/ppermute | solution.py:208
  129.7 6.6 %all-to-all-done.4 = f32[32,8,192]{2,1,0:T(8,128)S(1)} async-done(((f32[32,8,192]{2,1,0:T(8,128)}), f32[32,8,192]{2,1,0:T(8,128)S(1)}, u32[]{:S(2)}, u32[]{:S(2)}) %all-to-all-start.4) | async-done | bytes 196640 | tf_op jit(solution)/shard_map/all_to_all | solution.py:264
  136.5 7.2 %fusion.8 = f32[8,1,192,1]{2,1,3,0:T(1,128)S(1)} fusion(f32[8,4,192,192]{3,2,1,0:T(8,128)} %param.17, f32[8,4,192,1]{2,1,0,3:T(4,128)S(1)} %convolution_bitcast_fusion.1), kind=kOutput, calls=%fused_computation.23 | convolution fusion | flops 14155776 | bytes 4749312 | tf_op jit(solution)/shard_map/bnij,bnj->bi/dot_general | solution.py:268
  143.8 1.4 fusion.30
  145.9 2.6 %all-to-all-start.5 = ((f32[32,8,192]{2,1,0:T(8,128)}), f32[32,8,192]{2,1,0:T(8,128)S(1)}, u32[]{:S(2)}, u32[]{:S(2)}) async-start(f32[32,8,192]{2,1,0:T(8,128)} %tile.14), calls=%async_computation.5 | async-start | bytes 524288 | tf_op jit(solution)/shard_map/all_to_all | solution.py:264
  149.8 4.4 %collective-permute-done.1 = f32[3,1024]{1,0:T(4,128)S(1)} collective-permute-done((f32[3,1024]{1,0:T(4,128)S(1)}, f32[3,1024]{1,0:T(4,128)S(1)}, u32[]{:S(2)}, u32[]{:S(2)}) %collective-permute-start.1) | collective-permute-done | bytes 12320 | tf_op jit(solution)/shard_map/ppermute | solution.py:208
  155.4 3.4 %all-to-all-done.5 = f32[32,8,192]{2,1,0:T(8,128)S(1)} async-done(((f32[32,8,192]{2,1,0:T(8,128)}), f32[32,8,192]{2,1,0:T(8,128)S(1)}, u32[]{:S(2)}, u32[]{:S(2)}) %all-to-all-start.5) | async-done | bytes 196640 | tf_op jit(solution)/shard_map/all_to_all | solution.py:264
  159.1 7.2 %fusion.6 = f32[8,1,192,1]{2,1,3,0:T(1,128)S(1)} fusion(f32[8,4,192,192]{3,2,1,0:T(8,128)} %param.17, f32[8,4,192,1]{2,1,0,3:T(4,128)S(1)} %convolution_bitcast_fusion), kind=kOutput, calls=%fused_computation.21 | convolution fusion | flops 14155776 | bytes 4749312 | tf_op jit(solution)/shard_map/bnij,bnj->bi/dot_general | solution.py:268
  166.3 1.4 fusion.28
  (66 shorter events, 14.1 us)
Async XLA Ops:
  0.6 34.4 %copy-start = (f32[8,192,192]{2,1,0:T(8,128)S(1)}, f32[8,192,192]{2,1,0:T(8,128)}, u32[]{:S(2)}) copy-start(f32[8,192,192]{2,1,0:T(8,128)} %param.19) | copy-start | bytes 3538948
  16.6 9.3 %copy-start.5 = (f32[384]{0:T(512)S(1)}, f32[384]{0:T(512)}, u32[]{:S(2)}) copy-start(f32[384]{0:T(512)} %param.15) | copy-start | bytes 4612
  16.6 18.3 %copy-start.1 = (f32[192,192]{1,0:T(8,128)S(1)}, f32[192,192]{1,0:T(8,128)}, u32[]{:S(2)}) copy-start(f32[192,192]{1,0:T(8,128)} %param.16) | copy-start | bytes 442372
  18.6 21.3 %copy-start.6 = (s32[8,4]{0,1:T(4,128)S(1)}, s32[8,4]{0,1:T(4,128)}, u32[]{:S(2)}) copy-start(s32[8,4]{0,1:T(4,128)} %param.18) | copy-start | bytes 388
  18.6 16.0 %all-to-all-start = ((f32[32,4,384]{2,1,0:T(4,128)}), f32[32,4,384]{2,1,0:T(4,128)S(1)}, u32[]{:S(2)}, u32[]{:S(2)}) async-start(f32[32,4,384]{2,1,0:T(4,128)} %bitcast.9), calls=%async_computation | async-start | bytes 393216 | tf_op jit(solution)/shard_map/all_to_all | solution.py:234
  37.2 13.1 %all-to-all-start.1 = ((f32[32,8,192]{2,1,0:T(8,128)}), f32[32,8,192]{2,1,0:T(8,128)S(1)}, u32[]{:S(2)}, u32[]{:S(2)}) async-start(f32[32,8,192]{2,1,0:T(8,128)} %tile.10), calls=%async_computation.1 | async-start | bytes 524288 | tf_op jit(solution)/shard_map/all_to_all | solution.py:264
  57.7 4.7 %copy-start.2 = (f32[5,3072]{1,0:T(8,128)S(1)}, f32[5,3072]{1,0:T(8,128)}, u32[]{:S(2)}) copy-start(f32[5,3072]{1,0:T(8,128)} %param.12) | copy-start | bytes 184324
  59.9 13.0 %all-to-all-start.2 = ((f32[32,8,192]{2,1,0:T(8,128)}), f32[32,8,192]{2,1,0:T(8,128)S(1)}, u32[]{:S(2)}, u32[]{:S(2)}) async-start(f32[32,8,192]{2,1,0:T(8,128)} %tile.11), calls=%async_computation.2 | async-start | bytes 524288 | tf_op jit(solution)/shard_map/all_to_all | solution.py:264
  82.4 28.3 %all-to-all-start.3 = ((f32[32,8,192]{2,1,0:T(8,128)}), f32[32,8,192]{2,1,0:T(8,128)S(1)}, u32[]{:S(2)}, u32[]{:S(2)}) async-start(f32[32,8,192]{2,1,0:T(8,128)} %tile.12), calls=%async_computation.3 | async-start | bytes 524288 | tf_op jit(solution)/shard_map/all_to_all | solution.py:264
  118.1 7.8 %copy-start.3 = (f32[3,48,128]{2,1,0:T(8,128)S(1)}, f32[3,48,128]{2,1,0:T(8,128)}, u32[]{:S(2)}) copy-start(f32[3,48,128]{2,1,0:T(8,128)} %get-tuple-element.8) | copy-start | bytes 221188
  118.1 7.8 %copy-start.4 = (f32[3,48,128]{2,1,0:T(8,128)S(1)}, f32[3,48,128]{2,1,0:T(8,128)}, u32[]{:S(2)}) copy-start(f32[3,48,128]{2,1,0:T(8,128)} %get-tuple-element.9) | copy-start | bytes 221188
  120.3 16.0 %all-to-all-start.4 = ((f32[32,8,192]{2,1,0:T(8,128)}), f32[32,8,192]{2,1,0:T(8,128)S(1)}, u32[]{:S(2)}, u32[]{:S(2)}) async-start(f32[32,8,192]{2,1,0:T(8,128)} %tile.13), calls=%async_computation.4 | async-start | bytes 524288 | tf_op jit(solution)/shard_map/all_to_all | solution.py:264
  126.0 23.8 %collective-permute-start = (f32[3,1024]{1,0:T(4,128)S(1)}, f32[3,1024]{1,0:T(4,128)S(1)}, u32[]{:S(2)}, u32[]{:S(2)}) collective-permute-start(f32[3,1024]{1,0:T(4,128)S(1)} %bitcast.146), channel_id=1, source_target_pairs={{0,8},{8,16},{16,24},{1,9},{9,17},{17,25},{2,10},{10,18},{18,26},{... | collective-permute-start | bytes 36872 | tf_op jit(solution)/shard_map/ppermute | solution.py:208
  145.9 13.0 %all-to-all-start.5 = ((f32[32,8,192]{2,1,0:T(8,128)}), f32[32,8,192]{2,1,0:T(8,128)S(1)}, u32[]{:S(2)}, u32[]{:S(2)}) async-start(f32[32,8,192]{2,1,0:T(8,128)} %tile.14), calls=%async_computation.5 | async-start | bytes 524288 | tf_op jit(solution)/shard_map/all_to_all | solution.py:264
  148.5 5.7 %collective-permute-start.1 = (f32[3,1024]{1,0:T(4,128)S(1)}, f32[3,1024]{1,0:T(4,128)S(1)}, u32[]{:S(2)}, u32[]{:S(2)}) collective-permute-start(f32[3,1024]{1,0:T(4,128)S(1)} %bitcast.147), channel_id=1, source_target_pairs={{8,0},{16,8},{24,16},{9,1},{17,9},{25,17},{10,2},{18,10},{26,18},{... | collective-permute-start | bytes 36872 | tf_op jit(solution)/shard_map/ppermute | solution.py:208

commit v3 on v2

--- a/solution.py
+++ b/solution.py
@@ -202,6 +202,49 @@
     return q_next, unpack(up), unpack(down)
 
 
+def sweep_kernel(idx_ref, g_ref, s_ref, pt_ref, ft_ref, v_ref, vout_ref, send_ref):
+    total = g_ref.shape[0]
+    own = v_ref.shape[0]
+    width = s_ref.shape[1]
+    rows = []
+    for b in range(own):
+        acc = None
+        for n in range(width):
+            w = idx_ref[b * width + n]
+            inside = jnp.logical_and(w >= 0, w < total)
+            near = g_ref[pl.ds(jnp.clip(w, 0, total - 1), 1), :]
+            near = jnp.where(inside, near, 0.0)
+            term = s_ref[b, n] * near
+            acc = term if acc is None else acc + term
+        image = jnp.sum(acc, axis=1, keepdims=True)
+        rest = ft_ref[:, b : b + 1] - image
+        update = jnp.sum(pt_ref[b] * rest, axis=0, keepdims=True)
+        rows.append(v_ref[b : b + 1, :] + damping * update)
+    fresh = jnp.concatenate(rows, axis=0)
+    vout_ref[...] = fresh
+    for k in range(send_ref.shape[0] // own):
+        send_ref[k * own : (k + 1) * own, :] = fresh
+
+
+def sweep(where_read, gathered, stiffness, transposed, force_t, velocity, copies):
+    own = velocity.shape[0]
+    vmem = pl.BlockSpec(memory_space=pltpu.VMEM)
+    return pl.pallas_call(
+        sweep_kernel,
+        out_shape=(
+            jax.ShapeDtypeStruct(velocity.shape, jnp.float32),
+            jax.ShapeDtypeStruct((copies * own, velocity.shape[1]), jnp.float32),
+        ),
+        in_specs=[pl.BlockSpec(memory_space=pltpu.SMEM)] + [vmem] * 5,
+        out_specs=(vmem, vmem),
+        cost_estimate=pl.CostEstimate(
+            flops=2 * (stiffness.size + transposed.size),
+            transcendentals=0,
+            bytes_accessed=4 * (stiffness.size + transposed.size + gathered.size),
+        ),
+    )(where_read, gathered, stiffness, transposed, force_t, velocity)
+
+
 def passed_along(array, axis, by):
     size = lax.axis_size(axis)
     pairs = [(i, i + by) for i in range(size) if 0 <= i + by < size]
@@ -253,20 +296,18 @@
     def precondition(vector):
         return jnp.einsum("bij,bj->bi", preconditioner, vector, precision=highest)
 
-    slab_blocks = own_blocks * lax.axis_size("rad")
-    all_blocks = slab_blocks * n_slab
-    where_read = (slab - 1) * slab_blocks + pattern.reshape(-1)
-    selector = (
-        where_read[:, None] == jnp.arange(all_blocks, dtype=jnp.int32)[None, :]
-    ).astype(jnp.float32)
+    slab_blocks = own_blocks * n_rad
+    copies = n_slab * n_rad
+    where_read = ((slab - 1) * slab_blocks + pattern).reshape(-1).astype(jnp.int32)
+    transposed = jnp.swapaxes(preconditioner, 1, 2)
+    force_t = force.T
     velocity = damping * precondition(force)
+    send = jnp.tile(velocity, (copies, 1))
     for sweep_index in range(1, ITERS):
-        gathered = lax.all_to_all(
-            jnp.tile(velocity, (n_slab * n_rad, 1)), ("slab", "rad"), 0, 0, tiled=True
+        gathered = lax.all_to_all(send, ("slab", "rad"), 0, 0, tiled=True)
+        velocity, send = sweep(
+            where_read, gathered, stiffness, transposed, force_t, velocity, copies
         )
-        neighbours = jnp.dot(selector, gathered, precision=highest).reshape(own_blocks, -1, BLOCK)
-        image = jnp.einsum("bnij,bnj->bi", stiffness, neighbours, precision=highest)
-        velocity = velocity + damping * precondition(force - image)
     return (q_next, arrivals, element_stress, velocity)
 
 

time: 169 us -> 152 us (0.90)
  matrix products: 45.4 us -> 1.55 us
  Pallas kernels: 40.8 us -> 67.6 us
  local copies, waits for them, and re-layouts: 5.54 us -> 9.34 us
  waiting for transfers between devices: 43.7 us -> 40.6 us
    dot_general x10 -> x0, matrix products: 37.1 us -> none  [the longest x5 36 us: body(): image = jnp.einsum('bnij,bnj->bi', stiffness, neighbours, precision=highest)]
    pallas_call x0 -> x5, Pallas kernels: none -> 26.8 us  [sweep(): pl.pallas_call(sweep_kernel, out_shape=(jax.ShapeDtypeStruct(velocity.sha...]
    dot_general x6 -> x1, matrix products: 8.17 us -> 1.38 us  [precondition(): return jnp.einsum('bij,bj->bi', preconditioner, vector, precision=highest)]
    unnamed x20 -> x33, local copies, waits for them, and re-layouts: 0.69 us -> 6.08 us
    all_to_all x5, waiting for transfers between devices: 30.7 us -> 27.5 us  [body(): gathered = lax.all_to_all(send, ('slab', 'rad'), 0, 0, tiled=True)]
    another operation x5 -> x1, local copies, waits for them, and re-layouts: 3.76 us -> 0.75 us  [body(): send = jnp.tile(velocity, (copies, 1))]
  transfers between devices with their start and end apart: 8 -> 8, of which waited for: 6 -> 6; matrix products, arithmetic and copies ran while one was open for 7% -> 3% of each run, Pallas kernels for 15% -> 20%
where the time goes in v3:
time: 152 us; the launch traced here: 151 us
  Pallas kernels  67.6 us (44%)
  waiting for transfers between devices  40.6 us (27%)
  starting transfers between devices  28.6 us (19%)
  local copies, waits for them, and re-layouts  9.34 us (6%)
  other arithmetic  2.61 us (2%)
  matrix products  1.55 us (1%)
    all_to_all x5, waiting for transfers between devices, body(): gathered = lax.all_to_all(send, ('slab', 'rad'), 0, 0, tiled=True)  27.5 us
    pallas_call x5, Pallas kernels, sweep(): pl.pallas_call(sweep_kernel, out_shape=(jax.ShapeDtypeStruct(velocity.sha...  26.8 us
    pallas_call x1, Pallas kernels, update_and_pack(): pl.pallas_call(functools.partial(update_kernel, groups16=groups16, slots1...  24.9 us
    all_to_all x5, starting transfers between devices, body(): gathered = lax.all_to_all(send, ('slab', 'rad'), 0, 0, tiled=True)  16.3 us
    pallas_call x1, Pallas kernels, stress_partials(): pl.pallas_call(functools.partial(stress_kernel, groups=groups, rows=rows)...  15.9 us
    all_to_all x1, waiting for transfers between devices, body(): received = lax.all_to_all(spread, ('slab', 'rad'), 0, 0, tiled=True)  8.66 us
    all_to_all x1, starting transfers between devices, body(): received = lax.all_to_all(spread, ('slab', 'rad'), 0, 0, tiled=True)  7.3 us
    unnamed x33, local copies, waits for them, and re-layouts  6.08 us
  transfers between devices with their start and end apart: 8, of which 6 were waited for; matrix products, arithmetic and copies ran while one was open for 3% of the time, Pallas kernels for 20%

profile of v3, /device:TPU:0, one launch (start us, length us, event | category | flops | bytes accessed | tf_op | source)
XLA Modules:
  0.0 151.2 jit_solution(16345601747952214690)
XLA Ops:
  0.6 15.9 %shard_map.130 = f32[3,320,128]{2,1,0:T(8,128)} custom-call(f32[3,16384]{1,0:T(4,128)} %q_ref.3, s32[1,16384]{1,0:T(1,128)} %bitcast.81, s32[1,16384]{1,0:T(1,128)} %bitcast.83), custom_call_target="tpu_custom_call" | custom-call | flops 4026531840 | bytes 327680 | tf_op jit(solution)/shard_map/pallas_call | solution.py:157
  16.5 1.2 slice_add_fusion
  18.6 7.3 %all-to-all-start = ((f32[32,4,384]{2,1,0:T(4,128)}), f32[32,4,384]{2,1,0:T(4,128)S(1)}, u32[]{:S(2)}, u32[]{:S(2)}) async-start(f32[32,4,384]{2,1,0:T(4,128)} %bitcast.9), calls=%async_computation | async-start | bytes 393216 | tf_op jit(solution)/shard_map/all_to_all | solution.py:277
  26.0 8.7 %all-to-all-done = f32[32,4,384]{2,1,0:T(4,128)S(1)} async-done(((f32[32,4,384]{2,1,0:T(4,128)}), f32[32,4,384]{2,1,0:T(4,128)S(1)}, u32[]{:S(2)}, u32[]{:S(2)}) %all-to-all-start) | async-done | bytes 196640 | tf_op jit(solution)/shard_map/all_to_all | solution.py:277
  35.1 1.4 fusion.2
  37.2 2.7 %all-to-all-start.1 = ((f32[32,8,192]{2,1,0:T(8,128)}), f32[32,8,192]{2,1,0:T(8,128)S(1)}, u32[]{:S(2)}, u32[]{:S(2)}) async-start(f32[32,8,192]{2,1,0:T(8,128)} %tile.2), calls=%async_computation.1 | async-start | bytes 524288 | tf_op jit(solution)/shard_map/all_to_all | solution.py:307
  40.0 1.8 %copy.25 = f32[8,192,192]{1,2,0:T(8,128)} copy(f32[8,192,192]{2,1,0:T(8,128)S(1)} %copy-done.1) | data formatting | bytes 2359296 | tf_op args[9]
  43.2 7.2 %all-to-all-done.1 = f32[32,8,192]{2,1,0:T(8,128)S(1)} async-done(((f32[32,8,192]{2,1,0:T(8,128)}), f32[32,8,192]{2,1,0:T(8,128)S(1)}, u32[]{:S(2)}, u32[]{:S(2)}) %all-to-all-start.1) | async-done | bytes 196640 | tf_op jit(solution)/shard_map/all_to_all | solution.py:307
  51.1 5.4 %shard_map.131 = (f32[8,192]{1,0:T(8,128)}, f32[256,192]{1,0:T(8,128)}) custom-call(s32[32]{0:T(128)} %reshape.120.idx_ref, f32[256,192]{1,0:T(8,128)} %bitcast.62, f32[8,4,192,192]{3,2,1,0:T(8,128)} %s_ref.9, f32[8,192,192]{2,1,0:T(8,128)} %bitcast.51, f32[192,8]{1,0:T(8,128)} %bitcast.56, f32[8,192]{1,0:T(8,128)} %copy-done.8), custom_call_target="tpu_custom_call" | custom-call | flops 2949120 | bytes 6094848 | tf_op jit(solution)/shard_map/pallas_call | solution.py:232
  56.5 2.6 %all-to-all-start.2 = ((f32[32,8,192]{2,1,0:T(8,128)}), f32[32,8,192]{2,1,0:T(8,128)S(1)}, u32[]{:S(2)}, u32[]{:S(2)}) async-start(f32[32,8,192]{2,1,0:T(8,128)} %bitcast.71), calls=%async_computation.2 | async-start | bytes 524288 | tf_op jit(solution)/shard_map/all_to_all | solution.py:307
  59.1 10.3 %all-to-all-done.2 = f32[32,8,192]{2,1,0:T(8,128)S(1)} async-done(((f32[32,8,192]{2,1,0:T(8,128)}), f32[32,8,192]{2,1,0:T(8,128)S(1)}, u32[]{:S(2)}, u32[]{:S(2)}) %all-to-all-start.2) | async-done | bytes 196640 | tf_op jit(solution)/shard_map/all_to_all | solution.py:307
  70.1 5.4 %shard_map.132 = (f32[8,192]{1,0:T(8,128)}, f32[256,192]{1,0:T(8,128)}) custom-call(s32[32]{0:T(128)} %reshape.120.idx_ref, f32[256,192]{1,0:T(8,128)} %bitcast.65, f32[8,4,192,192]{3,2,1,0:T(8,128)} %s_ref.9, f32[8,192,192]{2,1,0:T(8,128)} %bitcast.52, f32[192,8]{1,0:T(8,128)} %bitcast.57, f32[8,192]{1,0:T(8,128)} %get-tuple-element.20.v_ref), custom_call_target="tpu_custom_call" | custom-call | flops 2949120 | bytes 6094848 | tf_op jit(solution)/shard_map/pallas_call | solution.py:232
  75.5 2.6 %all-to-all-start.3 = ((f32[32,8,192]{2,1,0:T(8,128)}), f32[32,8,192]{2,1,0:T(8,128)S(1)}, u32[]{:S(2)}, u32[]{:S(2)}) async-start(f32[32,8,192]{2,1,0:T(8,128)} %bitcast.70), calls=%async_computation.3 | async-start | bytes 524288 | tf_op jit(solution)/shard_map/all_to_all | solution.py:307
  78.8 24.9 %shard_map.129 = (f32[3,16384]{1,0:T(4,128)}, f32[3,48,128]{2,1,0:T(8,128)}, f32[3,48,128]{2,1,0:T(8,128)}) custom-call(f32[3,16384]{1,0:T(4,128)} %q_ref.3, f32[3,16384]{1,0:T(4,128)} %inc_ref.1, s32[1,16384]{1,0:T(1,128)} %bitcast.82, s32[1,16384]{1,0:T(1,128)} %bitcast.84, bf16[3,160,128]{2,1,0:T(8,128)(2,1)} %pad_maximum_fusion.tab_ref), custom_call_target="tpu_custom_call" | custom-call | flops 3221225472 | bytes 655360 | tf_op jit(solution)/shard_map/pallas_call | solution.py:183
  104.4 5.4 %shard_map.133 = (f32[8,192]{1,0:T(8,128)}, f32[256,192]{1,0:T(8,128)}) custom-call(s32[32]{0:T(128)} %reshape.120.idx_ref, f32[256,192]{1,0:T(8,128)} %bitcast.64, f32[8,4,192,192]{3,2,1,0:T(8,128)} %s_ref.9, f32[8,192,192]{2,1,0:T(8,128)} %bitcast.53, f32[192,8]{1,0:T(8,128)} %bitcast.58, f32[8,192]{1,0:T(8,128)} %get-tuple-element.22.v_ref), custom_call_target="tpu_custom_call" | custom-call | flops 2949120 | bytes 6094848 | tf_op jit(solution)/shard_map/pallas_call | solution.py:232
  109.8 5.8 %all-to-all-start.4 = ((f32[32,8,192]{2,1,0:T(8,128)}), f32[32,8,192]{2,1,0:T(8,128)S(1)}, u32[]{:S(2)}, u32[]{:S(2)}) async-start(f32[32,8,192]{2,1,0:T(8,128)} %bitcast.69), calls=%async_computation.4 | async-start | bytes 524288 | tf_op jit(solution)/shard_map/all_to_all | solution.py:307
  115.7 3.7 %collective-permute-start = (f32[3,1024]{1,0:T(4,128)S(1)}, f32[3,1024]{1,0:T(4,128)S(1)}, u32[]{:S(2)}, u32[]{:S(2)}) collective-permute-start(f32[3,1024]{1,0:T(4,128)S(1)} %bitcast.77), channel_id=1, source_target_pairs={{0,8},{8,16},{16,24},{1,9},{9,17},{17,25},{2,10},{10,18},{18,26},{... | collective-permute-start | bytes 36872 | tf_op jit(solution)/shard_map/ppermute | solution.py:251
  119.4 6.6 %all-to-all-done.4 = f32[32,8,192]{2,1,0:T(8,128)S(1)} async-done(((f32[32,8,192]{2,1,0:T(8,128)}), f32[32,8,192]{2,1,0:T(8,128)S(1)}, u32[]{:S(2)}, u32[]{:S(2)}) %all-to-all-start.4) | async-done | bytes 196640 | tf_op jit(solution)/shard_map/all_to_all | solution.py:307
  126.8 5.3 %shard_map.134 = (f32[8,192]{1,0:T(8,128)}, f32[256,192]{1,0:T(8,128)}) custom-call(s32[32]{0:T(128)} %reshape.120.idx_ref, f32[256,192]{1,0:T(8,128)} %bitcast.63, f32[8,4,192,192]{3,2,1,0:T(8,128)} %s_ref.9, f32[8,192,192]{2,1,0:T(8,128)} %bitcast.54, f32[192,8]{1,0:T(8,128)} %bitcast.59, f32[8,192]{1,0:T(8,128)} %get-tuple-element.24.v_ref), custom_call_target="tpu_custom_call" | custom-call | flops 2949120 | bytes 6094848 | tf_op jit(solution)/shard_map/pallas_call | solution.py:232
  132.1 2.6 %all-to-all-start.5 = ((f32[32,8,192]{2,1,0:T(8,128)}), f32[32,8,192]{2,1,0:T(8,128)S(1)}, u32[]{:S(2)}, u32[]{:S(2)}) async-start(f32[32,8,192]{2,1,0:T(8,128)} %bitcast.68), calls=%async_computation.5 | async-start | bytes 524288 | tf_op jit(solution)/shard_map/all_to_all | solution.py:307
  134.7 1.3 collective-permute-start.1
  136.0 4.4 %collective-permute-done.1 = f32[3,1024]{1,0:T(4,128)S(1)} collective-permute-done((f32[3,1024]{1,0:T(4,128)S(1)}, f32[3,1024]{1,0:T(4,128)S(1)}, u32[]{:S(2)}, u32[]{:S(2)}) %collective-permute-start.1) | collective-permute-done | bytes 12320 | tf_op jit(solution)/shard_map/ppermute | solution.py:251
  141.7 3.4 %all-to-all-done.5 = f32[32,8,192]{2,1,0:T(8,128)S(1)} async-done(((f32[32,8,192]{2,1,0:T(8,128)}), f32[32,8,192]{2,1,0:T(8,128)S(1)}, u32[]{:S(2)}, u32[]{:S(2)}) %all-to-all-start.5) | async-done | bytes 196640 | tf_op jit(solution)/shard_map/all_to_all | solution.py:307
  145.8 5.3 %shard_map.135 = (f32[8,192]{1,0:T(8,128)}, f32[256,192]{1,0:T(8,128)}) custom-call(s32[32]{0:T(128)} %reshape.120.idx_ref, f32[256,192]{1,0:T(8,128)} %bitcast.61, f32[8,4,192,192]{3,2,1,0:T(8,128)} %s_ref.9, f32[8,192,192]{2,1,0:T(8,128)} %bitcast.55, f32[192,8]{1,0:T(8,128)} %bitcast.60, f32[8,192]{1,0:T(8,128)} %get-tuple-element.26.v_ref), custom_call_target="tpu_custom_call" | custom-call | flops 2949120 | bytes 6094848 | tf_op jit(solution)/shard_map/pallas_call | solution.py:232
  (57 shorter events, 9.1 us)
Async XLA Ops:
  0.6 34.3 %copy-start = (f32[192,192]{1,0:T(8,128)S(1)}, f32[192,192]{1,0:T(8,128)}, u32[]{:S(2)}) copy-start(f32[192,192]{1,0:T(8,128)} %param.16) | copy-start | bytes 442372
  16.5 9.4 %copy-start.11 = (f32[384]{0:T(512)S(1)}, f32[384]{0:T(512)}, u32[]{:S(2)}) copy-start(f32[384]{0:T(512)} %param.15) | copy-start | bytes 4612
  16.5 18.6 %copy-start.1 = (f32[8,192,192]{2,1,0:T(8,128)S(1)}, f32[8,192,192]{2,1,0:T(8,128)}, u32[]{:S(2)}) copy-start(f32[8,192,192]{2,1,0:T(8,128)} %param.19) | copy-start | bytes 3538948
  18.6 16.1 %all-to-all-start = ((f32[32,4,384]{2,1,0:T(4,128)}), f32[32,4,384]{2,1,0:T(4,128)S(1)}, u32[]{:S(2)}, u32[]{:S(2)}) async-start(f32[32,4,384]{2,1,0:T(4,128)} %bitcast.9), calls=%async_computation | async-start | bytes 393216 | tf_op jit(solution)/shard_map/all_to_all | solution.py:277
  36.5 5.3 %copy-start.8 = (f32[8,192]{1,0:T(8,128)}, f32[8,192]{1,0:T(8,128)S(1)}, u32[]{:S(2)}) copy-start(f32[8,192]{1,0:T(8,128)S(1)} %bitcast_multiply_fusion.v_ref) | copy-start | bytes 18436
  37.2 13.1 %all-to-all-start.1 = ((f32[32,8,192]{2,1,0:T(8,128)}), f32[32,8,192]{2,1,0:T(8,128)S(1)}, u32[]{:S(2)}, u32[]{:S(2)}) async-start(f32[32,8,192]{2,1,0:T(8,128)} %tile.2), calls=%async_computation.1 | async-start | bytes 524288 | tf_op jit(solution)/shard_map/all_to_all | solution.py:307
  40.0 1.8 %copy-start.12 = (s32[8,4]{0,1:T(4,128)S(1)}, s32[8,4]{0,1:T(4,128)}, u32[]{:S(2)}) copy-start(s32[8,4]{0,1:T(4,128)} %param.18) | copy-start | bytes 388
  50.4 0.7 copy-start.3
  51.1 8.0 %copy-start.7 = (f32[5,3072]{1,0:T(8,128)S(1)}, f32[5,3072]{1,0:T(8,128)}, u32[]{:S(2)}) copy-start(f32[5,3072]{1,0:T(8,128)} %param.12) | copy-start | bytes 184324
  56.5 13.0 %all-to-all-start.2 = ((f32[32,8,192]{2,1,0:T(8,128)}), f32[32,8,192]{2,1,0:T(8,128)S(1)}, u32[]{:S(2)}, u32[]{:S(2)}) async-start(f32[32,8,192]{2,1,0:T(8,128)} %bitcast.71), calls=%async_computation.2 | async-start | bytes 524288 | tf_op jit(solution)/shard_map/all_to_all | solution.py:307
  69.4 0.7 copy-start.6
  75.5 28.2 %all-to-all-start.3 = ((f32[32,8,192]{2,1,0:T(8,128)}), f32[32,8,192]{2,1,0:T(8,128)S(1)}, u32[]{:S(2)}, u32[]{:S(2)}) async-start(f32[32,8,192]{2,1,0:T(8,128)} %bitcast.70), calls=%async_computation.3 | async-start | bytes 524288 | tf_op jit(solution)/shard_map/all_to_all | solution.py:307
  103.7 0.7 copy-start.5
  104.4 11.2 %copy-start.9 = (f32[3,48,128]{2,1,0:T(8,128)S(1)}, f32[3,48,128]{2,1,0:T(8,128)}, u32[]{:S(2)}) copy-start(f32[3,48,128]{2,1,0:T(8,128)} %get-tuple-element.17) | copy-start | bytes 221188
  104.4 11.3 %copy-start.10 = (f32[3,48,128]{2,1,0:T(8,128)S(1)}, f32[3,48,128]{2,1,0:T(8,128)}, u32[]{:S(2)}) copy-start(f32[3,48,128]{2,1,0:T(8,128)} %get-tuple-element.18) | copy-start | bytes 221188
  109.8 16.2 %all-to-all-start.4 = ((f32[32,8,192]{2,1,0:T(8,128)}), f32[32,8,192]{2,1,0:T(8,128)S(1)}, u32[]{:S(2)}, u32[]{:S(2)}) async-start(f32[32,8,192]{2,1,0:T(8,128)} %bitcast.69), calls=%async_computation.4 | async-start | bytes 524288 | tf_op jit(solution)/shard_map/all_to_all | solution.py:307
  115.7 20.3 %collective-permute-start = (f32[3,1024]{1,0:T(4,128)S(1)}, f32[3,1024]{1,0:T(4,128)S(1)}, u32[]{:S(2)}, u32[]{:S(2)}) collective-permute-start(f32[3,1024]{1,0:T(4,128)S(1)} %bitcast.77), channel_id=1, source_target_pairs={{0,8},{8,16},{16,24},{1,9},{9,17},{17,25},{2,10},{10,18},{18,26},{... | collective-permute-start | bytes 36872 | tf_op jit(solution)/shard_map/ppermute | solution.py:251
  126.0 0.7 copy-start.4
  132.1 13.0 %all-to-all-start.5 = ((f32[32,8,192]{2,1,0:T(8,128)}), f32[32,8,192]{2,1,0:T(8,128)S(1)}, u32[]{:S(2)}, u32[]{:S(2)}) async-start(f32[32,8,192]{2,1,0:T(8,128)} %bitcast.68), calls=%async_computation.5 | async-start | bytes 524288 | tf_op jit(solution)/shard_map/all_to_all | solution.py:307
  134.7 5.7 %collective-permute-start.1 = (f32[3,1024]{1,0:T(4,128)S(1)}, f32[3,1024]{1,0:T(4,128)S(1)}, u32[]{:S(2)}, u32[]{:S(2)}) collective-permute-start(f32[3,1024]{1,0:T(4,128)S(1)} %bitcast.78), channel_id=1, source_target_pairs={{8,0},{16,8},{24,16},{9,1},{17,9},{25,17},{10,2},{18,10},{26,18},{... | collective-permute-start | bytes 36872 | tf_op jit(solution)/shard_map/ppermute | solution.py:251
  145.1 0.7 copy-start.2

commit v4 on v3

--- a/solution.py
+++ b/solution.py
@@ -10,6 +10,7 @@
 BLOCK = 192
 ITERS = 6
 CHUNK = 512
+UPDATE_PARTS = 4
 
 extensibility = 50.0
 time_step = 0.01
@@ -77,9 +78,9 @@
 
 
 def update_kernel(
-    q_ref, inc_ref, e_ref, m_ref, tab_ref, qn_ref, up_ref, dn_ref, tri_ref, *, groups16, slots16
+    q_ref, inc_ref, e_ref, m_ref, tab_ref, start_ref, qn_ref, up_ref, dn_ref, tri_ref, *, groups16, slots16, first
 ):
-    count = q_ref.shape[1]
+    count = qn_ref.shape[1]
     up_ref[...] = jnp.zeros_like(up_ref)
     dn_ref[...] = jnp.zeros_like(dn_ref)
     before = lax.broadcasted_iota(jnp.int32, (CHUNK, CHUNK), 0)
@@ -92,7 +93,7 @@
     zero = jnp.zeros((), jnp.bfloat16)
 
     def body(step, offsets):
-        cols = pl.ds(pl.multiple_of(step * CHUNK, CHUNK), CHUNK)
+        cols = pl.ds(pl.multiple_of((first + step) * CHUNK, CHUNK), CHUNK)
         q = q_ref[:, cols]
         inc = inc_ref[:, cols]
         element = e_ref[:, cols]
@@ -123,7 +124,7 @@
             q[k : k + 1] + time_step * (drift[k] - 0.5 * spring * q[k : k + 1]) + noise_scale * inc[k : k + 1]
             for k in range(3)
         ]
-        qn_ref[:, cols] = jnp.concatenate(q_next, axis=0)
+        qn_ref[:, pl.ds(pl.multiple_of(step * CHUNK, CHUNK), CHUNK)] = jnp.concatenate(q_next, axis=0)
         going_up = move == 1
         going_down = move == -1
         flags = jnp.where(
@@ -147,7 +148,7 @@
                 )
         return offsets + jnp.sum(flags, axis=1, keepdims=True)
 
-    lax.fori_loop(0, count // CHUNK, body, jnp.zeros((8, 1), jnp.float32))
+    lax.fori_loop(0, count // CHUNK, body, start_ref[...])
 
 
 def stress_partials(q_state, element, migration, slab_elems):
@@ -180,20 +181,41 @@
     lo = rest - mid
     pieces = jnp.stack([hi, mid, lo]).astype(jnp.bfloat16)
     count = q_state.shape[1]
-    q_next, up, down = pl.pallas_call(
-        functools.partial(update_kernel, groups16=groups16, slots16=slots16),
-        out_shape=(
-            jax.ShapeDtypeStruct((3, count), jnp.float32),
-            jax.ShapeDtypeStruct((3, 3 * slots16, 128), jnp.float32),
-            jax.ShapeDtypeStruct((3, 3 * slots16, 128), jnp.float32),
-        ),
-        scratch_shapes=[pltpu.VMEM((CHUNK, CHUNK), jnp.bfloat16)],
-        cost_estimate=pl.CostEstimate(
-            flops=2 * 3 * (5 * groups16 + 6 * slots16) * 128 * count,
-            transcendentals=0,
-            bytes_accessed=40 * count,
-        ),
-    )(q_state, increments, element.reshape(1, -1), migration.reshape(1, -1), pieces)
+    parts = UPDATE_PARTS
+    share = count // parts
+    flags = jnp.stack([migration == 1, migration == -1]).astype(jnp.float32)
+    per_part = jnp.sum(flags.reshape(2, parts, share), axis=2)
+    starts = jnp.cumsum(per_part, axis=1) - per_part
+    starts = jnp.pad(starts.T, ((0, 0), (0, 6)))[:, :, None]
+    q_parts, up, down = [], 0.0, 0.0
+    for part in range(parts):
+        q_part, up_part, down_part = pl.pallas_call(
+            functools.partial(
+                update_kernel, groups16=groups16, slots16=slots16, first=part * share // CHUNK
+            ),
+            out_shape=(
+                jax.ShapeDtypeStruct((3, share), jnp.float32),
+                jax.ShapeDtypeStruct((3, 3 * slots16, 128), jnp.float32),
+                jax.ShapeDtypeStruct((3, 3 * slots16, 128), jnp.float32),
+            ),
+            scratch_shapes=[pltpu.VMEM((CHUNK, CHUNK), jnp.bfloat16)],
+            cost_estimate=pl.CostEstimate(
+                flops=16 * 3 * (5 * groups16 + 6 * slots16) * 128 * share,
+                transcendentals=0,
+                bytes_accessed=40 * share,
+            ),
+        )(
+            q_state,
+            increments,
+            element.reshape(1, -1),
+            migration.reshape(1, -1),
+            pieces,
+            starts[part],
+        )
+        q_parts.append(q_part)
+        up = up + up_part
+        down = down + down_part
+    q_next = jnp.concatenate(q_parts, axis=1)
 
     def unpack(acc):
         whole = acc[0] + acc[1] + acc[2]

time: 152 us -> 150 us (0.987)
  waiting for transfers between devices: 40.6 us -> 27.8 us
  Pallas kernels: 67.6 us -> 72.9 us
  starting transfers between devices: 28.6 us -> 31.2 us
  other arithmetic: 2.61 us -> 4.68 us
    all_to_all x1, waiting for transfers between devices: 8.66 us -> 0.01 us  [body(): received = lax.all_to_all(spread, ('slab', 'rad'), 0, 0, tiled=True)]
    pallas_call x1 -> x4, Pallas kernels: 24.9 us -> 30.4 us  [update_and_pack(): pl.pallas_call(functools.partial(update_kernel, groups16=groups16, slots1...]
    ppermute x2, waiting for transfers between devices: 4.38 us -> 0.01 us  [passed_along(): return lax.ppermute(array, axis, pairs)]
    all_to_all x5, starting transfers between devices: 16.3 us -> 19 us  [body(): gathered = lax.all_to_all(send, ('slab', 'rad'), 0, 0, tiled=True)]
    unnamed x33 -> x51, local copies, waits for them, and re-layouts: 6.08 us -> 6.02 us
  transfers between devices with their start and end apart: 8 -> 8, of which waited for: 6 -> 5; matrix products, arithmetic and copies ran while one was open for 3% -> 5% of each run, Pallas kernels for 20% -> 28%
where the time goes in v4:
time: 150 us; the launch traced here: 149 us
  Pallas kernels  72.9 us (49%)
  starting transfers between devices  31.2 us (21%)
  waiting for transfers between devices  27.8 us (19%)
  local copies, waits for them, and re-layouts  10.1 us (7%)
  other arithmetic  4.68 us (3%)
  matrix products  1.55 us (1%)
    pallas_call x4, Pallas kernels, update_and_pack(): pl.pallas_call(functools.partial(update_kernel, groups16=groups16, slots1...  30.4 us
    all_to_all x5, waiting for transfers between devices, body(): gathered = lax.all_to_all(send, ('slab', 'rad'), 0, 0, tiled=True)  27.8 us
    pallas_call x5, Pallas kernels, sweep(): pl.pallas_call(sweep_kernel, out_shape=(jax.ShapeDtypeStruct(velocity.sha...  26.7 us
    all_to_all x5, starting transfers between devices, body(): gathered = lax.all_to_all(send, ('slab', 'rad'), 0, 0, tiled=True)  19 us
    pallas_call x1, Pallas kernels, stress_partials(): pl.pallas_call(functools.partial(stress_kernel, groups=groups, rows=rows)...  15.9 us
    all_to_all x1, starting transfers between devices, body(): received = lax.all_to_all(spread, ('slab', 'rad'), 0, 0, tiled=True)  7.3 us
    unnamed x51, local copies, waits for them, and re-layouts  6.02 us
    ppermute x2, starting transfers between devices, passed_along(): return lax.ppermute(array, axis, pairs)  4.9 us
  transfers between devices with their start and end apart: 8, of which 5 were waited for; matrix products, arithmetic and copies ran while one was open for 5% of the time, Pallas kernels for 28%

profile of v4, /device:TPU:0, one launch (start us, length us, event | category | flops | bytes accessed | tf_op | source)
XLA Modules:
  0.0 149.2 jit_solution(16812080299813111124)
XLA Ops:
  0.6 15.9 %shard_map.133 = f32[3,320,128]{2,1,0:T(8,128)} custom-call(f32[3,16384]{1,0:T(4,128)} %q_ref.9, s32[1,16384]{1,0:T(1,128)} %bitcast.96, s32[1,16384]{1,0:T(1,128)} %bitcast.85), custom_call_target="tpu_custom_call" | custom-call | flops 4026531840 | bytes 327680 | tf_op jit(solution)/shard_map/pallas_call | solution.py:158
  18.6 7.3 %all-to-all-start = ((f32[32,4,384]{2,1,0:T(4,128)}), f32[32,4,384]{2,1,0:T(4,128)S(1)}, u32[]{:S(2)}, u32[]{:S(2)}) async-start(f32[32,4,384]{2,1,0:T(4,128)} %bitcast.14), calls=%async_computation | async-start | bytes 393216 | tf_op jit(solution)/shard_map/all_to_all | solution.py:299
  26.8 1.8 %copy.57 = f32[8,192,192]{1,2,0:T(8,128)} copy(f32[8,192,192]{2,1,0:T(8,128)S(1)} %copy-done.1) | data formatting | bytes 2359296 | tf_op args[9]
  30.4 7.6 %shard_map.129 = (f32[3,4096]{1,0:T(4,128)}, f32[3,48,128]{2,1,0:T(8,128)}, f32[3,48,128]{2,1,0:T(8,128)}) custom-call(f32[3,16384]{1,0:T(4,128)} %q_ref.9, f32[3,16384]{1,0:T(4,128)} %inc_ref.7, s32[1,16384]{1,0:T(1,128)} %bitcast.97, s32[1,16384]{1,0:T(1,128)} %bitcast.86, bf16[3,160,128]{2,1,0:T(8,128)(2,1)} %pad_maximum_fusion.1.tab_ref, ...), custom_call_target="tpu_custom_call" | custom-call | flops 6442450944 | bytes 163840 | tf_op jit(solution)/shard_map/pallas_call | solution.py:192
  37.9 7.6 %shard_map.130 = (f32[3,4096]{1,0:T(4,128)}, f32[3,48,128]{2,1,0:T(8,128)}, f32[3,48,128]{2,1,0:T(8,128)}) custom-call(f32[3,16384]{1,0:T(4,128)} %q_ref.9, f32[3,16384]{1,0:T(4,128)} %inc_ref.7, s32[1,16384]{1,0:T(1,128)} %bitcast.98, s32[1,16384]{1,0:T(1,128)} %bitcast.87, bf16[3,160,128]{2,1,0:T(8,128)(2,1)} %pad_maximum_fusion.1.tab_ref, ...), custom_call_target="tpu_custom_call" | custom-call | flops 6442450944 | bytes 163840 | tf_op jit(solution)/shard_map/pallas_call | solution.py:192
  45.9 1.4 fusion.2
  48.1 5.8 %all-to-all-start.1 = ((f32[32,8,192]{2,1,0:T(8,128)}), f32[32,8,192]{2,1,0:T(8,128)S(1)}, u32[]{:S(2)}, u32[]{:S(2)}) async-start(f32[32,8,192]{2,1,0:T(8,128)} %tile.2), calls=%async_computation.1 | async-start | bytes 524288 | tf_op jit(solution)/shard_map/all_to_all | solution.py:329
  53.9 7.6 %shard_map.131 = (f32[3,4096]{1,0:T(4,128)}, f32[3,48,128]{2,1,0:T(8,128)}, f32[3,48,128]{2,1,0:T(8,128)}) custom-call(f32[3,16384]{1,0:T(4,128)} %q_ref.9, f32[3,16384]{1,0:T(4,128)} %inc_ref.7, s32[1,16384]{1,0:T(1,128)} %bitcast.99, s32[1,16384]{1,0:T(1,128)} %bitcast.88, bf16[3,160,128]{2,1,0:T(8,128)(2,1)} %pad_maximum_fusion.1.tab_ref, ...), custom_call_target="tpu_custom_call" | custom-call | flops 6442450944 | bytes 163840 | tf_op jit(solution)/shard_map/pallas_call | solution.py:192
  62.2 2.0 %all-to-all-done.1 = f32[32,8,192]{2,1,0:T(8,128)S(1)} async-done(((f32[32,8,192]{2,1,0:T(8,128)}), f32[32,8,192]{2,1,0:T(8,128)S(1)}, u32[]{:S(2)}, u32[]{:S(2)}) %all-to-all-start.1) | async-done | bytes 196640 | tf_op jit(solution)/shard_map/all_to_all | solution.py:329
  65.0 5.3 %shard_map.134 = (f32[8,192]{1,0:T(8,128)}, f32[256,192]{1,0:T(8,128)}) custom-call(s32[32]{0:T(128)} %reshape.139.idx_ref, f32[256,192]{1,0:T(8,128)} %bitcast.75, f32[8,4,192,192]{3,2,1,0:T(8,128)} %s_ref.9, f32[8,192,192]{2,1,0:T(8,128)} %bitcast.61, f32[192,8]{1,0:T(8,128)} %bitcast.66, f32[8,192]{1,0:T(8,128)} %copy-done.8), custom_call_target="tpu_custom_call" | custom-call | flops 2949120 | bytes 6094848 | tf_op jit(solution)/shard_map/pallas_call | solution.py:254
  70.3 3.8 %all-to-all-start.2 = ((f32[32,8,192]{2,1,0:T(8,128)}), f32[32,8,192]{2,1,0:T(8,128)S(1)}, u32[]{:S(2)}, u32[]{:S(2)}) async-start(f32[32,8,192]{2,1,0:T(8,128)} %bitcast.79), calls=%async_computation.2 | async-start | bytes 524288 | tf_op jit(solution)/shard_map/all_to_all | solution.py:329
  74.2 7.7 %shard_map.132 = (f32[3,4096]{1,0:T(4,128)}, f32[3,48,128]{2,1,0:T(8,128)}, f32[3,48,128]{2,1,0:T(8,128)}) custom-call(f32[3,16384]{1,0:T(4,128)} %q_ref.9, f32[3,16384]{1,0:T(4,128)} %inc_ref.7, s32[1,16384]{1,0:T(1,128)} %bitcast.100, s32[1,16384]{1,0:T(1,128)} %bitcast.89, bf16[3,160,128]{2,1,0:T(8,128)(2,1)} %pad_maximum_fusion.1.tab_ref, ...), custom_call_target="tpu_custom_call" | custom-call | flops 6442450944 | bytes 163840 | tf_op jit(solution)/shard_map/pallas_call | solution.py:192
  82.8 1.7 %all-to-all-done.2 = f32[32,8,192]{2,1,0:T(8,128)S(1)} async-done(((f32[32,8,192]{2,1,0:T(8,128)}), f32[32,8,192]{2,1,0:T(8,128)S(1)}, u32[]{:S(2)}, u32[]{:S(2)}) %all-to-all-start.2) | async-done | bytes 196640 | tf_op jit(solution)/shard_map/all_to_all | solution.py:329
  85.2 5.3 %shard_map.135 = (f32[8,192]{1,0:T(8,128)}, f32[256,192]{1,0:T(8,128)}) custom-call(s32[32]{0:T(128)} %reshape.139.idx_ref, f32[256,192]{1,0:T(8,128)} %bitcast.72, f32[8,4,192,192]{3,2,1,0:T(8,128)} %s_ref.9, f32[8,192,192]{2,1,0:T(8,128)} %bitcast.62, f32[192,8]{1,0:T(8,128)} %bitcast.67, f32[8,192]{1,0:T(8,128)} %get-tuple-element.38.v_ref), custom_call_target="tpu_custom_call" | custom-call | flops 2949120 | bytes 6094848 | tf_op jit(solution)/shard_map/pallas_call | solution.py:254
  90.5 4.2 %all-to-all-start.3 = ((f32[32,8,192]{2,1,0:T(8,128)}), f32[32,8,192]{2,1,0:T(8,128)S(1)}, u32[]{:S(2)}, u32[]{:S(2)}) async-start(f32[32,8,192]{2,1,0:T(8,128)} %bitcast.81), calls=%async_computation.3 | async-start | bytes 524288 | tf_op jit(solution)/shard_map/all_to_all | solution.py:329
  96.1 9.0 %all-to-all-done.3 = f32[32,8,192]{2,1,0:T(8,128)S(1)} async-done(((f32[32,8,192]{2,1,0:T(8,128)}), f32[32,8,192]{2,1,0:T(8,128)S(1)}, u32[]{:S(2)}, u32[]{:S(2)}) %all-to-all-start.3) | async-done | bytes 196640 | tf_op jit(solution)/shard_map/all_to_all | solution.py:329
  105.8 5.3 %shard_map.136 = (f32[8,192]{1,0:T(8,128)}, f32[256,192]{1,0:T(8,128)}) custom-call(s32[32]{0:T(128)} %reshape.139.idx_ref, f32[256,192]{1,0:T(8,128)} %bitcast.74, f32[8,4,192,192]{3,2,1,0:T(8,128)} %s_ref.9, f32[8,192,192]{2,1,0:T(8,128)} %bitcast.63, f32[192,8]{1,0:T(8,128)} %bitcast.68, f32[8,192]{1,0:T(8,128)} %get-tuple-element.40.v_ref), custom_call_target="tpu_custom_call" | custom-call | flops 2949120 | bytes 6094848 | tf_op jit(solution)/shard_map/pallas_call | solution.py:254
  111.1 2.6 %all-to-all-start.4 = ((f32[32,8,192]{2,1,0:T(8,128)}), f32[32,8,192]{2,1,0:T(8,128)S(1)}, u32[]{:S(2)}, u32[]{:S(2)}) async-start(f32[32,8,192]{2,1,0:T(8,128)} %bitcast.80), calls=%async_computation.4 | async-start | bytes 524288 | tf_op jit(solution)/shard_map/all_to_all | solution.py:329
  113.8 3.6 %collective-permute-start = (f32[3,1024]{1,0:T(4,128)S(1)}, f32[3,1024]{1,0:T(4,128)S(1)}, u32[]{:S(2)}, u32[]{:S(2)}) collective-permute-start(f32[3,1024]{1,0:T(4,128)S(1)} %bitcast.93), channel_id=1, source_target_pairs={{0,8},{8,16},{16,24},{1,9},{9,17},{17,25},{2,10},{10,18},{18,26},{... | collective-permute-start | bytes 36872 | tf_op jit(solution)/shard_map/ppermute | solution.py:273
  117.4 6.7 %all-to-all-done.4 = f32[32,8,192]{2,1,0:T(8,128)S(1)} async-done(((f32[32,8,192]{2,1,0:T(8,128)}), f32[32,8,192]{2,1,0:T(8,128)S(1)}, u32[]{:S(2)}, u32[]{:S(2)}) %all-to-all-start.4) | async-done | bytes 196640 | tf_op jit(solution)/shard_map/all_to_all | solution.py:329
  124.8 5.4 %shard_map.137 = (f32[8,192]{1,0:T(8,128)}, f32[256,192]{1,0:T(8,128)}) custom-call(s32[32]{0:T(128)} %reshape.139.idx_ref, f32[256,192]{1,0:T(8,128)} %bitcast.73, f32[8,4,192,192]{3,2,1,0:T(8,128)} %s_ref.9, f32[8,192,192]{2,1,0:T(8,128)} %bitcast.64, f32[192,8]{1,0:T(8,128)} %bitcast.69, f32[8,192]{1,0:T(8,128)} %get-tuple-element.42.v_ref), custom_call_target="tpu_custom_call" | custom-call | flops 2949120 | bytes 6094848 | tf_op jit(solution)/shard_map/pallas_call | solution.py:254
  130.2 2.6 %all-to-all-start.5 = ((f32[32,8,192]{2,1,0:T(8,128)}), f32[32,8,192]{2,1,0:T(8,128)S(1)}, u32[]{:S(2)}, u32[]{:S(2)}) async-start(f32[32,8,192]{2,1,0:T(8,128)} %bitcast.78), calls=%async_computation.5 | async-start | bytes 524288 | tf_op jit(solution)/shard_map/all_to_all | solution.py:329
  134.9 8.3 %all-to-all-done.5 = f32[32,8,192]{2,1,0:T(8,128)S(1)} async-done(((f32[32,8,192]{2,1,0:T(8,128)}), f32[32,8,192]{2,1,0:T(8,128)S(1)}, u32[]{:S(2)}, u32[]{:S(2)}) %all-to-all-start.5) | async-done | bytes 196640 | tf_op jit(solution)/shard_map/all_to_all | solution.py:329
  143.9 5.3 %shard_map.138 = (f32[8,192]{1,0:T(8,128)}, f32[256,192]{1,0:T(8,128)}) custom-call(s32[32]{0:T(128)} %reshape.139.idx_ref, f32[256,192]{1,0:T(8,128)} %bitcast.71, f32[8,4,192,192]{3,2,1,0:T(8,128)} %s_ref.9, f32[8,192,192]{2,1,0:T(8,128)} %bitcast.65, f32[192,8]{1,0:T(8,128)} %bitcast.70, f32[8,192]{1,0:T(8,128)} %get-tuple-element.44.v_ref), custom_call_target="tpu_custom_call" | custom-call | flops 2949120 | bytes 6094848 | tf_op jit(solution)/shard_map/pallas_call | solution.py:254
  (88 shorter events, 14.4 us)
Async XLA Ops:
  0.6 45.1 %copy-start = (f32[192,192]{1,0:T(8,128)S(1)}, f32[192,192]{1,0:T(8,128)}, u32[]{:S(2)}) copy-start(f32[192,192]{1,0:T(8,128)} %param.16) | copy-start | bytes 442372
  16.5 9.4 %copy-start.15 = (s32[16384]{0:T(1024)S(1)}, s32[16384]{0:T(1024)}, u32[]{:S(2)}) copy-start(s32[16384]{0:T(1024)} %param.14) | copy-start | bytes 196612
  16.5 9.5 %copy-start.20 = (f32[384]{0:T(512)S(1)}, f32[384]{0:T(512)}, u32[]{:S(2)}) copy-start(f32[384]{0:T(512)} %param.15) | copy-start | bytes 4612
  16.5 9.5 %copy-start.21 = (s32[8,4]{0,1:T(4,128)S(1)}, s32[8,4]{0,1:T(4,128)}, u32[]{:S(2)}) copy-start(s32[8,4]{0,1:T(4,128)} %param.18) | copy-start | bytes 388
  16.5 10.3 %copy-start.1 = (f32[8,192,192]{2,1,0:T(8,128)S(1)}, f32[8,192,192]{2,1,0:T(8,128)}, u32[]{:S(2)}) copy-start(f32[8,192,192]{2,1,0:T(8,128)} %param.19) | copy-start | bytes 3538948
  18.6 26.9 %all-to-all-start = ((f32[32,4,384]{2,1,0:T(4,128)}), f32[32,4,384]{2,1,0:T(4,128)S(1)}, u32[]{:S(2)}, u32[]{:S(2)}) async-start(f32[32,4,384]{2,1,0:T(4,128)} %bitcast.14), calls=%async_computation | async-start | bytes 393216 | tf_op jit(solution)/shard_map/all_to_all | solution.py:299
  47.3 14.2 %copy-start.8 = (f32[8,192]{1,0:T(8,128)}, f32[8,192]{1,0:T(8,128)S(1)}, u32[]{:S(2)}) copy-start(f32[8,192]{1,0:T(8,128)S(1)} %bitcast_multiply_fusion.v_ref) | copy-start | bytes 18436
  48.1 16.2 %all-to-all-start.1 = ((f32[32,8,192]{2,1,0:T(8,128)}), f32[32,8,192]{2,1,0:T(8,128)S(1)}, u32[]{:S(2)}, u32[]{:S(2)}) async-start(f32[32,8,192]{2,1,0:T(8,128)} %tile.2), calls=%async_computation.1 | async-start | bytes 524288 | tf_op jit(solution)/shard_map/all_to_all | solution.py:329
  70.3 14.2 %all-to-all-start.2 = ((f32[32,8,192]{2,1,0:T(8,128)}), f32[32,8,192]{2,1,0:T(8,128)S(1)}, u32[]{:S(2)}, u32[]{:S(2)}) async-start(f32[32,8,192]{2,1,0:T(8,128)} %bitcast.79), calls=%async_computation.2 | async-start | bytes 524288 | tf_op jit(solution)/shard_map/all_to_all | solution.py:329
  74.1 7.7 %copy-start.9 = (f32[3,48,128]{2,1,0:T(8,128)S(1)}, f32[3,48,128]{2,1,0:T(8,128)}, u32[]{:S(2)}) copy-start(f32[3,48,128]{2,1,0:T(8,128)} %get-tuple-element.29) | copy-start | bytes 221188
  74.1 7.7 %copy-start.10 = (f32[3,48,128]{2,1,0:T(8,128)S(1)}, f32[3,48,128]{2,1,0:T(8,128)}, u32[]{:S(2)}) copy-start(f32[3,48,128]{2,1,0:T(8,128)} %get-tuple-element.33) | copy-start | bytes 221188
  74.1 7.7 %copy-start.11 = (f32[3,48,128]{2,1,0:T(8,128)S(1)}, f32[3,48,128]{2,1,0:T(8,128)}, u32[]{:S(2)}) copy-start(f32[3,48,128]{2,1,0:T(8,128)} %get-tuple-element.30) | copy-start | bytes 221188
  74.1 7.7 %copy-start.12 = (f32[3,48,128]{2,1,0:T(8,128)S(1)}, f32[3,48,128]{2,1,0:T(8,128)}, u32[]{:S(2)}) copy-start(f32[3,48,128]{2,1,0:T(8,128)} %get-tuple-element.34) | copy-start | bytes 221188
  74.2 7.7 %copy-start.13 = (f32[3,48,128]{2,1,0:T(8,128)S(1)}, f32[3,48,128]{2,1,0:T(8,128)}, u32[]{:S(2)}) copy-start(f32[3,48,128]{2,1,0:T(8,128)} %get-tuple-element.31) | copy-start | bytes 221188
  74.2 7.7 %copy-start.14 = (f32[3,48,128]{2,1,0:T(8,128)S(1)}, f32[3,48,128]{2,1,0:T(8,128)}, u32[]{:S(2)}) copy-start(f32[3,48,128]{2,1,0:T(8,128)} %get-tuple-element.35) | copy-start | bytes 221188
  90.5 14.6 %all-to-all-start.3 = ((f32[32,8,192]{2,1,0:T(8,128)}), f32[32,8,192]{2,1,0:T(8,128)S(1)}, u32[]{:S(2)}, u32[]{:S(2)}) async-start(f32[32,8,192]{2,1,0:T(8,128)} %bitcast.81), calls=%async_computation.3 | async-start | bytes 524288 | tf_op jit(solution)/shard_map/all_to_all | solution.py:329
  94.8 38.8 %collective-permute-start.1 = (f32[3,1024]{1,0:T(4,128)S(1)}, f32[3,1024]{1,0:T(4,128)S(1)}, u32[]{:S(2)}, u32[]{:S(2)}) collective-permute-start(f32[3,1024]{1,0:T(4,128)S(1)} %bitcast.92), channel_id=1, source_target_pairs={{8,0},{16,8},{24,16},{9,1},{17,9},{25,17},{10,2},{18,10},{26,18},{... | collective-permute-start | bytes 36872 | tf_op jit(solution)/shard_map/ppermute | solution.py:273
  111.1 13.0 %all-to-all-start.4 = ((f32[32,8,192]{2,1,0:T(8,128)}), f32[32,8,192]{2,1,0:T(8,128)S(1)}, u32[]{:S(2)}, u32[]{:S(2)}) async-start(f32[32,8,192]{2,1,0:T(8,128)} %bitcast.80), calls=%async_computation.4 | async-start | bytes 524288 | tf_op jit(solution)/shard_map/all_to_all | solution.py:329
  113.8 19.8 %collective-permute-start = (f32[3,1024]{1,0:T(4,128)S(1)}, f32[3,1024]{1,0:T(4,128)S(1)}, u32[]{:S(2)}, u32[]{:S(2)}) collective-permute-start(f32[3,1024]{1,0:T(4,128)S(1)} %bitcast.93), channel_id=1, source_target_pairs={{0,8},{8,16},{16,24},{1,9},{9,17},{17,25},{2,10},{10,18},{18,26},{... | collective-permute-start | bytes 36872 | tf_op jit(solution)/shard_map/ppermute | solution.py:273
  124.8 8.0 %copy-start.16 = (f32[3,4096]{1,0:T(4,128)S(1)}, f32[3,4096]{1,0:T(4,128)}, u32[]{:S(2)}) copy-start(f32[3,4096]{1,0:T(4,128)} %get-tuple-element.25) | copy-start | bytes 147460
  124.8 8.0 %copy-start.17 = (f32[3,4096]{1,0:T(4,128)S(1)}, f32[3,4096]{1,0:T(4,128)}, u32[]{:S(2)}) copy-start(f32[3,4096]{1,0:T(4,128)} %get-tuple-element.26) | copy-start | bytes 147460
  124.8 8.0 %copy-start.18 = (f32[3,4096]{1,0:T(4,128)S(1)}, f32[3,4096]{1,0:T(4,128)}, u32[]{:S(2)}) copy-start(f32[3,4096]{1,0:T(4,128)} %get-tuple-element.27) | copy-start | bytes 147460
  124.8 8.0 %copy-start.19 = (f32[3,4096]{1,0:T(4,128)S(1)}, f32[3,4096]{1,0:T(4,128)}, u32[]{:S(2)}) copy-start(f32[3,4096]{1,0:T(4,128)} %get-tuple-element.28) | copy-start | bytes 147460
  130.2 13.0 %all-to-all-start.5 = ((f32[32,8,192]{2,1,0:T(8,128)}), f32[32,8,192]{2,1,0:T(8,128)S(1)}, u32[]{:S(2)}, u32[]{:S(2)}) async-start(f32[32,8,192]{2,1,0:T(8,128)} %bitcast.78), calls=%async_computation.5 | async-start | bytes 524288 | tf_op jit(solution)/shard_map/all_to_all | solution.py:329
  (6 other events, 5.3 us)

commit v5 on v4

--- a/solution.py
+++ b/solution.py
@@ -10,6 +10,7 @@
 BLOCK = 192
 ITERS = 6
 CHUNK = 512
+STRESS_CHUNK = 1024
 UPDATE_PARTS = 4
 
 extensibility = 50.0
@@ -50,12 +51,12 @@
 def stress_kernel(q_ref, e_ref, m_ref, out_ref, *, groups, rows):
     count = q_ref.shape[1]
     out_ref[...] = jnp.zeros_like(out_ref)
-    low_iota = lax.broadcasted_iota(jnp.int32, (128, CHUNK), 0)
-    row_iota = lax.broadcasted_iota(jnp.int32, (rows, CHUNK), 0)
+    low_iota = lax.broadcasted_iota(jnp.int32, (128, STRESS_CHUNK), 0)
+    row_iota = lax.broadcasted_iota(jnp.int32, (rows, STRESS_CHUNK), 0)
     zero = jnp.zeros((), jnp.bfloat16)
 
     def body(step, carry):
-        cols = pl.ds(pl.multiple_of(step * CHUNK, CHUNK), CHUNK)
+        cols = pl.ds(pl.multiple_of(step * STRESS_CHUNK, STRESS_CHUNK), STRESS_CHUNK)
         q = q_ref[:, cols]
         element = e_ref[:, cols]
         move = m_ref[:, cols]
@@ -63,18 +64,19 @@
         kind = jnp.where(move == 0, 1, jnp.where(move == 1, 2, 0))
         key = kind * groups + (element >> 7)
         low = (low_iota == (element & 127)).astype(jnp.bfloat16)
+        low = jnp.concatenate([low, low, low], axis=1)
         mask = row_iota == key
-        pieces = [bf16_pieces(term) for term in terms]
-        for p in range(3):
-            spread = jnp.concatenate(
-                [jnp.where(mask, pieces[c][p], zero) for c in range(4)], axis=0
-            )
-            out_ref[p] += lax.dot_general(
-                spread, low, nt_dims, preferred_element_type=jnp.float32
-            )
+        spread = jnp.concatenate(
+            [
+                jnp.concatenate([jnp.where(mask, piece, zero) for piece in bf16_pieces(term)], axis=1)
+                for term in terms
+            ],
+            axis=0,
+        )
+        out_ref[...] += lax.dot_general(spread, low, nt_dims, preferred_element_type=jnp.float32)
         return carry
 
-    lax.fori_loop(0, count // CHUNK, body, 0)
+    lax.fori_loop(0, count // STRESS_CHUNK, body, 0)
 
 
 def update_kernel(
@@ -99,9 +101,9 @@
         element = e_ref[:, cols]
         move = m_ref[:, cols]
         low = (low_iota == (element & 127)).astype(jnp.bfloat16)
-        picked = jnp.dot(tab_ref[0], low, preferred_element_type=jnp.float32)
-        picked = picked + jnp.dot(tab_ref[1], low, preferred_element_type=jnp.float32)
-        picked = picked + jnp.dot(tab_ref[2], low, preferred_element_type=jnp.float32)
+        picked = jnp.dot(
+            tab_ref[...], jnp.concatenate([low, low, low], axis=0), preferred_element_type=jnp.float32
+        )
         hit = group_iota == (element >> 7)
         grads = [
             jnp.sum(
@@ -138,14 +140,16 @@
         for direction, chosen, out_ref in ((0, going_up, up_ref), (1, going_down, dn_ref)):
             slot = slots[direction : direction + 1]
             place = ((low_iota == (slot & 127)) & chosen).astype(jnp.bfloat16)
+            place = jnp.concatenate([place, place, place], axis=1)
             which = slot_iota == (slot >> 7)
-            for p in range(3):
-                spread = jnp.concatenate(
-                    [jnp.where(which, pieces[k][p], zero) for k in range(3)], axis=0
-                )
-                out_ref[p] += lax.dot_general(
-                    spread, place, nt_dims, preferred_element_type=jnp.float32
-                )
+            spread = jnp.concatenate(
+                [
+                    jnp.concatenate([jnp.where(which, piece, zero) for piece in pieces[k]], axis=1)
+                    for k in range(3)
+                ],
+                axis=0,
+            )
+            out_ref[...] += lax.dot_general(spread, place, nt_dims, preferred_element_type=jnp.float32)
         return offsets + jnp.sum(flags, axis=1, keepdims=True)
 
     lax.fori_loop(0, count // CHUNK, body, start_ref[...])
@@ -157,13 +161,12 @@
     count = q_state.shape[1]
     out = pl.pallas_call(
         functools.partial(stress_kernel, groups=groups, rows=rows),
-        out_shape=jax.ShapeDtypeStruct((3, 4 * rows, 128), jnp.float32),
+        out_shape=jax.ShapeDtypeStruct((4 * rows, 128), jnp.float32),
         cost_estimate=pl.CostEstimate(
             flops=2 * 3 * 4 * rows * 128 * count, transcendentals=0, bytes_accessed=20 * count
         ),
     )(q_state, element.reshape(1, -1), migration.reshape(1, -1))
-    total = out[0] + out[1] + out[2]
-    total = total.reshape(4, rows, 128)[:, : 3 * groups].reshape(4, 3 * slab_elems)
+    total = out.reshape(4, rows, 128)[:, : 3 * groups].reshape(4, 3 * slab_elems)
     return total
 
 
@@ -179,7 +182,7 @@
     rest = arranged - hi
     mid = lax.reduce_precision(rest, exponent_bits=8, mantissa_bits=7)
     lo = rest - mid
-    pieces = jnp.stack([hi, mid, lo]).astype(jnp.bfloat16)
+    pieces = jnp.concatenate([hi, mid, lo], axis=1).astype(jnp.bfloat16)
     count = q_state.shape[1]
     parts = UPDATE_PARTS
     share = count // parts
@@ -195,8 +198,8 @@
             ),
             out_shape=(
                 jax.ShapeDtypeStruct((3, share), jnp.float32),
-                jax.ShapeDtypeStruct((3, 3 * slots16, 128), jnp.float32),
-                jax.ShapeDtypeStruct((3, 3 * slots16, 128), jnp.float32),
+                jax.ShapeDtypeStruct((3 * slots16, 128), jnp.float32),
+                jax.ShapeDtypeStruct((3 * slots16, 128), jnp.float32),
             ),
             scratch_shapes=[pltpu.VMEM((CHUNK, CHUNK), jnp.bfloat16)],
             cost_estimate=pl.CostEstimate(
@@ -218,8 +221,7 @@
     q_next = jnp.concatenate(q_parts, axis=1)
 
     def unpack(acc):
-        whole = acc[0] + acc[1] + acc[2]
-        return whole.reshape(3, slots16, 128)[:, :slots].reshape(3, slots * 128)
+        return acc.reshape(3, slots16, 128)[:, :slots].reshape(3, slots * 128)
 
     return q_next, unpack(up), unpack(down)
 

time: 150 us -> 138 us (0.920)
  waiting for transfers between devices: 27.8 us -> 20.2 us
  Pallas kernels: 72.9 us -> 68.9 us
    all_to_all x5, waiting for transfers between devices: 27.8 us -> 20.2 us  [body(): gathered = lax.all_to_all(send, ('slab', 'rad'), 0, 0, tiled=True)]
    pallas_call x1, Pallas kernels: 15.9 us -> 12.8 us  [stress_partials(): pl.pallas_call(functools.partial(stress_kernel, groups=groups, rows=rows)...]
  transfers between devices with their start and end apart: 8 -> 8, of which waited for: 5 -> 5; matrix products, arithmetic and copies ran while one was open for 5% -> 6% of each run, Pallas kernels for 28% -> 25%
where the time goes in v5:
time: 138 us
  Pallas kernels  68.9 us (50%)
  starting transfers between devices  31.6 us (23%)
  waiting for transfers between devices  20.2 us (15%)
  local copies, waits for them, and re-layouts  11 us (8%)
  other arithmetic  3.26 us (2%)
  matrix products  1.55 us (1%)
    pallas_call x4, Pallas kernels, update_and_pack(): pl.pallas_call(functools.partial(update_kernel, groups16=groups16, slots1...  29.4 us
    pallas_call x5, Pallas kernels, sweep(): pl.pallas_call(sweep_kernel, out_shape=(jax.ShapeDtypeStruct(velocity.sha...  26.7 us
    all_to_all x5, waiting for transfers between devices, body(): gathered = lax.all_to_all(send, ('slab', 'rad'), 0, 0, tiled=True)  20.2 us
    all_to_all x5, starting transfers between devices, body(): gathered = lax.all_to_all(send, ('slab', 'rad'), 0, 0, tiled=True)  18.5 us
    pallas_call x1, Pallas kernels, stress_partials(): pl.pallas_call(functools.partial(stress_kernel, groups=groups, rows=rows)...  12.8 us
    all_to_all x1, starting transfers between devices, body(): received = lax.all_to_all(spread, ('slab', 'rad'), 0, 0, tiled=True)  7.3 us
    unnamed x51, local copies, waits for them, and re-layouts  6.02 us
    ppermute x2, starting transfers between devices, passed_along(): return lax.ppermute(array, axis, pairs)  5.84 us
  transfers between devices with their start and end apart: 8, of which 5 were waited for; matrix products, arithmetic and copies ran while one was open for 6% of the time, Pallas kernels for 25%

profile of v5, /device:TPU:0, one launch (start us, length us, event | category | flops | bytes accessed | tf_op | source)
XLA Modules:
  0.0 137.6 jit_solution(13405776980137024405)
XLA Ops:
  0.6 12.8 %shard_map.133 = f32[320,128]{1,0:T(8,128)} custom-call(f32[3,16384]{1,0:T(4,128)} %q_ref.9, s32[1,16384]{1,0:T(1,128)} %bitcast.94, s32[1,16384]{1,0:T(1,128)} %bitcast.83), custom_call_target="tpu_custom_call" | custom-call | flops 4026531840 | bytes 327680 | tf_op jit(solution)/shard_map/pallas_call | solution.py:162
  15.3 7.3 %all-to-all-start = ((f32[32,4,384]{2,1,0:T(4,128)}), f32[32,4,384]{2,1,0:T(4,128)S(1)}, u32[]{:S(2)}, u32[]{:S(2)}) async-start(f32[32,4,384]{2,1,0:T(4,128)} %bitcast.14), calls=%async_computation | async-start | bytes 393216 | tf_op jit(solution)/shard_map/all_to_all | solution.py:301
  23.4 1.8 %copy.57 = f32[8,192,192]{1,2,0:T(8,128)} copy(f32[8,192,192]{2,1,0:T(8,128)S(1)} %copy-done.1) | data formatting | bytes 2359296 | tf_op args[9]
  27.0 7.3 %shard_map.129 = (f32[3,4096]{1,0:T(4,128)}, f32[48,128]{1,0:T(8,128)}, f32[48,128]{1,0:T(8,128)}) custom-call(f32[3,16384]{1,0:T(4,128)} %q_ref.9, f32[3,16384]{1,0:T(4,128)} %inc_ref.7, s32[1,16384]{1,0:T(1,128)} %bitcast.95, s32[1,16384]{1,0:T(1,128)} %bitcast.84, bf16[160,384]{1,0:T(8,128)(2,1)} %pad_maximum_fusion.1.tab_ref, ...), custom_call_target="tpu_custom_call" | custom-call | flops 6442450944 | bytes 163840 | tf_op jit(solution)/shard_map/pallas_call | solution.py:195
  34.7 1.4 %fusion.2 = f32[8,1,192]{2,1,0:T(1,128)S(1)} fusion(f32[8,192,192]{2,1,0:T(8,128)S(1)} %copy-done.1, f32[8,192,1]{1,0,2:T(8,128)S(1)} %bitcast.82), kind=kOutput, calls=%fused_computation.22 | convolution fusion | flops 3538944 | bytes 1191936 | tf_op jit(solution)/shard_map/bij,bj->bi/dot_general | solution.py:321
  36.9 5.8 %all-to-all-start.1 = ((f32[32,8,192]{2,1,0:T(8,128)}), f32[32,8,192]{2,1,0:T(8,128)S(1)}, u32[]{:S(2)}, u32[]{:S(2)}) async-start(f32[32,8,192]{2,1,0:T(8,128)} %tile.2), calls=%async_computation.1 | async-start | bytes 524288 | tf_op jit(solution)/shard_map/all_to_all | solution.py:331
  42.7 7.3 %shard_map.130 = (f32[3,4096]{1,0:T(4,128)}, f32[48,128]{1,0:T(8,128)}, f32[48,128]{1,0:T(8,128)}) custom-call(f32[3,16384]{1,0:T(4,128)} %q_ref.9, f32[3,16384]{1,0:T(4,128)} %inc_ref.7, s32[1,16384]{1,0:T(1,128)} %bitcast.96, s32[1,16384]{1,0:T(1,128)} %bitcast.85, bf16[160,384]{1,0:T(8,128)(2,1)} %pad_maximum_fusion.1.tab_ref, ...), custom_call_target="tpu_custom_call" | custom-call | flops 6442450944 | bytes 163840 | tf_op jit(solution)/shard_map/pallas_call | solution.py:195
  50.8 2.3 %all-to-all-done.1 = f32[32,8,192]{2,1,0:T(8,128)S(1)} async-done(((f32[32,8,192]{2,1,0:T(8,128)}), f32[32,8,192]{2,1,0:T(8,128)S(1)}, u32[]{:S(2)}, u32[]{:S(2)}) %all-to-all-start.1) | async-done | bytes 196640 | tf_op jit(solution)/shard_map/all_to_all | solution.py:331
  53.8 5.3 %shard_map.134 = (f32[8,192]{1,0:T(8,128)}, f32[256,192]{1,0:T(8,128)}) custom-call(s32[32]{0:T(128)} %reshape.97.idx_ref, f32[256,192]{1,0:T(8,128)} %bitcast.73, f32[8,4,192,192]{3,2,1,0:T(8,128)} %s_ref.9, f32[8,192,192]{2,1,0:T(8,128)} %bitcast.60, f32[192,8]{1,0:T(8,128)} %bitcast.65, f32[8,192]{1,0:T(8,128)} %copy-done.8), custom_call_target="tpu_custom_call" | custom-call | flops 2949120 | bytes 6094848 | tf_op jit(solution)/shard_map/pallas_call | solution.py:256
  59.1 3.6 %all-to-all-start.2 = ((f32[32,8,192]{2,1,0:T(8,128)}), f32[32,8,192]{2,1,0:T(8,128)S(1)}, u32[]{:S(2)}, u32[]{:S(2)}) async-start(f32[32,8,192]{2,1,0:T(8,128)} %bitcast.78), calls=%async_computation.2 | async-start | bytes 524288 | tf_op jit(solution)/shard_map/all_to_all | solution.py:331
  62.7 7.3 %shard_map.131 = (f32[3,4096]{1,0:T(4,128)}, f32[48,128]{1,0:T(8,128)}, f32[48,128]{1,0:T(8,128)}) custom-call(f32[3,16384]{1,0:T(4,128)} %q_ref.9, f32[3,16384]{1,0:T(4,128)} %inc_ref.7, s32[1,16384]{1,0:T(1,128)} %bitcast.97, s32[1,16384]{1,0:T(1,128)} %bitcast.86, bf16[160,384]{1,0:T(8,128)(2,1)} %pad_maximum_fusion.1.tab_ref, ...), custom_call_target="tpu_custom_call" | custom-call | flops 6442450944 | bytes 163840 | tf_op jit(solution)/shard_map/pallas_call | solution.py:195
  70.1 3.0 %all-to-all-done.2 = f32[32,8,192]{2,1,0:T(8,128)S(1)} async-done(((f32[32,8,192]{2,1,0:T(8,128)}), f32[32,8,192]{2,1,0:T(8,128)S(1)}, u32[]{:S(2)}, u32[]{:S(2)}) %all-to-all-start.2) | async-done | bytes 196640 | tf_op jit(solution)/shard_map/all_to_all | solution.py:331
  73.8 5.3 %shard_map.135 = (f32[8,192]{1,0:T(8,128)}, f32[256,192]{1,0:T(8,128)}) custom-call(s32[32]{0:T(128)} %reshape.97.idx_ref, f32[256,192]{1,0:T(8,128)} %bitcast.74, f32[8,4,192,192]{3,2,1,0:T(8,128)} %s_ref.9, f32[8,192,192]{2,1,0:T(8,128)} %bitcast.61, f32[192,8]{1,0:T(8,128)} %bitcast.66, f32[8,192]{1,0:T(8,128)} %get-tuple-element.38.v_ref), custom_call_target="tpu_custom_call" | custom-call | flops 2949120 | bytes 6094848 | tf_op jit(solution)/shard_map/pallas_call | solution.py:256
  79.1 2.8 %all-to-all-start.3 = ((f32[32,8,192]{2,1,0:T(8,128)}), f32[32,8,192]{2,1,0:T(8,128)S(1)}, u32[]{:S(2)}, u32[]{:S(2)}) async-start(f32[32,8,192]{2,1,0:T(8,128)} %bitcast.76), calls=%async_computation.3 | async-start | bytes 524288 | tf_op jit(solution)/shard_map/all_to_all | solution.py:331
  82.0 7.4 %shard_map.132 = (f32[3,4096]{1,0:T(4,128)}, f32[48,128]{1,0:T(8,128)}, f32[48,128]{1,0:T(8,128)}) custom-call(f32[3,16384]{1,0:T(4,128)} %q_ref.9, f32[3,16384]{1,0:T(4,128)} %inc_ref.7, s32[1,16384]{1,0:T(1,128)} %bitcast.98, s32[1,16384]{1,0:T(1,128)} %bitcast.87, bf16[160,384]{1,0:T(8,128)(2,1)} %pad_maximum_fusion.1.tab_ref, ...), custom_call_target="tpu_custom_call" | custom-call | flops 6442450944 | bytes 163840 | tf_op jit(solution)/shard_map/pallas_call | solution.py:195
  90.2 2.1 %all-to-all-done.3 = f32[32,8,192]{2,1,0:T(8,128)S(1)} async-done(((f32[32,8,192]{2,1,0:T(8,128)}), f32[32,8,192]{2,1,0:T(8,128)S(1)}, u32[]{:S(2)}, u32[]{:S(2)}) %all-to-all-start.3) | async-done | bytes 196640 | tf_op jit(solution)/shard_map/all_to_all | solution.py:331
  93.0 5.3 %shard_map.136 = (f32[8,192]{1,0:T(8,128)}, f32[256,192]{1,0:T(8,128)}) custom-call(s32[32]{0:T(128)} %reshape.97.idx_ref, f32[256,192]{1,0:T(8,128)} %bitcast.71, f32[8,4,192,192]{3,2,1,0:T(8,128)} %s_ref.9, f32[8,192,192]{2,1,0:T(8,128)} %bitcast.62, f32[192,8]{1,0:T(8,128)} %bitcast.67, f32[8,192]{1,0:T(8,128)} %get-tuple-element.40.v_ref), custom_call_target="tpu_custom_call" | custom-call | flops 2949120 | bytes 6094848 | tf_op jit(solution)/shard_map/pallas_call | solution.py:256
  98.4 3.7 %all-to-all-start.4 = ((f32[32,8,192]{2,1,0:T(8,128)}), f32[32,8,192]{2,1,0:T(8,128)S(1)}, u32[]{:S(2)}, u32[]{:S(2)}) async-start(f32[32,8,192]{2,1,0:T(8,128)} %bitcast.77), calls=%async_computation.4 | async-start | bytes 524288 | tf_op jit(solution)/shard_map/all_to_all | solution.py:331
  103.4 4.5 %collective-permute-start = (f32[3,1024]{1,0:T(4,128)S(1)}, f32[3,1024]{1,0:T(4,128)S(1)}, u32[]{:S(2)}, u32[]{:S(2)}) collective-permute-start(f32[3,1024]{1,0:T(4,128)S(1)} %bitcast.91), channel_id=1, source_target_pairs={{0,8},{8,16},{16,24},{1,9},{9,17},{17,25},{2,10},{10,18},{18,26},{... | collective-permute-start | bytes 36872 | tf_op jit(solution)/shard_map/ppermute | solution.py:275
  108.0 4.5 %all-to-all-done.4 = f32[32,8,192]{2,1,0:T(8,128)S(1)} async-done(((f32[32,8,192]{2,1,0:T(8,128)}), f32[32,8,192]{2,1,0:T(8,128)S(1)}, u32[]{:S(2)}, u32[]{:S(2)}) %all-to-all-start.4) | async-done | bytes 196640 | tf_op jit(solution)/shard_map/all_to_all | solution.py:331
  113.2 5.4 %shard_map.137 = (f32[8,192]{1,0:T(8,128)}, f32[256,192]{1,0:T(8,128)}) custom-call(s32[32]{0:T(128)} %reshape.97.idx_ref, f32[256,192]{1,0:T(8,128)} %bitcast.72, f32[8,4,192,192]{3,2,1,0:T(8,128)} %s_ref.9, f32[8,192,192]{2,1,0:T(8,128)} %bitcast.63, f32[192,8]{1,0:T(8,128)} %bitcast.68, f32[8,192]{1,0:T(8,128)} %get-tuple-element.42.v_ref), custom_call_target="tpu_custom_call" | custom-call | flops 2949120 | bytes 6094848 | tf_op jit(solution)/shard_map/pallas_call | solution.py:256
  118.6 2.6 %all-to-all-start.5 = ((f32[32,8,192]{2,1,0:T(8,128)}), f32[32,8,192]{2,1,0:T(8,128)S(1)}, u32[]{:S(2)}, u32[]{:S(2)}) async-start(f32[32,8,192]{2,1,0:T(8,128)} %bitcast.75), calls=%async_computation.5 | async-start | bytes 524288 | tf_op jit(solution)/shard_map/all_to_all | solution.py:331
  123.2 8.3 %all-to-all-done.5 = f32[32,8,192]{2,1,0:T(8,128)S(1)} async-done(((f32[32,8,192]{2,1,0:T(8,128)}), f32[32,8,192]{2,1,0:T(8,128)S(1)}, u32[]{:S(2)}, u32[]{:S(2)}) %all-to-all-start.5) | async-done | bytes 196640 | tf_op jit(solution)/shard_map/all_to_all | solution.py:331
  132.2 5.3 %shard_map.138 = (f32[8,192]{1,0:T(8,128)}, f32[256,192]{1,0:T(8,128)}) custom-call(s32[32]{0:T(128)} %reshape.97.idx_ref, f32[256,192]{1,0:T(8,128)} %bitcast.70, f32[8,4,192,192]{3,2,1,0:T(8,128)} %s_ref.9, f32[8,192,192]{2,1,0:T(8,128)} %bitcast.64, f32[192,8]{1,0:T(8,128)} %bitcast.69, f32[8,192]{1,0:T(8,128)} %get-tuple-element.44.v_ref), custom_call_target="tpu_custom_call" | custom-call | flops 2949120 | bytes 6094848 | tf_op jit(solution)/shard_map/pallas_call | solution.py:256
  (85 shorter events, 14.0 us)
Async XLA Ops:
  0.6 33.9 %copy-start = (f32[192,192]{1,0:T(8,128)S(1)}, f32[192,192]{1,0:T(8,128)}, u32[]{:S(2)}) copy-start(f32[192,192]{1,0:T(8,128)} %param.16) | copy-start | bytes 442372
  13.4 9.2 %copy-start.9 = (s32[16384]{0:T(1024)S(1)}, s32[16384]{0:T(1024)}, u32[]{:S(2)}) copy-start(s32[16384]{0:T(1024)} %param.14) | copy-start | bytes 196612
  13.4 9.3 %copy-start.20 = (f32[384]{0:T(512)S(1)}, f32[384]{0:T(512)}, u32[]{:S(2)}) copy-start(f32[384]{0:T(512)} %param.15) | copy-start | bytes 4612
  13.4 9.3 %copy-start.21 = (s32[8,4]{0,1:T(4,128)S(1)}, s32[8,4]{0,1:T(4,128)}, u32[]{:S(2)}) copy-start(s32[8,4]{0,1:T(4,128)} %param.18) | copy-start | bytes 388
  13.4 10.0 %copy-start.1 = (f32[8,192,192]{2,1,0:T(8,128)S(1)}, f32[8,192,192]{2,1,0:T(8,128)}, u32[]{:S(2)}) copy-start(f32[8,192,192]{2,1,0:T(8,128)} %param.19) | copy-start | bytes 3538948
  15.3 19.0 %all-to-all-start = ((f32[32,4,384]{2,1,0:T(4,128)}), f32[32,4,384]{2,1,0:T(4,128)S(1)}, u32[]{:S(2)}, u32[]{:S(2)}) async-start(f32[32,4,384]{2,1,0:T(4,128)} %bitcast.14), calls=%async_computation | async-start | bytes 393216 | tf_op jit(solution)/shard_map/all_to_all | solution.py:301
  36.1 13.9 %copy-start.8 = (f32[8,192]{1,0:T(8,128)}, f32[8,192]{1,0:T(8,128)S(1)}, u32[]{:S(2)}) copy-start(f32[8,192]{1,0:T(8,128)S(1)} %bitcast_multiply_fusion.v_ref) | copy-start | bytes 18436
  36.9 16.2 %all-to-all-start.1 = ((f32[32,8,192]{2,1,0:T(8,128)}), f32[32,8,192]{2,1,0:T(8,128)S(1)}, u32[]{:S(2)}, u32[]{:S(2)}) async-start(f32[32,8,192]{2,1,0:T(8,128)} %tile.2), calls=%async_computation.1 | async-start | bytes 524288 | tf_op jit(solution)/shard_map/all_to_all | solution.py:331
  59.1 14.0 %all-to-all-start.2 = ((f32[32,8,192]{2,1,0:T(8,128)}), f32[32,8,192]{2,1,0:T(8,128)S(1)}, u32[]{:S(2)}, u32[]{:S(2)}) async-start(f32[32,8,192]{2,1,0:T(8,128)} %bitcast.78), calls=%async_computation.2 | async-start | bytes 524288 | tf_op jit(solution)/shard_map/all_to_all | solution.py:331
  79.1 13.2 %all-to-all-start.3 = ((f32[32,8,192]{2,1,0:T(8,128)}), f32[32,8,192]{2,1,0:T(8,128)S(1)}, u32[]{:S(2)}, u32[]{:S(2)}) async-start(f32[32,8,192]{2,1,0:T(8,128)} %bitcast.76), calls=%async_computation.3 | async-start | bytes 524288 | tf_op jit(solution)/shard_map/all_to_all | solution.py:331
  81.9 7.4 %copy-start.14 = (f32[48,128]{1,0:T(8,128)S(1)}, f32[48,128]{1,0:T(8,128)}, u32[]{:S(2)}) copy-start(f32[48,128]{1,0:T(8,128)} %get-tuple-element.29) | copy-start | bytes 73732
  82.0 7.4 %copy-start.15 = (f32[48,128]{1,0:T(8,128)S(1)}, f32[48,128]{1,0:T(8,128)}, u32[]{:S(2)}) copy-start(f32[48,128]{1,0:T(8,128)} %get-tuple-element.33) | copy-start | bytes 73732
  82.0 7.4 %copy-start.16 = (f32[48,128]{1,0:T(8,128)S(1)}, f32[48,128]{1,0:T(8,128)}, u32[]{:S(2)}) copy-start(f32[48,128]{1,0:T(8,128)} %get-tuple-element.30) | copy-start | bytes 73732
  82.0 7.4 %copy-start.17 = (f32[48,128]{1,0:T(8,128)S(1)}, f32[48,128]{1,0:T(8,128)}, u32[]{:S(2)}) copy-start(f32[48,128]{1,0:T(8,128)} %get-tuple-element.34) | copy-start | bytes 73732
  82.0 7.4 %copy-start.18 = (f32[48,128]{1,0:T(8,128)S(1)}, f32[48,128]{1,0:T(8,128)}, u32[]{:S(2)}) copy-start(f32[48,128]{1,0:T(8,128)} %get-tuple-element.31) | copy-start | bytes 73732
  82.0 7.4 %copy-start.19 = (f32[48,128]{1,0:T(8,128)S(1)}, f32[48,128]{1,0:T(8,128)}, u32[]{:S(2)}) copy-start(f32[48,128]{1,0:T(8,128)} %get-tuple-element.35) | copy-start | bytes 73732
  98.4 14.1 %all-to-all-start.4 = ((f32[32,8,192]{2,1,0:T(8,128)}), f32[32,8,192]{2,1,0:T(8,128)S(1)}, u32[]{:S(2)}, u32[]{:S(2)}) async-start(f32[32,8,192]{2,1,0:T(8,128)} %bitcast.77), calls=%async_computation.4 | async-start | bytes 524288 | tf_op jit(solution)/shard_map/all_to_all | solution.py:331
  102.1 19.8 %collective-permute-start.1 = (f32[3,1024]{1,0:T(4,128)S(1)}, f32[3,1024]{1,0:T(4,128)S(1)}, u32[]{:S(2)}, u32[]{:S(2)}) collective-permute-start(f32[3,1024]{1,0:T(4,128)S(1)} %bitcast.90), channel_id=1, source_target_pairs={{8,0},{16,8},{24,16},{9,1},{17,9},{25,17},{10,2},{18,10},{26,18},{... | collective-permute-start | bytes 36872 | tf_op jit(solution)/shard_map/ppermute | solution.py:275
  103.4 18.5 %collective-permute-start = (f32[3,1024]{1,0:T(4,128)S(1)}, f32[3,1024]{1,0:T(4,128)S(1)}, u32[]{:S(2)}, u32[]{:S(2)}) collective-permute-start(f32[3,1024]{1,0:T(4,128)S(1)} %bitcast.91), channel_id=1, source_target_pairs={{0,8},{8,16},{16,24},{1,9},{9,17},{17,25},{2,10},{10,18},{18,26},{... | collective-permute-start | bytes 36872 | tf_op jit(solution)/shard_map/ppermute | solution.py:275
  113.2 8.0 %copy-start.10 = (f32[3,4096]{1,0:T(4,128)S(1)}, f32[3,4096]{1,0:T(4,128)}, u32[]{:S(2)}) copy-start(f32[3,4096]{1,0:T(4,128)} %get-tuple-element.25) | copy-start | bytes 147460
  113.2 8.0 %copy-start.11 = (f32[3,4096]{1,0:T(4,128)S(1)}, f32[3,4096]{1,0:T(4,128)}, u32[]{:S(2)}) copy-start(f32[3,4096]{1,0:T(4,128)} %get-tuple-element.26) | copy-start | bytes 147460
  113.2 8.0 %copy-start.12 = (f32[3,4096]{1,0:T(4,128)S(1)}, f32[3,4096]{1,0:T(4,128)}, u32[]{:S(2)}) copy-start(f32[3,4096]{1,0:T(4,128)} %get-tuple-element.27) | copy-start | bytes 147460
  113.2 8.0 %copy-start.13 = (f32[3,4096]{1,0:T(4,128)S(1)}, f32[3,4096]{1,0:T(4,128)}, u32[]{:S(2)}) copy-start(f32[3,4096]{1,0:T(4,128)} %get-tuple-element.28) | copy-start | bytes 147460
  118.6 13.0 %all-to-all-start.5 = ((f32[32,8,192]{2,1,0:T(8,128)}), f32[32,8,192]{2,1,0:T(8,128)S(1)}, u32[]{:S(2)}, u32[]{:S(2)}) async-start(f32[32,8,192]{2,1,0:T(8,128)} %bitcast.75), calls=%async_computation.5 | async-start | bytes 524288 | tf_op jit(solution)/shard_map/all_to_all | solution.py:331
  (6 other events, 5.3 us)

commit v6 on v5

--- a/solution.py
+++ b/solution.py
@@ -230,44 +230,55 @@
     total = g_ref.shape[0]
     own = v_ref.shape[0]
     width = s_ref.shape[1]
-    rows = []
-    for b in range(own):
-        acc = None
-        for n in range(width):
-            w = idx_ref[b * width + n]
-            inside = jnp.logical_and(w >= 0, w < total)
-            near = g_ref[pl.ds(jnp.clip(w, 0, total - 1), 1), :]
-            near = jnp.where(inside, near, 0.0)
-            term = s_ref[b, n] * near
-            acc = term if acc is None else acc + term
-        image = jnp.sum(acc, axis=1, keepdims=True)
-        rest = ft_ref[:, b : b + 1] - image
-        update = jnp.sum(pt_ref[b] * rest, axis=0, keepdims=True)
-        rows.append(v_ref[b : b + 1, :] + damping * update)
-    fresh = jnp.concatenate(rows, axis=0)
-    vout_ref[...] = fresh
-    for k in range(send_ref.shape[0] // own):
-        send_ref[k * own : (k + 1) * own, :] = fresh
+    b = pl.program_id(0)
+    acc = None
+    for n in range(width):
+        w = idx_ref[b * width + n]
+        inside = jnp.logical_and(w >= 0, w < total)
+        near = g_ref[pl.ds(jnp.clip(w, 0, total - 1), 1), :]
+        near = jnp.where(inside, near, 0.0)
+        term = s_ref[0, n] * near
+        acc = term if acc is None else acc + term
+    image = jnp.sum(acc, axis=1, keepdims=True)
+    rest = ft_ref[0] - image
+    update = jnp.sum(pt_ref[0] * rest, axis=0, keepdims=True)
+    vout_ref[pl.ds(b, 1), :] = v_ref[pl.ds(b, 1), :] + damping * update
+
+    @pl.when(b == own - 1)
+    def _():
+        fresh = vout_ref[...]
+        for k in range(send_ref.shape[0] // own):
+            send_ref[k * own : (k + 1) * own, :] = fresh
 
 
 def sweep(where_read, gathered, stiffness, transposed, force_t, velocity, copies):
-    own = velocity.shape[0]
-    vmem = pl.BlockSpec(memory_space=pltpu.VMEM)
+    own, size = velocity.shape
+    width = stiffness.shape[1]
+    whole = lambda shape: pl.BlockSpec(shape, lambda b, idx: (0,) * len(shape))
     return pl.pallas_call(
         sweep_kernel,
         out_shape=(
             jax.ShapeDtypeStruct(velocity.shape, jnp.float32),
-            jax.ShapeDtypeStruct((copies * own, velocity.shape[1]), jnp.float32),
-        ),
-        in_specs=[pl.BlockSpec(memory_space=pltpu.SMEM)] + [vmem] * 5,
-        out_specs=(vmem, vmem),
+            jax.ShapeDtypeStruct((copies * own, size), jnp.float32),
+        ),
+        grid_spec=pltpu.PrefetchScalarGridSpec(
+            num_scalar_prefetch=1,
+            grid=(own,),
+            in_specs=[
+                whole(gathered.shape),
+                pl.BlockSpec((1, width, size, size), lambda b, idx: (b, 0, 0, 0)),
+                pl.BlockSpec((1, size, size), lambda b, idx: (b, 0, 0)),
+                pl.BlockSpec((1, size, 1), lambda b, idx: (b, 0, 0)),
+                whole(velocity.shape),
+            ],
+            out_specs=(whole(velocity.shape), whole((copies * own, size))),
+        ),
         cost_estimate=pl.CostEstimate(
             flops=2 * (stiffness.size + transposed.size),
             transcendentals=0,
             bytes_accessed=4 * (stiffness.size + transposed.size + gathered.size),
         ),
     )(where_read, gathered, stiffness, transposed, force_t, velocity)
-
 
 def passed_along(array, axis, by):
     size = lax.axis_size(axis)
@@ -324,7 +335,7 @@
     copies = n_slab * n_rad
     where_read = ((slab - 1) * slab_blocks + pattern).reshape(-1).astype(jnp.int32)
     transposed = jnp.swapaxes(preconditioner, 1, 2)
-    force_t = force.T
+    force_t = force[:, :, None]
     velocity = damping * precondition(force)
     send = jnp.tile(velocity, (copies, 1))
     for sweep_index in range(1, ITERS):

time: 138 us -> 154 us (1.12)
  Pallas kernels: 68.9 us -> 83.7 us
    pallas_call x5, Pallas kernels: 26.7 us -> 41.6 us  [sweep(): pl.pallas_call(sweep_kernel, out_shape=(jax.ShapeDtypeStruct(velocity.sha...]
    unnamed x51 -> x53, local copies, waits for them, and re-layouts: 6.02 us -> 6.03 us
  transfers between devices with their start and end apart: 8 -> 8, of which waited for: 5 -> 5; matrix products, arithmetic and copies ran while one was open for 6% -> 5% of each run, Pallas kernels for 25% -> 25%
where the time goes in v6:
time: 154 us; the launch traced here: 152 us
  Pallas kernels  83.7 us (54%)
  starting transfers between devices  30.8 us (20%)
  waiting for transfers between devices  21 us (14%)
  local copies, waits for them, and re-layouts  10.7 us (7%)
  other arithmetic  3.26 us (2%)
  matrix products  1.58 us (1%)
    pallas_call x5, Pallas kernels, sweep(): pl.pallas_call(sweep_kernel, out_shape=(jax.ShapeDtypeStruct(velocity.sha...  41.6 us
    pallas_call x4, Pallas kernels, update_and_pack(): pl.pallas_call(functools.partial(update_kernel, groups16=groups16, slots1...  29.4 us
    all_to_all x5, waiting for transfers between devices, body(): gathered = lax.all_to_all(send, ('slab', 'rad'), 0, 0, tiled=True)  21 us
    all_to_all x5, starting transfers between devices, body(): gathered = lax.all_to_all(send, ('slab', 'rad'), 0, 0, tiled=True)  17.7 us
    pallas_call x1, Pallas kernels, stress_partials(): pl.pallas_call(functools.partial(stress_kernel, groups=groups, rows=rows)...  12.8 us
    all_to_all x1, starting transfers between devices, body(): received = lax.all_to_all(spread, ('slab', 'rad'), 0, 0, tiled=True)  7.3 us
    unnamed x53, local copies, waits for them, and re-layouts  6.03 us
    ppermute x2, starting transfers between devices, passed_along(): return lax.ppermute(array, axis, pairs)  5.84 us
  transfers between devices with their start and end apart: 8, of which 5 were waited for; matrix products, arithmetic and copies ran while one was open for 5% of the time, Pallas kernels for 25%

profile of v6, /device:TPU:0, one launch (start us, length us, event | category | flops | bytes accessed | tf_op | source)
XLA Modules:
  0.0 152.1 jit_solution(16791942117178115364)
XLA Ops:
  0.6 12.8 %shard_map.133 = f32[320,128]{1,0:T(8,128)} custom-call(f32[3,16384]{1,0:T(4,128)} %q_ref.9, s32[1,16384]{1,0:T(1,128)} %bitcast.89, s32[1,16384]{1,0:T(1,128)} %bitcast.78), custom_call_target="tpu_custom_call" | custom-call | flops 4026531840 | bytes 327680 | tf_op jit(solution)/shard_map/pallas_call | solution.py:162
  15.3 7.3 %all-to-all-start = ((f32[32,4,384]{2,1,0:T(4,128)}), f32[32,4,384]{2,1,0:T(4,128)S(1)}, u32[]{:S(2)}, u32[]{:S(2)}) async-start(f32[32,4,384]{2,1,0:T(4,128)} %bitcast.14), calls=%async_computation | async-start | bytes 393216 | tf_op jit(solution)/shard_map/all_to_all | solution.py:312
  23.5 1.8 %copy.68 = f32[8,192,192]{1,2,0:T(8,128)} copy(f32[8,192,192]{2,1,0:T(8,128)S(1)} %copy-done.2) | data formatting | bytes 2359296 | tf_op args[9]
  27.1 7.3 %shard_map.129 = (f32[3,4096]{1,0:T(4,128)}, f32[48,128]{1,0:T(8,128)}, f32[48,128]{1,0:T(8,128)}) custom-call(f32[3,16384]{1,0:T(4,128)} %q_ref.9, f32[3,16384]{1,0:T(4,128)} %inc_ref.7, s32[1,16384]{1,0:T(1,128)} %bitcast.90, s32[1,16384]{1,0:T(1,128)} %bitcast.79, bf16[160,384]{1,0:T(8,128)(2,1)} %pad_maximum_fusion.1.tab_ref, ...), custom_call_target="tpu_custom_call" | custom-call | flops 6442450944 | bytes 163840 | tf_op jit(solution)/shard_map/pallas_call | solution.py:195
  35.2 1.4 fusion.6
  37.3 5.8 %all-to-all-start.1 = ((f32[32,8,192]{2,1,0:T(8,128)}), f32[32,8,192]{2,1,0:T(8,128)S(1)}, u32[]{:S(2)}, u32[]{:S(2)}) async-start(f32[32,8,192]{2,1,0:T(8,128)} %tile.2), calls=%async_computation.1 | async-start | bytes 524288 | tf_op jit(solution)/shard_map/all_to_all | solution.py:342
  43.2 7.3 %shard_map.130 = (f32[3,4096]{1,0:T(4,128)}, f32[48,128]{1,0:T(8,128)}, f32[48,128]{1,0:T(8,128)}) custom-call(f32[3,16384]{1,0:T(4,128)} %q_ref.9, f32[3,16384]{1,0:T(4,128)} %inc_ref.7, s32[1,16384]{1,0:T(1,128)} %bitcast.91, s32[1,16384]{1,0:T(1,128)} %bitcast.80, bf16[160,384]{1,0:T(8,128)(2,1)} %pad_maximum_fusion.1.tab_ref, ...), custom_call_target="tpu_custom_call" | custom-call | flops 6442450944 | bytes 163840 | tf_op jit(solution)/shard_map/pallas_call | solution.py:195
  50.5 3.0 %all-to-all-done.1 = f32[32,8,192]{2,1,0:T(8,128)S(1)} async-done(((f32[32,8,192]{2,1,0:T(8,128)}), f32[32,8,192]{2,1,0:T(8,128)S(1)}, u32[]{:S(2)}, u32[]{:S(2)}) %all-to-all-start.1) | async-done | bytes 196640 | tf_op jit(solution)/shard_map/all_to_all | solution.py:342
  54.3 8.3 %shard_map.134 = (f32[8,192]{1,0:T(8,128)}, f32[256,192]{1,0:T(8,128)}) custom-call(s32[32]{0:T(128)} %reshape.97.idx_ref, f32[256,192]{1,0:T(8,128)} %bitcast.70, f32[8,4,192,192]{3,2,1,0:T(8,128)} %s_ref.9, f32[8,192,192]{2,1,0:T(8,128)} %bitcast.61, f32[8,192,1]{2,1,0:T(8,128)} %copy-done.1, f32[8,192]{1,0:T(8,128)} %copy-done.9), custom_call_target="tpu_custom_call" | custom-call | flops 2949120 | bytes 6094848 | tf_op jit(solution)/shard_map/pallas_call | solution.py:258
  62.6 2.8 %all-to-all-start.2 = ((f32[32,8,192]{2,1,0:T(8,128)}), f32[32,8,192]{2,1,0:T(8,128)S(1)}, u32[]{:S(2)}, u32[]{:S(2)}) async-start(f32[32,8,192]{2,1,0:T(8,128)} %bitcast.74), calls=%async_computation.2 | async-start | bytes 524288 | tf_op jit(solution)/shard_map/all_to_all | solution.py:342
  65.4 7.3 %shard_map.131 = (f32[3,4096]{1,0:T(4,128)}, f32[48,128]{1,0:T(8,128)}, f32[48,128]{1,0:T(8,128)}) custom-call(f32[3,16384]{1,0:T(4,128)} %q_ref.9, f32[3,16384]{1,0:T(4,128)} %inc_ref.7, s32[1,16384]{1,0:T(1,128)} %bitcast.92, s32[1,16384]{1,0:T(1,128)} %bitcast.81, bf16[160,384]{1,0:T(8,128)(2,1)} %pad_maximum_fusion.1.tab_ref, ...), custom_call_target="tpu_custom_call" | custom-call | flops 6442450944 | bytes 163840 | tf_op jit(solution)/shard_map/pallas_call | solution.py:195
  72.7 3.1 %all-to-all-done.2 = f32[32,8,192]{2,1,0:T(8,128)S(1)} async-done(((f32[32,8,192]{2,1,0:T(8,128)}), f32[32,8,192]{2,1,0:T(8,128)S(1)}, u32[]{:S(2)}, u32[]{:S(2)}) %all-to-all-start.2) | async-done | bytes 196640 | tf_op jit(solution)/shard_map/all_to_all | solution.py:342
  76.5 8.3 %shard_map.135 = (f32[8,192]{1,0:T(8,128)}, f32[256,192]{1,0:T(8,128)}) custom-call(s32[32]{0:T(128)} %reshape.97.idx_ref, f32[256,192]{1,0:T(8,128)} %bitcast.69, f32[8,4,192,192]{3,2,1,0:T(8,128)} %s_ref.9, f32[8,192,192]{2,1,0:T(8,128)} %bitcast.62, f32[8,192,1]{2,1,0:T(8,128)} %copy-done.1, f32[8,192]{1,0:T(8,128)} %get-tuple-element.38.v_ref), custom_call_target="tpu_custom_call" | custom-call | flops 2949120 | bytes 6094848 | tf_op jit(solution)/shard_map/pallas_call | solution.py:258
  84.7 2.8 %all-to-all-start.3 = ((f32[32,8,192]{2,1,0:T(8,128)}), f32[32,8,192]{2,1,0:T(8,128)S(1)}, u32[]{:S(2)}, u32[]{:S(2)}) async-start(f32[32,8,192]{2,1,0:T(8,128)} %bitcast.72), calls=%async_computation.3 | async-start | bytes 524288 | tf_op jit(solution)/shard_map/all_to_all | solution.py:342
  87.6 7.4 %shard_map.132 = (f32[3,4096]{1,0:T(4,128)}, f32[48,128]{1,0:T(8,128)}, f32[48,128]{1,0:T(8,128)}) custom-call(f32[3,16384]{1,0:T(4,128)} %q_ref.9, f32[3,16384]{1,0:T(4,128)} %inc_ref.7, s32[1,16384]{1,0:T(1,128)} %bitcast.93, s32[1,16384]{1,0:T(1,128)} %bitcast.82, bf16[160,384]{1,0:T(8,128)(2,1)} %pad_maximum_fusion.1.tab_ref, ...), custom_call_target="tpu_custom_call" | custom-call | flops 6442450944 | bytes 163840 | tf_op jit(solution)/shard_map/pallas_call | solution.py:195
  95.8 2.1 %all-to-all-done.3 = f32[32,8,192]{2,1,0:T(8,128)S(1)} async-done(((f32[32,8,192]{2,1,0:T(8,128)}), f32[32,8,192]{2,1,0:T(8,128)S(1)}, u32[]{:S(2)}, u32[]{:S(2)}) %all-to-all-start.3) | async-done | bytes 196640 | tf_op jit(solution)/shard_map/all_to_all | solution.py:342
  98.6 8.3 %shard_map.136 = (f32[8,192]{1,0:T(8,128)}, f32[256,192]{1,0:T(8,128)}) custom-call(s32[32]{0:T(128)} %reshape.97.idx_ref, f32[256,192]{1,0:T(8,128)} %bitcast.67, f32[8,4,192,192]{3,2,1,0:T(8,128)} %s_ref.9, f32[8,192,192]{2,1,0:T(8,128)} %bitcast.63, f32[8,192,1]{2,1,0:T(8,128)} %copy-done.1, f32[8,192]{1,0:T(8,128)} %get-tuple-element.40.v_ref), custom_call_target="tpu_custom_call" | custom-call | flops 2949120 | bytes 6094848 | tf_op jit(solution)/shard_map/pallas_call | solution.py:258
  106.9 3.7 %all-to-all-start.4 = ((f32[32,8,192]{2,1,0:T(8,128)}), f32[32,8,192]{2,1,0:T(8,128)S(1)}, u32[]{:S(2)}, u32[]{:S(2)}) async-start(f32[32,8,192]{2,1,0:T(8,128)} %bitcast.73), calls=%async_computation.4 | async-start | bytes 524288 | tf_op jit(solution)/shard_map/all_to_all | solution.py:342
  112.0 4.5 %collective-permute-start = (f32[3,1024]{1,0:T(4,128)S(1)}, f32[3,1024]{1,0:T(4,128)S(1)}, u32[]{:S(2)}, u32[]{:S(2)}) collective-permute-start(f32[3,1024]{1,0:T(4,128)S(1)} %bitcast.86), channel_id=1, source_target_pairs={{0,8},{8,16},{16,24},{1,9},{9,17},{17,25},{2,10},{10,18},{18,26},{... | collective-permute-start | bytes 36872 | tf_op jit(solution)/shard_map/ppermute | solution.py:286
  116.5 4.5 %all-to-all-done.4 = f32[32,8,192]{2,1,0:T(8,128)S(1)} async-done(((f32[32,8,192]{2,1,0:T(8,128)}), f32[32,8,192]{2,1,0:T(8,128)S(1)}, u32[]{:S(2)}, u32[]{:S(2)}) %all-to-all-start.4) | async-done | bytes 196640 | tf_op jit(solution)/shard_map/all_to_all | solution.py:342
  121.7 8.4 %shard_map.137 = (f32[8,192]{1,0:T(8,128)}, f32[256,192]{1,0:T(8,128)}) custom-call(s32[32]{0:T(128)} %reshape.97.idx_ref, f32[256,192]{1,0:T(8,128)} %bitcast.68, f32[8,4,192,192]{3,2,1,0:T(8,128)} %s_ref.9, f32[8,192,192]{2,1,0:T(8,128)} %bitcast.64, f32[8,192,1]{2,1,0:T(8,128)} %copy-done.1, f32[8,192]{1,0:T(8,128)} %get-tuple-element.42.v_ref), custom_call_target="tpu_custom_call" | custom-call | flops 2949120 | bytes 6094848 | tf_op jit(solution)/shard_map/pallas_call | solution.py:258
  130.2 2.6 %all-to-all-start.5 = ((f32[32,8,192]{2,1,0:T(8,128)}), f32[32,8,192]{2,1,0:T(8,128)S(1)}, u32[]{:S(2)}, u32[]{:S(2)}) async-start(f32[32,8,192]{2,1,0:T(8,128)} %bitcast.71), calls=%async_computation.5 | async-start | bytes 524288 | tf_op jit(solution)/shard_map/all_to_all | solution.py:342
  134.8 8.3 %all-to-all-done.5 = f32[32,8,192]{2,1,0:T(8,128)S(1)} async-done(((f32[32,8,192]{2,1,0:T(8,128)}), f32[32,8,192]{2,1,0:T(8,128)S(1)}, u32[]{:S(2)}, u32[]{:S(2)}) %all-to-all-start.5) | async-done | bytes 196640 | tf_op jit(solution)/shard_map/all_to_all | solution.py:342
  143.8 8.3 %shard_map.138 = (f32[8,192]{1,0:T(8,128)}, f32[256,192]{1,0:T(8,128)}) custom-call(s32[32]{0:T(128)} %reshape.97.idx_ref, f32[256,192]{1,0:T(8,128)} %bitcast.66, f32[8,4,192,192]{3,2,1,0:T(8,128)} %s_ref.9, f32[8,192,192]{2,1,0:T(8,128)} %bitcast.65, f32[8,192,1]{2,1,0:T(8,128)} %copy-done.1, f32[8,192]{1,0:T(8,128)} %get-tuple-element.44.v_ref), custom_call_target="tpu_custom_call" | custom-call | flops 2949120 | bytes 6094848 | tf_op jit(solution)/shard_map/pallas_call | solution.py:258
  (87 shorter events, 13.7 us)
Async XLA Ops:
  0.6 34.0 %copy-start = (f32[192,192]{1,0:T(8,128)S(1)}, f32[192,192]{1,0:T(8,128)}, u32[]{:S(2)}) copy-start(f32[192,192]{1,0:T(8,128)} %param.16) | copy-start | bytes 442372
  13.4 9.2 %copy-start.10 = (s32[16384]{0:T(1024)S(1)}, s32[16384]{0:T(1024)}, u32[]{:S(2)}) copy-start(s32[16384]{0:T(1024)} %param.14) | copy-start | bytes 196612
  13.4 9.3 %copy-start.21 = (f32[384]{0:T(512)S(1)}, f32[384]{0:T(512)}, u32[]{:S(2)}) copy-start(f32[384]{0:T(512)} %param.15) | copy-start | bytes 4612
  13.4 9.3 %copy-start.22 = (s32[8,4]{0,1:T(4,128)S(1)}, s32[8,4]{0,1:T(4,128)}, u32[]{:S(2)}) copy-start(s32[8,4]{0,1:T(4,128)} %param.18) | copy-start | bytes 388
  13.4 10.1 %copy-start.2 = (f32[8,192,192]{2,1,0:T(8,128)S(1)}, f32[8,192,192]{2,1,0:T(8,128)}, u32[]{:S(2)}) copy-start(f32[8,192,192]{2,1,0:T(8,128)} %param.19) | copy-start | bytes 3538948
  15.3 19.1 %all-to-all-start = ((f32[32,4,384]{2,1,0:T(4,128)}), f32[32,4,384]{2,1,0:T(4,128)S(1)}, u32[]{:S(2)}, u32[]{:S(2)}) async-start(f32[32,4,384]{2,1,0:T(4,128)} %bitcast.14), calls=%async_computation | async-start | bytes 393216 | tf_op jit(solution)/shard_map/all_to_all | solution.py:312
  36.6 13.9 %copy-start.9 = (f32[8,192]{1,0:T(8,128)}, f32[8,192]{1,0:T(8,128)S(1)}, u32[]{:S(2)}) copy-start(f32[8,192]{1,0:T(8,128)S(1)} %bitcast_multiply_fusion.v_ref) | copy-start | bytes 18436
  37.3 16.2 %all-to-all-start.1 = ((f32[32,8,192]{2,1,0:T(8,128)}), f32[32,8,192]{2,1,0:T(8,128)S(1)}, u32[]{:S(2)}, u32[]{:S(2)}) async-start(f32[32,8,192]{2,1,0:T(8,128)} %tile.2), calls=%async_computation.1 | async-start | bytes 524288 | tf_op jit(solution)/shard_map/all_to_all | solution.py:342
  62.6 13.2 %all-to-all-start.2 = ((f32[32,8,192]{2,1,0:T(8,128)}), f32[32,8,192]{2,1,0:T(8,128)S(1)}, u32[]{:S(2)}, u32[]{:S(2)}) async-start(f32[32,8,192]{2,1,0:T(8,128)} %bitcast.74), calls=%async_computation.2 | async-start | bytes 524288 | tf_op jit(solution)/shard_map/all_to_all | solution.py:342
  84.7 13.2 %all-to-all-start.3 = ((f32[32,8,192]{2,1,0:T(8,128)}), f32[32,8,192]{2,1,0:T(8,128)S(1)}, u32[]{:S(2)}, u32[]{:S(2)}) async-start(f32[32,8,192]{2,1,0:T(8,128)} %bitcast.72), calls=%async_computation.3 | async-start | bytes 524288 | tf_op jit(solution)/shard_map/all_to_all | solution.py:342
  87.5 7.4 %copy-start.15 = (f32[48,128]{1,0:T(8,128)S(1)}, f32[48,128]{1,0:T(8,128)}, u32[]{:S(2)}) copy-start(f32[48,128]{1,0:T(8,128)} %get-tuple-element.29) | copy-start | bytes 73732
  87.5 7.4 %copy-start.16 = (f32[48,128]{1,0:T(8,128)S(1)}, f32[48,128]{1,0:T(8,128)}, u32[]{:S(2)}) copy-start(f32[48,128]{1,0:T(8,128)} %get-tuple-element.33) | copy-start | bytes 73732
  87.6 7.4 %copy-start.17 = (f32[48,128]{1,0:T(8,128)S(1)}, f32[48,128]{1,0:T(8,128)}, u32[]{:S(2)}) copy-start(f32[48,128]{1,0:T(8,128)} %get-tuple-element.30) | copy-start | bytes 73732
  87.6 7.4 %copy-start.18 = (f32[48,128]{1,0:T(8,128)S(1)}, f32[48,128]{1,0:T(8,128)}, u32[]{:S(2)}) copy-start(f32[48,128]{1,0:T(8,128)} %get-tuple-element.34) | copy-start | bytes 73732
  87.6 7.4 %copy-start.19 = (f32[48,128]{1,0:T(8,128)S(1)}, f32[48,128]{1,0:T(8,128)}, u32[]{:S(2)}) copy-start(f32[48,128]{1,0:T(8,128)} %get-tuple-element.31) | copy-start | bytes 73732
  87.6 7.4 %copy-start.20 = (f32[48,128]{1,0:T(8,128)S(1)}, f32[48,128]{1,0:T(8,128)}, u32[]{:S(2)}) copy-start(f32[48,128]{1,0:T(8,128)} %get-tuple-element.35) | copy-start | bytes 73732
  106.9 14.1 %all-to-all-start.4 = ((f32[32,8,192]{2,1,0:T(8,128)}), f32[32,8,192]{2,1,0:T(8,128)S(1)}, u32[]{:S(2)}, u32[]{:S(2)}) async-start(f32[32,8,192]{2,1,0:T(8,128)} %bitcast.73), calls=%async_computation.4 | async-start | bytes 524288 | tf_op jit(solution)/shard_map/all_to_all | solution.py:342
  110.7 22.9 %collective-permute-start.1 = (f32[3,1024]{1,0:T(4,128)S(1)}, f32[3,1024]{1,0:T(4,128)S(1)}, u32[]{:S(2)}, u32[]{:S(2)}) collective-permute-start(f32[3,1024]{1,0:T(4,128)S(1)} %bitcast.85), channel_id=1, source_target_pairs={{8,0},{16,8},{24,16},{9,1},{17,9},{25,17},{10,2},{18,10},{26,18},{... | collective-permute-start | bytes 36872 | tf_op jit(solution)/shard_map/ppermute | solution.py:286
  112.0 21.6 %collective-permute-start = (f32[3,1024]{1,0:T(4,128)S(1)}, f32[3,1024]{1,0:T(4,128)S(1)}, u32[]{:S(2)}, u32[]{:S(2)}) collective-permute-start(f32[3,1024]{1,0:T(4,128)S(1)} %bitcast.86), channel_id=1, source_target_pairs={{0,8},{8,16},{16,24},{1,9},{9,17},{17,25},{2,10},{10,18},{18,26},{... | collective-permute-start | bytes 36872 | tf_op jit(solution)/shard_map/ppermute | solution.py:286
  121.7 11.0 %copy-start.11 = (f32[3,4096]{1,0:T(4,128)S(1)}, f32[3,4096]{1,0:T(4,128)}, u32[]{:S(2)}) copy-start(f32[3,4096]{1,0:T(4,128)} %get-tuple-element.25) | copy-start | bytes 147460
  121.7 11.0 %copy-start.12 = (f32[3,4096]{1,0:T(4,128)S(1)}, f32[3,4096]{1,0:T(4,128)}, u32[]{:S(2)}) copy-start(f32[3,4096]{1,0:T(4,128)} %get-tuple-element.26) | copy-start | bytes 147460
  121.7 11.0 %copy-start.13 = (f32[3,4096]{1,0:T(4,128)S(1)}, f32[3,4096]{1,0:T(4,128)}, u32[]{:S(2)}) copy-start(f32[3,4096]{1,0:T(4,128)} %get-tuple-element.27) | copy-start | bytes 147460
  121.7 11.1 %copy-start.14 = (f32[3,4096]{1,0:T(4,128)S(1)}, f32[3,4096]{1,0:T(4,128)}, u32[]{:S(2)}) copy-start(f32[3,4096]{1,0:T(4,128)} %get-tuple-element.28) | copy-start | bytes 147460
  130.2 13.0 %all-to-all-start.5 = ((f32[32,8,192]{2,1,0:T(8,128)}), f32[32,8,192]{2,1,0:T(8,128)S(1)}, u32[]{:S(2)}, u32[]{:S(2)}) async-start(f32[32,8,192]{2,1,0:T(8,128)} %bitcast.71), calls=%async_computation.5 | async-start | bytes 524288 | tf_op jit(solution)/shard_map/all_to_all | solution.py:342
  (7 other events, 7.5 us)

commit v7 on v5

--- a/solution.py
+++ b/solution.py
@@ -48,9 +48,11 @@
     return spring, terms
 
 
-def stress_kernel(q_ref, e_ref, m_ref, out_ref, *, groups, rows):
+def stress_kernel(slab_ref, q_ref, e_ref, m_ref, send_ref, acc_ref, *, groups, rows):
     count = q_ref.shape[1]
-    out_ref[...] = jnp.zeros_like(out_ref)
+    n_dev = send_ref.shape[0]
+    n_rad = groups // 3
+    acc_ref[...] = jnp.zeros_like(acc_ref)
     low_iota = lax.broadcasted_iota(jnp.int32, (128, STRESS_CHUNK), 0)
     row_iota = lax.broadcasted_iota(jnp.int32, (rows, STRESS_CHUNK), 0)
     zero = jnp.zeros((), jnp.bfloat16)
@@ -73,10 +75,21 @@
             ],
             axis=0,
         )
-        out_ref[...] += lax.dot_general(spread, low, nt_dims, preferred_element_type=jnp.float32)
+        acc_ref[...] += lax.dot_general(spread, low, nt_dims, preferred_element_type=jnp.float32)
         return carry
 
     lax.fori_loop(0, count // STRESS_CHUNK, body, 0)
+    send_ref[...] = jnp.zeros_like(send_ref)
+    slab = slab_ref[0]
+    for kind in range(3):
+        target = slab - 1 + kind
+
+        @pl.when(jnp.logical_and(target >= 0, target * n_rad < n_dev))
+        def _():
+            for r in range(n_rad):
+                for c in range(4):
+                    start = c * rows + kind * groups + r * 3
+                    send_ref[target * n_rad + r, c * 3 : c * 3 + 3, :] = acc_ref[start : start + 3, :]
 
 
 def update_kernel(
@@ -155,19 +168,47 @@
     lax.fori_loop(0, count // CHUNK, body, start_ref[...])
 
 
-def stress_partials(q_state, element, migration, slab_elems):
+def stress_partials(slab, q_state, element, migration, slab_elems, n_dev):
     groups = slab_elems // 128
     rows = round_up(3 * groups, 16)
     count = q_state.shape[1]
-    out = pl.pallas_call(
+    vmem = pl.BlockSpec(memory_space=pltpu.VMEM)
+    return pl.pallas_call(
         functools.partial(stress_kernel, groups=groups, rows=rows),
-        out_shape=jax.ShapeDtypeStruct((4 * rows, 128), jnp.float32),
+        out_shape=jax.ShapeDtypeStruct((n_dev, 12, 128), jnp.float32),
+        in_specs=[pl.BlockSpec(memory_space=pltpu.SMEM)] + [vmem] * 3,
+        out_specs=vmem,
+        scratch_shapes=[pltpu.VMEM((4 * rows, 128), jnp.float32)],
         cost_estimate=pl.CostEstimate(
             flops=2 * 3 * 4 * rows * 128 * count, transcendentals=0, bytes_accessed=20 * count
         ),
-    )(q_state, element.reshape(1, -1), migration.reshape(1, -1))
-    total = out.reshape(4, rows, 128)[:, : 3 * groups].reshape(4, 3 * slab_elems)
-    return total
+    )(slab, q_state, element.reshape(1, -1), migration.reshape(1, -1))
+
+
+def first_kernel(pt_ref, ft_ref, vout_ref, send_ref):
+    own = vout_ref.shape[0]
+    rows = [
+        damping * jnp.sum(pt_ref[b] * ft_ref[:, b : b + 1], axis=0, keepdims=True)
+        for b in range(own)
+    ]
+    fresh = jnp.concatenate(rows, axis=0)
+    vout_ref[...] = fresh
+    for k in range(send_ref.shape[0] // own):
+        send_ref[k * own : (k + 1) * own, :] = fresh
+
+
+def first_velocity(transposed, force_t, copies):
+    own, size = transposed.shape[0], transposed.shape[1]
+    return pl.pallas_call(
+        first_kernel,
+        out_shape=(
+            jax.ShapeDtypeStruct((own, size), jnp.float32),
+            jax.ShapeDtypeStruct((copies * own, size), jnp.float32),
+        ),
+        cost_estimate=pl.CostEstimate(
+            flops=2 * transposed.size, transcendentals=0, bytes_accessed=4 * transposed.size
+        ),
+    )(transposed, force_t)
 
 
 def update_and_pack(q_state, increments, element, migration, table, capacity):
@@ -293,13 +334,11 @@
     slab = lax.axis_index("slab")
 
     n_rad = lax.axis_size("rad")
-    near = stress_partials(q_state, element, migration, slab_elems)
-    near = near.reshape(4, 3, n_rad, slab_elems // n_rad).transpose(1, 2, 0, 3)
-    spread = jnp.zeros((n_slab + 2,) + near.shape[1:], jnp.float32)
-    spread = lax.dynamic_update_slice(spread, near, (slab, 0, 0, 0))
-    spread = spread[1 : n_slab + 1].reshape((n_slab * n_rad,) + near.shape[2:])
-    received = lax.all_to_all(spread, ("slab", "rad"), 0, 0, tiled=True)
-    sums = jnp.sum(received, axis=0)
+    send = stress_partials(
+        slab.reshape(1).astype(jnp.int32), q_state, element, migration, slab_elems, n_slab * n_rad
+    )
+    received = lax.all_to_all(send, ("slab", "rad"), 0, 0, tiled=True)
+    sums = jnp.sum(received, axis=0).reshape(4, slab_elems // n_rad)
     element_stress = sums / volume
 
     q_next, upward, downward = update_and_pack(
@@ -325,8 +364,7 @@
     where_read = ((slab - 1) * slab_blocks + pattern).reshape(-1).astype(jnp.int32)
     transposed = jnp.swapaxes(preconditioner, 1, 2)
     force_t = force.T
-    velocity = damping * precondition(force)
-    send = jnp.tile(velocity, (copies, 1))
+    velocity, send = first_velocity(transposed, force_t, copies)
     for sweep_index in range(1, ITERS):
         gathered = lax.all_to_all(send, ("slab", "rad"), 0, 0, tiled=True)
         velocity, send = sweep(

time: 138 us -> 137 us (level)
  local copies, waits for them, and re-layouts: 11 us -> 7.64 us
  Pallas kernels: 68.9 us -> 71.4 us
    pallas_call x0 -> x1, Pallas kernels: none -> 2.42 us  [first_velocity(): pl.pallas_call(first_kernel, out_shape=(jax.ShapeDtypeStruct((own, size),...]
    slice x2 -> x0, local copies, waits for them, and re-layouts: 1.74 us -> none  [the longest x1 1.05 us: stress_partials(): total = out.reshape(4, rows, 128)[:, :3 * groups].reshape(4, 3 * slab_elems)]
    dot_general x1 -> x0, matrix products: 1.39 us -> none  [precondition(): return jnp.einsum('bij,bj->bi', preconditioner, vector, precision=highest)]
    unnamed x51 -> x49, local copies, waits for them, and re-layouts: 6.02 us -> 6.02 us
  transfers between devices with their start and end apart: 8 -> 8, of which waited for: 5 -> 5; matrix products, arithmetic and copies ran while one was open for 6% -> 5% of each run, Pallas kernels for 25% -> 25%
where the time goes in v7:
time: 137 us; the launch traced here: 136 us
  Pallas kernels  71.4 us (52%)
  starting transfers between devices  30.9 us (23%)
  waiting for transfers between devices  21 us (15%)
  local copies, waits for them, and re-layouts  7.64 us (6%)
  other arithmetic  3.24 us (2%)
    pallas_call x4, Pallas kernels, update_and_pack(): pl.pallas_call(functools.partial(update_kernel, groups16=groups16, slots1...  29.4 us
    pallas_call x5, Pallas kernels, sweep(): pl.pallas_call(sweep_kernel, out_shape=(jax.ShapeDtypeStruct(velocity.sha...  26.7 us
    all_to_all x5, waiting for transfers between devices, body(): gathered = lax.all_to_all(send, ('slab', 'rad'), 0, 0, tiled=True)  21 us
    all_to_all x5, starting transfers between devices, body(): gathered = lax.all_to_all(send, ('slab', 'rad'), 0, 0, tiled=True)  17.7 us
    pallas_call x1, Pallas kernels, stress_partials(): pl.pallas_call(functools.partial(stress_kernel, groups=groups, rows=rows)...  12.9 us
    all_to_all x1, starting transfers between devices, body(): received = lax.all_to_all(send, ('slab', 'rad'), 0, 0, tiled=True)  7.3 us
    unnamed x49, local copies, waits for them, and re-layouts  6.02 us
    ppermute x2, starting transfers between devices, passed_along(): return lax.ppermute(array, axis, pairs)  5.84 us
  transfers between devices with their start and end apart: 8, of which 5 were waited for; matrix products, arithmetic and copies ran while one was open for 5% of the time, Pallas kernels for 25%

profile of v7, /device:TPU:0, one launch (start us, length us, event | category | flops | bytes accessed | tf_op | source)
XLA Modules:
  0.0 136.4 jit_solution(7175876881803904487)
XLA Ops:
  0.7 12.9 %shard_map.133 = f32[32,12,128]{2,1,0:T(8,128)} custom-call(s32[1]{0:T(128)} %bitcast.12.slab_ref, f32[3,16384]{1,0:T(4,128)} %q_ref.9, s32[1,16384]{1,0:T(1,128)} %bitcast.84, s32[1,16384]{1,0:T(1,128)} %bitcast.73), custom_call_target="tpu_custom_call" | custom-call | flops 4026531840 | bytes 327680 | tf_op jit(solution)/shard_map/pallas_call | solution.py:176
  13.6 7.3 %all-to-all-start = ((f32[32,12,128]{2,1,0:T(8,128)}), f32[32,12,128]{2,1,0:T(8,128)S(1)}, u32[]{:S(2)}, u32[]{:S(2)}) async-start(f32[32,12,128]{2,1,0:T(8,128)} %shard_map.133), calls=%async_computation | async-start | bytes 524288 | tf_op jit(solution)/shard_map/all_to_all | solution.py:340
  21.1 1.8 %copy.52 = f32[8,192,192]{1,2,0:T(8,128)} copy(f32[8,192,192]{2,1,0:T(8,128)S(1)} %copy-done.1) | data formatting | bytes 2359296 | tf_op args[9]
  25.3 7.3 %shard_map.129 = (f32[3,4096]{1,0:T(4,128)}, f32[48,128]{1,0:T(8,128)}, f32[48,128]{1,0:T(8,128)}) custom-call(f32[3,16384]{1,0:T(4,128)} %q_ref.9, f32[3,16384]{1,0:T(4,128)} %inc_ref.7, s32[1,16384]{1,0:T(1,128)} %bitcast.85, s32[1,16384]{1,0:T(1,128)} %bitcast.74, bf16[160,384]{1,0:T(8,128)(2,1)} %pad_maximum_fusion.1.tab_ref, ...), custom_call_target="tpu_custom_call" | custom-call | flops 6442450944 | bytes 163840 | tf_op jit(solution)/shard_map/pallas_call | solution.py:236
  34.1 2.4 %shard_map.134 = (f32[8,192]{1,0:T(8,128)}, f32[256,192]{1,0:T(8,128)}) custom-call(f32[8,192,192]{2,1,0:T(8,128)} %bitcast.55, f32[192,8]{1,0:T(8,128)} %convolution_bitcast_fusion.ft_ref), custom_call_target="tpu_custom_call" | custom-call | flops 589824 | bytes 1179648 | tf_op jit(solution)/shard_map/pallas_call | solution.py:202
  36.5 5.8 %all-to-all-start.1 = ((f32[32,8,192]{2,1,0:T(8,128)}), f32[32,8,192]{2,1,0:T(8,128)S(1)}, u32[]{:S(2)}, u32[]{:S(2)}) async-start(f32[32,8,192]{2,1,0:T(8,128)} %bitcast.70), calls=%async_computation.1 | async-start | bytes 524288 | tf_op jit(solution)/shard_map/all_to_all | solution.py:369
  42.3 7.3 %shard_map.130 = (f32[3,4096]{1,0:T(4,128)}, f32[48,128]{1,0:T(8,128)}, f32[48,128]{1,0:T(8,128)}) custom-call(f32[3,16384]{1,0:T(4,128)} %q_ref.9, f32[3,16384]{1,0:T(4,128)} %inc_ref.7, s32[1,16384]{1,0:T(1,128)} %bitcast.86, s32[1,16384]{1,0:T(1,128)} %bitcast.75, bf16[160,384]{1,0:T(8,128)(2,1)} %pad_maximum_fusion.1.tab_ref, ...), custom_call_target="tpu_custom_call" | custom-call | flops 6442450944 | bytes 163840 | tf_op jit(solution)/shard_map/pallas_call | solution.py:236
  49.7 3.0 %all-to-all-done.1 = f32[32,8,192]{2,1,0:T(8,128)S(1)} async-done(((f32[32,8,192]{2,1,0:T(8,128)}), f32[32,8,192]{2,1,0:T(8,128)S(1)}, u32[]{:S(2)}, u32[]{:S(2)}) %all-to-all-start.1) | async-done | bytes 196640 | tf_op jit(solution)/shard_map/all_to_all | solution.py:369
  53.4 5.3 %shard_map.135 = (f32[8,192]{1,0:T(8,128)}, f32[256,192]{1,0:T(8,128)}) custom-call(s32[32]{0:T(128)} %reshape.94.idx_ref, f32[256,192]{1,0:T(8,128)} %bitcast.64, f32[8,4,192,192]{3,2,1,0:T(8,128)} %s_ref.9, f32[8,192,192]{2,1,0:T(8,128)} %bitcast.56, f32[192,8]{1,0:T(8,128)} %convolution_bitcast_fusion.ft_ref, f32[8,192]{1,0:T(8,128)} %get-tuple-element.40.v_ref), custom_call_target="tpu_custom_call" | custom-call | flops 2949120 | bytes 6094848 | tf_op jit(solution)/shard_map/pallas_call | solution.py:297
  58.8 2.8 %all-to-all-start.2 = ((f32[32,8,192]{2,1,0:T(8,128)}), f32[32,8,192]{2,1,0:T(8,128)S(1)}, u32[]{:S(2)}, u32[]{:S(2)}) async-start(f32[32,8,192]{2,1,0:T(8,128)} %bitcast.69), calls=%async_computation.2 | async-start | bytes 524288 | tf_op jit(solution)/shard_map/all_to_all | solution.py:369
  61.6 7.3 %shard_map.131 = (f32[3,4096]{1,0:T(4,128)}, f32[48,128]{1,0:T(8,128)}, f32[48,128]{1,0:T(8,128)}) custom-call(f32[3,16384]{1,0:T(4,128)} %q_ref.9, f32[3,16384]{1,0:T(4,128)} %inc_ref.7, s32[1,16384]{1,0:T(1,128)} %bitcast.87, s32[1,16384]{1,0:T(1,128)} %bitcast.76, bf16[160,384]{1,0:T(8,128)(2,1)} %pad_maximum_fusion.1.tab_ref, ...), custom_call_target="tpu_custom_call" | custom-call | flops 6442450944 | bytes 163840 | tf_op jit(solution)/shard_map/pallas_call | solution.py:236
  68.9 3.0 %all-to-all-done.2 = f32[32,8,192]{2,1,0:T(8,128)S(1)} async-done(((f32[32,8,192]{2,1,0:T(8,128)}), f32[32,8,192]{2,1,0:T(8,128)S(1)}, u32[]{:S(2)}, u32[]{:S(2)}) %all-to-all-start.2) | async-done | bytes 196640 | tf_op jit(solution)/shard_map/all_to_all | solution.py:369
  72.7 5.3 %shard_map.136 = (f32[8,192]{1,0:T(8,128)}, f32[256,192]{1,0:T(8,128)}) custom-call(s32[32]{0:T(128)} %reshape.94.idx_ref, f32[256,192]{1,0:T(8,128)} %bitcast.65, f32[8,4,192,192]{3,2,1,0:T(8,128)} %s_ref.9, f32[8,192,192]{2,1,0:T(8,128)} %bitcast.57, f32[192,8]{1,0:T(8,128)} %convolution_bitcast_fusion.ft_ref, f32[8,192]{1,0:T(8,128)} %get-tuple-element.42.v_ref), custom_call_target="tpu_custom_call" | custom-call | flops 2949120 | bytes 6094848 | tf_op jit(solution)/shard_map/pallas_call | solution.py:297
  78.0 2.8 %all-to-all-start.3 = ((f32[32,8,192]{2,1,0:T(8,128)}), f32[32,8,192]{2,1,0:T(8,128)S(1)}, u32[]{:S(2)}, u32[]{:S(2)}) async-start(f32[32,8,192]{2,1,0:T(8,128)} %bitcast.67), calls=%async_computation.3 | async-start | bytes 524288 | tf_op jit(solution)/shard_map/all_to_all | solution.py:369
  80.8 7.4 %shard_map.132 = (f32[3,4096]{1,0:T(4,128)}, f32[48,128]{1,0:T(8,128)}, f32[48,128]{1,0:T(8,128)}) custom-call(f32[3,16384]{1,0:T(4,128)} %q_ref.9, f32[3,16384]{1,0:T(4,128)} %inc_ref.7, s32[1,16384]{1,0:T(1,128)} %bitcast.88, s32[1,16384]{1,0:T(1,128)} %bitcast.77, bf16[160,384]{1,0:T(8,128)(2,1)} %pad_maximum_fusion.1.tab_ref, ...), custom_call_target="tpu_custom_call" | custom-call | flops 6442450944 | bytes 163840 | tf_op jit(solution)/shard_map/pallas_call | solution.py:236
  89.0 2.1 %all-to-all-done.3 = f32[32,8,192]{2,1,0:T(8,128)S(1)} async-done(((f32[32,8,192]{2,1,0:T(8,128)}), f32[32,8,192]{2,1,0:T(8,128)S(1)}, u32[]{:S(2)}, u32[]{:S(2)}) %all-to-all-start.3) | async-done | bytes 196640 | tf_op jit(solution)/shard_map/all_to_all | solution.py:369
  91.9 5.3 %shard_map.137 = (f32[8,192]{1,0:T(8,128)}, f32[256,192]{1,0:T(8,128)}) custom-call(s32[32]{0:T(128)} %reshape.94.idx_ref, f32[256,192]{1,0:T(8,128)} %bitcast.62, f32[8,4,192,192]{3,2,1,0:T(8,128)} %s_ref.9, f32[8,192,192]{2,1,0:T(8,128)} %bitcast.58, f32[192,8]{1,0:T(8,128)} %convolution_bitcast_fusion.ft_ref, f32[8,192]{1,0:T(8,128)} %get-tuple-element.44.v_ref), custom_call_target="tpu_custom_call" | custom-call | flops 2949120 | bytes 6094848 | tf_op jit(solution)/shard_map/pallas_call | solution.py:297
  97.2 3.7 %all-to-all-start.4 = ((f32[32,8,192]{2,1,0:T(8,128)}), f32[32,8,192]{2,1,0:T(8,128)S(1)}, u32[]{:S(2)}, u32[]{:S(2)}) async-start(f32[32,8,192]{2,1,0:T(8,128)} %bitcast.68), calls=%async_computation.4 | async-start | bytes 524288 | tf_op jit(solution)/shard_map/all_to_all | solution.py:369
  102.3 4.5 %collective-permute-start = (f32[3,1024]{1,0:T(4,128)S(1)}, f32[3,1024]{1,0:T(4,128)S(1)}, u32[]{:S(2)}, u32[]{:S(2)}) collective-permute-start(f32[3,1024]{1,0:T(4,128)S(1)} %bitcast.81), channel_id=1, source_target_pairs={{0,8},{8,16},{16,24},{1,9},{9,17},{17,25},{2,10},{10,18},{18,26},{... | collective-permute-start | bytes 36872 | tf_op jit(solution)/shard_map/ppermute | solution.py:316
  106.8 4.5 %all-to-all-done.4 = f32[32,8,192]{2,1,0:T(8,128)S(1)} async-done(((f32[32,8,192]{2,1,0:T(8,128)}), f32[32,8,192]{2,1,0:T(8,128)S(1)}, u32[]{:S(2)}, u32[]{:S(2)}) %all-to-all-start.4) | async-done | bytes 196640 | tf_op jit(solution)/shard_map/all_to_all | solution.py:369
  112.0 5.4 %shard_map.138 = (f32[8,192]{1,0:T(8,128)}, f32[256,192]{1,0:T(8,128)}) custom-call(s32[32]{0:T(128)} %reshape.94.idx_ref, f32[256,192]{1,0:T(8,128)} %bitcast.63, f32[8,4,192,192]{3,2,1,0:T(8,128)} %s_ref.9, f32[8,192,192]{2,1,0:T(8,128)} %bitcast.59, f32[192,8]{1,0:T(8,128)} %convolution_bitcast_fusion.ft_ref, f32[8,192]{1,0:T(8,128)} %get-tuple-element.46.v_ref), custom_call_target="tpu_custom_call" | custom-call | flops 2949120 | bytes 6094848 | tf_op jit(solution)/shard_map/pallas_call | solution.py:297
  117.4 2.6 %all-to-all-start.5 = ((f32[32,8,192]{2,1,0:T(8,128)}), f32[32,8,192]{2,1,0:T(8,128)S(1)}, u32[]{:S(2)}, u32[]{:S(2)}) async-start(f32[32,8,192]{2,1,0:T(8,128)} %bitcast.66), calls=%async_computation.5 | async-start | bytes 524288 | tf_op jit(solution)/shard_map/all_to_all | solution.py:369
  122.0 8.3 %all-to-all-done.5 = f32[32,8,192]{2,1,0:T(8,128)S(1)} async-done(((f32[32,8,192]{2,1,0:T(8,128)}), f32[32,8,192]{2,1,0:T(8,128)S(1)}, u32[]{:S(2)}, u32[]{:S(2)}) %all-to-all-start.5) | async-done | bytes 196640 | tf_op jit(solution)/shard_map/all_to_all | solution.py:369
  131.1 5.3 %shard_map.139 = (f32[8,192]{1,0:T(8,128)}, f32[256,192]{1,0:T(8,128)}) custom-call(s32[32]{0:T(128)} %reshape.94.idx_ref, f32[256,192]{1,0:T(8,128)} %bitcast.61, f32[8,4,192,192]{3,2,1,0:T(8,128)} %s_ref.9, f32[8,192,192]{2,1,0:T(8,128)} %bitcast.60, f32[192,8]{1,0:T(8,128)} %convolution_bitcast_fusion.ft_ref, f32[8,192]{1,0:T(8,128)} %get-tuple-element.48.v_ref), custom_call_target="tpu_custom_call" | custom-call | flops 2949120 | bytes 6094848 | tf_op jit(solution)/shard_map/pallas_call | solution.py:297
  (77 shorter events, 11.6 us)
Async XLA Ops:
  0.6 32.2 %copy-start = (f32[192,192]{1,0:T(8,128)S(1)}, f32[192,192]{1,0:T(8,128)}, u32[]{:S(2)}) copy-start(f32[192,192]{1,0:T(8,128)} %param.16) | copy-start | bytes 442372
  0.7 20.3 %copy-start.8 = (s32[16384]{0:T(1024)S(1)}, s32[16384]{0:T(1024)}, u32[]{:S(2)}) copy-start(s32[16384]{0:T(1024)} %param.14) | copy-start | bytes 196612
  0.7 20.3 %copy-start.19 = (f32[384]{0:T(512)S(1)}, f32[384]{0:T(512)}, u32[]{:S(2)}) copy-start(f32[384]{0:T(512)} %param.15) | copy-start | bytes 4612
  0.7 20.4 %copy-start.1 = (f32[8,192,192]{2,1,0:T(8,128)S(1)}, f32[8,192,192]{2,1,0:T(8,128)}, u32[]{:S(2)}) copy-start(f32[8,192,192]{2,1,0:T(8,128)} %param.19) | copy-start | bytes 3538948
  13.6 19.0 %all-to-all-start = ((f32[32,12,128]{2,1,0:T(8,128)}), f32[32,12,128]{2,1,0:T(8,128)S(1)}, u32[]{:S(2)}, u32[]{:S(2)}) async-start(f32[32,12,128]{2,1,0:T(8,128)} %shard_map.133), calls=%async_computation | async-start | bytes 524288 | tf_op jit(solution)/shard_map/all_to_all | solution.py:340
  21.1 1.8 %copy-start.20 = (s32[8,4]{0,1:T(4,128)S(1)}, s32[8,4]{0,1:T(4,128)}, u32[]{:S(2)}) copy-start(s32[8,4]{0,1:T(4,128)} %param.18) | copy-start | bytes 388
  21.1 2.4 %copy-start.7 = (f32[5,3072]{1,0:T(8,128)S(1)}, f32[5,3072]{1,0:T(8,128)}, u32[]{:S(2)}) copy-start(f32[5,3072]{1,0:T(8,128)} %param.12) | copy-start | bytes 184324
  36.5 16.2 %all-to-all-start.1 = ((f32[32,8,192]{2,1,0:T(8,128)}), f32[32,8,192]{2,1,0:T(8,128)S(1)}, u32[]{:S(2)}, u32[]{:S(2)}) async-start(f32[32,8,192]{2,1,0:T(8,128)} %bitcast.70), calls=%async_computation.1 | async-start | bytes 524288 | tf_op jit(solution)/shard_map/all_to_all | solution.py:369
  58.8 13.2 %all-to-all-start.2 = ((f32[32,8,192]{2,1,0:T(8,128)}), f32[32,8,192]{2,1,0:T(8,128)S(1)}, u32[]{:S(2)}, u32[]{:S(2)}) async-start(f32[32,8,192]{2,1,0:T(8,128)} %bitcast.69), calls=%async_computation.2 | async-start | bytes 524288 | tf_op jit(solution)/shard_map/all_to_all | solution.py:369
  78.0 13.2 %all-to-all-start.3 = ((f32[32,8,192]{2,1,0:T(8,128)}), f32[32,8,192]{2,1,0:T(8,128)S(1)}, u32[]{:S(2)}, u32[]{:S(2)}) async-start(f32[32,8,192]{2,1,0:T(8,128)} %bitcast.67), calls=%async_computation.3 | async-start | bytes 524288 | tf_op jit(solution)/shard_map/all_to_all | solution.py:369
  80.8 7.4 %copy-start.13 = (f32[48,128]{1,0:T(8,128)S(1)}, f32[48,128]{1,0:T(8,128)}, u32[]{:S(2)}) copy-start(f32[48,128]{1,0:T(8,128)} %get-tuple-element.31) | copy-start | bytes 73732
  80.8 7.4 %copy-start.14 = (f32[48,128]{1,0:T(8,128)S(1)}, f32[48,128]{1,0:T(8,128)}, u32[]{:S(2)}) copy-start(f32[48,128]{1,0:T(8,128)} %get-tuple-element.35) | copy-start | bytes 73732
  80.8 7.4 %copy-start.15 = (f32[48,128]{1,0:T(8,128)S(1)}, f32[48,128]{1,0:T(8,128)}, u32[]{:S(2)}) copy-start(f32[48,128]{1,0:T(8,128)} %get-tuple-element.32) | copy-start | bytes 73732
  80.8 7.4 %copy-start.16 = (f32[48,128]{1,0:T(8,128)S(1)}, f32[48,128]{1,0:T(8,128)}, u32[]{:S(2)}) copy-start(f32[48,128]{1,0:T(8,128)} %get-tuple-element.36) | copy-start | bytes 73732
  80.8 7.4 %copy-start.17 = (f32[48,128]{1,0:T(8,128)S(1)}, f32[48,128]{1,0:T(8,128)}, u32[]{:S(2)}) copy-start(f32[48,128]{1,0:T(8,128)} %get-tuple-element.33) | copy-start | bytes 73732
  80.8 7.4 %copy-start.18 = (f32[48,128]{1,0:T(8,128)S(1)}, f32[48,128]{1,0:T(8,128)}, u32[]{:S(2)}) copy-start(f32[48,128]{1,0:T(8,128)} %get-tuple-element.37) | copy-start | bytes 73732
  97.2 14.1 %all-to-all-start.4 = ((f32[32,8,192]{2,1,0:T(8,128)}), f32[32,8,192]{2,1,0:T(8,128)S(1)}, u32[]{:S(2)}, u32[]{:S(2)}) async-start(f32[32,8,192]{2,1,0:T(8,128)} %bitcast.68), calls=%async_computation.4 | async-start | bytes 524288 | tf_op jit(solution)/shard_map/all_to_all | solution.py:369
  100.9 19.8 %collective-permute-start.1 = (f32[3,1024]{1,0:T(4,128)S(1)}, f32[3,1024]{1,0:T(4,128)S(1)}, u32[]{:S(2)}, u32[]{:S(2)}) collective-permute-start(f32[3,1024]{1,0:T(4,128)S(1)} %bitcast.80), channel_id=1, source_target_pairs={{8,0},{16,8},{24,16},{9,1},{17,9},{25,17},{10,2},{18,10},{26,18},{... | collective-permute-start | bytes 36872 | tf_op jit(solution)/shard_map/ppermute | solution.py:316
  102.3 18.5 %collective-permute-start = (f32[3,1024]{1,0:T(4,128)S(1)}, f32[3,1024]{1,0:T(4,128)S(1)}, u32[]{:S(2)}, u32[]{:S(2)}) collective-permute-start(f32[3,1024]{1,0:T(4,128)S(1)} %bitcast.81), channel_id=1, source_target_pairs={{0,8},{8,16},{16,24},{1,9},{9,17},{17,25},{2,10},{10,18},{18,26},{... | collective-permute-start | bytes 36872 | tf_op jit(solution)/shard_map/ppermute | solution.py:316
  112.0 8.0 %copy-start.9 = (f32[3,4096]{1,0:T(4,128)S(1)}, f32[3,4096]{1,0:T(4,128)}, u32[]{:S(2)}) copy-start(f32[3,4096]{1,0:T(4,128)} %get-tuple-element.27) | copy-start | bytes 147460
  112.0 8.0 %copy-start.10 = (f32[3,4096]{1,0:T(4,128)S(1)}, f32[3,4096]{1,0:T(4,128)}, u32[]{:S(2)}) copy-start(f32[3,4096]{1,0:T(4,128)} %get-tuple-element.28) | copy-start | bytes 147460
  112.0 8.0 %copy-start.11 = (f32[3,4096]{1,0:T(4,128)S(1)}, f32[3,4096]{1,0:T(4,128)}, u32[]{:S(2)}) copy-start(f32[3,4096]{1,0:T(4,128)} %get-tuple-element.29) | copy-start | bytes 147460
  112.0 8.0 %copy-start.12 = (f32[3,4096]{1,0:T(4,128)S(1)}, f32[3,4096]{1,0:T(4,128)}, u32[]{:S(2)}) copy-start(f32[3,4096]{1,0:T(4,128)} %get-tuple-element.30) | copy-start | bytes 147460
  117.4 13.0 %all-to-all-start.5 = ((f32[32,8,192]{2,1,0:T(8,128)}), f32[32,8,192]{2,1,0:T(8,128)S(1)}, u32[]{:S(2)}, u32[]{:S(2)}) async-start(f32[32,8,192]{2,1,0:T(8,128)} %bitcast.66), calls=%async_computation.5 | async-start | bytes 524288 | tf_op jit(solution)/shard_map/all_to_all | solution.py:369
  (5 other events, 3.5 us)

commit v8 on v7

--- a/solution.py
+++ b/solution.py
@@ -267,23 +267,37 @@
     return q_next, unpack(up), unpack(down)
 
 
-def sweep_kernel(idx_ref, g_ref, s_ref, pt_ref, ft_ref, v_ref, vout_ref, send_ref):
-    total = g_ref.shape[0]
+def sweep_kernel(
+    idx_ref, g_hbm, s_hbm, pt_hbm, ft_ref, v_ref, vout_ref, send_ref, g_buf, s_buf, pt_buf, sems
+):
+    total = g_buf.shape[0]
     own = v_ref.shape[0]
-    width = s_ref.shape[1]
+    width = s_buf.shape[1]
+    g_copy = pltpu.make_async_copy(g_hbm, g_buf, sems.at[0])
+    g_copy.start()
+    s_copies = [pltpu.make_async_copy(s_hbm.at[b], s_buf.at[b], sems.at[1 + b]) for b in range(own)]
+    p_copies = [
+        pltpu.make_async_copy(pt_hbm.at[b], pt_buf.at[b], sems.at[1 + own + b]) for b in range(own)
+    ]
+    for b in range(own):
+        s_copies[b].start()
+        p_copies[b].start()
+    g_copy.wait()
     rows = []
     for b in range(own):
+        s_copies[b].wait()
         acc = None
         for n in range(width):
             w = idx_ref[b * width + n]
             inside = jnp.logical_and(w >= 0, w < total)
-            near = g_ref[pl.ds(jnp.clip(w, 0, total - 1), 1), :]
+            near = g_buf[pl.ds(jnp.clip(w, 0, total - 1), 1), :]
             near = jnp.where(inside, near, 0.0)
-            term = s_ref[b, n] * near
+            term = s_buf[b, n] * near
             acc = term if acc is None else acc + term
         image = jnp.sum(acc, axis=1, keepdims=True)
         rest = ft_ref[:, b : b + 1] - image
-        update = jnp.sum(pt_ref[b] * rest, axis=0, keepdims=True)
+        p_copies[b].wait()
+        update = jnp.sum(pt_buf[b] * rest, axis=0, keepdims=True)
         rows.append(v_ref[b : b + 1, :] + damping * update)
     fresh = jnp.concatenate(rows, axis=0)
     vout_ref[...] = fresh
@@ -294,21 +308,27 @@
 def sweep(where_read, gathered, stiffness, transposed, force_t, velocity, copies):
     own = velocity.shape[0]
     vmem = pl.BlockSpec(memory_space=pltpu.VMEM)
+    anywhere = pl.BlockSpec(memory_space=pl.ANY)
     return pl.pallas_call(
         sweep_kernel,
         out_shape=(
             jax.ShapeDtypeStruct(velocity.shape, jnp.float32),
             jax.ShapeDtypeStruct((copies * own, velocity.shape[1]), jnp.float32),
         ),
-        in_specs=[pl.BlockSpec(memory_space=pltpu.SMEM)] + [vmem] * 5,
+        in_specs=[pl.BlockSpec(memory_space=pltpu.SMEM), anywhere, anywhere, anywhere, vmem, vmem],
         out_specs=(vmem, vmem),
+        scratch_shapes=[
+            pltpu.VMEM(gathered.shape, jnp.float32),
+            pltpu.VMEM(stiffness.shape, jnp.float32),
+            pltpu.VMEM(transposed.shape, jnp.float32),
+            pltpu.SemaphoreType.DMA((1 + 2 * own,)),
+        ],
         cost_estimate=pl.CostEstimate(
             flops=2 * (stiffness.size + transposed.size),
             transcendentals=0,
             bytes_accessed=4 * (stiffness.size + transposed.size + gathered.size),
         ),
     )(where_read, gathered, stiffness, transposed, force_t, velocity)
-
 
 def passed_along(array, axis, by):
     size = lax.axis_size(axis)

time: 137 us -> 137 us (level)
  no operation moved by 1% of the time
where the time goes in v8:
time: 137 us; the launch traced here: 136 us
  Pallas kernels  71.3 us (52%)
  starting transfers between devices  30.9 us (23%)
  waiting for transfers between devices  21 us (15%)
  local copies, waits for them, and re-layouts  7.64 us (6%)
  other arithmetic  3.24 us (2%)
    pallas_call x4, Pallas kernels, update_and_pack(): pl.pallas_call(functools.partial(update_kernel, groups16=groups16, slots1...  29.4 us
    pallas_call x5, Pallas kernels, sweep(): pl.pallas_call(sweep_kernel, out_shape=(jax.ShapeDtypeStruct(velocity.sha...  26.5 us
    all_to_all x5, waiting for transfers between devices, body(): gathered = lax.all_to_all(send, ('slab', 'rad'), 0, 0, tiled=True)  21 us
    all_to_all x5, starting transfers between devices, body(): gathered = lax.all_to_all(send, ('slab', 'rad'), 0, 0, tiled=True)  17.8 us
    pallas_call x1, Pallas kernels, stress_partials(): pl.pallas_call(functools.partial(stress_kernel, groups=groups, rows=rows)...  12.9 us
    all_to_all x1, starting transfers between devices, body(): received = lax.all_to_all(send, ('slab', 'rad'), 0, 0, tiled=True)  7.3 us
    unnamed x49, local copies, waits for them, and re-layouts  6.02 us
    ppermute x2, starting transfers between devices, passed_along(): return lax.ppermute(array, axis, pairs)  5.84 us
  transfers between devices with their start and end apart: 8, of which 5 were waited for; matrix products, arithmetic and copies ran while one was open for 5% of the time, Pallas kernels for 25%

profile of v8, /device:TPU:0, one launch (start us, length us, event | category | flops | bytes accessed | tf_op | source)
XLA Modules:
  0.0 136.3 jit_solution(13421867227469774036)
XLA Ops:
  0.7 12.9 %shard_map.133 = f32[32,12,128]{2,1,0:T(8,128)} custom-call(s32[1]{0:T(128)} %bitcast.12.slab_ref, f32[3,16384]{1,0:T(4,128)} %q_ref.9, s32[1,16384]{1,0:T(1,128)} %bitcast.84, s32[1,16384]{1,0:T(1,128)} %bitcast.73), custom_call_target="tpu_custom_call" | custom-call | flops 4026531840 | bytes 327680 | tf_op jit(solution)/shard_map/pallas_call | solution.py:176
  13.6 7.3 %all-to-all-start = ((f32[32,12,128]{2,1,0:T(8,128)}), f32[32,12,128]{2,1,0:T(8,128)S(1)}, u32[]{:S(2)}, u32[]{:S(2)}) async-start(f32[32,12,128]{2,1,0:T(8,128)} %shard_map.133), calls=%async_computation | async-start | bytes 524288 | tf_op jit(solution)/shard_map/all_to_all | solution.py:360
  21.1 1.8 %copy.52 = f32[8,192,192]{1,2,0:T(8,128)} copy(f32[8,192,192]{2,1,0:T(8,128)S(1)} %copy-done.1) | data formatting | bytes 2359296 | tf_op args[9]
  25.3 7.3 %shard_map.129 = (f32[3,4096]{1,0:T(4,128)}, f32[48,128]{1,0:T(8,128)}, f32[48,128]{1,0:T(8,128)}) custom-call(f32[3,16384]{1,0:T(4,128)} %q_ref.9, f32[3,16384]{1,0:T(4,128)} %inc_ref.7, s32[1,16384]{1,0:T(1,128)} %bitcast.85, s32[1,16384]{1,0:T(1,128)} %bitcast.74, bf16[160,384]{1,0:T(8,128)(2,1)} %pad_maximum_fusion.1.tab_ref, ...), custom_call_target="tpu_custom_call" | custom-call | flops 6442450944 | bytes 163840 | tf_op jit(solution)/shard_map/pallas_call | solution.py:236
  34.1 2.4 %shard_map.134 = (f32[8,192]{1,0:T(8,128)}, f32[256,192]{1,0:T(8,128)}) custom-call(f32[8,192,192]{2,1,0:T(8,128)} %bitcast.55, f32[192,8]{1,0:T(8,128)} %convolution_bitcast_fusion.ft_ref), custom_call_target="tpu_custom_call" | custom-call | flops 589824 | bytes 1179648 | tf_op jit(solution)/shard_map/pallas_call | solution.py:202
  36.5 5.8 %all-to-all-start.1 = ((f32[32,8,192]{2,1,0:T(8,128)}), f32[32,8,192]{2,1,0:T(8,128)S(1)}, u32[]{:S(2)}, u32[]{:S(2)}) async-start(f32[32,8,192]{2,1,0:T(8,128)} %bitcast.70), calls=%async_computation.1 | async-start | bytes 524288 | tf_op jit(solution)/shard_map/all_to_all | solution.py:389
  42.3 7.3 %shard_map.130 = (f32[3,4096]{1,0:T(4,128)}, f32[48,128]{1,0:T(8,128)}, f32[48,128]{1,0:T(8,128)}) custom-call(f32[3,16384]{1,0:T(4,128)} %q_ref.9, f32[3,16384]{1,0:T(4,128)} %inc_ref.7, s32[1,16384]{1,0:T(1,128)} %bitcast.86, s32[1,16384]{1,0:T(1,128)} %bitcast.75, bf16[160,384]{1,0:T(8,128)(2,1)} %pad_maximum_fusion.1.tab_ref, ...), custom_call_target="tpu_custom_call" | custom-call | flops 6442450944 | bytes 163840 | tf_op jit(solution)/shard_map/pallas_call | solution.py:236
  49.7 3.0 %all-to-all-done.1 = f32[32,8,192]{2,1,0:T(8,128)S(1)} async-done(((f32[32,8,192]{2,1,0:T(8,128)}), f32[32,8,192]{2,1,0:T(8,128)S(1)}, u32[]{:S(2)}, u32[]{:S(2)}) %all-to-all-start.1) | async-done | bytes 196640 | tf_op jit(solution)/shard_map/all_to_all | solution.py:389
  53.4 5.3 %shard_map.135 = (f32[8,192]{1,0:T(8,128)}, f32[256,192]{1,0:T(8,128)}) custom-call(s32[32]{0:T(128)} %reshape.94.idx_ref, f32[256,192]{1,0:T(8,128)} %bitcast.64, f32[8,4,192,192]{3,2,1,0:T(8,128)} %s_hbm.9, f32[8,192,192]{2,1,0:T(8,128)} %bitcast.56, f32[192,8]{1,0:T(8,128)} %convolution_bitcast_fusion.ft_ref, f32[8,192]{1,0:T(8,128)} %get-tuple-element.40.v_ref), custom_call_target="tpu_custom_call" | custom-call | flops 2949120 | bytes 6094848 | tf_op jit(solution)/shard_map/pallas_call | solution.py:312
  58.7 2.8 %all-to-all-start.2 = ((f32[32,8,192]{2,1,0:T(8,128)}), f32[32,8,192]{2,1,0:T(8,128)S(1)}, u32[]{:S(2)}, u32[]{:S(2)}) async-start(f32[32,8,192]{2,1,0:T(8,128)} %bitcast.69), calls=%async_computation.2 | async-start | bytes 524288 | tf_op jit(solution)/shard_map/all_to_all | solution.py:389
  61.5 7.3 %shard_map.131 = (f32[3,4096]{1,0:T(4,128)}, f32[48,128]{1,0:T(8,128)}, f32[48,128]{1,0:T(8,128)}) custom-call(f32[3,16384]{1,0:T(4,128)} %q_ref.9, f32[3,16384]{1,0:T(4,128)} %inc_ref.7, s32[1,16384]{1,0:T(1,128)} %bitcast.87, s32[1,16384]{1,0:T(1,128)} %bitcast.76, bf16[160,384]{1,0:T(8,128)(2,1)} %pad_maximum_fusion.1.tab_ref, ...), custom_call_target="tpu_custom_call" | custom-call | flops 6442450944 | bytes 163840 | tf_op jit(solution)/shard_map/pallas_call | solution.py:236
  68.9 3.0 %all-to-all-done.2 = f32[32,8,192]{2,1,0:T(8,128)S(1)} async-done(((f32[32,8,192]{2,1,0:T(8,128)}), f32[32,8,192]{2,1,0:T(8,128)S(1)}, u32[]{:S(2)}, u32[]{:S(2)}) %all-to-all-start.2) | async-done | bytes 196640 | tf_op jit(solution)/shard_map/all_to_all | solution.py:389
  72.6 5.3 %shard_map.136 = (f32[8,192]{1,0:T(8,128)}, f32[256,192]{1,0:T(8,128)}) custom-call(s32[32]{0:T(128)} %reshape.94.idx_ref, f32[256,192]{1,0:T(8,128)} %bitcast.65, f32[8,4,192,192]{3,2,1,0:T(8,128)} %s_hbm.9, f32[8,192,192]{2,1,0:T(8,128)} %bitcast.57, f32[192,8]{1,0:T(8,128)} %convolution_bitcast_fusion.ft_ref, f32[8,192]{1,0:T(8,128)} %get-tuple-element.42.v_ref), custom_call_target="tpu_custom_call" | custom-call | flops 2949120 | bytes 6094848 | tf_op jit(solution)/shard_map/pallas_call | solution.py:312
  77.9 2.8 %all-to-all-start.3 = ((f32[32,8,192]{2,1,0:T(8,128)}), f32[32,8,192]{2,1,0:T(8,128)S(1)}, u32[]{:S(2)}, u32[]{:S(2)}) async-start(f32[32,8,192]{2,1,0:T(8,128)} %bitcast.67), calls=%async_computation.3 | async-start | bytes 524288 | tf_op jit(solution)/shard_map/all_to_all | solution.py:389
  80.8 7.4 %shard_map.132 = (f32[3,4096]{1,0:T(4,128)}, f32[48,128]{1,0:T(8,128)}, f32[48,128]{1,0:T(8,128)}) custom-call(f32[3,16384]{1,0:T(4,128)} %q_ref.9, f32[3,16384]{1,0:T(4,128)} %inc_ref.7, s32[1,16384]{1,0:T(1,128)} %bitcast.88, s32[1,16384]{1,0:T(1,128)} %bitcast.77, bf16[160,384]{1,0:T(8,128)(2,1)} %pad_maximum_fusion.1.tab_ref, ...), custom_call_target="tpu_custom_call" | custom-call | flops 6442450944 | bytes 163840 | tf_op jit(solution)/shard_map/pallas_call | solution.py:236
  89.0 2.1 %all-to-all-done.3 = f32[32,8,192]{2,1,0:T(8,128)S(1)} async-done(((f32[32,8,192]{2,1,0:T(8,128)}), f32[32,8,192]{2,1,0:T(8,128)S(1)}, u32[]{:S(2)}, u32[]{:S(2)}) %all-to-all-start.3) | async-done | bytes 196640 | tf_op jit(solution)/shard_map/all_to_all | solution.py:389
  91.8 5.3 %shard_map.137 = (f32[8,192]{1,0:T(8,128)}, f32[256,192]{1,0:T(8,128)}) custom-call(s32[32]{0:T(128)} %reshape.94.idx_ref, f32[256,192]{1,0:T(8,128)} %bitcast.62, f32[8,4,192,192]{3,2,1,0:T(8,128)} %s_hbm.9, f32[8,192,192]{2,1,0:T(8,128)} %bitcast.58, f32[192,8]{1,0:T(8,128)} %convolution_bitcast_fusion.ft_ref, f32[8,192]{1,0:T(8,128)} %get-tuple-element.44.v_ref), custom_call_target="tpu_custom_call" | custom-call | flops 2949120 | bytes 6094848 | tf_op jit(solution)/shard_map/pallas_call | solution.py:312
  97.1 3.7 %all-to-all-start.4 = ((f32[32,8,192]{2,1,0:T(8,128)}), f32[32,8,192]{2,1,0:T(8,128)S(1)}, u32[]{:S(2)}, u32[]{:S(2)}) async-start(f32[32,8,192]{2,1,0:T(8,128)} %bitcast.68), calls=%async_computation.4 | async-start | bytes 524288 | tf_op jit(solution)/shard_map/all_to_all | solution.py:389
  102.2 4.5 %collective-permute-start = (f32[3,1024]{1,0:T(4,128)S(1)}, f32[3,1024]{1,0:T(4,128)S(1)}, u32[]{:S(2)}, u32[]{:S(2)}) collective-permute-start(f32[3,1024]{1,0:T(4,128)S(1)} %bitcast.81), channel_id=1, source_target_pairs={{0,8},{8,16},{16,24},{1,9},{9,17},{17,25},{2,10},{10,18},{18,26},{... | collective-permute-start | bytes 36872 | tf_op jit(solution)/shard_map/ppermute | solution.py:336
  106.8 4.5 %all-to-all-done.4 = f32[32,8,192]{2,1,0:T(8,128)S(1)} async-done(((f32[32,8,192]{2,1,0:T(8,128)}), f32[32,8,192]{2,1,0:T(8,128)S(1)}, u32[]{:S(2)}, u32[]{:S(2)}) %all-to-all-start.4) | async-done | bytes 196640 | tf_op jit(solution)/shard_map/all_to_all | solution.py:389
  112.0 5.3 %shard_map.138 = (f32[8,192]{1,0:T(8,128)}, f32[256,192]{1,0:T(8,128)}) custom-call(s32[32]{0:T(128)} %reshape.94.idx_ref, f32[256,192]{1,0:T(8,128)} %bitcast.63, f32[8,4,192,192]{3,2,1,0:T(8,128)} %s_hbm.9, f32[8,192,192]{2,1,0:T(8,128)} %bitcast.59, f32[192,8]{1,0:T(8,128)} %convolution_bitcast_fusion.ft_ref, f32[8,192]{1,0:T(8,128)} %get-tuple-element.46.v_ref), custom_call_target="tpu_custom_call" | custom-call | flops 2949120 | bytes 6094848 | tf_op jit(solution)/shard_map/pallas_call | solution.py:312
  117.3 2.6 %all-to-all-start.5 = ((f32[32,8,192]{2,1,0:T(8,128)}), f32[32,8,192]{2,1,0:T(8,128)S(1)}, u32[]{:S(2)}, u32[]{:S(2)}) async-start(f32[32,8,192]{2,1,0:T(8,128)} %bitcast.66), calls=%async_computation.5 | async-start | bytes 524288 | tf_op jit(solution)/shard_map/all_to_all | solution.py:389
  122.0 8.3 %all-to-all-done.5 = f32[32,8,192]{2,1,0:T(8,128)S(1)} async-done(((f32[32,8,192]{2,1,0:T(8,128)}), f32[32,8,192]{2,1,0:T(8,128)S(1)}, u32[]{:S(2)}, u32[]{:S(2)}) %all-to-all-start.5) | async-done | bytes 196640 | tf_op jit(solution)/shard_map/all_to_all | solution.py:389
  131.0 5.3 %shard_map.139 = (f32[8,192]{1,0:T(8,128)}, f32[256,192]{1,0:T(8,128)}) custom-call(s32[32]{0:T(128)} %reshape.94.idx_ref, f32[256,192]{1,0:T(8,128)} %bitcast.61, f32[8,4,192,192]{3,2,1,0:T(8,128)} %s_hbm.9, f32[8,192,192]{2,1,0:T(8,128)} %bitcast.60, f32[192,8]{1,0:T(8,128)} %convolution_bitcast_fusion.ft_ref, f32[8,192]{1,0:T(8,128)} %get-tuple-element.48.v_ref), custom_call_target="tpu_custom_call" | custom-call | flops 2949120 | bytes 6094848 | tf_op jit(solution)/shard_map/pallas_call | solution.py:312
  (77 shorter events, 11.6 us)
Async XLA Ops:
  0.6 32.2 %copy-start = (f32[192,192]{1,0:T(8,128)S(1)}, f32[192,192]{1,0:T(8,128)}, u32[]{:S(2)}) copy-start(f32[192,192]{1,0:T(8,128)} %param.16) | copy-start | bytes 442372
  0.7 20.3 %copy-start.8 = (s32[16384]{0:T(1024)S(1)}, s32[16384]{0:T(1024)}, u32[]{:S(2)}) copy-start(s32[16384]{0:T(1024)} %param.14) | copy-start | bytes 196612
  0.7 20.3 %copy-start.19 = (f32[384]{0:T(512)S(1)}, f32[384]{0:T(512)}, u32[]{:S(2)}) copy-start(f32[384]{0:T(512)} %param.15) | copy-start | bytes 4612
  0.7 20.4 %copy-start.1 = (f32[8,192,192]{2,1,0:T(8,128)S(1)}, f32[8,192,192]{2,1,0:T(8,128)}, u32[]{:S(2)}) copy-start(f32[8,192,192]{2,1,0:T(8,128)} %param.19) | copy-start | bytes 3538948
  13.6 19.0 %all-to-all-start = ((f32[32,12,128]{2,1,0:T(8,128)}), f32[32,12,128]{2,1,0:T(8,128)S(1)}, u32[]{:S(2)}, u32[]{:S(2)}) async-start(f32[32,12,128]{2,1,0:T(8,128)} %shard_map.133), calls=%async_computation | async-start | bytes 524288 | tf_op jit(solution)/shard_map/all_to_all | solution.py:360
  21.1 1.8 %copy-start.20 = (s32[8,4]{0,1:T(4,128)S(1)}, s32[8,4]{0,1:T(4,128)}, u32[]{:S(2)}) copy-start(s32[8,4]{0,1:T(4,128)} %param.18) | copy-start | bytes 388
  21.1 2.4 %copy-start.7 = (f32[5,3072]{1,0:T(8,128)S(1)}, f32[5,3072]{1,0:T(8,128)}, u32[]{:S(2)}) copy-start(f32[5,3072]{1,0:T(8,128)} %param.12) | copy-start | bytes 184324
  36.5 16.2 %all-to-all-start.1 = ((f32[32,8,192]{2,1,0:T(8,128)}), f32[32,8,192]{2,1,0:T(8,128)S(1)}, u32[]{:S(2)}, u32[]{:S(2)}) async-start(f32[32,8,192]{2,1,0:T(8,128)} %bitcast.70), calls=%async_computation.1 | async-start | bytes 524288 | tf_op jit(solution)/shard_map/all_to_all | solution.py:389
  58.7 13.2 %all-to-all-start.2 = ((f32[32,8,192]{2,1,0:T(8,128)}), f32[32,8,192]{2,1,0:T(8,128)S(1)}, u32[]{:S(2)}, u32[]{:S(2)}) async-start(f32[32,8,192]{2,1,0:T(8,128)} %bitcast.69), calls=%async_computation.2 | async-start | bytes 524288 | tf_op jit(solution)/shard_map/all_to_all | solution.py:389
  77.9 13.2 %all-to-all-start.3 = ((f32[32,8,192]{2,1,0:T(8,128)}), f32[32,8,192]{2,1,0:T(8,128)S(1)}, u32[]{:S(2)}, u32[]{:S(2)}) async-start(f32[32,8,192]{2,1,0:T(8,128)} %bitcast.67), calls=%async_computation.3 | async-start | bytes 524288 | tf_op jit(solution)/shard_map/all_to_all | solution.py:389
  80.7 7.4 %copy-start.13 = (f32[48,128]{1,0:T(8,128)S(1)}, f32[48,128]{1,0:T(8,128)}, u32[]{:S(2)}) copy-start(f32[48,128]{1,0:T(8,128)} %get-tuple-element.31) | copy-start | bytes 73732
  80.8 7.4 %copy-start.14 = (f32[48,128]{1,0:T(8,128)S(1)}, f32[48,128]{1,0:T(8,128)}, u32[]{:S(2)}) copy-start(f32[48,128]{1,0:T(8,128)} %get-tuple-element.35) | copy-start | bytes 73732
  80.8 7.4 %copy-start.15 = (f32[48,128]{1,0:T(8,128)S(1)}, f32[48,128]{1,0:T(8,128)}, u32[]{:S(2)}) copy-start(f32[48,128]{1,0:T(8,128)} %get-tuple-element.32) | copy-start | bytes 73732
  80.8 7.4 %copy-start.16 = (f32[48,128]{1,0:T(8,128)S(1)}, f32[48,128]{1,0:T(8,128)}, u32[]{:S(2)}) copy-start(f32[48,128]{1,0:T(8,128)} %get-tuple-element.36) | copy-start | bytes 73732
  80.8 7.4 %copy-start.17 = (f32[48,128]{1,0:T(8,128)S(1)}, f32[48,128]{1,0:T(8,128)}, u32[]{:S(2)}) copy-start(f32[48,128]{1,0:T(8,128)} %get-tuple-element.33) | copy-start | bytes 73732
  80.8 7.4 %copy-start.18 = (f32[48,128]{1,0:T(8,128)S(1)}, f32[48,128]{1,0:T(8,128)}, u32[]{:S(2)}) copy-start(f32[48,128]{1,0:T(8,128)} %get-tuple-element.37) | copy-start | bytes 73732
  97.1 14.1 %all-to-all-start.4 = ((f32[32,8,192]{2,1,0:T(8,128)}), f32[32,8,192]{2,1,0:T(8,128)S(1)}, u32[]{:S(2)}, u32[]{:S(2)}) async-start(f32[32,8,192]{2,1,0:T(8,128)} %bitcast.68), calls=%async_computation.4 | async-start | bytes 524288 | tf_op jit(solution)/shard_map/all_to_all | solution.py:389
  100.9 19.8 %collective-permute-start.1 = (f32[3,1024]{1,0:T(4,128)S(1)}, f32[3,1024]{1,0:T(4,128)S(1)}, u32[]{:S(2)}, u32[]{:S(2)}) collective-permute-start(f32[3,1024]{1,0:T(4,128)S(1)} %bitcast.80), channel_id=1, source_target_pairs={{8,0},{16,8},{24,16},{9,1},{17,9},{25,17},{10,2},{18,10},{26,18},{... | collective-permute-start | bytes 36872 | tf_op jit(solution)/shard_map/ppermute | solution.py:336
  102.2 18.5 %collective-permute-start = (f32[3,1024]{1,0:T(4,128)S(1)}, f32[3,1024]{1,0:T(4,128)S(1)}, u32[]{:S(2)}, u32[]{:S(2)}) collective-permute-start(f32[3,1024]{1,0:T(4,128)S(1)} %bitcast.81), channel_id=1, source_target_pairs={{0,8},{8,16},{16,24},{1,9},{9,17},{17,25},{2,10},{10,18},{18,26},{... | collective-permute-start | bytes 36872 | tf_op jit(solution)/shard_map/ppermute | solution.py:336
  112.0 8.0 %copy-start.9 = (f32[3,4096]{1,0:T(4,128)S(1)}, f32[3,4096]{1,0:T(4,128)}, u32[]{:S(2)}) copy-start(f32[3,4096]{1,0:T(4,128)} %get-tuple-element.27) | copy-start | bytes 147460
  112.0 8.0 %copy-start.10 = (f32[3,4096]{1,0:T(4,128)S(1)}, f32[3,4096]{1,0:T(4,128)}, u32[]{:S(2)}) copy-start(f32[3,4096]{1,0:T(4,128)} %get-tuple-element.28) | copy-start | bytes 147460
  112.0 8.0 %copy-start.11 = (f32[3,4096]{1,0:T(4,128)S(1)}, f32[3,4096]{1,0:T(4,128)}, u32[]{:S(2)}) copy-start(f32[3,4096]{1,0:T(4,128)} %get-tuple-element.29) | copy-start | bytes 147460
  112.0 8.0 %copy-start.12 = (f32[3,4096]{1,0:T(4,128)S(1)}, f32[3,4096]{1,0:T(4,128)}, u32[]{:S(2)}) copy-start(f32[3,4096]{1,0:T(4,128)} %get-tuple-element.30) | copy-start | bytes 147460
  117.3 13.0 %all-to-all-start.5 = ((f32[32,8,192]{2,1,0:T(8,128)}), f32[32,8,192]{2,1,0:T(8,128)S(1)}, u32[]{:S(2)}, u32[]{:S(2)}) async-start(f32[32,8,192]{2,1,0:T(8,128)} %bitcast.66), calls=%async_computation.5 | async-start | bytes 524288 | tf_op jit(solution)/shard_map/all_to_all | solution.py:389
  (5 other events, 3.5 us)

commit v9 on v8

--- a/solution.py
+++ b/solution.py
@@ -267,35 +267,62 @@
     return q_next, unpack(up), unpack(down)
 
 
+def own_kernel(v_ref, ft_ref, s_hbm, rest_ref, s_buf, sems):
+    own = v_ref.shape[0]
+    copies = [pltpu.make_async_copy(s_hbm.at[b, 0], s_buf.at[b], sems.at[b]) for b in range(own)]
+    for copy in copies:
+        copy.start()
+    for b in range(own):
+        copies[b].wait()
+        image = jnp.sum(s_buf[b] * v_ref[b : b + 1, :], axis=1, keepdims=True)
+        rest_ref[:, b : b + 1] = ft_ref[:, b : b + 1] - image
+
+
+def own_term(velocity, force_t, stiffness):
+    own, size = velocity.shape
+    vmem = pl.BlockSpec(memory_space=pltpu.VMEM)
+    return pl.pallas_call(
+        own_kernel,
+        out_shape=jax.ShapeDtypeStruct(force_t.shape, jnp.float32),
+        in_specs=[vmem, vmem, pl.BlockSpec(memory_space=pl.ANY)],
+        out_specs=vmem,
+        scratch_shapes=[
+            pltpu.VMEM((own, size, size), jnp.float32),
+            pltpu.SemaphoreType.DMA((own,)),
+        ],
+        cost_estimate=pl.CostEstimate(
+            flops=2 * own * size * size, transcendentals=0, bytes_accessed=4 * own * size * size
+        ),
+    )(velocity, force_t, stiffness)
+
+
 def sweep_kernel(
-    idx_ref, g_hbm, s_hbm, pt_hbm, ft_ref, v_ref, vout_ref, send_ref, g_buf, s_buf, pt_buf, sems
+    idx_ref, g_ref, s_hbm, pt_hbm, rest_ref, v_ref, vout_ref, send_ref, s_buf, pt_buf, sems
 ):
-    total = g_buf.shape[0]
+    total = g_ref.shape[0]
     own = v_ref.shape[0]
-    width = s_buf.shape[1]
-    g_copy = pltpu.make_async_copy(g_hbm, g_buf, sems.at[0])
-    g_copy.start()
-    s_copies = [pltpu.make_async_copy(s_hbm.at[b], s_buf.at[b], sems.at[1 + b]) for b in range(own)]
-    p_copies = [
-        pltpu.make_async_copy(pt_hbm.at[b], pt_buf.at[b], sems.at[1 + own + b]) for b in range(own)
+    width = s_buf.shape[1] + 1
+    s_copies = [
+        pltpu.make_async_copy(s_hbm.at[b, pl.ds(1, width - 1)], s_buf.at[b], sems.at[b])
+        for b in range(own)
     ]
+    p_copies = [pltpu.make_async_copy(pt_hbm.at[b], pt_buf.at[b], sems.at[own + b]) for b in range(own)]
     for b in range(own):
         s_copies[b].start()
         p_copies[b].start()
-    g_copy.wait()
     rows = []
     for b in range(own):
         s_copies[b].wait()
         acc = None
-        for n in range(width):
+        for n in range(1, width):
             w = idx_ref[b * width + n]
             inside = jnp.logical_and(w >= 0, w < total)
-            near = g_buf[pl.ds(jnp.clip(w, 0, total - 1), 1), :]
+            near = g_ref[pl.ds(jnp.clip(w, 0, total - 1), 1), :]
             near = jnp.where(inside, near, 0.0)
-            term = s_buf[b, n] * near
+            term = s_buf[b, n - 1] * near
             acc = term if acc is None else acc + term
         image = jnp.sum(acc, axis=1, keepdims=True)
-        rest = ft_ref[:, b : b + 1] - image
+        rest = rest_ref[:, b : b + 1] - image
         p_copies[b].wait()
         update = jnp.sum(pt_buf[b] * rest, axis=0, keepdims=True)
         rows.append(v_ref[b : b + 1, :] + damping * update)
@@ -305,30 +332,30 @@
         send_ref[k * own : (k + 1) * own, :] = fresh
 
 
-def sweep(where_read, gathered, stiffness, transposed, force_t, velocity, copies):
-    own = velocity.shape[0]
+def sweep(where_read, gathered, stiffness, transposed, rest_t, velocity, copies):
+    own, size = velocity.shape
+    width = stiffness.shape[1]
     vmem = pl.BlockSpec(memory_space=pltpu.VMEM)
     anywhere = pl.BlockSpec(memory_space=pl.ANY)
     return pl.pallas_call(
         sweep_kernel,
         out_shape=(
             jax.ShapeDtypeStruct(velocity.shape, jnp.float32),
-            jax.ShapeDtypeStruct((copies * own, velocity.shape[1]), jnp.float32),
-        ),
-        in_specs=[pl.BlockSpec(memory_space=pltpu.SMEM), anywhere, anywhere, anywhere, vmem, vmem],
+            jax.ShapeDtypeStruct((copies * own, size), jnp.float32),
+        ),
+        in_specs=[pl.BlockSpec(memory_space=pltpu.SMEM), vmem, anywhere, anywhere, vmem, vmem],
         out_specs=(vmem, vmem),
         scratch_shapes=[
-            pltpu.VMEM(gathered.shape, jnp.float32),
-            pltpu.VMEM(stiffness.shape, jnp.float32),
+            pltpu.VMEM((own, width - 1, size, size), jnp.float32),
             pltpu.VMEM(transposed.shape, jnp.float32),
-            pltpu.SemaphoreType.DMA((1 + 2 * own,)),
+            pltpu.SemaphoreType.DMA((2 * own,)),
         ],
         cost_estimate=pl.CostEstimate(
             flops=2 * (stiffness.size + transposed.size),
             transcendentals=0,
             bytes_accessed=4 * (stiffness.size + transposed.size + gathered.size),
         ),
-    )(where_read, gathered, stiffness, transposed, force_t, velocity)
+    )(where_read, gathered, stiffness, transposed, rest_t, velocity)
 
 def passed_along(array, axis, by):
     size = lax.axis_size(axis)
@@ -387,8 +414,9 @@
     velocity, send = first_velocity(transposed, force_t, copies)
     for sweep_index in range(1, ITERS):
         gathered = lax.all_to_all(send, ("slab", "rad"), 0, 0, tiled=True)
+        rest_t = own_term(velocity, force_t, stiffness)
         velocity, send = sweep(
-            where_read, gathered, stiffness, transposed, force_t, velocity, copies
+            where_read, gathered, stiffness, transposed, rest_t, velocity, copies
         )
     return (q_next, arrivals, element_stress, velocity)
 

time: 137 us -> 148 us (1.080)
  waiting for transfers between devices: 21 us -> 5.84 us
  Pallas kernels: 71.3 us -> 85.9 us
  starting transfers between devices: 30.9 us -> 41.6 us
    pallas_call x0 -> x5, Pallas kernels: none -> 16.9 us  [own_term(): pl.pallas_call(own_kernel, out_shape=jax.ShapeDtypeStruct(force_t.shape,...]
    all_to_all x5, waiting for transfers between devices: 21 us -> 5.83 us  [body(): gathered = lax.all_to_all(send, ('slab', 'rad'), 0, 0, tiled=True)]
    all_to_all x5, starting transfers between devices: 17.8 us -> 28.3 us  [body(): gathered = lax.all_to_all(send, ('slab', 'rad'), 0, 0, tiled=True)]
    pallas_call x5, Pallas kernels: 26.5 us -> 24.2 us  [sweep(): pl.pallas_call(sweep_kernel, out_shape=(jax.ShapeDtypeStruct(velocity.sha...]
  transfers between devices with their start and end apart: 8 -> 8, of which waited for: 5 -> 2; matrix products, arithmetic and copies ran while one was open for 5% -> 5% of each run, Pallas kernels for 25% -> 35%
where the time goes in v9:
time: 148 us; the launch traced here: 147 us
  Pallas kernels  85.9 us (58%)
  starting transfers between devices  41.6 us (28%)
  local copies, waits for them, and re-layouts  7.66 us (5%)
  waiting for transfers between devices  5.84 us (4%)
  other arithmetic  3.24 us (2%)
    pallas_call x4, Pallas kernels, update_and_pack(): pl.pallas_call(functools.partial(update_kernel, groups16=groups16, slots1...  29.4 us
    all_to_all x5, starting transfers between devices, body(): gathered = lax.all_to_all(send, ('slab', 'rad'), 0, 0, tiled=True)  28.3 us
    pallas_call x5, Pallas kernels, sweep(): pl.pallas_call(sweep_kernel, out_shape=(jax.ShapeDtypeStruct(velocity.sha...  24.2 us
    pallas_call x5, Pallas kernels, own_term(): pl.pallas_call(own_kernel, out_shape=jax.ShapeDtypeStruct(force_t.shape,...  16.9 us
    pallas_call x1, Pallas kernels, stress_partials(): pl.pallas_call(functools.partial(stress_kernel, groups=groups, rows=rows)...  12.9 us
    all_to_all x1, starting transfers between devices, body(): received = lax.all_to_all(send, ('slab', 'rad'), 0, 0, tiled=True)  7.3 us
    ppermute x2, starting transfers between devices, passed_along(): return lax.ppermute(array, axis, pairs)  6.02 us
    unnamed x49, local copies, waits for them, and re-layouts  6.01 us
  transfers between devices with their start and end apart: 8, of which 2 were waited for; matrix products, arithmetic and copies ran while one was open for 5% of the time, Pallas kernels for 35%

profile of v9, /device:TPU:0, one launch (start us, length us, event | category | flops | bytes accessed | tf_op | source)
XLA Modules:
  0.0 146.7 jit_solution(17883404993360272123)
XLA Ops:
  0.7 12.9 %shard_map.133 = f32[32,12,128]{2,1,0:T(8,128)} custom-call(s32[1]{0:T(128)} %bitcast.12.slab_ref, f32[3,16384]{1,0:T(4,128)} %q_ref.9, s32[1,16384]{1,0:T(1,128)} %bitcast.84, s32[1,16384]{1,0:T(1,128)} %bitcast.73), custom_call_target="tpu_custom_call" | custom-call | flops 4026531840 | bytes 327680 | tf_op jit(solution)/shard_map/pallas_call | solution.py:176
  13.6 7.3 %all-to-all-start = ((f32[32,12,128]{2,1,0:T(8,128)}), f32[32,12,128]{2,1,0:T(8,128)S(1)}, u32[]{:S(2)}, u32[]{:S(2)}) async-start(f32[32,12,128]{2,1,0:T(8,128)} %shard_map.133), calls=%async_computation | async-start | bytes 524288 | tf_op jit(solution)/shard_map/all_to_all | solution.py:387
  25.3 7.3 %shard_map.129 = (f32[3,4096]{1,0:T(4,128)}, f32[48,128]{1,0:T(8,128)}, f32[48,128]{1,0:T(8,128)}) custom-call(f32[3,16384]{1,0:T(4,128)} %q_ref.9, f32[3,16384]{1,0:T(4,128)} %inc_ref.7, s32[1,16384]{1,0:T(1,128)} %bitcast.85, s32[1,16384]{1,0:T(1,128)} %bitcast.74, bf16[160,384]{1,0:T(8,128)(2,1)} %pad_maximum_fusion.1.tab_ref, ...), custom_call_target="tpu_custom_call" | custom-call | flops 6442450944 | bytes 163840 | tf_op jit(solution)/shard_map/pallas_call | solution.py:236
  34.1 2.4 %shard_map.134 = (f32[8,192]{1,0:T(8,128)}, f32[256,192]{1,0:T(8,128)}) custom-call(f32[8,192,192]{2,1,0:T(8,128)} %bitcast.55, f32[192,8]{1,0:T(8,128)} %convolution_bitcast_fusion.ft_ref), custom_call_target="tpu_custom_call" | custom-call | flops 589824 | bytes 1179648 | tf_op jit(solution)/shard_map/pallas_call | solution.py:202
  36.5 5.8 %all-to-all-start.1 = ((f32[32,8,192]{2,1,0:T(8,128)}), f32[32,8,192]{2,1,0:T(8,128)S(1)}, u32[]{:S(2)}, u32[]{:S(2)}) async-start(f32[32,8,192]{2,1,0:T(8,128)} %bitcast.70), calls=%async_computation.1 | async-start | bytes 524288 | tf_op jit(solution)/shard_map/all_to_all | solution.py:416
  42.4 7.4 %shard_map.130 = (f32[3,4096]{1,0:T(4,128)}, f32[48,128]{1,0:T(8,128)}, f32[48,128]{1,0:T(8,128)}) custom-call(f32[3,16384]{1,0:T(4,128)} %q_ref.9, f32[3,16384]{1,0:T(4,128)} %inc_ref.7, s32[1,16384]{1,0:T(1,128)} %bitcast.86, s32[1,16384]{1,0:T(1,128)} %bitcast.75, bf16[160,384]{1,0:T(8,128)(2,1)} %pad_maximum_fusion.1.tab_ref, ...), custom_call_target="tpu_custom_call" | custom-call | flops 6442450944 | bytes 163840 | tf_op jit(solution)/shard_map/pallas_call | solution.py:236
  49.7 3.4 %shard_map.135.rest_ref = f32[192,8]{1,0:T(8,128)} custom-call(f32[8,192]{1,0:T(8,128)} %get-tuple-element.40.v_ref, f32[192,8]{1,0:T(8,128)} %convolution_bitcast_fusion.ft_ref, f32[8,4,192,192]{3,2,1,0:T(8,128)} %s_hbm.19), custom_call_target="tpu_custom_call" | custom-call | flops 589824 | bytes 1179648 | tf_op jit(solution)/shard_map/pallas_call | solution.py:284
  53.8 4.8 %shard_map.136 = (f32[8,192]{1,0:T(8,128)}, f32[256,192]{1,0:T(8,128)}) custom-call(s32[32]{0:T(128)} %reshape.94.idx_ref, f32[256,192]{1,0:T(8,128)} %bitcast.64, f32[8,4,192,192]{3,2,1,0:T(8,128)} %s_hbm.19, f32[8,192,192]{2,1,0:T(8,128)} %bitcast.56, f32[192,8]{1,0:T(8,128)} %shard_map.135.rest_ref, f32[8,192]{1,0:T(8,128)} %get-tuple-element.40.v_ref), custom_call_target="tpu_custom_call" | custom-call | flops 2949120 | bytes 6094848 | tf_op jit(solution)/shard_map/pallas_call | solution.py:340
  58.7 5.8 %all-to-all-start.2 = ((f32[32,8,192]{2,1,0:T(8,128)}), f32[32,8,192]{2,1,0:T(8,128)S(1)}, u32[]{:S(2)}, u32[]{:S(2)}) async-start(f32[32,8,192]{2,1,0:T(8,128)} %bitcast.69), calls=%async_computation.2 | async-start | bytes 524288 | tf_op jit(solution)/shard_map/all_to_all | solution.py:416
  64.5 7.4 %shard_map.131 = (f32[3,4096]{1,0:T(4,128)}, f32[48,128]{1,0:T(8,128)}, f32[48,128]{1,0:T(8,128)}) custom-call(f32[3,16384]{1,0:T(4,128)} %q_ref.9, f32[3,16384]{1,0:T(4,128)} %inc_ref.7, s32[1,16384]{1,0:T(1,128)} %bitcast.87, s32[1,16384]{1,0:T(1,128)} %bitcast.76, bf16[160,384]{1,0:T(8,128)(2,1)} %pad_maximum_fusion.1.tab_ref, ...), custom_call_target="tpu_custom_call" | custom-call | flops 6442450944 | bytes 163840 | tf_op jit(solution)/shard_map/pallas_call | solution.py:236
  71.9 3.4 %shard_map.137.rest_ref = f32[192,8]{1,0:T(8,128)} custom-call(f32[8,192]{1,0:T(8,128)} %get-tuple-element.42.v_ref, f32[192,8]{1,0:T(8,128)} %convolution_bitcast_fusion.ft_ref, f32[8,4,192,192]{3,2,1,0:T(8,128)} %s_hbm.19), custom_call_target="tpu_custom_call" | custom-call | flops 589824 | bytes 1179648 | tf_op jit(solution)/shard_map/pallas_call | solution.py:284
  76.0 4.8 %shard_map.138 = (f32[8,192]{1,0:T(8,128)}, f32[256,192]{1,0:T(8,128)}) custom-call(s32[32]{0:T(128)} %reshape.94.idx_ref, f32[256,192]{1,0:T(8,128)} %bitcast.65, f32[8,4,192,192]{3,2,1,0:T(8,128)} %s_hbm.19, f32[8,192,192]{2,1,0:T(8,128)} %bitcast.57, f32[192,8]{1,0:T(8,128)} %shard_map.137.rest_ref, f32[8,192]{1,0:T(8,128)} %get-tuple-element.42.v_ref), custom_call_target="tpu_custom_call" | custom-call | flops 2949120 | bytes 6094848 | tf_op jit(solution)/shard_map/pallas_call | solution.py:340
  80.8 5.8 %all-to-all-start.3 = ((f32[32,8,192]{2,1,0:T(8,128)}), f32[32,8,192]{2,1,0:T(8,128)S(1)}, u32[]{:S(2)}, u32[]{:S(2)}) async-start(f32[32,8,192]{2,1,0:T(8,128)} %bitcast.67), calls=%async_computation.3 | async-start | bytes 524288 | tf_op jit(solution)/shard_map/all_to_all | solution.py:416
  86.8 7.4 %shard_map.132 = (f32[3,4096]{1,0:T(4,128)}, f32[48,128]{1,0:T(8,128)}, f32[48,128]{1,0:T(8,128)}) custom-call(f32[3,16384]{1,0:T(4,128)} %q_ref.9, f32[3,16384]{1,0:T(4,128)} %inc_ref.7, s32[1,16384]{1,0:T(1,128)} %bitcast.88, s32[1,16384]{1,0:T(1,128)} %bitcast.77, bf16[160,384]{1,0:T(8,128)(2,1)} %pad_maximum_fusion.1.tab_ref, ...), custom_call_target="tpu_custom_call" | custom-call | flops 6442450944 | bytes 163840 | tf_op jit(solution)/shard_map/pallas_call | solution.py:236
  94.9 3.4 %shard_map.139.rest_ref = f32[192,8]{1,0:T(8,128)} custom-call(f32[8,192]{1,0:T(8,128)} %get-tuple-element.44.v_ref, f32[192,8]{1,0:T(8,128)} %convolution_bitcast_fusion.ft_ref, f32[8,4,192,192]{3,2,1,0:T(8,128)} %s_hbm.19), custom_call_target="tpu_custom_call" | custom-call | flops 589824 | bytes 1179648 | tf_op jit(solution)/shard_map/pallas_call | solution.py:284
  99.1 4.8 %shard_map.140 = (f32[8,192]{1,0:T(8,128)}, f32[256,192]{1,0:T(8,128)}) custom-call(s32[32]{0:T(128)} %reshape.94.idx_ref, f32[256,192]{1,0:T(8,128)} %bitcast.62, f32[8,4,192,192]{3,2,1,0:T(8,128)} %s_hbm.19, f32[8,192,192]{2,1,0:T(8,128)} %bitcast.58, f32[192,8]{1,0:T(8,128)} %shard_map.139.rest_ref, f32[8,192]{1,0:T(8,128)} %get-tuple-element.44.v_ref), custom_call_target="tpu_custom_call" | custom-call | flops 2949120 | bytes 6094848 | tf_op jit(solution)/shard_map/pallas_call | solution.py:340
  103.9 5.8 %all-to-all-start.4 = ((f32[32,8,192]{2,1,0:T(8,128)}), f32[32,8,192]{2,1,0:T(8,128)S(1)}, u32[]{:S(2)}, u32[]{:S(2)}) async-start(f32[32,8,192]{2,1,0:T(8,128)} %bitcast.68), calls=%async_computation.4 | async-start | bytes 524288 | tf_op jit(solution)/shard_map/all_to_all | solution.py:416
  111.1 4.7 %collective-permute-start = (f32[3,1024]{1,0:T(4,128)S(1)}, f32[3,1024]{1,0:T(4,128)S(1)}, u32[]{:S(2)}, u32[]{:S(2)}) collective-permute-start(f32[3,1024]{1,0:T(4,128)S(1)} %bitcast.81), channel_id=1, source_target_pairs={{0,8},{8,16},{16,24},{1,9},{9,17},{17,25},{2,10},{10,18},{18,26},{... | collective-permute-start | bytes 36872 | tf_op jit(solution)/shard_map/ppermute | solution.py:363
  115.8 3.4 %shard_map.141.rest_ref = f32[192,8]{1,0:T(8,128)} custom-call(f32[8,192]{1,0:T(8,128)} %get-tuple-element.46.v_ref, f32[192,8]{1,0:T(8,128)} %convolution_bitcast_fusion.ft_ref, f32[8,4,192,192]{3,2,1,0:T(8,128)} %s_hbm.19), custom_call_target="tpu_custom_call" | custom-call | flops 589824 | bytes 1179648 | tf_op jit(solution)/shard_map/pallas_call | solution.py:284
  120.8 4.9 %shard_map.142 = (f32[8,192]{1,0:T(8,128)}, f32[256,192]{1,0:T(8,128)}) custom-call(s32[32]{0:T(128)} %reshape.94.idx_ref, f32[256,192]{1,0:T(8,128)} %bitcast.63, f32[8,4,192,192]{3,2,1,0:T(8,128)} %s_hbm.19, f32[8,192,192]{2,1,0:T(8,128)} %bitcast.59, f32[192,8]{1,0:T(8,128)} %shard_map.141.rest_ref, f32[8,192]{1,0:T(8,128)} %get-tuple-element.46.v_ref), custom_call_target="tpu_custom_call" | custom-call | flops 2949120 | bytes 6094848 | tf_op jit(solution)/shard_map/pallas_call | solution.py:340
  125.7 4.9 %all-to-all-start.5 = ((f32[32,8,192]{2,1,0:T(8,128)}), f32[32,8,192]{2,1,0:T(8,128)S(1)}, u32[]{:S(2)}, u32[]{:S(2)}) async-start(f32[32,8,192]{2,1,0:T(8,128)} %bitcast.66), calls=%async_computation.5 | async-start | bytes 524288 | tf_op jit(solution)/shard_map/all_to_all | solution.py:416
  132.7 3.4 %shard_map.143.rest_ref = f32[192,8]{1,0:T(8,128)} custom-call(f32[8,192]{1,0:T(8,128)} %get-tuple-element.48.v_ref, f32[192,8]{1,0:T(8,128)} %convolution_bitcast_fusion.ft_ref, f32[8,4,192,192]{3,2,1,0:T(8,128)} %s_hbm.19), custom_call_target="tpu_custom_call" | custom-call | flops 589824 | bytes 1179648 | tf_op jit(solution)/shard_map/pallas_call | solution.py:284
  136.1 4.9 %all-to-all-done.5 = f32[32,8,192]{2,1,0:T(8,128)S(1)} async-done(((f32[32,8,192]{2,1,0:T(8,128)}), f32[32,8,192]{2,1,0:T(8,128)S(1)}, u32[]{:S(2)}, u32[]{:S(2)}) %all-to-all-start.5) | async-done | bytes 196640 | tf_op jit(solution)/shard_map/all_to_all | solution.py:416
  141.7 4.8 %shard_map.144 = (f32[8,192]{1,0:T(8,128)}, f32[256,192]{1,0:T(8,128)}) custom-call(s32[32]{0:T(128)} %reshape.94.idx_ref, f32[256,192]{1,0:T(8,128)} %bitcast.61, f32[8,4,192,192]{3,2,1,0:T(8,128)} %s_hbm.19, f32[8,192,192]{2,1,0:T(8,128)} %bitcast.60, f32[192,8]{1,0:T(8,128)} %shard_map.143.rest_ref, f32[8,192]{1,0:T(8,128)} %get-tuple-element.48.v_ref), custom_call_target="tpu_custom_call" | custom-call | flops 2949120 | bytes 6094848 | tf_op jit(solution)/shard_map/pallas_call | solution.py:340
  (82 shorter events, 14.3 us)
Async XLA Ops:
  0.6 32.3 %copy-start = (f32[192,192]{1,0:T(8,128)S(1)}, f32[192,192]{1,0:T(8,128)}, u32[]{:S(2)}) copy-start(f32[192,192]{1,0:T(8,128)} %param.16) | copy-start | bytes 442372
  0.7 20.3 %copy-start.8 = (s32[16384]{0:T(1024)S(1)}, s32[16384]{0:T(1024)}, u32[]{:S(2)}) copy-start(s32[16384]{0:T(1024)} %param.14) | copy-start | bytes 196612
  0.7 20.3 %copy-start.19 = (f32[384]{0:T(512)S(1)}, f32[384]{0:T(512)}, u32[]{:S(2)}) copy-start(f32[384]{0:T(512)} %param.15) | copy-start | bytes 4612
  0.7 20.4 %copy-start.1 = (f32[8,192,192]{2,1,0:T(8,128)S(1)}, f32[8,192,192]{2,1,0:T(8,128)}, u32[]{:S(2)}) copy-start(f32[8,192,192]{2,1,0:T(8,128)} %param.19) | copy-start | bytes 3538948
  13.6 19.1 %all-to-all-start = ((f32[32,12,128]{2,1,0:T(8,128)}), f32[32,12,128]{2,1,0:T(8,128)S(1)}, u32[]{:S(2)}, u32[]{:S(2)}) async-start(f32[32,12,128]{2,1,0:T(8,128)} %shard_map.133), calls=%async_computation | async-start | bytes 524288 | tf_op jit(solution)/shard_map/all_to_all | solution.py:387
  21.1 1.8 %copy-start.20 = (s32[8,4]{0,1:T(4,128)S(1)}, s32[8,4]{0,1:T(4,128)}, u32[]{:S(2)}) copy-start(s32[8,4]{0,1:T(4,128)} %param.18) | copy-start | bytes 388
  21.1 2.5 %copy-start.7 = (f32[5,3072]{1,0:T(8,128)S(1)}, f32[5,3072]{1,0:T(8,128)}, u32[]{:S(2)}) copy-start(f32[5,3072]{1,0:T(8,128)} %param.12) | copy-start | bytes 184324
  36.5 16.6 %all-to-all-start.1 = ((f32[32,8,192]{2,1,0:T(8,128)}), f32[32,8,192]{2,1,0:T(8,128)S(1)}, u32[]{:S(2)}, u32[]{:S(2)}) async-start(f32[32,8,192]{2,1,0:T(8,128)} %bitcast.70), calls=%async_computation.1 | async-start | bytes 524288 | tf_op jit(solution)/shard_map/all_to_all | solution.py:416
  58.7 16.6 %all-to-all-start.2 = ((f32[32,8,192]{2,1,0:T(8,128)}), f32[32,8,192]{2,1,0:T(8,128)S(1)}, u32[]{:S(2)}, u32[]{:S(2)}) async-start(f32[32,8,192]{2,1,0:T(8,128)} %bitcast.69), calls=%async_computation.2 | async-start | bytes 524288 | tf_op jit(solution)/shard_map/all_to_all | solution.py:416
  80.8 17.5 %all-to-all-start.3 = ((f32[32,8,192]{2,1,0:T(8,128)}), f32[32,8,192]{2,1,0:T(8,128)S(1)}, u32[]{:S(2)}, u32[]{:S(2)}) async-start(f32[32,8,192]{2,1,0:T(8,128)} %bitcast.67), calls=%async_computation.3 | async-start | bytes 524288 | tf_op jit(solution)/shard_map/all_to_all | solution.py:416
  86.7 7.4 %copy-start.13 = (f32[48,128]{1,0:T(8,128)S(1)}, f32[48,128]{1,0:T(8,128)}, u32[]{:S(2)}) copy-start(f32[48,128]{1,0:T(8,128)} %get-tuple-element.31) | copy-start | bytes 73732
  86.7 7.4 %copy-start.14 = (f32[48,128]{1,0:T(8,128)S(1)}, f32[48,128]{1,0:T(8,128)}, u32[]{:S(2)}) copy-start(f32[48,128]{1,0:T(8,128)} %get-tuple-element.35) | copy-start | bytes 73732
  86.7 7.4 %copy-start.15 = (f32[48,128]{1,0:T(8,128)S(1)}, f32[48,128]{1,0:T(8,128)}, u32[]{:S(2)}) copy-start(f32[48,128]{1,0:T(8,128)} %get-tuple-element.32) | copy-start | bytes 73732
  86.7 7.4 %copy-start.16 = (f32[48,128]{1,0:T(8,128)S(1)}, f32[48,128]{1,0:T(8,128)}, u32[]{:S(2)}) copy-start(f32[48,128]{1,0:T(8,128)} %get-tuple-element.36) | copy-start | bytes 73732
  86.7 7.4 %copy-start.17 = (f32[48,128]{1,0:T(8,128)S(1)}, f32[48,128]{1,0:T(8,128)}, u32[]{:S(2)}) copy-start(f32[48,128]{1,0:T(8,128)} %get-tuple-element.33) | copy-start | bytes 73732
  86.7 7.4 %copy-start.18 = (f32[48,128]{1,0:T(8,128)S(1)}, f32[48,128]{1,0:T(8,128)}, u32[]{:S(2)}) copy-start(f32[48,128]{1,0:T(8,128)} %get-tuple-element.37) | copy-start | bytes 73732
  103.9 16.2 %all-to-all-start.4 = ((f32[32,8,192]{2,1,0:T(8,128)}), f32[32,8,192]{2,1,0:T(8,128)S(1)}, u32[]{:S(2)}, u32[]{:S(2)}) async-start(f32[32,8,192]{2,1,0:T(8,128)} %bitcast.68), calls=%async_computation.4 | async-start | bytes 524288 | tf_op jit(solution)/shard_map/all_to_all | solution.py:416
  109.8 21.7 %collective-permute-start.1 = (f32[3,1024]{1,0:T(4,128)S(1)}, f32[3,1024]{1,0:T(4,128)S(1)}, u32[]{:S(2)}, u32[]{:S(2)}) collective-permute-start(f32[3,1024]{1,0:T(4,128)S(1)} %bitcast.80), channel_id=1, source_target_pairs={{8,0},{16,8},{24,16},{9,1},{17,9},{25,17},{10,2},{18,10},{26,18},{... | collective-permute-start | bytes 36872 | tf_op jit(solution)/shard_map/ppermute | solution.py:363
  111.1 20.4 %collective-permute-start = (f32[3,1024]{1,0:T(4,128)S(1)}, f32[3,1024]{1,0:T(4,128)S(1)}, u32[]{:S(2)}, u32[]{:S(2)}) collective-permute-start(f32[3,1024]{1,0:T(4,128)S(1)} %bitcast.81), channel_id=1, source_target_pairs={{0,8},{8,16},{16,24},{1,9},{9,17},{17,25},{2,10},{10,18},{18,26},{... | collective-permute-start | bytes 36872 | tf_op jit(solution)/shard_map/ppermute | solution.py:363
  120.8 9.8 %copy-start.9 = (f32[3,4096]{1,0:T(4,128)S(1)}, f32[3,4096]{1,0:T(4,128)}, u32[]{:S(2)}) copy-start(f32[3,4096]{1,0:T(4,128)} %get-tuple-element.27) | copy-start | bytes 147460
  120.8 9.8 %copy-start.10 = (f32[3,4096]{1,0:T(4,128)S(1)}, f32[3,4096]{1,0:T(4,128)}, u32[]{:S(2)}) copy-start(f32[3,4096]{1,0:T(4,128)} %get-tuple-element.28) | copy-start | bytes 147460
  120.8 9.8 %copy-start.11 = (f32[3,4096]{1,0:T(4,128)S(1)}, f32[3,4096]{1,0:T(4,128)}, u32[]{:S(2)}) copy-start(f32[3,4096]{1,0:T(4,128)} %get-tuple-element.29) | copy-start | bytes 147460
  120.8 9.9 %copy-start.12 = (f32[3,4096]{1,0:T(4,128)S(1)}, f32[3,4096]{1,0:T(4,128)}, u32[]{:S(2)}) copy-start(f32[3,4096]{1,0:T(4,128)} %get-tuple-element.30) | copy-start | bytes 147460
  125.7 15.3 %all-to-all-start.5 = ((f32[32,8,192]{2,1,0:T(8,128)}), f32[32,8,192]{2,1,0:T(8,128)S(1)}, u32[]{:S(2)}, u32[]{:S(2)}) async-start(f32[32,8,192]{2,1,0:T(8,128)} %bitcast.66), calls=%async_computation.5 | async-start | bytes 524288 | tf_op jit(solution)/shard_map/all_to_all | solution.py:416
  (5 other events, 3.5 us)

commit v10 on v7

--- a/solution.py
+++ b/solution.py
@@ -93,7 +93,7 @@
 
 
 def update_kernel(
-    q_ref, inc_ref, e_ref, m_ref, tab_ref, start_ref, qn_ref, up_ref, dn_ref, tri_ref, *, groups16, slots16, first
+    q_ref, inc_ref, e_ref, m_ref, tab_ref, start_ref, after_ref, qn_ref, up_ref, dn_ref, tri_ref, *, groups16, slots16, first
 ):
     count = qn_ref.shape[1]
     up_ref[...] = jnp.zeros_like(up_ref)
@@ -211,7 +211,7 @@
     )(transposed, force_t)
 
 
-def update_and_pack(q_state, increments, element, migration, table, capacity):
+def update_prepare(migration, table, capacity, count):
     rows, slab_elems = table.shape
     groups = slab_elems // 128
     groups16 = round_up(groups, 16)
@@ -224,47 +224,49 @@
     mid = lax.reduce_precision(rest, exponent_bits=8, mantissa_bits=7)
     lo = rest - mid
     pieces = jnp.concatenate([hi, mid, lo], axis=1).astype(jnp.bfloat16)
-    count = q_state.shape[1]
-    parts = UPDATE_PARTS
-    share = count // parts
+    share = count // UPDATE_PARTS
     flags = jnp.stack([migration == 1, migration == -1]).astype(jnp.float32)
-    per_part = jnp.sum(flags.reshape(2, parts, share), axis=2)
+    per_part = jnp.sum(flags.reshape(2, UPDATE_PARTS, share), axis=2)
     starts = jnp.cumsum(per_part, axis=1) - per_part
     starts = jnp.pad(starts.T, ((0, 0), (0, 6)))[:, :, None]
-    q_parts, up, down = [], 0.0, 0.0
-    for part in range(parts):
-        q_part, up_part, down_part = pl.pallas_call(
-            functools.partial(
-                update_kernel, groups16=groups16, slots16=slots16, first=part * share // CHUNK
-            ),
-            out_shape=(
-                jax.ShapeDtypeStruct((3, share), jnp.float32),
-                jax.ShapeDtypeStruct((3 * slots16, 128), jnp.float32),
-                jax.ShapeDtypeStruct((3 * slots16, 128), jnp.float32),
-            ),
-            scratch_shapes=[pltpu.VMEM((CHUNK, CHUNK), jnp.bfloat16)],
-            cost_estimate=pl.CostEstimate(
-                flops=16 * 3 * (5 * groups16 + 6 * slots16) * 128 * share,
-                transcendentals=0,
-                bytes_accessed=40 * share,
-            ),
-        )(
-            q_state,
-            increments,
-            element.reshape(1, -1),
-            migration.reshape(1, -1),
-            pieces,
-            starts[part],
-        )
-        q_parts.append(q_part)
-        up = up + up_part
-        down = down + down_part
-    q_next = jnp.concatenate(q_parts, axis=1)
-
-    def unpack(acc):
-        return acc.reshape(3, slots16, 128)[:, :slots].reshape(3, slots * 128)
-
-    return q_next, unpack(up), unpack(down)
+    return pieces, starts, groups16, slots16
+
+
+def update_part(part, prepared, after, q_state, increments, element, migration):
+    pieces, starts, groups16, slots16 = prepared
+    share = q_state.shape[1] // UPDATE_PARTS
+    vmem = pl.BlockSpec(memory_space=pltpu.VMEM)
+    return pl.pallas_call(
+        functools.partial(
+            update_kernel, groups16=groups16, slots16=slots16, first=part * share // CHUNK
+        ),
+        out_shape=(
+            jax.ShapeDtypeStruct((3, share), jnp.float32),
+            jax.ShapeDtypeStruct((3 * slots16, 128), jnp.float32),
+            jax.ShapeDtypeStruct((3 * slots16, 128), jnp.float32),
+        ),
+        in_specs=[vmem] * 6 + [pl.BlockSpec(memory_space=pl.ANY)],
+        out_specs=(vmem, vmem, vmem),
+        scratch_shapes=[pltpu.VMEM((CHUNK, CHUNK), jnp.bfloat16)],
+        cost_estimate=pl.CostEstimate(
+            flops=16 * 3 * (5 * groups16 + 6 * slots16) * 128 * share,
+            transcendentals=0,
+            bytes_accessed=40 * share,
+        ),
+    )(
+        q_state,
+        increments,
+        element.reshape(1, -1),
+        migration.reshape(1, -1),
+        pieces,
+        starts[part],
+        after,
+    )
+
+
+def unpack(acc, capacity):
+    slots = capacity // 128
+    return acc.reshape(3, -1, 128)[:, :slots].reshape(3, slots * 128)
 
 
 def sweep_kernel(idx_ref, g_ref, s_ref, pt_ref, ft_ref, v_ref, vout_ref, send_ref):
@@ -341,12 +343,7 @@
     sums = jnp.sum(received, axis=0).reshape(4, slab_elems // n_rad)
     element_stress = sums / volume
 
-    q_next, upward, downward = update_and_pack(
-        q_state, increments, element, migration, velocity_grad, capacity
-    )
-    from_lower = passed_along(upward, "slab", 1)
-    from_upper = passed_along(downward, "slab", -1)
-    arrivals = jnp.stack([from_lower, from_upper])
+    prepared = update_prepare(migration, velocity_grad, capacity, q_state.shape[1])
 
     own_blocks = stiffness.shape[0]
     groups = (
@@ -365,11 +362,30 @@
     transposed = jnp.swapaxes(preconditioner, 1, 2)
     force_t = force.T
     velocity, send = first_velocity(transposed, force_t, copies)
+    q_parts, upward, downward = [], 0.0, 0.0
     for sweep_index in range(1, ITERS):
+        if len(q_parts) < UPDATE_PARTS:
+            q_part, up_part, down_part = update_part(
+                len(q_parts), prepared, velocity, q_state, increments, element, migration
+            )
+            q_parts.append(q_part)
+            upward = upward + up_part
+            downward = downward + down_part
         gathered = lax.all_to_all(send, ("slab", "rad"), 0, 0, tiled=True)
         velocity, send = sweep(
             where_read, gathered, stiffness, transposed, force_t, velocity, copies
         )
+    while len(q_parts) < UPDATE_PARTS:
+        q_part, up_part, down_part = update_part(
+            len(q_parts), prepared, velocity, q_state, increments, element, migration
+        )
+        q_parts.append(q_part)
+        upward = upward + up_part
+        downward = downward + down_part
+    q_next = jnp.concatenate(q_parts, axis=1)
+    from_lower = passed_along(unpack(upward, capacity), "slab", 1)
+    from_upper = passed_along(unpack(downward, capacity), "slab", -1)
+    arrivals = jnp.stack([from_lower, from_upper])
     return (q_next, arrivals, element_stress, velocity)
 
 

time: 137 us -> 139 us (1.015)
  waiting for transfers between devices: 21 us -> 23.4 us
    all_to_all x1, waiting for transfers between devices: 0.01 us -> 5.94 us  [body(): received = lax.all_to_all(send, ('slab', 'rad'), 0, 0, tiled=True)]
    all_to_all x5, waiting for transfers between devices: 21 us -> 17.4 us  [body(): gathered = lax.all_to_all(send, ('slab', 'rad'), 0, 0, tiled=True)]
where the time goes in v10:
time: 139 us
  Pallas kernels  71.4 us (51%)
  starting transfers between devices  30.6 us (22%)
  waiting for transfers between devices  23.4 us (17%)
  local copies, waits for them, and re-layouts  7.72 us (6%)
  other arithmetic  3.24 us (2%)
    pallas_call x4, Pallas kernels, update_part(): pl.pallas_call(functools.partial(update_kernel, groups16=groups16, slots1...  29.4 us
    pallas_call x5, Pallas kernels, sweep(): pl.pallas_call(sweep_kernel, out_shape=(jax.ShapeDtypeStruct(velocity.sha...  26.7 us
    all_to_all x5, starting transfers between devices, body(): gathered = lax.all_to_all(send, ('slab', 'rad'), 0, 0, tiled=True)  18.3 us
    all_to_all x5, waiting for transfers between devices, body(): gathered = lax.all_to_all(send, ('slab', 'rad'), 0, 0, tiled=True)  17.4 us
    pallas_call x1, Pallas kernels, stress_partials(): pl.pallas_call(functools.partial(stress_kernel, groups=groups, rows=rows)...  12.9 us
    all_to_all x1, starting transfers between devices, body(): received = lax.all_to_all(send, ('slab', 'rad'), 0, 0, tiled=True)  7.3 us
    unnamed x49, local copies, waits for them, and re-layouts  6.02 us
    all_to_all x1, waiting for transfers between devices, body(): received = lax.all_to_all(send, ('slab', 'rad'), 0, 0, tiled=True)  5.94 us
  transfers between devices with their start and end apart: 8, of which 5 were waited for; matrix products, arithmetic and copies ran while one was open for 5% of the time, Pallas kernels for 25%

profile of v10, /device:TPU:0, one launch (start us, length us, event | category | flops | bytes accessed | tf_op | source)
XLA Modules:
  0.0 138.6 jit_solution(936235368542991690)
XLA Ops:
  0.7 12.9 %shard_map.129 = f32[32,12,128]{2,1,0:T(8,128)} custom-call(s32[1]{0:T(128)} %bitcast.6.slab_ref, f32[3,16384]{1,0:T(4,128)} %q_ref.9, s32[1,16384]{1,0:T(1,128)} %bitcast.84, s32[1,16384]{1,0:T(1,128)} %bitcast.73), custom_call_target="tpu_custom_call" | custom-call | flops 4026531840 | bytes 327680 | tf_op jit(solution)/shard_map/pallas_call | solution.py:176
  13.6 7.3 %all-to-all-start = ((f32[32,12,128]{2,1,0:T(8,128)}), f32[32,12,128]{2,1,0:T(8,128)S(1)}, u32[]{:S(2)}, u32[]{:S(2)}) async-start(f32[32,12,128]{2,1,0:T(8,128)} %shard_map.129), calls=%async_computation | async-start | bytes 524288 | tf_op jit(solution)/shard_map/all_to_all | solution.py:342
  22.1 1.8 %copy.47 = f32[8,192,192]{1,2,0:T(8,128)} copy(f32[8,192,192]{2,1,0:T(8,128)S(1)} %copy-done.1) | data formatting | bytes 2359296 | tf_op args[9]
  25.4 5.9 %all-to-all-done = f32[32,12,128]{2,1,0:T(8,128)S(1)} async-done(((f32[32,12,128]{2,1,0:T(8,128)}), f32[32,12,128]{2,1,0:T(8,128)S(1)}, u32[]{:S(2)}, u32[]{:S(2)}) %all-to-all-start) | async-done | bytes 196640 | tf_op jit(solution)/shard_map/all_to_all | solution.py:342
  32.8 2.4 %shard_map.130 = (f32[8,192]{1,0:T(8,128)}, f32[256,192]{1,0:T(8,128)}) custom-call(f32[8,192,192]{2,1,0:T(8,128)} %bitcast.55, f32[192,8]{1,0:T(8,128)} %convolution_bitcast_fusion.ft_ref), custom_call_target="tpu_custom_call" | custom-call | flops 589824 | bytes 1179648 | tf_op jit(solution)/shard_map/pallas_call | solution.py:202
  35.2 2.6 %all-to-all-start.1 = ((f32[32,8,192]{2,1,0:T(8,128)}), f32[32,8,192]{2,1,0:T(8,128)S(1)}, u32[]{:S(2)}, u32[]{:S(2)}) async-start(f32[32,8,192]{2,1,0:T(8,128)} %bitcast.68), calls=%async_computation.1 | async-start | bytes 524288 | tf_op jit(solution)/shard_map/all_to_all | solution.py:374
  37.8 7.3 %shard_map.131 = (f32[3,4096]{1,0:T(4,128)}, f32[48,128]{1,0:T(8,128)}, f32[48,128]{1,0:T(8,128)}) custom-call(f32[3,16384]{1,0:T(4,128)} %q_ref.9, f32[3,16384]{1,0:T(4,128)} %inc_ref.7, s32[1,16384]{1,0:T(1,128)} %bitcast.85, s32[1,16384]{1,0:T(1,128)} %bitcast.74, bf16[160,384]{1,0:T(8,128)(2,1)} %pad_maximum_fusion.1.tab_ref, ...), custom_call_target="tpu_custom_call" | custom-call | flops 6442450944 | bytes 163840 | tf_op jit(solution)/shard_map/pallas_call | solution.py:239
  45.7 2.4 %all-to-all-done.1 = f32[32,8,192]{2,1,0:T(8,128)S(1)} async-done(((f32[32,8,192]{2,1,0:T(8,128)}), f32[32,8,192]{2,1,0:T(8,128)S(1)}, u32[]{:S(2)}, u32[]{:S(2)}) %all-to-all-start.1) | async-done | bytes 196640 | tf_op jit(solution)/shard_map/all_to_all | solution.py:374
  48.9 5.3 %shard_map.132 = (f32[8,192]{1,0:T(8,128)}, f32[256,192]{1,0:T(8,128)}) custom-call(s32[32]{0:T(128)} %reshape.92.idx_ref, f32[256,192]{1,0:T(8,128)} %bitcast.63, f32[8,4,192,192]{3,2,1,0:T(8,128)} %s_ref.9, f32[8,192,192]{2,1,0:T(8,128)} %bitcast.56, f32[192,8]{1,0:T(8,128)} %convolution_bitcast_fusion.ft_ref, f32[8,192]{1,0:T(8,128)} %get-tuple-element.27.after_ref.v_ref), custom_call_target="tpu_custom_call" | custom-call | flops 2949120 | bytes 6094848 | tf_op jit(solution)/shard_map/pallas_call | solution.py:299
  54.2 3.4 %all-to-all-start.2 = ((f32[32,8,192]{2,1,0:T(8,128)}), f32[32,8,192]{2,1,0:T(8,128)S(1)}, u32[]{:S(2)}, u32[]{:S(2)}) async-start(f32[32,8,192]{2,1,0:T(8,128)} %bitcast.69), calls=%async_computation.2 | async-start | bytes 524288 | tf_op jit(solution)/shard_map/all_to_all | solution.py:374
  57.6 7.4 %shard_map.133 = (f32[3,4096]{1,0:T(4,128)}, f32[48,128]{1,0:T(8,128)}, f32[48,128]{1,0:T(8,128)}) custom-call(f32[3,16384]{1,0:T(4,128)} %q_ref.9, f32[3,16384]{1,0:T(4,128)} %inc_ref.7, s32[1,16384]{1,0:T(1,128)} %bitcast.86, s32[1,16384]{1,0:T(1,128)} %bitcast.75, bf16[160,384]{1,0:T(8,128)(2,1)} %pad_maximum_fusion.1.tab_ref, ...), custom_call_target="tpu_custom_call" | custom-call | flops 6442450944 | bytes 163840 | tf_op jit(solution)/shard_map/pallas_call | solution.py:239
  65.0 3.0 %all-to-all-done.2 = f32[32,8,192]{2,1,0:T(8,128)S(1)} async-done(((f32[32,8,192]{2,1,0:T(8,128)}), f32[32,8,192]{2,1,0:T(8,128)S(1)}, u32[]{:S(2)}, u32[]{:S(2)}) %all-to-all-start.2) | async-done | bytes 196640 | tf_op jit(solution)/shard_map/all_to_all | solution.py:374
  68.7 5.3 %shard_map.134 = (f32[8,192]{1,0:T(8,128)}, f32[256,192]{1,0:T(8,128)}) custom-call(s32[32]{0:T(128)} %reshape.92.idx_ref, f32[256,192]{1,0:T(8,128)} %bitcast.64, f32[8,4,192,192]{3,2,1,0:T(8,128)} %s_ref.9, f32[8,192,192]{2,1,0:T(8,128)} %bitcast.57, f32[192,8]{1,0:T(8,128)} %convolution_bitcast_fusion.ft_ref, f32[8,192]{1,0:T(8,128)} %get-tuple-element.30.after_ref.v_ref), custom_call_target="tpu_custom_call" | custom-call | flops 2949120 | bytes 6094848 | tf_op jit(solution)/shard_map/pallas_call | solution.py:299
  74.0 2.8 %all-to-all-start.3 = ((f32[32,8,192]{2,1,0:T(8,128)}), f32[32,8,192]{2,1,0:T(8,128)S(1)}, u32[]{:S(2)}, u32[]{:S(2)}) async-start(f32[32,8,192]{2,1,0:T(8,128)} %bitcast.70), calls=%async_computation.3 | async-start | bytes 524288 | tf_op jit(solution)/shard_map/all_to_all | solution.py:374
  76.9 7.3 %shard_map.135 = (f32[3,4096]{1,0:T(4,128)}, f32[48,128]{1,0:T(8,128)}, f32[48,128]{1,0:T(8,128)}) custom-call(f32[3,16384]{1,0:T(4,128)} %q_ref.9, f32[3,16384]{1,0:T(4,128)} %inc_ref.7, s32[1,16384]{1,0:T(1,128)} %bitcast.87, s32[1,16384]{1,0:T(1,128)} %bitcast.76, bf16[160,384]{1,0:T(8,128)(2,1)} %pad_maximum_fusion.1.tab_ref, ...), custom_call_target="tpu_custom_call" | custom-call | flops 6442450944 | bytes 163840 | tf_op jit(solution)/shard_map/pallas_call | solution.py:239
  84.2 3.0 %all-to-all-done.3 = f32[32,8,192]{2,1,0:T(8,128)S(1)} async-done(((f32[32,8,192]{2,1,0:T(8,128)}), f32[32,8,192]{2,1,0:T(8,128)S(1)}, u32[]{:S(2)}, u32[]{:S(2)}) %all-to-all-start.3) | async-done | bytes 196640 | tf_op jit(solution)/shard_map/all_to_all | solution.py:374
  87.9 5.3 %shard_map.136 = (f32[8,192]{1,0:T(8,128)}, f32[256,192]{1,0:T(8,128)}) custom-call(s32[32]{0:T(128)} %reshape.92.idx_ref, f32[256,192]{1,0:T(8,128)} %bitcast.65, f32[8,4,192,192]{3,2,1,0:T(8,128)} %s_ref.9, f32[8,192,192]{2,1,0:T(8,128)} %bitcast.58, f32[192,8]{1,0:T(8,128)} %convolution_bitcast_fusion.ft_ref, f32[8,192]{1,0:T(8,128)} %get-tuple-element.33.after_ref.v_ref), custom_call_target="tpu_custom_call" | custom-call | flops 2949120 | bytes 6094848 | tf_op jit(solution)/shard_map/pallas_call | solution.py:299
  93.3 2.8 %all-to-all-start.4 = ((f32[32,8,192]{2,1,0:T(8,128)}), f32[32,8,192]{2,1,0:T(8,128)S(1)}, u32[]{:S(2)}, u32[]{:S(2)}) async-start(f32[32,8,192]{2,1,0:T(8,128)} %bitcast.66), calls=%async_computation.4 | async-start | bytes 524288 | tf_op jit(solution)/shard_map/all_to_all | solution.py:374
  96.1 7.4 %shard_map.137 = (f32[3,4096]{1,0:T(4,128)}, f32[48,128]{1,0:T(8,128)}, f32[48,128]{1,0:T(8,128)}) custom-call(f32[3,16384]{1,0:T(4,128)} %q_ref.9, f32[3,16384]{1,0:T(4,128)} %inc_ref.7, s32[1,16384]{1,0:T(1,128)} %bitcast.88, s32[1,16384]{1,0:T(1,128)} %bitcast.77, bf16[160,384]{1,0:T(8,128)(2,1)} %pad_maximum_fusion.1.tab_ref, ...), custom_call_target="tpu_custom_call" | custom-call | flops 6442450944 | bytes 163840 | tf_op jit(solution)/shard_map/pallas_call | solution.py:239
  104.4 3.7 %collective-permute-start = (f32[3,1024]{1,0:T(4,128)S(1)}, f32[3,1024]{1,0:T(4,128)S(1)}, u32[]{:S(2)}, u32[]{:S(2)}) collective-permute-start(f32[3,1024]{1,0:T(4,128)S(1)} %bitcast.80), channel_id=1, source_target_pairs={{0,8},{8,16},{16,24},{1,9},{9,17},{17,25},{2,10},{10,18},{18,26},{... | collective-permute-start | bytes 36872 | tf_op jit(solution)/shard_map/ppermute | solution.py:318
  110.1 5.4 %shard_map.138 = (f32[8,192]{1,0:T(8,128)}, f32[256,192]{1,0:T(8,128)}) custom-call(s32[32]{0:T(128)} %reshape.92.idx_ref, f32[256,192]{1,0:T(8,128)} %bitcast.61, f32[8,4,192,192]{3,2,1,0:T(8,128)} %s_ref.9, f32[8,192,192]{2,1,0:T(8,128)} %bitcast.59, f32[192,8]{1,0:T(8,128)} %convolution_bitcast_fusion.ft_ref, f32[8,192]{1,0:T(8,128)} %get-tuple-element.36.after_ref.v_ref), custom_call_target="tpu_custom_call" | custom-call | flops 2949120 | bytes 6094848 | tf_op jit(solution)/shard_map/pallas_call | solution.py:299
  115.5 6.7 %all-to-all-start.5 = ((f32[32,8,192]{2,1,0:T(8,128)}), f32[32,8,192]{2,1,0:T(8,128)S(1)}, u32[]{:S(2)}, u32[]{:S(2)}) async-start(f32[32,8,192]{2,1,0:T(8,128)} %bitcast.67), calls=%async_computation.5 | async-start | bytes 524288 | tf_op jit(solution)/shard_map/all_to_all | solution.py:374
  123.6 8.9 %all-to-all-done.5 = f32[32,8,192]{2,1,0:T(8,128)S(1)} async-done(((f32[32,8,192]{2,1,0:T(8,128)}), f32[32,8,192]{2,1,0:T(8,128)S(1)}, u32[]{:S(2)}, u32[]{:S(2)}) %all-to-all-start.5) | async-done | bytes 196640 | tf_op jit(solution)/shard_map/all_to_all | solution.py:374
  133.3 5.3 %shard_map.139 = (f32[8,192]{1,0:T(8,128)}, f32[256,192]{1,0:T(8,128)}) custom-call(s32[32]{0:T(128)} %reshape.92.idx_ref, f32[256,192]{1,0:T(8,128)} %bitcast.62, f32[8,4,192,192]{3,2,1,0:T(8,128)} %s_ref.9, f32[8,192,192]{2,1,0:T(8,128)} %bitcast.60, f32[192,8]{1,0:T(8,128)} %convolution_bitcast_fusion.ft_ref, f32[8,192]{1,0:T(8,128)} %get-tuple-element.48.v_ref), custom_call_target="tpu_custom_call" | custom-call | flops 2949120 | bytes 6094848 | tf_op jit(solution)/shard_map/pallas_call | solution.py:299
  (77 shorter events, 11.7 us)
Async XLA Ops:
  0.6 30.9 %copy-start = (f32[192,192]{1,0:T(8,128)S(1)}, f32[192,192]{1,0:T(8,128)}, u32[]{:S(2)}) copy-start(f32[192,192]{1,0:T(8,128)} %param.16) | copy-start | bytes 442372
  0.7 20.3 %copy-start.8 = (s32[16384]{0:T(1024)S(1)}, s32[16384]{0:T(1024)}, u32[]{:S(2)}) copy-start(s32[16384]{0:T(1024)} %param.14) | copy-start | bytes 196612
  0.7 20.7 %copy-start.20 = (s32[8,4]{0,1:T(4,128)S(1)}, s32[8,4]{0,1:T(4,128)}, u32[]{:S(2)}) copy-start(s32[8,4]{0,1:T(4,128)} %param.18) | copy-start | bytes 388
  0.7 21.4 %copy-start.19 = (f32[384]{0:T(512)S(1)}, f32[384]{0:T(512)}, u32[]{:S(2)}) copy-start(f32[384]{0:T(512)} %param.15) | copy-start | bytes 4612
  0.7 21.4 %copy-start.1 = (f32[8,192,192]{2,1,0:T(8,128)S(1)}, f32[8,192,192]{2,1,0:T(8,128)}, u32[]{:S(2)}) copy-start(f32[8,192,192]{2,1,0:T(8,128)} %param.19) | copy-start | bytes 3538948
  13.6 17.7 %all-to-all-start = ((f32[32,12,128]{2,1,0:T(8,128)}), f32[32,12,128]{2,1,0:T(8,128)S(1)}, u32[]{:S(2)}, u32[]{:S(2)}) async-start(f32[32,12,128]{2,1,0:T(8,128)} %shard_map.129), calls=%async_computation | async-start | bytes 524288 | tf_op jit(solution)/shard_map/all_to_all | solution.py:342
  22.1 2.5 %copy-start.7 = (f32[5,3072]{1,0:T(8,128)S(1)}, f32[5,3072]{1,0:T(8,128)}, u32[]{:S(2)}) copy-start(f32[5,3072]{1,0:T(8,128)} %param.12) | copy-start | bytes 184324
  35.2 13.0 %all-to-all-start.1 = ((f32[32,8,192]{2,1,0:T(8,128)}), f32[32,8,192]{2,1,0:T(8,128)S(1)}, u32[]{:S(2)}, u32[]{:S(2)}) async-start(f32[32,8,192]{2,1,0:T(8,128)} %bitcast.68), calls=%async_computation.1 | async-start | bytes 524288 | tf_op jit(solution)/shard_map/all_to_all | solution.py:374
  54.2 13.8 %all-to-all-start.2 = ((f32[32,8,192]{2,1,0:T(8,128)}), f32[32,8,192]{2,1,0:T(8,128)S(1)}, u32[]{:S(2)}, u32[]{:S(2)}) async-start(f32[32,8,192]{2,1,0:T(8,128)} %bitcast.69), calls=%async_computation.2 | async-start | bytes 524288 | tf_op jit(solution)/shard_map/all_to_all | solution.py:374
  74.0 13.2 %all-to-all-start.3 = ((f32[32,8,192]{2,1,0:T(8,128)}), f32[32,8,192]{2,1,0:T(8,128)S(1)}, u32[]{:S(2)}, u32[]{:S(2)}) async-start(f32[32,8,192]{2,1,0:T(8,128)} %bitcast.70), calls=%async_computation.3 | async-start | bytes 524288 | tf_op jit(solution)/shard_map/all_to_all | solution.py:374
  93.3 16.1 %all-to-all-start.4 = ((f32[32,8,192]{2,1,0:T(8,128)}), f32[32,8,192]{2,1,0:T(8,128)S(1)}, u32[]{:S(2)}, u32[]{:S(2)}) async-start(f32[32,8,192]{2,1,0:T(8,128)} %bitcast.66), calls=%async_computation.4 | async-start | bytes 524288 | tf_op jit(solution)/shard_map/all_to_all | solution.py:374
  96.1 7.4 %copy-start.13 = (f32[48,128]{1,0:T(8,128)S(1)}, f32[48,128]{1,0:T(8,128)}, u32[]{:S(2)}) copy-start(f32[48,128]{1,0:T(8,128)} %get-tuple-element.38) | copy-start | bytes 73732
  96.1 7.4 %copy-start.14 = (f32[48,128]{1,0:T(8,128)S(1)}, f32[48,128]{1,0:T(8,128)}, u32[]{:S(2)}) copy-start(f32[48,128]{1,0:T(8,128)} %get-tuple-element.42) | copy-start | bytes 73732
  96.1 7.4 %copy-start.15 = (f32[48,128]{1,0:T(8,128)S(1)}, f32[48,128]{1,0:T(8,128)}, u32[]{:S(2)}) copy-start(f32[48,128]{1,0:T(8,128)} %get-tuple-element.39) | copy-start | bytes 73732
  96.1 7.4 %copy-start.16 = (f32[48,128]{1,0:T(8,128)S(1)}, f32[48,128]{1,0:T(8,128)}, u32[]{:S(2)}) copy-start(f32[48,128]{1,0:T(8,128)} %get-tuple-element.43) | copy-start | bytes 73732
  96.1 7.4 %copy-start.17 = (f32[48,128]{1,0:T(8,128)S(1)}, f32[48,128]{1,0:T(8,128)}, u32[]{:S(2)}) copy-start(f32[48,128]{1,0:T(8,128)} %get-tuple-element.40) | copy-start | bytes 73732
  96.1 7.4 %copy-start.18 = (f32[48,128]{1,0:T(8,128)S(1)}, f32[48,128]{1,0:T(8,128)}, u32[]{:S(2)}) copy-start(f32[48,128]{1,0:T(8,128)} %get-tuple-element.44) | copy-start | bytes 73732
  104.4 18.6 %collective-permute-start = (f32[3,1024]{1,0:T(4,128)S(1)}, f32[3,1024]{1,0:T(4,128)S(1)}, u32[]{:S(2)}, u32[]{:S(2)}) collective-permute-start(f32[3,1024]{1,0:T(4,128)S(1)} %bitcast.80), channel_id=1, source_target_pairs={{0,8},{8,16},{16,24},{1,9},{9,17},{17,25},{2,10},{10,18},{18,26},{... | collective-permute-start | bytes 36872 | tf_op jit(solution)/shard_map/ppermute | solution.py:318
  108.1 14.9 %collective-permute-start.1 = (f32[3,1024]{1,0:T(4,128)S(1)}, f32[3,1024]{1,0:T(4,128)S(1)}, u32[]{:S(2)}, u32[]{:S(2)}) collective-permute-start(f32[3,1024]{1,0:T(4,128)S(1)} %bitcast.81), channel_id=1, source_target_pairs={{8,0},{16,8},{24,16},{9,1},{17,9},{25,17},{10,2},{18,10},{26,18},{... | collective-permute-start | bytes 36872 | tf_op jit(solution)/shard_map/ppermute | solution.py:318
  110.1 12.1 %copy-start.9 = (f32[3,4096]{1,0:T(4,128)S(1)}, f32[3,4096]{1,0:T(4,128)}, u32[]{:S(2)}) copy-start(f32[3,4096]{1,0:T(4,128)} %get-tuple-element.28) | copy-start | bytes 147460
  110.1 12.1 %copy-start.10 = (f32[3,4096]{1,0:T(4,128)S(1)}, f32[3,4096]{1,0:T(4,128)}, u32[]{:S(2)}) copy-start(f32[3,4096]{1,0:T(4,128)} %get-tuple-element.31) | copy-start | bytes 147460
  110.1 12.1 %copy-start.11 = (f32[3,4096]{1,0:T(4,128)S(1)}, f32[3,4096]{1,0:T(4,128)}, u32[]{:S(2)}) copy-start(f32[3,4096]{1,0:T(4,128)} %get-tuple-element.34) | copy-start | bytes 147460
  110.1 12.1 %copy-start.12 = (f32[3,4096]{1,0:T(4,128)S(1)}, f32[3,4096]{1,0:T(4,128)}, u32[]{:S(2)}) copy-start(f32[3,4096]{1,0:T(4,128)} %get-tuple-element.37) | copy-start | bytes 147460
  115.5 17.1 %all-to-all-start.5 = ((f32[32,8,192]{2,1,0:T(8,128)}), f32[32,8,192]{2,1,0:T(8,128)S(1)}, u32[]{:S(2)}, u32[]{:S(2)}) async-start(f32[32,8,192]{2,1,0:T(8,128)} %bitcast.67), calls=%async_computation.5 | async-start | bytes 524288 | tf_op jit(solution)/shard_map/all_to_all | solution.py:374
  (5 other events, 3.5 us)

commit v11 on v7

--- a/solution.py
+++ b/solution.py
@@ -267,31 +267,36 @@
     return q_next, unpack(up), unpack(down)
 
 
-def sweep_kernel(idx_ref, g_ref, s_ref, pt_ref, ft_ref, v_ref, vout_ref, send_ref):
+def sweep_kernel(idx_ref, g_ref, m_ref, v1_ref, v_ref, vout_ref, send_ref):
     total = g_ref.shape[0]
-    own = v_ref.shape[0]
-    width = s_ref.shape[1]
+    own, size = v_ref.shape
+    width = m_ref.shape[1]
+    near = []
+    for k in range(own * width):
+        w = idx_ref[k]
+        inside = jnp.logical_and(w >= 0, w < total)
+        row = g_ref[pl.ds(jnp.clip(w, 0, total - 1), 1), :]
+        near.append(jnp.where(inside, row, 0.0))
+    lanes = round_up(size, 128)
+    near = jnp.concatenate(near, axis=0)
+    near = jnp.pad(near, ((0, 128 - own * width), (0, lanes - size)))
+    columns = near.T
     rows = []
     for b in range(own):
         acc = None
         for n in range(width):
-            w = idx_ref[b * width + n]
-            inside = jnp.logical_and(w >= 0, w < total)
-            near = g_ref[pl.ds(jnp.clip(w, 0, total - 1), 1), :]
-            near = jnp.where(inside, near, 0.0)
-            term = s_ref[b, n] * near
+            k = b * width + n
+            term = m_ref[b, n] * columns[:size, k : k + 1]
             acc = term if acc is None else acc + term
-        image = jnp.sum(acc, axis=1, keepdims=True)
-        rest = ft_ref[:, b : b + 1] - image
-        update = jnp.sum(pt_ref[b] * rest, axis=0, keepdims=True)
-        rows.append(v_ref[b : b + 1, :] + damping * update)
+        image = jnp.sum(acc, axis=0, keepdims=True)
+        rows.append(v_ref[b : b + 1, :] + v1_ref[b : b + 1, :] - damping * image)
     fresh = jnp.concatenate(rows, axis=0)
     vout_ref[...] = fresh
     for k in range(send_ref.shape[0] // own):
         send_ref[k * own : (k + 1) * own, :] = fresh
 
 
-def sweep(where_read, gathered, stiffness, transposed, force_t, velocity, copies):
+def sweep(where_read, gathered, merged, first, velocity, copies):
     own = velocity.shape[0]
     vmem = pl.BlockSpec(memory_space=pltpu.VMEM)
     return pl.pallas_call(
@@ -300,15 +305,12 @@
             jax.ShapeDtypeStruct(velocity.shape, jnp.float32),
             jax.ShapeDtypeStruct((copies * own, velocity.shape[1]), jnp.float32),
         ),
-        in_specs=[pl.BlockSpec(memory_space=pltpu.SMEM)] + [vmem] * 5,
+        in_specs=[pl.BlockSpec(memory_space=pltpu.SMEM)] + [vmem] * 4,
         out_specs=(vmem, vmem),
         cost_estimate=pl.CostEstimate(
-            flops=2 * (stiffness.size + transposed.size),
-            transcendentals=0,
-            bytes_accessed=4 * (stiffness.size + transposed.size + gathered.size),
-        ),
-    )(where_read, gathered, stiffness, transposed, force_t, velocity)
-
+            flops=2 * merged.size, transcendentals=0, bytes_accessed=4 * (merged.size + gathered.size)
+        ),
+    )(where_read, gathered, merged, first, velocity)
 
 def passed_along(array, axis, by):
     size = lax.axis_size(axis)
@@ -365,11 +367,11 @@
     transposed = jnp.swapaxes(preconditioner, 1, 2)
     force_t = force.T
     velocity, send = first_velocity(transposed, force_t, copies)
+    first = velocity
+    merged = jnp.einsum("bik,bnkj->bnji", preconditioner, stiffness, precision=highest)
     for sweep_index in range(1, ITERS):
         gathered = lax.all_to_all(send, ("slab", "rad"), 0, 0, tiled=True)
-        velocity, send = sweep(
-            where_read, gathered, stiffness, transposed, force_t, velocity, copies
-        )
+        velocity, send = sweep(where_read, gathered, merged, first, velocity, copies)
     return (q_next, arrivals, element_stress, velocity)
 
 

time: 137 us -> 150 us (1.095)
  matrix products: 1.24 us -> 16.7 us
  starting transfers between devices: 30.9 us -> 34.1 us
  waiting for transfers between devices: 21 us -> 17.8 us
  Pallas kernels: 71.4 us -> 68.6 us
    dot_general x0 -> x1, matrix products: none -> 15.5 us  [body(): jnp.einsum('bik,bnkj->bnji', preconditioner, stiffness, precision=highest)]
    all_to_all x5, starting transfers between devices: 17.7 us -> 21 us  [body(): gathered = lax.all_to_all(send, ('slab', 'rad'), 0, 0, tiled=True)]
    all_to_all x5, waiting for transfers between devices: 21 us -> 17.8 us  [body(): gathered = lax.all_to_all(send, ('slab', 'rad'), 0, 0, tiled=True)]
    pallas_call x5, Pallas kernels: 26.7 us -> 23.9 us  [sweep(): pl.pallas_call(sweep_kernel, out_shape=(jax.ShapeDtypeStruct(velocity.sha...]
  transfers between devices with their start and end apart: 8 -> 8, of which waited for: 5 -> 4; matrix products, arithmetic and copies ran while one was open for 5% -> 15% of each run, Pallas kernels for 25% -> 23%
where the time goes in v11:
time: 150 us; the launch traced here: 149 us
  Pallas kernels  68.6 us (46%)
  starting transfers between devices  34.1 us (23%)
  waiting for transfers between devices  17.8 us (12%)
  matrix products  16.7 us (11%)
  local copies, waits for them, and re-layouts  7.73 us (5%)
  other arithmetic  3.25 us (2%)
    pallas_call x4, Pallas kernels, update_and_pack(): pl.pallas_call(functools.partial(update_kernel, groups16=groups16, slots1...  29.4 us
    pallas_call x5, Pallas kernels, sweep(): pl.pallas_call(sweep_kernel, out_shape=(jax.ShapeDtypeStruct(velocity.sha...  23.9 us
    all_to_all x5, starting transfers between devices, body(): gathered = lax.all_to_all(send, ('slab', 'rad'), 0, 0, tiled=True)  21 us
    all_to_all x5, waiting for transfers between devices, body(): gathered = lax.all_to_all(send, ('slab', 'rad'), 0, 0, tiled=True)  17.8 us
    dot_general x1, matrix products, body(): jnp.einsum('bik,bnkj->bnji', preconditioner, stiffness, precision=highest)  15.5 us
    pallas_call x1, Pallas kernels, stress_partials(): pl.pallas_call(functools.partial(stress_kernel, groups=groups, rows=rows)...  12.9 us
    all_to_all x1, starting transfers between devices, body(): received = lax.all_to_all(send, ('slab', 'rad'), 0, 0, tiled=True)  7.3 us
    unnamed x49, local copies, waits for them, and re-layouts  6.03 us
  transfers between devices with their start and end apart: 8, of which 4 were waited for; matrix products, arithmetic and copies ran while one was open for 15% of the time, Pallas kernels for 23%

profile of v11, /device:TPU:0, one launch (start us, length us, event | category | flops | bytes accessed | tf_op | source)
XLA Modules:
  0.0 149.1 jit_solution(8539438591030068871)
XLA Ops:
  0.7 12.9 %shard_map.133 = f32[32,12,128]{2,1,0:T(8,128)} custom-call(s32[1]{0:T(128)} %bitcast.12.slab_ref, f32[3,16384]{1,0:T(4,128)} %q_ref.9, s32[1,16384]{1,0:T(1,128)} %bitcast.85, s32[1,16384]{1,0:T(1,128)} %bitcast.74), custom_call_target="tpu_custom_call" | custom-call | flops 4026531840 | bytes 327680 | tf_op jit(solution)/shard_map/pallas_call | solution.py:176
  13.6 7.3 %all-to-all-start = ((f32[32,12,128]{2,1,0:T(8,128)}), f32[32,12,128]{2,1,0:T(8,128)S(1)}, u32[]{:S(2)}, u32[]{:S(2)}) async-start(f32[32,12,128]{2,1,0:T(8,128)} %shard_map.133), calls=%async_computation | async-start | bytes 524288 | tf_op jit(solution)/shard_map/all_to_all | solution.py:342
  21.1 1.8 %copy.56 = f32[8,192,192]{1,2,0:T(8,128)} copy(f32[8,192,192]{2,1,0:T(8,128)S(1)} %copy-done.1) | data formatting | bytes 2359296 | tf_op args[9]
  25.4 7.3 %shard_map.129 = (f32[3,4096]{1,0:T(4,128)}, f32[48,128]{1,0:T(8,128)}, f32[48,128]{1,0:T(8,128)}) custom-call(f32[3,16384]{1,0:T(4,128)} %q_ref.9, f32[3,16384]{1,0:T(4,128)} %inc_ref.7, s32[1,16384]{1,0:T(1,128)} %bitcast.86, s32[1,16384]{1,0:T(1,128)} %bitcast.75, bf16[160,384]{1,0:T(8,128)(2,1)} %pad_maximum_fusion.1.tab_ref, ...), custom_call_target="tpu_custom_call" | custom-call | flops 6442450944 | bytes 163840 | tf_op jit(solution)/shard_map/pallas_call | solution.py:236
  32.7 7.3 %shard_map.130 = (f32[3,4096]{1,0:T(4,128)}, f32[48,128]{1,0:T(8,128)}, f32[48,128]{1,0:T(8,128)}) custom-call(f32[3,16384]{1,0:T(4,128)} %q_ref.9, f32[3,16384]{1,0:T(4,128)} %inc_ref.7, s32[1,16384]{1,0:T(1,128)} %bitcast.87, s32[1,16384]{1,0:T(1,128)} %bitcast.76, bf16[160,384]{1,0:T(8,128)(2,1)} %pad_maximum_fusion.1.tab_ref, ...), custom_call_target="tpu_custom_call" | custom-call | flops 6442450944 | bytes 163840 | tf_op jit(solution)/shard_map/pallas_call | solution.py:236
  41.5 2.4 %shard_map.134 = (f32[8,192]{1,0:T(8,128)}, f32[256,192]{1,0:T(8,128)}) custom-call(f32[8,192,192]{2,1,0:T(8,128)} %bitcast.61, f32[192,8]{1,0:T(8,128)} %convolution_bitcast_fusion.ft_ref), custom_call_target="tpu_custom_call" | custom-call | flops 589824 | bytes 1179648 | tf_op jit(solution)/shard_map/pallas_call | solution.py:202
  43.9 5.8 %all-to-all-start.1 = ((f32[32,8,192]{2,1,0:T(8,128)}), f32[32,8,192]{2,1,0:T(8,128)S(1)}, u32[]{:S(2)}, u32[]{:S(2)}) async-start(f32[32,8,192]{2,1,0:T(8,128)} %bitcast.71), calls=%async_computation.1 | async-start | bytes 524288 | tf_op jit(solution)/shard_map/all_to_all | solution.py:373
  49.8 15.5 %fusion.m_ref = f32[8,4,192,192]{3,2,1,0:T(8,128)} fusion(f32[8,4,192,192]{3,2,1,0:T(8,128)} %param.17, f32[8,192,192]{2,1,0:T(8,128)S(1)} %copy-done.1), kind=kOutput, calls=%fused_computation | convolution fusion | flops 2717908992 | bytes 10616832 | tf_op jit(solution)/shard_map/bik,bnkj->bnji/dot_general | solution.py:371
  65.9 4.8 %shard_map.135 = (f32[8,192]{1,0:T(8,128)}, f32[256,192]{1,0:T(8,128)}) custom-call(s32[32]{0:T(128)} %reshape.94.idx_ref, f32[256,192]{1,0:T(8,128)} %bitcast.66, f32[8,4,192,192]{3,2,1,0:T(8,128)} %fusion.m_ref, f32[8,192]{1,0:T(8,128)} %get-tuple-element.40.v1_ref.v_ref, f32[8,192]{1,0:T(8,128)} %get-tuple-element.40.v1_ref.v_ref), custom_call_target="tpu_custom_call" | custom-call | flops 2359296 | bytes 4915200 | tf_op jit(solution)/shard_map/pallas_call | solution.py:302
  70.7 6.0 %all-to-all-start.2 = ((f32[32,8,192]{2,1,0:T(8,128)}), f32[32,8,192]{2,1,0:T(8,128)S(1)}, u32[]{:S(2)}, u32[]{:S(2)}) async-start(f32[32,8,192]{2,1,0:T(8,128)} %bitcast.70), calls=%async_computation.2 | async-start | bytes 524288 | tf_op jit(solution)/shard_map/all_to_all | solution.py:373
  76.7 7.3 %shard_map.131 = (f32[3,4096]{1,0:T(4,128)}, f32[48,128]{1,0:T(8,128)}, f32[48,128]{1,0:T(8,128)}) custom-call(f32[3,16384]{1,0:T(4,128)} %q_ref.9, f32[3,16384]{1,0:T(4,128)} %inc_ref.7, s32[1,16384]{1,0:T(1,128)} %bitcast.88, s32[1,16384]{1,0:T(1,128)} %bitcast.77, bf16[160,384]{1,0:T(8,128)(2,1)} %pad_maximum_fusion.1.tab_ref, ...), custom_call_target="tpu_custom_call" | custom-call | flops 6442450944 | bytes 163840 | tf_op jit(solution)/shard_map/pallas_call | solution.py:236
  84.1 2.9 %all-to-all-done.2 = f32[32,8,192]{2,1,0:T(8,128)S(1)} async-done(((f32[32,8,192]{2,1,0:T(8,128)}), f32[32,8,192]{2,1,0:T(8,128)S(1)}, u32[]{:S(2)}, u32[]{:S(2)}) %all-to-all-start.2) | async-done | bytes 196640 | tf_op jit(solution)/shard_map/all_to_all | solution.py:373
  87.6 4.8 %shard_map.136 = (f32[8,192]{1,0:T(8,128)}, f32[256,192]{1,0:T(8,128)}) custom-call(s32[32]{0:T(128)} %reshape.94.idx_ref, f32[256,192]{1,0:T(8,128)} %bitcast.65, f32[8,4,192,192]{3,2,1,0:T(8,128)} %fusion.m_ref, f32[8,192]{1,0:T(8,128)} %get-tuple-element.40.v1_ref.v_ref, f32[8,192]{1,0:T(8,128)} %get-tuple-element.42.v_ref), custom_call_target="tpu_custom_call" | custom-call | flops 2359296 | bytes 4915200 | tf_op jit(solution)/shard_map/pallas_call | solution.py:302
  92.4 2.8 %all-to-all-start.3 = ((f32[32,8,192]{2,1,0:T(8,128)}), f32[32,8,192]{2,1,0:T(8,128)S(1)}, u32[]{:S(2)}, u32[]{:S(2)}) async-start(f32[32,8,192]{2,1,0:T(8,128)} %bitcast.68), calls=%async_computation.3 | async-start | bytes 524288 | tf_op jit(solution)/shard_map/all_to_all | solution.py:373
  95.3 7.4 %shard_map.132 = (f32[3,4096]{1,0:T(4,128)}, f32[48,128]{1,0:T(8,128)}, f32[48,128]{1,0:T(8,128)}) custom-call(f32[3,16384]{1,0:T(4,128)} %q_ref.9, f32[3,16384]{1,0:T(4,128)} %inc_ref.7, s32[1,16384]{1,0:T(1,128)} %bitcast.89, s32[1,16384]{1,0:T(1,128)} %bitcast.78, bf16[160,384]{1,0:T(8,128)(2,1)} %pad_maximum_fusion.1.tab_ref, ...), custom_call_target="tpu_custom_call" | custom-call | flops 6442450944 | bytes 163840 | tf_op jit(solution)/shard_map/pallas_call | solution.py:236
  103.4 2.1 %all-to-all-done.3 = f32[32,8,192]{2,1,0:T(8,128)S(1)} async-done(((f32[32,8,192]{2,1,0:T(8,128)}), f32[32,8,192]{2,1,0:T(8,128)S(1)}, u32[]{:S(2)}, u32[]{:S(2)}) %all-to-all-start.3) | async-done | bytes 196640 | tf_op jit(solution)/shard_map/all_to_all | solution.py:373
  106.3 4.8 %shard_map.137 = (f32[8,192]{1,0:T(8,128)}, f32[256,192]{1,0:T(8,128)}) custom-call(s32[32]{0:T(128)} %reshape.94.idx_ref, f32[256,192]{1,0:T(8,128)} %bitcast.63, f32[8,4,192,192]{3,2,1,0:T(8,128)} %fusion.m_ref, f32[8,192]{1,0:T(8,128)} %get-tuple-element.40.v1_ref.v_ref, f32[8,192]{1,0:T(8,128)} %get-tuple-element.44.v_ref), custom_call_target="tpu_custom_call" | custom-call | flops 2359296 | bytes 4915200 | tf_op jit(solution)/shard_map/pallas_call | solution.py:302
  111.1 3.7 %all-to-all-start.4 = ((f32[32,8,192]{2,1,0:T(8,128)}), f32[32,8,192]{2,1,0:T(8,128)S(1)}, u32[]{:S(2)}, u32[]{:S(2)}) async-start(f32[32,8,192]{2,1,0:T(8,128)} %bitcast.69), calls=%async_computation.4 | async-start | bytes 524288 | tf_op jit(solution)/shard_map/all_to_all | solution.py:373
  116.2 4.5 %collective-permute-start = (f32[3,1024]{1,0:T(4,128)S(1)}, f32[3,1024]{1,0:T(4,128)S(1)}, u32[]{:S(2)}, u32[]{:S(2)}) collective-permute-start(f32[3,1024]{1,0:T(4,128)S(1)} %bitcast.82), channel_id=1, source_target_pairs={{0,8},{8,16},{16,24},{1,9},{9,17},{17,25},{2,10},{10,18},{18,26},{... | collective-permute-start | bytes 36872 | tf_op jit(solution)/shard_map/ppermute | solution.py:318
  120.7 4.5 %all-to-all-done.4 = f32[32,8,192]{2,1,0:T(8,128)S(1)} async-done(((f32[32,8,192]{2,1,0:T(8,128)}), f32[32,8,192]{2,1,0:T(8,128)S(1)}, u32[]{:S(2)}, u32[]{:S(2)}) %all-to-all-start.4) | async-done | bytes 196640 | tf_op jit(solution)/shard_map/all_to_all | solution.py:373
  125.9 4.8 %shard_map.138 = (f32[8,192]{1,0:T(8,128)}, f32[256,192]{1,0:T(8,128)}) custom-call(s32[32]{0:T(128)} %reshape.94.idx_ref, f32[256,192]{1,0:T(8,128)} %bitcast.64, f32[8,4,192,192]{3,2,1,0:T(8,128)} %fusion.m_ref, f32[8,192]{1,0:T(8,128)} %get-tuple-element.40.v1_ref.v_ref, f32[8,192]{1,0:T(8,128)} %get-tuple-element.46.v_ref), custom_call_target="tpu_custom_call" | custom-call | flops 2359296 | bytes 4915200 | tf_op jit(solution)/shard_map/pallas_call | solution.py:302
  130.7 2.6 %all-to-all-start.5 = ((f32[32,8,192]{2,1,0:T(8,128)}), f32[32,8,192]{2,1,0:T(8,128)S(1)}, u32[]{:S(2)}, u32[]{:S(2)}) async-start(f32[32,8,192]{2,1,0:T(8,128)} %bitcast.67), calls=%async_computation.5 | async-start | bytes 524288 | tf_op jit(solution)/shard_map/all_to_all | solution.py:373
  135.3 8.3 %all-to-all-done.5 = f32[32,8,192]{2,1,0:T(8,128)S(1)} async-done(((f32[32,8,192]{2,1,0:T(8,128)}), f32[32,8,192]{2,1,0:T(8,128)S(1)}, u32[]{:S(2)}, u32[]{:S(2)}) %all-to-all-start.5) | async-done | bytes 196640 | tf_op jit(solution)/shard_map/all_to_all | solution.py:373
  144.3 4.8 %shard_map.139 = (f32[8,192]{1,0:T(8,128)}, f32[256,192]{1,0:T(8,128)}) custom-call(s32[32]{0:T(128)} %reshape.94.idx_ref, f32[256,192]{1,0:T(8,128)} %bitcast.62, f32[8,4,192,192]{3,2,1,0:T(8,128)} %fusion.m_ref, f32[8,192]{1,0:T(8,128)} %get-tuple-element.40.v1_ref.v_ref, f32[8,192]{1,0:T(8,128)} %get-tuple-element.48.v_ref), custom_call_target="tpu_custom_call" | custom-call | flops 2359296 | bytes 4915200 | tf_op jit(solution)/shard_map/pallas_call | solution.py:302
  (78 shorter events, 11.7 us)
Async XLA Ops:
  0.6 39.7 %copy-start = (f32[192,192]{1,0:T(8,128)S(1)}, f32[192,192]{1,0:T(8,128)}, u32[]{:S(2)}) copy-start(f32[192,192]{1,0:T(8,128)} %param.16) | copy-start | bytes 442372
  0.7 20.3 %copy-start.8 = (s32[16384]{0:T(1024)S(1)}, s32[16384]{0:T(1024)}, u32[]{:S(2)}) copy-start(s32[16384]{0:T(1024)} %param.14) | copy-start | bytes 196612
  0.7 20.3 %copy-start.19 = (f32[384]{0:T(512)S(1)}, f32[384]{0:T(512)}, u32[]{:S(2)}) copy-start(f32[384]{0:T(512)} %param.15) | copy-start | bytes 4612
  0.7 20.4 %copy-start.1 = (f32[8,192,192]{2,1,0:T(8,128)S(1)}, f32[8,192,192]{2,1,0:T(8,128)}, u32[]{:S(2)}) copy-start(f32[8,192,192]{2,1,0:T(8,128)} %param.19) | copy-start | bytes 3538948
  0.7 22.2 %copy-start.20 = (s32[8,4]{0,1:T(4,128)S(1)}, s32[8,4]{0,1:T(4,128)}, u32[]{:S(2)}) copy-start(s32[8,4]{0,1:T(4,128)} %param.18) | copy-start | bytes 388
  0.7 22.9 %copy-start.7 = (f32[5,3072]{1,0:T(8,128)S(1)}, f32[5,3072]{1,0:T(8,128)}, u32[]{:S(2)}) copy-start(f32[5,3072]{1,0:T(8,128)} %param.12) | copy-start | bytes 184324
  13.6 26.4 %all-to-all-start = ((f32[32,12,128]{2,1,0:T(8,128)}), f32[32,12,128]{2,1,0:T(8,128)S(1)}, u32[]{:S(2)}, u32[]{:S(2)}) async-start(f32[32,12,128]{2,1,0:T(8,128)} %shard_map.133), calls=%async_computation | async-start | bytes 524288 | tf_op jit(solution)/shard_map/all_to_all | solution.py:342
  43.9 21.3 %all-to-all-start.1 = ((f32[32,8,192]{2,1,0:T(8,128)}), f32[32,8,192]{2,1,0:T(8,128)S(1)}, u32[]{:S(2)}, u32[]{:S(2)}) async-start(f32[32,8,192]{2,1,0:T(8,128)} %bitcast.71), calls=%async_computation.1 | async-start | bytes 524288 | tf_op jit(solution)/shard_map/all_to_all | solution.py:373
  70.7 16.2 %all-to-all-start.2 = ((f32[32,8,192]{2,1,0:T(8,128)}), f32[32,8,192]{2,1,0:T(8,128)S(1)}, u32[]{:S(2)}, u32[]{:S(2)}) async-start(f32[32,8,192]{2,1,0:T(8,128)} %bitcast.70), calls=%async_computation.2 | async-start | bytes 524288 | tf_op jit(solution)/shard_map/all_to_all | solution.py:373
  92.4 13.2 %all-to-all-start.3 = ((f32[32,8,192]{2,1,0:T(8,128)}), f32[32,8,192]{2,1,0:T(8,128)S(1)}, u32[]{:S(2)}, u32[]{:S(2)}) async-start(f32[32,8,192]{2,1,0:T(8,128)} %bitcast.68), calls=%async_computation.3 | async-start | bytes 524288 | tf_op jit(solution)/shard_map/all_to_all | solution.py:373
  95.2 7.4 %copy-start.13 = (f32[48,128]{1,0:T(8,128)S(1)}, f32[48,128]{1,0:T(8,128)}, u32[]{:S(2)}) copy-start(f32[48,128]{1,0:T(8,128)} %get-tuple-element.31) | copy-start | bytes 73732
  95.2 7.4 %copy-start.14 = (f32[48,128]{1,0:T(8,128)S(1)}, f32[48,128]{1,0:T(8,128)}, u32[]{:S(2)}) copy-start(f32[48,128]{1,0:T(8,128)} %get-tuple-element.35) | copy-start | bytes 73732
  95.2 7.4 %copy-start.15 = (f32[48,128]{1,0:T(8,128)S(1)}, f32[48,128]{1,0:T(8,128)}, u32[]{:S(2)}) copy-start(f32[48,128]{1,0:T(8,128)} %get-tuple-element.32) | copy-start | bytes 73732
  95.2 7.4 %copy-start.16 = (f32[48,128]{1,0:T(8,128)S(1)}, f32[48,128]{1,0:T(8,128)}, u32[]{:S(2)}) copy-start(f32[48,128]{1,0:T(8,128)} %get-tuple-element.36) | copy-start | bytes 73732
  95.2 7.4 %copy-start.17 = (f32[48,128]{1,0:T(8,128)S(1)}, f32[48,128]{1,0:T(8,128)}, u32[]{:S(2)}) copy-start(f32[48,128]{1,0:T(8,128)} %get-tuple-element.33) | copy-start | bytes 73732
  95.2 7.4 %copy-start.18 = (f32[48,128]{1,0:T(8,128)S(1)}, f32[48,128]{1,0:T(8,128)}, u32[]{:S(2)}) copy-start(f32[48,128]{1,0:T(8,128)} %get-tuple-element.37) | copy-start | bytes 73732
  106.3 27.0 %copy-start.9 = (f32[3,4096]{1,0:T(4,128)S(1)}, f32[3,4096]{1,0:T(4,128)}, u32[]{:S(2)}) copy-start(f32[3,4096]{1,0:T(4,128)} %get-tuple-element.27) | copy-start | bytes 147460
  106.3 27.0 %copy-start.10 = (f32[3,4096]{1,0:T(4,128)S(1)}, f32[3,4096]{1,0:T(4,128)}, u32[]{:S(2)}) copy-start(f32[3,4096]{1,0:T(4,128)} %get-tuple-element.28) | copy-start | bytes 147460
  106.3 27.0 %copy-start.11 = (f32[3,4096]{1,0:T(4,128)S(1)}, f32[3,4096]{1,0:T(4,128)}, u32[]{:S(2)}) copy-start(f32[3,4096]{1,0:T(4,128)} %get-tuple-element.29) | copy-start | bytes 147460
  106.3 27.0 %copy-start.12 = (f32[3,4096]{1,0:T(4,128)S(1)}, f32[3,4096]{1,0:T(4,128)}, u32[]{:S(2)}) copy-start(f32[3,4096]{1,0:T(4,128)} %get-tuple-element.30) | copy-start | bytes 147460
  111.1 14.1 %all-to-all-start.4 = ((f32[32,8,192]{2,1,0:T(8,128)}), f32[32,8,192]{2,1,0:T(8,128)S(1)}, u32[]{:S(2)}, u32[]{:S(2)}) async-start(f32[32,8,192]{2,1,0:T(8,128)} %bitcast.69), calls=%async_computation.4 | async-start | bytes 524288 | tf_op jit(solution)/shard_map/all_to_all | solution.py:373
  114.8 19.2 %collective-permute-start.1 = (f32[3,1024]{1,0:T(4,128)S(1)}, f32[3,1024]{1,0:T(4,128)S(1)}, u32[]{:S(2)}, u32[]{:S(2)}) collective-permute-start(f32[3,1024]{1,0:T(4,128)S(1)} %bitcast.81), channel_id=1, source_target_pairs={{8,0},{16,8},{24,16},{9,1},{17,9},{25,17},{10,2},{18,10},{26,18},{... | collective-permute-start | bytes 36872 | tf_op jit(solution)/shard_map/ppermute | solution.py:318
  116.2 17.9 %collective-permute-start = (f32[3,1024]{1,0:T(4,128)S(1)}, f32[3,1024]{1,0:T(4,128)S(1)}, u32[]{:S(2)}, u32[]{:S(2)}) collective-permute-start(f32[3,1024]{1,0:T(4,128)S(1)} %bitcast.82), channel_id=1, source_target_pairs={{0,8},{8,16},{16,24},{1,9},{9,17},{17,25},{2,10},{10,18},{18,26},{... | collective-permute-start | bytes 36872 | tf_op jit(solution)/shard_map/ppermute | solution.py:318
  130.7 13.0 %all-to-all-start.5 = ((f32[32,8,192]{2,1,0:T(8,128)}), f32[32,8,192]{2,1,0:T(8,128)S(1)}, u32[]{:S(2)}, u32[]{:S(2)}) async-start(f32[32,8,192]{2,1,0:T(8,128)} %bitcast.67), calls=%async_computation.5 | async-start | bytes 524288 | tf_op jit(solution)/shard_map/all_to_all | solution.py:373
  (5 other events, 3.5 us)

commit v12 on v7

--- a/solution.py
+++ b/solution.py
@@ -66,11 +66,13 @@
         kind = jnp.where(move == 0, 1, jnp.where(move == 1, 2, 0))
         key = kind * groups + (element >> 7)
         low = (low_iota == (element & 127)).astype(jnp.bfloat16)
-        low = jnp.concatenate([low, low, low], axis=1)
+        low = jnp.concatenate([low, low], axis=1)
         mask = row_iota == key
         spread = jnp.concatenate(
             [
-                jnp.concatenate([jnp.where(mask, piece, zero) for piece in bf16_pieces(term)], axis=1)
+                jnp.concatenate(
+                    [jnp.where(mask, piece, zero) for piece in bf16_pieces(term)[:2]], axis=1
+                )
                 for term in terms
             ],
             axis=0,

time: 137 us -> 134 us (0.978)
  Pallas kernels: 71.4 us -> 68.8 us
    pallas_call x1, Pallas kernels: 12.9 us -> 10.3 us  [stress_partials(): pl.pallas_call(functools.partial(stress_kernel, groups=groups, rows=rows)...]
  transfers between devices with their start and end apart: 8 -> 8, of which waited for: 5 -> 5; matrix products, arithmetic and copies ran while one was open for 5% -> 5% of each run, Pallas kernels for 25% -> 26%
where the time goes in v12:
time: 134 us
  Pallas kernels  68.8 us (51%)
  starting transfers between devices  30.9 us (23%)
  waiting for transfers between devices  21 us (16%)
  local copies, waits for them, and re-layouts  7.64 us (6%)
  other arithmetic  3.24 us (2%)
    pallas_call x4, Pallas kernels, update_and_pack(): pl.pallas_call(functools.partial(update_kernel, groups16=groups16, slots1...  29.4 us
    pallas_call x5, Pallas kernels, sweep(): pl.pallas_call(sweep_kernel, out_shape=(jax.ShapeDtypeStruct(velocity.sha...  26.7 us
    all_to_all x5, waiting for transfers between devices, body(): gathered = lax.all_to_all(send, ('slab', 'rad'), 0, 0, tiled=True)  21 us
    all_to_all x5, starting transfers between devices, body(): gathered = lax.all_to_all(send, ('slab', 'rad'), 0, 0, tiled=True)  17.7 us
    pallas_call x1, Pallas kernels, stress_partials(): pl.pallas_call(functools.partial(stress_kernel, groups=groups, rows=rows)...  10.3 us
    all_to_all x1, starting transfers between devices, body(): received = lax.all_to_all(send, ('slab', 'rad'), 0, 0, tiled=True)  7.3 us
    unnamed x49, local copies, waits for them, and re-layouts  6.02 us
    ppermute x2, starting transfers between devices, passed_along(): return lax.ppermute(array, axis, pairs)  5.84 us
  transfers between devices with their start and end apart: 8, of which 5 were waited for; matrix products, arithmetic and copies ran while one was open for 5% of the time, Pallas kernels for 26%

profile of v12, /device:TPU:0, one launch (start us, length us, event | category | flops | bytes accessed | tf_op | source)
XLA Modules:
  0.0 133.8 jit_solution(1383570810923420211)
XLA Ops:
  0.7 10.3 %shard_map.133 = f32[32,12,128]{2,1,0:T(8,128)} custom-call(s32[1]{0:T(128)} %bitcast.12.slab_ref, f32[3,16384]{1,0:T(4,128)} %q_ref.9, s32[1,16384]{1,0:T(1,128)} %bitcast.84, s32[1,16384]{1,0:T(1,128)} %bitcast.73), custom_call_target="tpu_custom_call" | custom-call | flops 4026531840 | bytes 327680 | tf_op jit(solution)/shard_map/pallas_call | solution.py:178
  11.0 7.3 %all-to-all-start = ((f32[32,12,128]{2,1,0:T(8,128)}), f32[32,12,128]{2,1,0:T(8,128)S(1)}, u32[]{:S(2)}, u32[]{:S(2)}) async-start(f32[32,12,128]{2,1,0:T(8,128)} %shard_map.133), calls=%async_computation | async-start | bytes 524288 | tf_op jit(solution)/shard_map/all_to_all | solution.py:342
  18.4 1.8 %copy.52 = f32[8,192,192]{1,2,0:T(8,128)} copy(f32[8,192,192]{2,1,0:T(8,128)S(1)} %copy-done.1) | data formatting | bytes 2359296 | tf_op args[9]
  22.7 7.3 %shard_map.129 = (f32[3,4096]{1,0:T(4,128)}, f32[48,128]{1,0:T(8,128)}, f32[48,128]{1,0:T(8,128)}) custom-call(f32[3,16384]{1,0:T(4,128)} %q_ref.9, f32[3,16384]{1,0:T(4,128)} %inc_ref.7, s32[1,16384]{1,0:T(1,128)} %bitcast.85, s32[1,16384]{1,0:T(1,128)} %bitcast.74, bf16[160,384]{1,0:T(8,128)(2,1)} %pad_maximum_fusion.1.tab_ref, ...), custom_call_target="tpu_custom_call" | custom-call | flops 6442450944 | bytes 163840 | tf_op jit(solution)/shard_map/pallas_call | solution.py:238
  31.5 2.4 %shard_map.134 = (f32[8,192]{1,0:T(8,128)}, f32[256,192]{1,0:T(8,128)}) custom-call(f32[8,192,192]{2,1,0:T(8,128)} %bitcast.55, f32[192,8]{1,0:T(8,128)} %convolution_bitcast_fusion.ft_ref), custom_call_target="tpu_custom_call" | custom-call | flops 589824 | bytes 1179648 | tf_op jit(solution)/shard_map/pallas_call | solution.py:204
  33.9 5.8 %all-to-all-start.1 = ((f32[32,8,192]{2,1,0:T(8,128)}), f32[32,8,192]{2,1,0:T(8,128)S(1)}, u32[]{:S(2)}, u32[]{:S(2)}) async-start(f32[32,8,192]{2,1,0:T(8,128)} %bitcast.70), calls=%async_computation.1 | async-start | bytes 524288 | tf_op jit(solution)/shard_map/all_to_all | solution.py:371
  39.7 7.3 %shard_map.130 = (f32[3,4096]{1,0:T(4,128)}, f32[48,128]{1,0:T(8,128)}, f32[48,128]{1,0:T(8,128)}) custom-call(f32[3,16384]{1,0:T(4,128)} %q_ref.9, f32[3,16384]{1,0:T(4,128)} %inc_ref.7, s32[1,16384]{1,0:T(1,128)} %bitcast.86, s32[1,16384]{1,0:T(1,128)} %bitcast.75, bf16[160,384]{1,0:T(8,128)(2,1)} %pad_maximum_fusion.1.tab_ref, ...), custom_call_target="tpu_custom_call" | custom-call | flops 6442450944 | bytes 163840 | tf_op jit(solution)/shard_map/pallas_call | solution.py:238
  47.1 3.0 %all-to-all-done.1 = f32[32,8,192]{2,1,0:T(8,128)S(1)} async-done(((f32[32,8,192]{2,1,0:T(8,128)}), f32[32,8,192]{2,1,0:T(8,128)S(1)}, u32[]{:S(2)}, u32[]{:S(2)}) %all-to-all-start.1) | async-done | bytes 196640 | tf_op jit(solution)/shard_map/all_to_all | solution.py:371
  50.8 5.3 %shard_map.135 = (f32[8,192]{1,0:T(8,128)}, f32[256,192]{1,0:T(8,128)}) custom-call(s32[32]{0:T(128)} %reshape.94.idx_ref, f32[256,192]{1,0:T(8,128)} %bitcast.64, f32[8,4,192,192]{3,2,1,0:T(8,128)} %s_ref.9, f32[8,192,192]{2,1,0:T(8,128)} %bitcast.56, f32[192,8]{1,0:T(8,128)} %convolution_bitcast_fusion.ft_ref, f32[8,192]{1,0:T(8,128)} %get-tuple-element.40.v_ref), custom_call_target="tpu_custom_call" | custom-call | flops 2949120 | bytes 6094848 | tf_op jit(solution)/shard_map/pallas_call | solution.py:299
  56.1 2.8 %all-to-all-start.2 = ((f32[32,8,192]{2,1,0:T(8,128)}), f32[32,8,192]{2,1,0:T(8,128)S(1)}, u32[]{:S(2)}, u32[]{:S(2)}) async-start(f32[32,8,192]{2,1,0:T(8,128)} %bitcast.69), calls=%async_computation.2 | async-start | bytes 524288 | tf_op jit(solution)/shard_map/all_to_all | solution.py:371
  58.9 7.3 %shard_map.131 = (f32[3,4096]{1,0:T(4,128)}, f32[48,128]{1,0:T(8,128)}, f32[48,128]{1,0:T(8,128)}) custom-call(f32[3,16384]{1,0:T(4,128)} %q_ref.9, f32[3,16384]{1,0:T(4,128)} %inc_ref.7, s32[1,16384]{1,0:T(1,128)} %bitcast.87, s32[1,16384]{1,0:T(1,128)} %bitcast.76, bf16[160,384]{1,0:T(8,128)(2,1)} %pad_maximum_fusion.1.tab_ref, ...), custom_call_target="tpu_custom_call" | custom-call | flops 6442450944 | bytes 163840 | tf_op jit(solution)/shard_map/pallas_call | solution.py:238
  66.3 3.0 %all-to-all-done.2 = f32[32,8,192]{2,1,0:T(8,128)S(1)} async-done(((f32[32,8,192]{2,1,0:T(8,128)}), f32[32,8,192]{2,1,0:T(8,128)S(1)}, u32[]{:S(2)}, u32[]{:S(2)}) %all-to-all-start.2) | async-done | bytes 196640 | tf_op jit(solution)/shard_map/all_to_all | solution.py:371
  70.0 5.3 %shard_map.136 = (f32[8,192]{1,0:T(8,128)}, f32[256,192]{1,0:T(8,128)}) custom-call(s32[32]{0:T(128)} %reshape.94.idx_ref, f32[256,192]{1,0:T(8,128)} %bitcast.65, f32[8,4,192,192]{3,2,1,0:T(8,128)} %s_ref.9, f32[8,192,192]{2,1,0:T(8,128)} %bitcast.57, f32[192,8]{1,0:T(8,128)} %convolution_bitcast_fusion.ft_ref, f32[8,192]{1,0:T(8,128)} %get-tuple-element.42.v_ref), custom_call_target="tpu_custom_call" | custom-call | flops 2949120 | bytes 6094848 | tf_op jit(solution)/shard_map/pallas_call | solution.py:299
  75.4 2.8 %all-to-all-start.3 = ((f32[32,8,192]{2,1,0:T(8,128)}), f32[32,8,192]{2,1,0:T(8,128)S(1)}, u32[]{:S(2)}, u32[]{:S(2)}) async-start(f32[32,8,192]{2,1,0:T(8,128)} %bitcast.67), calls=%async_computation.3 | async-start | bytes 524288 | tf_op jit(solution)/shard_map/all_to_all | solution.py:371
  78.2 7.4 %shard_map.132 = (f32[3,4096]{1,0:T(4,128)}, f32[48,128]{1,0:T(8,128)}, f32[48,128]{1,0:T(8,128)}) custom-call(f32[3,16384]{1,0:T(4,128)} %q_ref.9, f32[3,16384]{1,0:T(4,128)} %inc_ref.7, s32[1,16384]{1,0:T(1,128)} %bitcast.88, s32[1,16384]{1,0:T(1,128)} %bitcast.77, bf16[160,384]{1,0:T(8,128)(2,1)} %pad_maximum_fusion.1.tab_ref, ...), custom_call_target="tpu_custom_call" | custom-call | flops 6442450944 | bytes 163840 | tf_op jit(solution)/shard_map/pallas_call | solution.py:238
  86.4 2.1 %all-to-all-done.3 = f32[32,8,192]{2,1,0:T(8,128)S(1)} async-done(((f32[32,8,192]{2,1,0:T(8,128)}), f32[32,8,192]{2,1,0:T(8,128)S(1)}, u32[]{:S(2)}, u32[]{:S(2)}) %all-to-all-start.3) | async-done | bytes 196640 | tf_op jit(solution)/shard_map/all_to_all | solution.py:371
  89.2 5.3 %shard_map.137 = (f32[8,192]{1,0:T(8,128)}, f32[256,192]{1,0:T(8,128)}) custom-call(s32[32]{0:T(128)} %reshape.94.idx_ref, f32[256,192]{1,0:T(8,128)} %bitcast.62, f32[8,4,192,192]{3,2,1,0:T(8,128)} %s_ref.9, f32[8,192,192]{2,1,0:T(8,128)} %bitcast.58, f32[192,8]{1,0:T(8,128)} %convolution_bitcast_fusion.ft_ref, f32[8,192]{1,0:T(8,128)} %get-tuple-element.44.v_ref), custom_call_target="tpu_custom_call" | custom-call | flops 2949120 | bytes 6094848 | tf_op jit(solution)/shard_map/pallas_call | solution.py:299
  94.6 3.7 %all-to-all-start.4 = ((f32[32,8,192]{2,1,0:T(8,128)}), f32[32,8,192]{2,1,0:T(8,128)S(1)}, u32[]{:S(2)}, u32[]{:S(2)}) async-start(f32[32,8,192]{2,1,0:T(8,128)} %bitcast.68), calls=%async_computation.4 | async-start | bytes 524288 | tf_op jit(solution)/shard_map/all_to_all | solution.py:371
  99.6 4.5 %collective-permute-start = (f32[3,1024]{1,0:T(4,128)S(1)}, f32[3,1024]{1,0:T(4,128)S(1)}, u32[]{:S(2)}, u32[]{:S(2)}) collective-permute-start(f32[3,1024]{1,0:T(4,128)S(1)} %bitcast.81), channel_id=1, source_target_pairs={{0,8},{8,16},{16,24},{1,9},{9,17},{17,25},{2,10},{10,18},{18,26},{... | collective-permute-start | bytes 36872 | tf_op jit(solution)/shard_map/ppermute | solution.py:318
  104.2 4.5 %all-to-all-done.4 = f32[32,8,192]{2,1,0:T(8,128)S(1)} async-done(((f32[32,8,192]{2,1,0:T(8,128)}), f32[32,8,192]{2,1,0:T(8,128)S(1)}, u32[]{:S(2)}, u32[]{:S(2)}) %all-to-all-start.4) | async-done | bytes 196640 | tf_op jit(solution)/shard_map/all_to_all | solution.py:371
  109.4 5.4 %shard_map.138 = (f32[8,192]{1,0:T(8,128)}, f32[256,192]{1,0:T(8,128)}) custom-call(s32[32]{0:T(128)} %reshape.94.idx_ref, f32[256,192]{1,0:T(8,128)} %bitcast.63, f32[8,4,192,192]{3,2,1,0:T(8,128)} %s_ref.9, f32[8,192,192]{2,1,0:T(8,128)} %bitcast.59, f32[192,8]{1,0:T(8,128)} %convolution_bitcast_fusion.ft_ref, f32[8,192]{1,0:T(8,128)} %get-tuple-element.46.v_ref), custom_call_target="tpu_custom_call" | custom-call | flops 2949120 | bytes 6094848 | tf_op jit(solution)/shard_map/pallas_call | solution.py:299
  114.8 2.6 %all-to-all-start.5 = ((f32[32,8,192]{2,1,0:T(8,128)}), f32[32,8,192]{2,1,0:T(8,128)S(1)}, u32[]{:S(2)}, u32[]{:S(2)}) async-start(f32[32,8,192]{2,1,0:T(8,128)} %bitcast.66), calls=%async_computation.5 | async-start | bytes 524288 | tf_op jit(solution)/shard_map/all_to_all | solution.py:371
  119.4 8.3 %all-to-all-done.5 = f32[32,8,192]{2,1,0:T(8,128)S(1)} async-done(((f32[32,8,192]{2,1,0:T(8,128)}), f32[32,8,192]{2,1,0:T(8,128)S(1)}, u32[]{:S(2)}, u32[]{:S(2)}) %all-to-all-start.5) | async-done | bytes 196640 | tf_op jit(solution)/shard_map/all_to_all | solution.py:371
  128.4 5.3 %shard_map.139 = (f32[8,192]{1,0:T(8,128)}, f32[256,192]{1,0:T(8,128)}) custom-call(s32[32]{0:T(128)} %reshape.94.idx_ref, f32[256,192]{1,0:T(8,128)} %bitcast.61, f32[8,4,192,192]{3,2,1,0:T(8,128)} %s_ref.9, f32[8,192,192]{2,1,0:T(8,128)} %bitcast.60, f32[192,8]{1,0:T(8,128)} %convolution_bitcast_fusion.ft_ref, f32[8,192]{1,0:T(8,128)} %get-tuple-element.48.v_ref), custom_call_target="tpu_custom_call" | custom-call | flops 2949120 | bytes 6094848 | tf_op jit(solution)/shard_map/pallas_call | solution.py:299
  (77 shorter events, 11.6 us)
Async XLA Ops:
  0.6 29.6 %copy-start = (f32[192,192]{1,0:T(8,128)S(1)}, f32[192,192]{1,0:T(8,128)}, u32[]{:S(2)}) copy-start(f32[192,192]{1,0:T(8,128)} %param.16) | copy-start | bytes 442372
  0.7 17.6 %copy-start.8 = (s32[16384]{0:T(1024)S(1)}, s32[16384]{0:T(1024)}, u32[]{:S(2)}) copy-start(s32[16384]{0:T(1024)} %param.14) | copy-start | bytes 196612
  0.7 17.7 %copy-start.19 = (f32[384]{0:T(512)S(1)}, f32[384]{0:T(512)}, u32[]{:S(2)}) copy-start(f32[384]{0:T(512)} %param.15) | copy-start | bytes 4612
  0.7 17.7 %copy-start.1 = (f32[8,192,192]{2,1,0:T(8,128)S(1)}, f32[8,192,192]{2,1,0:T(8,128)}, u32[]{:S(2)}) copy-start(f32[8,192,192]{2,1,0:T(8,128)} %param.19) | copy-start | bytes 3538948
  11.0 19.0 %all-to-all-start = ((f32[32,12,128]{2,1,0:T(8,128)}), f32[32,12,128]{2,1,0:T(8,128)S(1)}, u32[]{:S(2)}, u32[]{:S(2)}) async-start(f32[32,12,128]{2,1,0:T(8,128)} %shard_map.133), calls=%async_computation | async-start | bytes 524288 | tf_op jit(solution)/shard_map/all_to_all | solution.py:342
  18.4 1.8 %copy-start.20 = (s32[8,4]{0,1:T(4,128)S(1)}, s32[8,4]{0,1:T(4,128)}, u32[]{:S(2)}) copy-start(s32[8,4]{0,1:T(4,128)} %param.18) | copy-start | bytes 388
  18.4 2.4 %copy-start.7 = (f32[5,3072]{1,0:T(8,128)S(1)}, f32[5,3072]{1,0:T(8,128)}, u32[]{:S(2)}) copy-start(f32[5,3072]{1,0:T(8,128)} %param.12) | copy-start | bytes 184324
  33.9 16.2 %all-to-all-start.1 = ((f32[32,8,192]{2,1,0:T(8,128)}), f32[32,8,192]{2,1,0:T(8,128)S(1)}, u32[]{:S(2)}, u32[]{:S(2)}) async-start(f32[32,8,192]{2,1,0:T(8,128)} %bitcast.70), calls=%async_computation.1 | async-start | bytes 524288 | tf_op jit(solution)/shard_map/all_to_all | solution.py:371
  56.1 13.2 %all-to-all-start.2 = ((f32[32,8,192]{2,1,0:T(8,128)}), f32[32,8,192]{2,1,0:T(8,128)S(1)}, u32[]{:S(2)}, u32[]{:S(2)}) async-start(f32[32,8,192]{2,1,0:T(8,128)} %bitcast.69), calls=%async_computation.2 | async-start | bytes 524288 | tf_op jit(solution)/shard_map/all_to_all | solution.py:371
  75.4 13.2 %all-to-all-start.3 = ((f32[32,8,192]{2,1,0:T(8,128)}), f32[32,8,192]{2,1,0:T(8,128)S(1)}, u32[]{:S(2)}, u32[]{:S(2)}) async-start(f32[32,8,192]{2,1,0:T(8,128)} %bitcast.67), calls=%async_computation.3 | async-start | bytes 524288 | tf_op jit(solution)/shard_map/all_to_all | solution.py:371
  78.2 7.4 %copy-start.13 = (f32[48,128]{1,0:T(8,128)S(1)}, f32[48,128]{1,0:T(8,128)}, u32[]{:S(2)}) copy-start(f32[48,128]{1,0:T(8,128)} %get-tuple-element.31) | copy-start | bytes 73732
  78.2 7.4 %copy-start.14 = (f32[48,128]{1,0:T(8,128)S(1)}, f32[48,128]{1,0:T(8,128)}, u32[]{:S(2)}) copy-start(f32[48,128]{1,0:T(8,128)} %get-tuple-element.35) | copy-start | bytes 73732
  78.2 7.4 %copy-start.15 = (f32[48,128]{1,0:T(8,128)S(1)}, f32[48,128]{1,0:T(8,128)}, u32[]{:S(2)}) copy-start(f32[48,128]{1,0:T(8,128)} %get-tuple-element.32) | copy-start | bytes 73732
  78.2 7.4 %copy-start.16 = (f32[48,128]{1,0:T(8,128)S(1)}, f32[48,128]{1,0:T(8,128)}, u32[]{:S(2)}) copy-start(f32[48,128]{1,0:T(8,128)} %get-tuple-element.36) | copy-start | bytes 73732
  78.2 7.4 %copy-start.17 = (f32[48,128]{1,0:T(8,128)S(1)}, f32[48,128]{1,0:T(8,128)}, u32[]{:S(2)}) copy-start(f32[48,128]{1,0:T(8,128)} %get-tuple-element.33) | copy-start | bytes 73732
  78.2 7.4 %copy-start.18 = (f32[48,128]{1,0:T(8,128)S(1)}, f32[48,128]{1,0:T(8,128)}, u32[]{:S(2)}) copy-start(f32[48,128]{1,0:T(8,128)} %get-tuple-element.37) | copy-start | bytes 73732
  94.6 14.1 %all-to-all-start.4 = ((f32[32,8,192]{2,1,0:T(8,128)}), f32[32,8,192]{2,1,0:T(8,128)S(1)}, u32[]{:S(2)}, u32[]{:S(2)}) async-start(f32[32,8,192]{2,1,0:T(8,128)} %bitcast.68), calls=%async_computation.4 | async-start | bytes 524288 | tf_op jit(solution)/shard_map/all_to_all | solution.py:371
  98.3 19.8 %collective-permute-start.1 = (f32[3,1024]{1,0:T(4,128)S(1)}, f32[3,1024]{1,0:T(4,128)S(1)}, u32[]{:S(2)}, u32[]{:S(2)}) collective-permute-start(f32[3,1024]{1,0:T(4,128)S(1)} %bitcast.80), channel_id=1, source_target_pairs={{8,0},{16,8},{24,16},{9,1},{17,9},{25,17},{10,2},{18,10},{26,18},{... | collective-permute-start | bytes 36872 | tf_op jit(solution)/shard_map/ppermute | solution.py:318
  99.6 18.5 %collective-permute-start = (f32[3,1024]{1,0:T(4,128)S(1)}, f32[3,1024]{1,0:T(4,128)S(1)}, u32[]{:S(2)}, u32[]{:S(2)}) collective-permute-start(f32[3,1024]{1,0:T(4,128)S(1)} %bitcast.81), channel_id=1, source_target_pairs={{0,8},{8,16},{16,24},{1,9},{9,17},{17,25},{2,10},{10,18},{18,26},{... | collective-permute-start | bytes 36872 | tf_op jit(solution)/shard_map/ppermute | solution.py:318
  109.4 8.0 %copy-start.9 = (f32[3,4096]{1,0:T(4,128)S(1)}, f32[3,4096]{1,0:T(4,128)}, u32[]{:S(2)}) copy-start(f32[3,4096]{1,0:T(4,128)} %get-tuple-element.27) | copy-start | bytes 147460
  109.4 8.0 %copy-start.10 = (f32[3,4096]{1,0:T(4,128)S(1)}, f32[3,4096]{1,0:T(4,128)}, u32[]{:S(2)}) copy-start(f32[3,4096]{1,0:T(4,128)} %get-tuple-element.28) | copy-start | bytes 147460
  109.4 8.0 %copy-start.11 = (f32[3,4096]{1,0:T(4,128)S(1)}, f32[3,4096]{1,0:T(4,128)}, u32[]{:S(2)}) copy-start(f32[3,4096]{1,0:T(4,128)} %get-tuple-element.29) | copy-start | bytes 147460
  109.4 8.0 %copy-start.12 = (f32[3,4096]{1,0:T(4,128)S(1)}, f32[3,4096]{1,0:T(4,128)}, u32[]{:S(2)}) copy-start(f32[3,4096]{1,0:T(4,128)} %get-tuple-element.30) | copy-start | bytes 147460
  114.8 13.0 %all-to-all-start.5 = ((f32[32,8,192]{2,1,0:T(8,128)}), f32[32,8,192]{2,1,0:T(8,128)S(1)}, u32[]{:S(2)}, u32[]{:S(2)}) async-start(f32[32,8,192]{2,1,0:T(8,128)} %bitcast.66), calls=%async_computation.5 | async-start | bytes 524288 | tf_op jit(solution)/shard_map/all_to_all | solution.py:371
  (5 other events, 3.5 us)

commit v13 on v12

--- a/solution.py
+++ b/solution.py
@@ -10,7 +10,7 @@
 BLOCK = 192
 ITERS = 6
 CHUNK = 512
-STRESS_CHUNK = 1024
+STRESS_CHUNK = 2048
 UPDATE_PARTS = 4
 
 extensibility = 50.0

time: 134 us -> 133 us (level)
  no operation moved by 1% of the time
where the time goes in v13:
time: 133 us
  Pallas kernels  67.7 us (51%)
  starting transfers between devices  30.9 us (23%)
  waiting for transfers between devices  21 us (16%)
  local copies, waits for them, and re-layouts  7.64 us (6%)
  other arithmetic  3.24 us (2%)
    pallas_call x4, Pallas kernels, update_and_pack(): pl.pallas_call(functools.partial(update_kernel, groups16=groups16, slots1...  29.4 us
    pallas_call x5, Pallas kernels, sweep(): pl.pallas_call(sweep_kernel, out_shape=(jax.ShapeDtypeStruct(velocity.sha...  26.7 us
    all_to_all x5, waiting for transfers between devices, body(): gathered = lax.all_to_all(send, ('slab', 'rad'), 0, 0, tiled=True)  21 us
    all_to_all x5, starting transfers between devices, body(): gathered = lax.all_to_all(send, ('slab', 'rad'), 0, 0, tiled=True)  17.7 us
    pallas_call x1, Pallas kernels, stress_partials(): pl.pallas_call(functools.partial(stress_kernel, groups=groups, rows=rows)...  9.2 us
    all_to_all x1, starting transfers between devices, body(): received = lax.all_to_all(send, ('slab', 'rad'), 0, 0, tiled=True)  7.3 us
    unnamed x49, local copies, waits for them, and re-layouts  6.02 us
    ppermute x2, starting transfers between devices, passed_along(): return lax.ppermute(array, axis, pairs)  5.84 us
  transfers between devices with their start and end apart: 8, of which 5 were waited for; matrix products, arithmetic and copies ran while one was open for 5% of the time, Pallas kernels for 26%

profile of v13, /device:TPU:0, one launch (start us, length us, event | category | flops | bytes accessed | tf_op | source)
XLA Modules:
  0.0 132.7 jit_solution(8549266222145976233)
XLA Ops:
  0.7 9.2 %shard_map.133 = f32[32,12,128]{2,1,0:T(8,128)} custom-call(s32[1]{0:T(128)} %bitcast.12.slab_ref, f32[3,16384]{1,0:T(4,128)} %q_ref.9, s32[1,16384]{1,0:T(1,128)} %bitcast.84, s32[1,16384]{1,0:T(1,128)} %bitcast.73), custom_call_target="tpu_custom_call" | custom-call | flops 4026531840 | bytes 327680 | tf_op jit(solution)/shard_map/pallas_call | solution.py:178
  9.9 7.3 %all-to-all-start = ((f32[32,12,128]{2,1,0:T(8,128)}), f32[32,12,128]{2,1,0:T(8,128)S(1)}, u32[]{:S(2)}, u32[]{:S(2)}) async-start(f32[32,12,128]{2,1,0:T(8,128)} %shard_map.133), calls=%async_computation | async-start | bytes 524288 | tf_op jit(solution)/shard_map/all_to_all | solution.py:342
  17.3 1.8 %copy.52 = f32[8,192,192]{1,2,0:T(8,128)} copy(f32[8,192,192]{2,1,0:T(8,128)S(1)} %copy-done.1) | data formatting | bytes 2359296 | tf_op args[9]
  21.5 7.3 %shard_map.129 = (f32[3,4096]{1,0:T(4,128)}, f32[48,128]{1,0:T(8,128)}, f32[48,128]{1,0:T(8,128)}) custom-call(f32[3,16384]{1,0:T(4,128)} %q_ref.9, f32[3,16384]{1,0:T(4,128)} %inc_ref.7, s32[1,16384]{1,0:T(1,128)} %bitcast.85, s32[1,16384]{1,0:T(1,128)} %bitcast.74, bf16[160,384]{1,0:T(8,128)(2,1)} %pad_maximum_fusion.1.tab_ref, ...), custom_call_target="tpu_custom_call" | custom-call | flops 6442450944 | bytes 163840 | tf_op jit(solution)/shard_map/pallas_call | solution.py:238
  30.4 2.4 %shard_map.134 = (f32[8,192]{1,0:T(8,128)}, f32[256,192]{1,0:T(8,128)}) custom-call(f32[8,192,192]{2,1,0:T(8,128)} %bitcast.55, f32[192,8]{1,0:T(8,128)} %convolution_bitcast_fusion.ft_ref), custom_call_target="tpu_custom_call" | custom-call | flops 589824 | bytes 1179648 | tf_op jit(solution)/shard_map/pallas_call | solution.py:204
  32.8 5.8 %all-to-all-start.1 = ((f32[32,8,192]{2,1,0:T(8,128)}), f32[32,8,192]{2,1,0:T(8,128)S(1)}, u32[]{:S(2)}, u32[]{:S(2)}) async-start(f32[32,8,192]{2,1,0:T(8,128)} %bitcast.70), calls=%async_computation.1 | async-start | bytes 524288 | tf_op jit(solution)/shard_map/all_to_all | solution.py:371
  38.6 7.3 %shard_map.130 = (f32[3,4096]{1,0:T(4,128)}, f32[48,128]{1,0:T(8,128)}, f32[48,128]{1,0:T(8,128)}) custom-call(f32[3,16384]{1,0:T(4,128)} %q_ref.9, f32[3,16384]{1,0:T(4,128)} %inc_ref.7, s32[1,16384]{1,0:T(1,128)} %bitcast.86, s32[1,16384]{1,0:T(1,128)} %bitcast.75, bf16[160,384]{1,0:T(8,128)(2,1)} %pad_maximum_fusion.1.tab_ref, ...), custom_call_target="tpu_custom_call" | custom-call | flops 6442450944 | bytes 163840 | tf_op jit(solution)/shard_map/pallas_call | solution.py:238
  46.0 3.0 %all-to-all-done.1 = f32[32,8,192]{2,1,0:T(8,128)S(1)} async-done(((f32[32,8,192]{2,1,0:T(8,128)}), f32[32,8,192]{2,1,0:T(8,128)S(1)}, u32[]{:S(2)}, u32[]{:S(2)}) %all-to-all-start.1) | async-done | bytes 196640 | tf_op jit(solution)/shard_map/all_to_all | solution.py:371
  49.7 5.3 %shard_map.135 = (f32[8,192]{1,0:T(8,128)}, f32[256,192]{1,0:T(8,128)}) custom-call(s32[32]{0:T(128)} %reshape.94.idx_ref, f32[256,192]{1,0:T(8,128)} %bitcast.64, f32[8,4,192,192]{3,2,1,0:T(8,128)} %s_ref.9, f32[8,192,192]{2,1,0:T(8,128)} %bitcast.56, f32[192,8]{1,0:T(8,128)} %convolution_bitcast_fusion.ft_ref, f32[8,192]{1,0:T(8,128)} %get-tuple-element.40.v_ref), custom_call_target="tpu_custom_call" | custom-call | flops 2949120 | bytes 6094848 | tf_op jit(solution)/shard_map/pallas_call | solution.py:299
  55.0 2.8 %all-to-all-start.2 = ((f32[32,8,192]{2,1,0:T(8,128)}), f32[32,8,192]{2,1,0:T(8,128)S(1)}, u32[]{:S(2)}, u32[]{:S(2)}) async-start(f32[32,8,192]{2,1,0:T(8,128)} %bitcast.69), calls=%async_computation.2 | async-start | bytes 524288 | tf_op jit(solution)/shard_map/all_to_all | solution.py:371
  57.8 7.3 %shard_map.131 = (f32[3,4096]{1,0:T(4,128)}, f32[48,128]{1,0:T(8,128)}, f32[48,128]{1,0:T(8,128)}) custom-call(f32[3,16384]{1,0:T(4,128)} %q_ref.9, f32[3,16384]{1,0:T(4,128)} %inc_ref.7, s32[1,16384]{1,0:T(1,128)} %bitcast.87, s32[1,16384]{1,0:T(1,128)} %bitcast.76, bf16[160,384]{1,0:T(8,128)(2,1)} %pad_maximum_fusion.1.tab_ref, ...), custom_call_target="tpu_custom_call" | custom-call | flops 6442450944 | bytes 163840 | tf_op jit(solution)/shard_map/pallas_call | solution.py:238
  65.2 3.0 %all-to-all-done.2 = f32[32,8,192]{2,1,0:T(8,128)S(1)} async-done(((f32[32,8,192]{2,1,0:T(8,128)}), f32[32,8,192]{2,1,0:T(8,128)S(1)}, u32[]{:S(2)}, u32[]{:S(2)}) %all-to-all-start.2) | async-done | bytes 196640 | tf_op jit(solution)/shard_map/all_to_all | solution.py:371
  68.9 5.3 %shard_map.136 = (f32[8,192]{1,0:T(8,128)}, f32[256,192]{1,0:T(8,128)}) custom-call(s32[32]{0:T(128)} %reshape.94.idx_ref, f32[256,192]{1,0:T(8,128)} %bitcast.65, f32[8,4,192,192]{3,2,1,0:T(8,128)} %s_ref.9, f32[8,192,192]{2,1,0:T(8,128)} %bitcast.57, f32[192,8]{1,0:T(8,128)} %convolution_bitcast_fusion.ft_ref, f32[8,192]{1,0:T(8,128)} %get-tuple-element.42.v_ref), custom_call_target="tpu_custom_call" | custom-call | flops 2949120 | bytes 6094848 | tf_op jit(solution)/shard_map/pallas_call | solution.py:299
  74.3 2.8 %all-to-all-start.3 = ((f32[32,8,192]{2,1,0:T(8,128)}), f32[32,8,192]{2,1,0:T(8,128)S(1)}, u32[]{:S(2)}, u32[]{:S(2)}) async-start(f32[32,8,192]{2,1,0:T(8,128)} %bitcast.67), calls=%async_computation.3 | async-start | bytes 524288 | tf_op jit(solution)/shard_map/all_to_all | solution.py:371
  77.1 7.4 %shard_map.132 = (f32[3,4096]{1,0:T(4,128)}, f32[48,128]{1,0:T(8,128)}, f32[48,128]{1,0:T(8,128)}) custom-call(f32[3,16384]{1,0:T(4,128)} %q_ref.9, f32[3,16384]{1,0:T(4,128)} %inc_ref.7, s32[1,16384]{1,0:T(1,128)} %bitcast.88, s32[1,16384]{1,0:T(1,128)} %bitcast.77, bf16[160,384]{1,0:T(8,128)(2,1)} %pad_maximum_fusion.1.tab_ref, ...), custom_call_target="tpu_custom_call" | custom-call | flops 6442450944 | bytes 163840 | tf_op jit(solution)/shard_map/pallas_call | solution.py:238
  85.3 2.1 %all-to-all-done.3 = f32[32,8,192]{2,1,0:T(8,128)S(1)} async-done(((f32[32,8,192]{2,1,0:T(8,128)}), f32[32,8,192]{2,1,0:T(8,128)S(1)}, u32[]{:S(2)}, u32[]{:S(2)}) %all-to-all-start.3) | async-done | bytes 196640 | tf_op jit(solution)/shard_map/all_to_all | solution.py:371
  88.2 5.3 %shard_map.137 = (f32[8,192]{1,0:T(8,128)}, f32[256,192]{1,0:T(8,128)}) custom-call(s32[32]{0:T(128)} %reshape.94.idx_ref, f32[256,192]{1,0:T(8,128)} %bitcast.62, f32[8,4,192,192]{3,2,1,0:T(8,128)} %s_ref.9, f32[8,192,192]{2,1,0:T(8,128)} %bitcast.58, f32[192,8]{1,0:T(8,128)} %convolution_bitcast_fusion.ft_ref, f32[8,192]{1,0:T(8,128)} %get-tuple-element.44.v_ref), custom_call_target="tpu_custom_call" | custom-call | flops 2949120 | bytes 6094848 | tf_op jit(solution)/shard_map/pallas_call | solution.py:299
  93.5 3.7 %all-to-all-start.4 = ((f32[32,8,192]{2,1,0:T(8,128)}), f32[32,8,192]{2,1,0:T(8,128)S(1)}, u32[]{:S(2)}, u32[]{:S(2)}) async-start(f32[32,8,192]{2,1,0:T(8,128)} %bitcast.68), calls=%async_computation.4 | async-start | bytes 524288 | tf_op jit(solution)/shard_map/all_to_all | solution.py:371
  98.6 4.5 %collective-permute-start = (f32[3,1024]{1,0:T(4,128)S(1)}, f32[3,1024]{1,0:T(4,128)S(1)}, u32[]{:S(2)}, u32[]{:S(2)}) collective-permute-start(f32[3,1024]{1,0:T(4,128)S(1)} %bitcast.81), channel_id=1, source_target_pairs={{0,8},{8,16},{16,24},{1,9},{9,17},{17,25},{2,10},{10,18},{18,26},{... | collective-permute-start | bytes 36872 | tf_op jit(solution)/shard_map/ppermute | solution.py:318
  103.1 4.5 %all-to-all-done.4 = f32[32,8,192]{2,1,0:T(8,128)S(1)} async-done(((f32[32,8,192]{2,1,0:T(8,128)}), f32[32,8,192]{2,1,0:T(8,128)S(1)}, u32[]{:S(2)}, u32[]{:S(2)}) %all-to-all-start.4) | async-done | bytes 196640 | tf_op jit(solution)/shard_map/all_to_all | solution.py:371
  108.3 5.4 %shard_map.138 = (f32[8,192]{1,0:T(8,128)}, f32[256,192]{1,0:T(8,128)}) custom-call(s32[32]{0:T(128)} %reshape.94.idx_ref, f32[256,192]{1,0:T(8,128)} %bitcast.63, f32[8,4,192,192]{3,2,1,0:T(8,128)} %s_ref.9, f32[8,192,192]{2,1,0:T(8,128)} %bitcast.59, f32[192,8]{1,0:T(8,128)} %convolution_bitcast_fusion.ft_ref, f32[8,192]{1,0:T(8,128)} %get-tuple-element.46.v_ref), custom_call_target="tpu_custom_call" | custom-call | flops 2949120 | bytes 6094848 | tf_op jit(solution)/shard_map/pallas_call | solution.py:299
  113.7 2.6 %all-to-all-start.5 = ((f32[32,8,192]{2,1,0:T(8,128)}), f32[32,8,192]{2,1,0:T(8,128)S(1)}, u32[]{:S(2)}, u32[]{:S(2)}) async-start(f32[32,8,192]{2,1,0:T(8,128)} %bitcast.66), calls=%async_computation.5 | async-start | bytes 524288 | tf_op jit(solution)/shard_map/all_to_all | solution.py:371
  118.3 8.3 %all-to-all-done.5 = f32[32,8,192]{2,1,0:T(8,128)S(1)} async-done(((f32[32,8,192]{2,1,0:T(8,128)}), f32[32,8,192]{2,1,0:T(8,128)S(1)}, u32[]{:S(2)}, u32[]{:S(2)}) %all-to-all-start.5) | async-done | bytes 196640 | tf_op jit(solution)/shard_map/all_to_all | solution.py:371
  127.4 5.3 %shard_map.139 = (f32[8,192]{1,0:T(8,128)}, f32[256,192]{1,0:T(8,128)}) custom-call(s32[32]{0:T(128)} %reshape.94.idx_ref, f32[256,192]{1,0:T(8,128)} %bitcast.61, f32[8,4,192,192]{3,2,1,0:T(8,128)} %s_ref.9, f32[8,192,192]{2,1,0:T(8,128)} %bitcast.60, f32[192,8]{1,0:T(8,128)} %convolution_bitcast_fusion.ft_ref, f32[8,192]{1,0:T(8,128)} %get-tuple-element.48.v_ref), custom_call_target="tpu_custom_call" | custom-call | flops 2949120 | bytes 6094848 | tf_op jit(solution)/shard_map/pallas_call | solution.py:299
  (77 shorter events, 11.6 us)
Async XLA Ops:
  0.6 28.5 %copy-start = (f32[192,192]{1,0:T(8,128)S(1)}, f32[192,192]{1,0:T(8,128)}, u32[]{:S(2)}) copy-start(f32[192,192]{1,0:T(8,128)} %param.16) | copy-start | bytes 442372
  0.7 16.5 %copy-start.8 = (s32[16384]{0:T(1024)S(1)}, s32[16384]{0:T(1024)}, u32[]{:S(2)}) copy-start(s32[16384]{0:T(1024)} %param.14) | copy-start | bytes 196612
  0.7 16.6 %copy-start.19 = (f32[384]{0:T(512)S(1)}, f32[384]{0:T(512)}, u32[]{:S(2)}) copy-start(f32[384]{0:T(512)} %param.15) | copy-start | bytes 4612
  0.7 16.6 %copy-start.1 = (f32[8,192,192]{2,1,0:T(8,128)S(1)}, f32[8,192,192]{2,1,0:T(8,128)}, u32[]{:S(2)}) copy-start(f32[8,192,192]{2,1,0:T(8,128)} %param.19) | copy-start | bytes 3538948
  9.9 19.0 %all-to-all-start = ((f32[32,12,128]{2,1,0:T(8,128)}), f32[32,12,128]{2,1,0:T(8,128)S(1)}, u32[]{:S(2)}, u32[]{:S(2)}) async-start(f32[32,12,128]{2,1,0:T(8,128)} %shard_map.133), calls=%async_computation | async-start | bytes 524288 | tf_op jit(solution)/shard_map/all_to_all | solution.py:342
  17.3 1.8 %copy-start.20 = (s32[8,4]{0,1:T(4,128)S(1)}, s32[8,4]{0,1:T(4,128)}, u32[]{:S(2)}) copy-start(s32[8,4]{0,1:T(4,128)} %param.18) | copy-start | bytes 388
  17.3 2.4 %copy-start.7 = (f32[5,3072]{1,0:T(8,128)S(1)}, f32[5,3072]{1,0:T(8,128)}, u32[]{:S(2)}) copy-start(f32[5,3072]{1,0:T(8,128)} %param.12) | copy-start | bytes 184324
  32.8 16.2 %all-to-all-start.1 = ((f32[32,8,192]{2,1,0:T(8,128)}), f32[32,8,192]{2,1,0:T(8,128)S(1)}, u32[]{:S(2)}, u32[]{:S(2)}) async-start(f32[32,8,192]{2,1,0:T(8,128)} %bitcast.70), calls=%async_computation.1 | async-start | bytes 524288 | tf_op jit(solution)/shard_map/all_to_all | solution.py:371
  55.0 13.2 %all-to-all-start.2 = ((f32[32,8,192]{2,1,0:T(8,128)}), f32[32,8,192]{2,1,0:T(8,128)S(1)}, u32[]{:S(2)}, u32[]{:S(2)}) async-start(f32[32,8,192]{2,1,0:T(8,128)} %bitcast.69), calls=%async_computation.2 | async-start | bytes 524288 | tf_op jit(solution)/shard_map/all_to_all | solution.py:371
  74.3 13.2 %all-to-all-start.3 = ((f32[32,8,192]{2,1,0:T(8,128)}), f32[32,8,192]{2,1,0:T(8,128)S(1)}, u32[]{:S(2)}, u32[]{:S(2)}) async-start(f32[32,8,192]{2,1,0:T(8,128)} %bitcast.67), calls=%async_computation.3 | async-start | bytes 524288 | tf_op jit(solution)/shard_map/all_to_all | solution.py:371
  77.1 7.4 %copy-start.13 = (f32[48,128]{1,0:T(8,128)S(1)}, f32[48,128]{1,0:T(8,128)}, u32[]{:S(2)}) copy-start(f32[48,128]{1,0:T(8,128)} %get-tuple-element.31) | copy-start | bytes 73732
  77.1 7.4 %copy-start.14 = (f32[48,128]{1,0:T(8,128)S(1)}, f32[48,128]{1,0:T(8,128)}, u32[]{:S(2)}) copy-start(f32[48,128]{1,0:T(8,128)} %get-tuple-element.35) | copy-start | bytes 73732
  77.1 7.4 %copy-start.15 = (f32[48,128]{1,0:T(8,128)S(1)}, f32[48,128]{1,0:T(8,128)}, u32[]{:S(2)}) copy-start(f32[48,128]{1,0:T(8,128)} %get-tuple-element.32) | copy-start | bytes 73732
  77.1 7.4 %copy-start.16 = (f32[48,128]{1,0:T(8,128)S(1)}, f32[48,128]{1,0:T(8,128)}, u32[]{:S(2)}) copy-start(f32[48,128]{1,0:T(8,128)} %get-tuple-element.36) | copy-start | bytes 73732
  77.1 7.4 %copy-start.17 = (f32[48,128]{1,0:T(8,128)S(1)}, f32[48,128]{1,0:T(8,128)}, u32[]{:S(2)}) copy-start(f32[48,128]{1,0:T(8,128)} %get-tuple-element.33) | copy-start | bytes 73732
  77.1 7.4 %copy-start.18 = (f32[48,128]{1,0:T(8,128)S(1)}, f32[48,128]{1,0:T(8,128)}, u32[]{:S(2)}) copy-start(f32[48,128]{1,0:T(8,128)} %get-tuple-element.37) | copy-start | bytes 73732
  93.5 14.1 %all-to-all-start.4 = ((f32[32,8,192]{2,1,0:T(8,128)}), f32[32,8,192]{2,1,0:T(8,128)S(1)}, u32[]{:S(2)}, u32[]{:S(2)}) async-start(f32[32,8,192]{2,1,0:T(8,128)} %bitcast.68), calls=%async_computation.4 | async-start | bytes 524288 | tf_op jit(solution)/shard_map/all_to_all | solution.py:371
  97.2 19.8 %collective-permute-start.1 = (f32[3,1024]{1,0:T(4,128)S(1)}, f32[3,1024]{1,0:T(4,128)S(1)}, u32[]{:S(2)}, u32[]{:S(2)}) collective-permute-start(f32[3,1024]{1,0:T(4,128)S(1)} %bitcast.80), channel_id=1, source_target_pairs={{8,0},{16,8},{24,16},{9,1},{17,9},{25,17},{10,2},{18,10},{26,18},{... | collective-permute-start | bytes 36872 | tf_op jit(solution)/shard_map/ppermute | solution.py:318
  98.6 18.5 %collective-permute-start = (f32[3,1024]{1,0:T(4,128)S(1)}, f32[3,1024]{1,0:T(4,128)S(1)}, u32[]{:S(2)}, u32[]{:S(2)}) collective-permute-start(f32[3,1024]{1,0:T(4,128)S(1)} %bitcast.81), channel_id=1, source_target_pairs={{0,8},{8,16},{16,24},{1,9},{9,17},{17,25},{2,10},{10,18},{18,26},{... | collective-permute-start | bytes 36872 | tf_op jit(solution)/shard_map/ppermute | solution.py:318
  108.3 8.0 %copy-start.9 = (f32[3,4096]{1,0:T(4,128)S(1)}, f32[3,4096]{1,0:T(4,128)}, u32[]{:S(2)}) copy-start(f32[3,4096]{1,0:T(4,128)} %get-tuple-element.27) | copy-start | bytes 147460
  108.3 8.0 %copy-start.10 = (f32[3,4096]{1,0:T(4,128)S(1)}, f32[3,4096]{1,0:T(4,128)}, u32[]{:S(2)}) copy-start(f32[3,4096]{1,0:T(4,128)} %get-tuple-element.28) | copy-start | bytes 147460
  108.3 8.0 %copy-start.11 = (f32[3,4096]{1,0:T(4,128)S(1)}, f32[3,4096]{1,0:T(4,128)}, u32[]{:S(2)}) copy-start(f32[3,4096]{1,0:T(4,128)} %get-tuple-element.29) | copy-start | bytes 147460
  108.3 8.0 %copy-start.12 = (f32[3,4096]{1,0:T(4,128)S(1)}, f32[3,4096]{1,0:T(4,128)}, u32[]{:S(2)}) copy-start(f32[3,4096]{1,0:T(4,128)} %get-tuple-element.30) | copy-start | bytes 147460
  113.7 13.0 %all-to-all-start.5 = ((f32[32,8,192]{2,1,0:T(8,128)}), f32[32,8,192]{2,1,0:T(8,128)S(1)}, u32[]{:S(2)}, u32[]{:S(2)}) async-start(f32[32,8,192]{2,1,0:T(8,128)} %bitcast.66), calls=%async_computation.5 | async-start | bytes 524288 | tf_op jit(solution)/shard_map/all_to_all | solution.py:371
  (5 other events, 3.5 us)

commit v14 on v13

--- a/solution.py
+++ b/solution.py
@@ -10,7 +10,7 @@
 BLOCK = 192
 ITERS = 6
 CHUNK = 512
-STRESS_CHUNK = 2048
+STRESS_CHUNK = 4096
 UPDATE_PARTS = 4
 
 extensibility = 50.0

time: 133 us -> 133 us (level)
  no operation moved by 1% of the time
where the time goes in v14:
time: 133 us; the launch traced here: 132 us
  Pallas kernels  67.1 us (50%)
  starting transfers between devices  30.9 us (23%)
  waiting for transfers between devices  21 us (16%)
  local copies, waits for them, and re-layouts  7.64 us (6%)
  other arithmetic  3.24 us (2%)
    pallas_call x4, Pallas kernels, update_and_pack(): pl.pallas_call(functools.partial(update_kernel, groups16=groups16, slots1...  29.4 us
    pallas_call x5, Pallas kernels, sweep(): pl.pallas_call(sweep_kernel, out_shape=(jax.ShapeDtypeStruct(velocity.sha...  26.7 us
    all_to_all x5, waiting for transfers between devices, body(): gathered = lax.all_to_all(send, ('slab', 'rad'), 0, 0, tiled=True)  21 us
    all_to_all x5, starting transfers between devices, body(): gathered = lax.all_to_all(send, ('slab', 'rad'), 0, 0, tiled=True)  17.7 us
    pallas_call x1, Pallas kernels, stress_partials(): pl.pallas_call(functools.partial(stress_kernel, groups=groups, rows=rows)...  8.58 us
    all_to_all x1, starting transfers between devices, body(): received = lax.all_to_all(send, ('slab', 'rad'), 0, 0, tiled=True)  7.3 us
    unnamed x49, local copies, waits for them, and re-layouts  6.02 us
    ppermute x2, starting transfers between devices, passed_along(): return lax.ppermute(array, axis, pairs)  5.84 us
  transfers between devices with their start and end apart: 8, of which 5 were waited for; matrix products, arithmetic and copies ran while one was open for 5% of the time, Pallas kernels for 26%

profile of v14, /device:TPU:0, one launch (start us, length us, event | category | flops | bytes accessed | tf_op | source)
XLA Modules:
  0.0 132.1 jit_solution(3590230026159508348)
XLA Ops:
  0.7 8.6 %shard_map.133 = f32[32,12,128]{2,1,0:T(8,128)} custom-call(s32[1]{0:T(128)} %bitcast.12.slab_ref, f32[3,16384]{1,0:T(4,128)} %q_ref.9, s32[1,16384]{1,0:T(1,128)} %bitcast.84, s32[1,16384]{1,0:T(1,128)} %bitcast.73), custom_call_target="tpu_custom_call" | custom-call | flops 4026531840 | bytes 327680 | tf_op jit(solution)/shard_map/pallas_call | solution.py:178
  9.3 7.3 %all-to-all-start = ((f32[32,12,128]{2,1,0:T(8,128)}), f32[32,12,128]{2,1,0:T(8,128)S(1)}, u32[]{:S(2)}, u32[]{:S(2)}) async-start(f32[32,12,128]{2,1,0:T(8,128)} %shard_map.133), calls=%async_computation | async-start | bytes 524288 | tf_op jit(solution)/shard_map/all_to_all | solution.py:342
  16.7 1.8 %copy.52 = f32[8,192,192]{1,2,0:T(8,128)} copy(f32[8,192,192]{2,1,0:T(8,128)S(1)} %copy-done.1) | data formatting | bytes 2359296 | tf_op args[9]
  20.9 7.3 %shard_map.129 = (f32[3,4096]{1,0:T(4,128)}, f32[48,128]{1,0:T(8,128)}, f32[48,128]{1,0:T(8,128)}) custom-call(f32[3,16384]{1,0:T(4,128)} %q_ref.9, f32[3,16384]{1,0:T(4,128)} %inc_ref.7, s32[1,16384]{1,0:T(1,128)} %bitcast.85, s32[1,16384]{1,0:T(1,128)} %bitcast.74, bf16[160,384]{1,0:T(8,128)(2,1)} %pad_maximum_fusion.1.tab_ref, ...), custom_call_target="tpu_custom_call" | custom-call | flops 6442450944 | bytes 163840 | tf_op jit(solution)/shard_map/pallas_call | solution.py:238
  29.7 2.4 %shard_map.134 = (f32[8,192]{1,0:T(8,128)}, f32[256,192]{1,0:T(8,128)}) custom-call(f32[8,192,192]{2,1,0:T(8,128)} %bitcast.55, f32[192,8]{1,0:T(8,128)} %convolution_bitcast_fusion.ft_ref), custom_call_target="tpu_custom_call" | custom-call | flops 589824 | bytes 1179648 | tf_op jit(solution)/shard_map/pallas_call | solution.py:204
  32.2 5.8 %all-to-all-start.1 = ((f32[32,8,192]{2,1,0:T(8,128)}), f32[32,8,192]{2,1,0:T(8,128)S(1)}, u32[]{:S(2)}, u32[]{:S(2)}) async-start(f32[32,8,192]{2,1,0:T(8,128)} %bitcast.70), calls=%async_computation.1 | async-start | bytes 524288 | tf_op jit(solution)/shard_map/all_to_all | solution.py:371
  38.0 7.3 %shard_map.130 = (f32[3,4096]{1,0:T(4,128)}, f32[48,128]{1,0:T(8,128)}, f32[48,128]{1,0:T(8,128)}) custom-call(f32[3,16384]{1,0:T(4,128)} %q_ref.9, f32[3,16384]{1,0:T(4,128)} %inc_ref.7, s32[1,16384]{1,0:T(1,128)} %bitcast.86, s32[1,16384]{1,0:T(1,128)} %bitcast.75, bf16[160,384]{1,0:T(8,128)(2,1)} %pad_maximum_fusion.1.tab_ref, ...), custom_call_target="tpu_custom_call" | custom-call | flops 6442450944 | bytes 163840 | tf_op jit(solution)/shard_map/pallas_call | solution.py:238
  45.3 3.0 %all-to-all-done.1 = f32[32,8,192]{2,1,0:T(8,128)S(1)} async-done(((f32[32,8,192]{2,1,0:T(8,128)}), f32[32,8,192]{2,1,0:T(8,128)S(1)}, u32[]{:S(2)}, u32[]{:S(2)}) %all-to-all-start.1) | async-done | bytes 196640 | tf_op jit(solution)/shard_map/all_to_all | solution.py:371
  49.1 5.3 %shard_map.135 = (f32[8,192]{1,0:T(8,128)}, f32[256,192]{1,0:T(8,128)}) custom-call(s32[32]{0:T(128)} %reshape.94.idx_ref, f32[256,192]{1,0:T(8,128)} %bitcast.64, f32[8,4,192,192]{3,2,1,0:T(8,128)} %s_ref.9, f32[8,192,192]{2,1,0:T(8,128)} %bitcast.56, f32[192,8]{1,0:T(8,128)} %convolution_bitcast_fusion.ft_ref, f32[8,192]{1,0:T(8,128)} %get-tuple-element.40.v_ref), custom_call_target="tpu_custom_call" | custom-call | flops 2949120 | bytes 6094848 | tf_op jit(solution)/shard_map/pallas_call | solution.py:299
  54.4 2.8 %all-to-all-start.2 = ((f32[32,8,192]{2,1,0:T(8,128)}), f32[32,8,192]{2,1,0:T(8,128)S(1)}, u32[]{:S(2)}, u32[]{:S(2)}) async-start(f32[32,8,192]{2,1,0:T(8,128)} %bitcast.69), calls=%async_computation.2 | async-start | bytes 524288 | tf_op jit(solution)/shard_map/all_to_all | solution.py:371
  57.2 7.4 %shard_map.131 = (f32[3,4096]{1,0:T(4,128)}, f32[48,128]{1,0:T(8,128)}, f32[48,128]{1,0:T(8,128)}) custom-call(f32[3,16384]{1,0:T(4,128)} %q_ref.9, f32[3,16384]{1,0:T(4,128)} %inc_ref.7, s32[1,16384]{1,0:T(1,128)} %bitcast.87, s32[1,16384]{1,0:T(1,128)} %bitcast.76, bf16[160,384]{1,0:T(8,128)(2,1)} %pad_maximum_fusion.1.tab_ref, ...), custom_call_target="tpu_custom_call" | custom-call | flops 6442450944 | bytes 163840 | tf_op jit(solution)/shard_map/pallas_call | solution.py:238
  64.6 3.0 %all-to-all-done.2 = f32[32,8,192]{2,1,0:T(8,128)S(1)} async-done(((f32[32,8,192]{2,1,0:T(8,128)}), f32[32,8,192]{2,1,0:T(8,128)S(1)}, u32[]{:S(2)}, u32[]{:S(2)}) %all-to-all-start.2) | async-done | bytes 196640 | tf_op jit(solution)/shard_map/all_to_all | solution.py:371
  68.3 5.3 %shard_map.136 = (f32[8,192]{1,0:T(8,128)}, f32[256,192]{1,0:T(8,128)}) custom-call(s32[32]{0:T(128)} %reshape.94.idx_ref, f32[256,192]{1,0:T(8,128)} %bitcast.65, f32[8,4,192,192]{3,2,1,0:T(8,128)} %s_ref.9, f32[8,192,192]{2,1,0:T(8,128)} %bitcast.57, f32[192,8]{1,0:T(8,128)} %convolution_bitcast_fusion.ft_ref, f32[8,192]{1,0:T(8,128)} %get-tuple-element.42.v_ref), custom_call_target="tpu_custom_call" | custom-call | flops 2949120 | bytes 6094848 | tf_op jit(solution)/shard_map/pallas_call | solution.py:299
  73.6 2.8 %all-to-all-start.3 = ((f32[32,8,192]{2,1,0:T(8,128)}), f32[32,8,192]{2,1,0:T(8,128)S(1)}, u32[]{:S(2)}, u32[]{:S(2)}) async-start(f32[32,8,192]{2,1,0:T(8,128)} %bitcast.67), calls=%async_computation.3 | async-start | bytes 524288 | tf_op jit(solution)/shard_map/all_to_all | solution.py:371
  76.5 7.4 %shard_map.132 = (f32[3,4096]{1,0:T(4,128)}, f32[48,128]{1,0:T(8,128)}, f32[48,128]{1,0:T(8,128)}) custom-call(f32[3,16384]{1,0:T(4,128)} %q_ref.9, f32[3,16384]{1,0:T(4,128)} %inc_ref.7, s32[1,16384]{1,0:T(1,128)} %bitcast.88, s32[1,16384]{1,0:T(1,128)} %bitcast.77, bf16[160,384]{1,0:T(8,128)(2,1)} %pad_maximum_fusion.1.tab_ref, ...), custom_call_target="tpu_custom_call" | custom-call | flops 6442450944 | bytes 163840 | tf_op jit(solution)/shard_map/pallas_call | solution.py:238
  84.7 2.1 %all-to-all-done.3 = f32[32,8,192]{2,1,0:T(8,128)S(1)} async-done(((f32[32,8,192]{2,1,0:T(8,128)}), f32[32,8,192]{2,1,0:T(8,128)S(1)}, u32[]{:S(2)}, u32[]{:S(2)}) %all-to-all-start.3) | async-done | bytes 196640 | tf_op jit(solution)/shard_map/all_to_all | solution.py:371
  87.5 5.3 %shard_map.137 = (f32[8,192]{1,0:T(8,128)}, f32[256,192]{1,0:T(8,128)}) custom-call(s32[32]{0:T(128)} %reshape.94.idx_ref, f32[256,192]{1,0:T(8,128)} %bitcast.62, f32[8,4,192,192]{3,2,1,0:T(8,128)} %s_ref.9, f32[8,192,192]{2,1,0:T(8,128)} %bitcast.58, f32[192,8]{1,0:T(8,128)} %convolution_bitcast_fusion.ft_ref, f32[8,192]{1,0:T(8,128)} %get-tuple-element.44.v_ref), custom_call_target="tpu_custom_call" | custom-call | flops 2949120 | bytes 6094848 | tf_op jit(solution)/shard_map/pallas_call | solution.py:299
  92.9 3.7 %all-to-all-start.4 = ((f32[32,8,192]{2,1,0:T(8,128)}), f32[32,8,192]{2,1,0:T(8,128)S(1)}, u32[]{:S(2)}, u32[]{:S(2)}) async-start(f32[32,8,192]{2,1,0:T(8,128)} %bitcast.68), calls=%async_computation.4 | async-start | bytes 524288 | tf_op jit(solution)/shard_map/all_to_all | solution.py:371
  97.9 4.5 %collective-permute-start = (f32[3,1024]{1,0:T(4,128)S(1)}, f32[3,1024]{1,0:T(4,128)S(1)}, u32[]{:S(2)}, u32[]{:S(2)}) collective-permute-start(f32[3,1024]{1,0:T(4,128)S(1)} %bitcast.81), channel_id=1, source_target_pairs={{0,8},{8,16},{16,24},{1,9},{9,17},{17,25},{2,10},{10,18},{18,26},{... | collective-permute-start | bytes 36872 | tf_op jit(solution)/shard_map/ppermute | solution.py:318
  102.5 4.5 %all-to-all-done.4 = f32[32,8,192]{2,1,0:T(8,128)S(1)} async-done(((f32[32,8,192]{2,1,0:T(8,128)}), f32[32,8,192]{2,1,0:T(8,128)S(1)}, u32[]{:S(2)}, u32[]{:S(2)}) %all-to-all-start.4) | async-done | bytes 196640 | tf_op jit(solution)/shard_map/all_to_all | solution.py:371
  107.7 5.4 %shard_map.138 = (f32[8,192]{1,0:T(8,128)}, f32[256,192]{1,0:T(8,128)}) custom-call(s32[32]{0:T(128)} %reshape.94.idx_ref, f32[256,192]{1,0:T(8,128)} %bitcast.63, f32[8,4,192,192]{3,2,1,0:T(8,128)} %s_ref.9, f32[8,192,192]{2,1,0:T(8,128)} %bitcast.59, f32[192,8]{1,0:T(8,128)} %convolution_bitcast_fusion.ft_ref, f32[8,192]{1,0:T(8,128)} %get-tuple-element.46.v_ref), custom_call_target="tpu_custom_call" | custom-call | flops 2949120 | bytes 6094848 | tf_op jit(solution)/shard_map/pallas_call | solution.py:299
  113.1 2.6 %all-to-all-start.5 = ((f32[32,8,192]{2,1,0:T(8,128)}), f32[32,8,192]{2,1,0:T(8,128)S(1)}, u32[]{:S(2)}, u32[]{:S(2)}) async-start(f32[32,8,192]{2,1,0:T(8,128)} %bitcast.66), calls=%async_computation.5 | async-start | bytes 524288 | tf_op jit(solution)/shard_map/all_to_all | solution.py:371
  117.7 8.3 %all-to-all-done.5 = f32[32,8,192]{2,1,0:T(8,128)S(1)} async-done(((f32[32,8,192]{2,1,0:T(8,128)}), f32[32,8,192]{2,1,0:T(8,128)S(1)}, u32[]{:S(2)}, u32[]{:S(2)}) %all-to-all-start.5) | async-done | bytes 196640 | tf_op jit(solution)/shard_map/all_to_all | solution.py:371
  126.7 5.3 %shard_map.139 = (f32[8,192]{1,0:T(8,128)}, f32[256,192]{1,0:T(8,128)}) custom-call(s32[32]{0:T(128)} %reshape.94.idx_ref, f32[256,192]{1,0:T(8,128)} %bitcast.61, f32[8,4,192,192]{3,2,1,0:T(8,128)} %s_ref.9, f32[8,192,192]{2,1,0:T(8,128)} %bitcast.60, f32[192,8]{1,0:T(8,128)} %convolution_bitcast_fusion.ft_ref, f32[8,192]{1,0:T(8,128)} %get-tuple-element.48.v_ref), custom_call_target="tpu_custom_call" | custom-call | flops 2949120 | bytes 6094848 | tf_op jit(solution)/shard_map/pallas_call | solution.py:299
  (77 shorter events, 11.6 us)
Async XLA Ops:
  0.6 27.9 %copy-start = (f32[192,192]{1,0:T(8,128)S(1)}, f32[192,192]{1,0:T(8,128)}, u32[]{:S(2)}) copy-start(f32[192,192]{1,0:T(8,128)} %param.16) | copy-start | bytes 442372
  0.7 15.9 %copy-start.8 = (s32[16384]{0:T(1024)S(1)}, s32[16384]{0:T(1024)}, u32[]{:S(2)}) copy-start(s32[16384]{0:T(1024)} %param.14) | copy-start | bytes 196612
  0.7 15.9 %copy-start.19 = (f32[384]{0:T(512)S(1)}, f32[384]{0:T(512)}, u32[]{:S(2)}) copy-start(f32[384]{0:T(512)} %param.15) | copy-start | bytes 4612
  0.7 16.0 %copy-start.1 = (f32[8,192,192]{2,1,0:T(8,128)S(1)}, f32[8,192,192]{2,1,0:T(8,128)}, u32[]{:S(2)}) copy-start(f32[8,192,192]{2,1,0:T(8,128)} %param.19) | copy-start | bytes 3538948
  9.3 19.0 %all-to-all-start = ((f32[32,12,128]{2,1,0:T(8,128)}), f32[32,12,128]{2,1,0:T(8,128)S(1)}, u32[]{:S(2)}, u32[]{:S(2)}) async-start(f32[32,12,128]{2,1,0:T(8,128)} %shard_map.133), calls=%async_computation | async-start | bytes 524288 | tf_op jit(solution)/shard_map/all_to_all | solution.py:342
  16.7 1.8 %copy-start.20 = (s32[8,4]{0,1:T(4,128)S(1)}, s32[8,4]{0,1:T(4,128)}, u32[]{:S(2)}) copy-start(s32[8,4]{0,1:T(4,128)} %param.18) | copy-start | bytes 388
  16.7 2.4 %copy-start.7 = (f32[5,3072]{1,0:T(8,128)S(1)}, f32[5,3072]{1,0:T(8,128)}, u32[]{:S(2)}) copy-start(f32[5,3072]{1,0:T(8,128)} %param.12) | copy-start | bytes 184324
  32.2 16.2 %all-to-all-start.1 = ((f32[32,8,192]{2,1,0:T(8,128)}), f32[32,8,192]{2,1,0:T(8,128)S(1)}, u32[]{:S(2)}, u32[]{:S(2)}) async-start(f32[32,8,192]{2,1,0:T(8,128)} %bitcast.70), calls=%async_computation.1 | async-start | bytes 524288 | tf_op jit(solution)/shard_map/all_to_all | solution.py:371
  54.4 13.2 %all-to-all-start.2 = ((f32[32,8,192]{2,1,0:T(8,128)}), f32[32,8,192]{2,1,0:T(8,128)S(1)}, u32[]{:S(2)}, u32[]{:S(2)}) async-start(f32[32,8,192]{2,1,0:T(8,128)} %bitcast.69), calls=%async_computation.2 | async-start | bytes 524288 | tf_op jit(solution)/shard_map/all_to_all | solution.py:371
  73.6 13.2 %all-to-all-start.3 = ((f32[32,8,192]{2,1,0:T(8,128)}), f32[32,8,192]{2,1,0:T(8,128)S(1)}, u32[]{:S(2)}, u32[]{:S(2)}) async-start(f32[32,8,192]{2,1,0:T(8,128)} %bitcast.67), calls=%async_computation.3 | async-start | bytes 524288 | tf_op jit(solution)/shard_map/all_to_all | solution.py:371
  76.5 7.4 %copy-start.13 = (f32[48,128]{1,0:T(8,128)S(1)}, f32[48,128]{1,0:T(8,128)}, u32[]{:S(2)}) copy-start(f32[48,128]{1,0:T(8,128)} %get-tuple-element.31) | copy-start | bytes 73732
  76.5 7.4 %copy-start.14 = (f32[48,128]{1,0:T(8,128)S(1)}, f32[48,128]{1,0:T(8,128)}, u32[]{:S(2)}) copy-start(f32[48,128]{1,0:T(8,128)} %get-tuple-element.35) | copy-start | bytes 73732
  76.5 7.4 %copy-start.15 = (f32[48,128]{1,0:T(8,128)S(1)}, f32[48,128]{1,0:T(8,128)}, u32[]{:S(2)}) copy-start(f32[48,128]{1,0:T(8,128)} %get-tuple-element.32) | copy-start | bytes 73732
  76.5 7.4 %copy-start.16 = (f32[48,128]{1,0:T(8,128)S(1)}, f32[48,128]{1,0:T(8,128)}, u32[]{:S(2)}) copy-start(f32[48,128]{1,0:T(8,128)} %get-tuple-element.36) | copy-start | bytes 73732
  76.5 7.4 %copy-start.17 = (f32[48,128]{1,0:T(8,128)S(1)}, f32[48,128]{1,0:T(8,128)}, u32[]{:S(2)}) copy-start(f32[48,128]{1,0:T(8,128)} %get-tuple-element.33) | copy-start | bytes 73732
  76.5 7.4 %copy-start.18 = (f32[48,128]{1,0:T(8,128)S(1)}, f32[48,128]{1,0:T(8,128)}, u32[]{:S(2)}) copy-start(f32[48,128]{1,0:T(8,128)} %get-tuple-element.37) | copy-start | bytes 73732
  92.9 14.1 %all-to-all-start.4 = ((f32[32,8,192]{2,1,0:T(8,128)}), f32[32,8,192]{2,1,0:T(8,128)S(1)}, u32[]{:S(2)}, u32[]{:S(2)}) async-start(f32[32,8,192]{2,1,0:T(8,128)} %bitcast.68), calls=%async_computation.4 | async-start | bytes 524288 | tf_op jit(solution)/shard_map/all_to_all | solution.py:371
  96.6 19.8 %collective-permute-start.1 = (f32[3,1024]{1,0:T(4,128)S(1)}, f32[3,1024]{1,0:T(4,128)S(1)}, u32[]{:S(2)}, u32[]{:S(2)}) collective-permute-start(f32[3,1024]{1,0:T(4,128)S(1)} %bitcast.80), channel_id=1, source_target_pairs={{8,0},{16,8},{24,16},{9,1},{17,9},{25,17},{10,2},{18,10},{26,18},{... | collective-permute-start | bytes 36872 | tf_op jit(solution)/shard_map/ppermute | solution.py:318
  97.9 18.5 %collective-permute-start = (f32[3,1024]{1,0:T(4,128)S(1)}, f32[3,1024]{1,0:T(4,128)S(1)}, u32[]{:S(2)}, u32[]{:S(2)}) collective-permute-start(f32[3,1024]{1,0:T(4,128)S(1)} %bitcast.81), channel_id=1, source_target_pairs={{0,8},{8,16},{16,24},{1,9},{9,17},{17,25},{2,10},{10,18},{18,26},{... | collective-permute-start | bytes 36872 | tf_op jit(solution)/shard_map/ppermute | solution.py:318
  107.7 8.0 %copy-start.9 = (f32[3,4096]{1,0:T(4,128)S(1)}, f32[3,4096]{1,0:T(4,128)}, u32[]{:S(2)}) copy-start(f32[3,4096]{1,0:T(4,128)} %get-tuple-element.27) | copy-start | bytes 147460
  107.7 8.0 %copy-start.10 = (f32[3,4096]{1,0:T(4,128)S(1)}, f32[3,4096]{1,0:T(4,128)}, u32[]{:S(2)}) copy-start(f32[3,4096]{1,0:T(4,128)} %get-tuple-element.28) | copy-start | bytes 147460
  107.7 8.0 %copy-start.11 = (f32[3,4096]{1,0:T(4,128)S(1)}, f32[3,4096]{1,0:T(4,128)}, u32[]{:S(2)}) copy-start(f32[3,4096]{1,0:T(4,128)} %get-tuple-element.29) | copy-start | bytes 147460
  107.7 8.0 %copy-start.12 = (f32[3,4096]{1,0:T(4,128)S(1)}, f32[3,4096]{1,0:T(4,128)}, u32[]{:S(2)}) copy-start(f32[3,4096]{1,0:T(4,128)} %get-tuple-element.30) | copy-start | bytes 147460
  113.1 13.0 %all-to-all-start.5 = ((f32[32,8,192]{2,1,0:T(8,128)}), f32[32,8,192]{2,1,0:T(8,128)S(1)}, u32[]{:S(2)}, u32[]{:S(2)}) async-start(f32[32,8,192]{2,1,0:T(8,128)} %bitcast.66), calls=%async_computation.5 | async-start | bytes 524288 | tf_op jit(solution)/shard_map/all_to_all | solution.py:371
  (5 other events, 3.5 us)

commit v15 on v14

--- a/solution.py
+++ b/solution.py
@@ -187,13 +187,15 @@
     )(slab, q_state, element.reshape(1, -1), migration.reshape(1, -1))
 
 
-def first_kernel(pt_ref, ft_ref, vout_ref, send_ref):
-    own = vout_ref.shape[0]
-    rows = [
-        damping * jnp.sum(pt_ref[b] * ft_ref[:, b : b + 1], axis=0, keepdims=True)
-        for b in range(own)
-    ]
-    fresh = jnp.concatenate(rows, axis=0)
+def first_kernel(p_ref, f_ref, vout_ref, send_ref):
+    own, size = vout_ref.shape
+    lanes = lax.broadcasted_iota(jnp.int32, (size, 128), 1)
+    block = jnp.zeros((size, 128), jnp.float32)
+    for b in range(own):
+        column = damping * jnp.sum(p_ref[b] * f_ref[b : b + 1, :], axis=1, keepdims=True)
+        block = jnp.where(lanes == b, column, block)
+    block = jnp.pad(block, ((0, round_up(size, 128) - size), (0, 0)))
+    fresh = block.T[:own, :size]
     vout_ref[...] = fresh
     for k in range(send_ref.shape[0] // own):
         send_ref[k * own : (k + 1) * own, :] = fresh
@@ -364,9 +366,10 @@
     slab_blocks = own_blocks * n_rad
     copies = n_slab * n_rad
     where_read = ((slab - 1) * slab_blocks + pattern).reshape(-1).astype(jnp.int32)
-    transposed = jnp.swapaxes(preconditioner, 1, 2)
     force_t = force.T
-    velocity, send = first_velocity(transposed, force_t, copies)
+    velocity, send = first_velocity(preconditioner, force, copies)
+    held, velocity = lax.optimization_barrier((preconditioner, velocity))
+    transposed = jnp.swapaxes(held, 1, 2)
     for sweep_index in range(1, ITERS):
         gathered = lax.all_to_all(send, ("slab", "rad"), 0, 0, tiled=True)
         velocity, send = sweep(

time: 133 us -> 133 us (level)
  starting transfers between devices: 30.9 us -> 33.2 us
  waiting for transfers between devices: 21 us -> 18.7 us
    all_to_all x5, waiting for transfers between devices: 21 us -> 18.3 us  [body(): gathered = lax.all_to_all(send, ('slab', 'rad'), 0, 0, tiled=True)]
    all_to_all x5, starting transfers between devices: 17.7 us -> 20 us  [body(): gathered = lax.all_to_all(send, ('slab', 'rad'), 0, 0, tiled=True)]
    unnamed x49 -> x50, local copies, waits for them, and re-layouts: 6.02 us -> 4.25 us
    optimization_barrier x0 -> x1, local copies, waits for them, and re-layouts: none -> 1.77 us  [body(): held, velocity = lax.optimization_barrier((preconditioner, velocity))]
  transfers between devices with their start and end apart: 8 -> 8, of which waited for: 5 -> 6; matrix products, arithmetic and copies ran while one was open for 5% -> 6% of each run, Pallas kernels for 26% -> 26%
where the time goes in v15:
time: 133 us
  Pallas kernels  67.2 us (51%)
  starting transfers between devices  33.2 us (25%)
  waiting for transfers between devices  18.7 us (14%)
  local copies, waits for them, and re-layouts  8.5 us (6%)
  other arithmetic  3.25 us (2%)
    pallas_call x4, Pallas kernels, update_and_pack(): pl.pallas_call(functools.partial(update_kernel, groups16=groups16, slots1...  29.5 us
    pallas_call x5, Pallas kernels, sweep(): pl.pallas_call(sweep_kernel, out_shape=(jax.ShapeDtypeStruct(velocity.sha...  26.6 us
    all_to_all x5, starting transfers between devices, body(): gathered = lax.all_to_all(send, ('slab', 'rad'), 0, 0, tiled=True)  20 us
    all_to_all x5, waiting for transfers between devices, body(): gathered = lax.all_to_all(send, ('slab', 'rad'), 0, 0, tiled=True)  18.3 us
    pallas_call x1, Pallas kernels, stress_partials(): pl.pallas_call(functools.partial(stress_kernel, groups=groups, rows=rows)...  8.54 us
    all_to_all x1, starting transfers between devices, body(): received = lax.all_to_all(send, ('slab', 'rad'), 0, 0, tiled=True)  7.3 us
    ppermute x2, starting transfers between devices, passed_along(): return lax.ppermute(array, axis, pairs)  5.84 us
    unnamed x50, local copies, waits for them, and re-layouts  4.25 us
  transfers between devices with their start and end apart: 8, of which 6 were waited for; matrix products, arithmetic and copies ran while one was open for 6% of the time, Pallas kernels for 26%

profile of v15, /device:TPU:0, one launch (start us, length us, event | category | flops | bytes accessed | tf_op | source)
XLA Modules:
  0.0 132.6 jit_solution(7894729530985989927)
XLA Ops:
  0.7 8.5 %shard_map.133 = f32[32,12,128]{2,1,0:T(8,128)} custom-call(s32[1]{0:T(128)} %bitcast.12.slab_ref, f32[3,16384]{1,0:T(4,128)} %q_ref.9, s32[1,16384]{1,0:T(1,128)} %bitcast.87, s32[1,16384]{1,0:T(1,128)} %bitcast.76), custom_call_target="tpu_custom_call" | custom-call | flops 4026531840 | bytes 327680 | tf_op jit(solution)/shard_map/pallas_call | solution.py:178
  9.2 7.3 %all-to-all-start = ((f32[32,12,128]{2,1,0:T(8,128)}), f32[32,12,128]{2,1,0:T(8,128)S(1)}, u32[]{:S(2)}, u32[]{:S(2)}) async-start(f32[32,12,128]{2,1,0:T(8,128)} %shard_map.133), calls=%async_computation | async-start | bytes 524288 | tf_op jit(solution)/shard_map/all_to_all | solution.py:344
  19.2 7.3 %shard_map.129 = (f32[3,4096]{1,0:T(4,128)}, f32[48,128]{1,0:T(8,128)}, f32[48,128]{1,0:T(8,128)}) custom-call(f32[3,16384]{1,0:T(4,128)} %q_ref.9, f32[3,16384]{1,0:T(4,128)} %inc_ref.7, s32[1,16384]{1,0:T(1,128)} %bitcast.88, s32[1,16384]{1,0:T(1,128)} %bitcast.77, bf16[160,384]{1,0:T(8,128)(2,1)} %pad_maximum_fusion.1.tab_ref, ...), custom_call_target="tpu_custom_call" | custom-call | flops 6442450944 | bytes 163840 | tf_op jit(solution)/shard_map/pallas_call | solution.py:240
  27.9 2.5 %shard_map.134 = (f32[8,192]{1,0:T(8,128)}, f32[256,192]{1,0:T(8,128)}) custom-call(f32[8,192,192]{2,1,0:T(8,128)} %p_ref.1, f32[8,192]{1,0:T(8,128)} %fusion.5.f_ref), custom_call_target="tpu_custom_call" | custom-call | flops 589824 | bytes 1179648 | tf_op jit(solution)/shard_map/pallas_call | solution.py:206
  30.4 5.5 %all-to-all-start.1 = ((f32[32,8,192]{2,1,0:T(8,128)}), f32[32,8,192]{2,1,0:T(8,128)S(1)}, u32[]{:S(2)}, u32[]{:S(2)}) async-start(f32[32,8,192]{2,1,0:T(8,128)} %bitcast.72), calls=%async_computation.1 | async-start | bytes 524288 | tf_op jit(solution)/shard_map/all_to_all | solution.py:374
  35.9 7.5 %shard_map.130 = (f32[3,4096]{1,0:T(4,128)}, f32[48,128]{1,0:T(8,128)}, f32[48,128]{1,0:T(8,128)}) custom-call(f32[3,16384]{1,0:T(4,128)} %q_ref.9, f32[3,16384]{1,0:T(4,128)} %inc_ref.7, s32[1,16384]{1,0:T(1,128)} %bitcast.89, s32[1,16384]{1,0:T(1,128)} %bitcast.78, bf16[160,384]{1,0:T(8,128)(2,1)} %pad_maximum_fusion.1.tab_ref, ...), custom_call_target="tpu_custom_call" | custom-call | flops 6442450944 | bytes 163840 | tf_op jit(solution)/shard_map/pallas_call | solution.py:240
  44.1 1.8 %copy.53 = f32[8,192,192]{1,2,0:T(8,128)} copy(f32[8,192,192]{2,1,0:T(8,128)S(1)} %copy-done.1) | data formatting | bytes 2359296 | tf_op jit(solution)/shard_map/optimization_barrier | solution.py:371
  47.0 5.3 %shard_map.135 = (f32[8,192]{1,0:T(8,128)}, f32[256,192]{1,0:T(8,128)}) custom-call(s32[32]{0:T(128)} %reshape.94.idx_ref, f32[256,192]{1,0:T(8,128)} %bitcast.67, f32[8,4,192,192]{3,2,1,0:T(8,128)} %s_ref.9, f32[8,192,192]{2,1,0:T(8,128)} %bitcast.54, f32[192,8]{1,0:T(8,128)} %bitcast.59, f32[8,192]{1,0:T(8,128)} %get-tuple-element.44.v_ref), custom_call_target="tpu_custom_call" | custom-call | flops 2949120 | bytes 6094848 | tf_op jit(solution)/shard_map/pallas_call | solution.py:301
  52.3 5.5 %all-to-all-start.2 = ((f32[32,8,192]{2,1,0:T(8,128)}), f32[32,8,192]{2,1,0:T(8,128)S(1)}, u32[]{:S(2)}, u32[]{:S(2)}) async-start(f32[32,8,192]{2,1,0:T(8,128)} %bitcast.73), calls=%async_computation.2 | async-start | bytes 524288 | tf_op jit(solution)/shard_map/all_to_all | solution.py:374
  57.8 7.4 %shard_map.131 = (f32[3,4096]{1,0:T(4,128)}, f32[48,128]{1,0:T(8,128)}, f32[48,128]{1,0:T(8,128)}) custom-call(f32[3,16384]{1,0:T(4,128)} %q_ref.9, f32[3,16384]{1,0:T(4,128)} %inc_ref.7, s32[1,16384]{1,0:T(1,128)} %bitcast.90, s32[1,16384]{1,0:T(1,128)} %bitcast.79, bf16[160,384]{1,0:T(8,128)(2,1)} %pad_maximum_fusion.1.tab_ref, ...), custom_call_target="tpu_custom_call" | custom-call | flops 6442450944 | bytes 163840 | tf_op jit(solution)/shard_map/pallas_call | solution.py:240
  65.1 3.0 %all-to-all-done.2 = f32[32,8,192]{2,1,0:T(8,128)S(1)} async-done(((f32[32,8,192]{2,1,0:T(8,128)}), f32[32,8,192]{2,1,0:T(8,128)S(1)}, u32[]{:S(2)}, u32[]{:S(2)}) %all-to-all-start.2) | async-done | bytes 196640 | tf_op jit(solution)/shard_map/all_to_all | solution.py:374
  68.9 5.3 %shard_map.136 = (f32[8,192]{1,0:T(8,128)}, f32[256,192]{1,0:T(8,128)}) custom-call(s32[32]{0:T(128)} %reshape.94.idx_ref, f32[256,192]{1,0:T(8,128)} %bitcast.68, f32[8,4,192,192]{3,2,1,0:T(8,128)} %s_ref.9, f32[8,192,192]{2,1,0:T(8,128)} %bitcast.55, f32[192,8]{1,0:T(8,128)} %bitcast.60, f32[8,192]{1,0:T(8,128)} %get-tuple-element.46.v_ref), custom_call_target="tpu_custom_call" | custom-call | flops 2949120 | bytes 6094848 | tf_op jit(solution)/shard_map/pallas_call | solution.py:301
  74.2 2.8 %all-to-all-start.3 = ((f32[32,8,192]{2,1,0:T(8,128)}), f32[32,8,192]{2,1,0:T(8,128)S(1)}, u32[]{:S(2)}, u32[]{:S(2)}) async-start(f32[32,8,192]{2,1,0:T(8,128)} %bitcast.70), calls=%async_computation.3 | async-start | bytes 524288 | tf_op jit(solution)/shard_map/all_to_all | solution.py:374
  77.1 7.4 %shard_map.132 = (f32[3,4096]{1,0:T(4,128)}, f32[48,128]{1,0:T(8,128)}, f32[48,128]{1,0:T(8,128)}) custom-call(f32[3,16384]{1,0:T(4,128)} %q_ref.9, f32[3,16384]{1,0:T(4,128)} %inc_ref.7, s32[1,16384]{1,0:T(1,128)} %bitcast.91, s32[1,16384]{1,0:T(1,128)} %bitcast.80, bf16[160,384]{1,0:T(8,128)(2,1)} %pad_maximum_fusion.1.tab_ref, ...), custom_call_target="tpu_custom_call" | custom-call | flops 6442450944 | bytes 163840 | tf_op jit(solution)/shard_map/pallas_call | solution.py:240
  85.2 2.1 %all-to-all-done.3 = f32[32,8,192]{2,1,0:T(8,128)S(1)} async-done(((f32[32,8,192]{2,1,0:T(8,128)}), f32[32,8,192]{2,1,0:T(8,128)S(1)}, u32[]{:S(2)}, u32[]{:S(2)}) %all-to-all-start.3) | async-done | bytes 196640 | tf_op jit(solution)/shard_map/all_to_all | solution.py:374
  88.1 5.3 %shard_map.137 = (f32[8,192]{1,0:T(8,128)}, f32[256,192]{1,0:T(8,128)}) custom-call(s32[32]{0:T(128)} %reshape.94.idx_ref, f32[256,192]{1,0:T(8,128)} %bitcast.65, f32[8,4,192,192]{3,2,1,0:T(8,128)} %s_ref.9, f32[8,192,192]{2,1,0:T(8,128)} %bitcast.56, f32[192,8]{1,0:T(8,128)} %bitcast.61, f32[8,192]{1,0:T(8,128)} %get-tuple-element.48.v_ref), custom_call_target="tpu_custom_call" | custom-call | flops 2949120 | bytes 6094848 | tf_op jit(solution)/shard_map/pallas_call | solution.py:301
  93.4 3.7 %all-to-all-start.4 = ((f32[32,8,192]{2,1,0:T(8,128)}), f32[32,8,192]{2,1,0:T(8,128)S(1)}, u32[]{:S(2)}, u32[]{:S(2)}) async-start(f32[32,8,192]{2,1,0:T(8,128)} %bitcast.71), calls=%async_computation.4 | async-start | bytes 524288 | tf_op jit(solution)/shard_map/all_to_all | solution.py:374
  97.2 1.3 collective-permute-start.1
  98.5 4.5 %collective-permute-start = (f32[3,1024]{1,0:T(4,128)S(1)}, f32[3,1024]{1,0:T(4,128)S(1)}, u32[]{:S(2)}, u32[]{:S(2)}) collective-permute-start(f32[3,1024]{1,0:T(4,128)S(1)} %bitcast.84), channel_id=1, source_target_pairs={{0,8},{8,16},{16,24},{1,9},{9,17},{17,25},{2,10},{10,18},{18,26},{... | collective-permute-start | bytes 36872 | tf_op jit(solution)/shard_map/ppermute | solution.py:320
  103.0 4.5 %all-to-all-done.4 = f32[32,8,192]{2,1,0:T(8,128)S(1)} async-done(((f32[32,8,192]{2,1,0:T(8,128)}), f32[32,8,192]{2,1,0:T(8,128)S(1)}, u32[]{:S(2)}, u32[]{:S(2)}) %all-to-all-start.4) | async-done | bytes 196640 | tf_op jit(solution)/shard_map/all_to_all | solution.py:374
  108.2 5.4 %shard_map.138 = (f32[8,192]{1,0:T(8,128)}, f32[256,192]{1,0:T(8,128)}) custom-call(s32[32]{0:T(128)} %reshape.94.idx_ref, f32[256,192]{1,0:T(8,128)} %bitcast.66, f32[8,4,192,192]{3,2,1,0:T(8,128)} %s_ref.9, f32[8,192,192]{2,1,0:T(8,128)} %bitcast.57, f32[192,8]{1,0:T(8,128)} %bitcast.62, f32[8,192]{1,0:T(8,128)} %get-tuple-element.50.v_ref), custom_call_target="tpu_custom_call" | custom-call | flops 2949120 | bytes 6094848 | tf_op jit(solution)/shard_map/pallas_call | solution.py:301
  113.6 2.6 %all-to-all-start.5 = ((f32[32,8,192]{2,1,0:T(8,128)}), f32[32,8,192]{2,1,0:T(8,128)S(1)}, u32[]{:S(2)}, u32[]{:S(2)}) async-start(f32[32,8,192]{2,1,0:T(8,128)} %bitcast.69), calls=%async_computation.5 | async-start | bytes 524288 | tf_op jit(solution)/shard_map/all_to_all | solution.py:374
  118.2 8.3 %all-to-all-done.5 = f32[32,8,192]{2,1,0:T(8,128)S(1)} async-done(((f32[32,8,192]{2,1,0:T(8,128)}), f32[32,8,192]{2,1,0:T(8,128)S(1)}, u32[]{:S(2)}, u32[]{:S(2)}) %all-to-all-start.5) | async-done | bytes 196640 | tf_op jit(solution)/shard_map/all_to_all | solution.py:374
  127.3 5.3 %shard_map.139 = (f32[8,192]{1,0:T(8,128)}, f32[256,192]{1,0:T(8,128)}) custom-call(s32[32]{0:T(128)} %reshape.94.idx_ref, f32[256,192]{1,0:T(8,128)} %bitcast.64, f32[8,4,192,192]{3,2,1,0:T(8,128)} %s_ref.9, f32[8,192,192]{2,1,0:T(8,128)} %bitcast.58, f32[192,8]{1,0:T(8,128)} %bitcast.63, f32[8,192]{1,0:T(8,128)} %get-tuple-element.52.v_ref), custom_call_target="tpu_custom_call" | custom-call | flops 2949120 | bytes 6094848 | tf_op jit(solution)/shard_map/pallas_call | solution.py:301
  (80 shorter events, 11.5 us)
Async XLA Ops:
  0.6 26.5 %copy-start = (f32[192,192]{1,0:T(8,128)S(1)}, f32[192,192]{1,0:T(8,128)}, u32[]{:S(2)}) copy-start(f32[192,192]{1,0:T(8,128)} %param.16) | copy-start | bytes 442372
  0.7 15.9 %copy-start.9 = (s32[16384]{0:T(1024)S(1)}, s32[16384]{0:T(1024)}, u32[]{:S(2)}) copy-start(s32[16384]{0:T(1024)} %param.14) | copy-start | bytes 196612
  0.7 15.9 %copy-start.20 = (f32[384]{0:T(512)S(1)}, f32[384]{0:T(512)}, u32[]{:S(2)}) copy-start(f32[384]{0:T(512)} %param.15) | copy-start | bytes 4612
  0.7 16.0 %copy-start.21 = (s32[8,4]{0,1:T(4,128)S(1)}, s32[8,4]{0,1:T(4,128)}, u32[]{:S(2)}) copy-start(s32[8,4]{0,1:T(4,128)} %param.18) | copy-start | bytes 388
  0.7 16.8 %copy-start.7 = (f32[5,3072]{1,0:T(8,128)S(1)}, f32[5,3072]{1,0:T(8,128)}, u32[]{:S(2)}) copy-start(f32[5,3072]{1,0:T(8,128)} %param.12) | copy-start | bytes 184324
  9.2 17.7 %all-to-all-start = ((f32[32,12,128]{2,1,0:T(8,128)}), f32[32,12,128]{2,1,0:T(8,128)S(1)}, u32[]{:S(2)}, u32[]{:S(2)}) async-start(f32[32,12,128]{2,1,0:T(8,128)} %shard_map.133), calls=%async_computation | async-start | bytes 524288 | tf_op jit(solution)/shard_map/all_to_all | solution.py:344
  30.4 15.9 %all-to-all-start.1 = ((f32[32,8,192]{2,1,0:T(8,128)}), f32[32,8,192]{2,1,0:T(8,128)S(1)}, u32[]{:S(2)}, u32[]{:S(2)}) async-start(f32[32,8,192]{2,1,0:T(8,128)} %bitcast.72), calls=%async_computation.1 | async-start | bytes 524288 | tf_op jit(solution)/shard_map/all_to_all | solution.py:374
  35.9 7.5 %copy-start.8 = (f32[8,192]{1,0:T(8,128)S(1)}, f32[8,192]{1,0:T(8,128)}, u32[]{:S(2)}) copy-start(f32[8,192]{1,0:T(8,128)} %fusion.5.f_ref) | copy-start | bytes 18436
  35.9 8.2 %copy-start.1 = (f32[8,192,192]{2,1,0:T(8,128)S(1)}, f32[8,192,192]{2,1,0:T(8,128)}, u32[]{:S(2)}) copy-start(f32[8,192,192]{2,1,0:T(8,128)} %p_ref.1) | copy-start | bytes 3538948
  52.3 15.9 %all-to-all-start.2 = ((f32[32,8,192]{2,1,0:T(8,128)}), f32[32,8,192]{2,1,0:T(8,128)S(1)}, u32[]{:S(2)}, u32[]{:S(2)}) async-start(f32[32,8,192]{2,1,0:T(8,128)} %bitcast.73), calls=%async_computation.2 | async-start | bytes 524288 | tf_op jit(solution)/shard_map/all_to_all | solution.py:374
  74.2 13.2 %all-to-all-start.3 = ((f32[32,8,192]{2,1,0:T(8,128)}), f32[32,8,192]{2,1,0:T(8,128)S(1)}, u32[]{:S(2)}, u32[]{:S(2)}) async-start(f32[32,8,192]{2,1,0:T(8,128)} %bitcast.70), calls=%async_computation.3 | async-start | bytes 524288 | tf_op jit(solution)/shard_map/all_to_all | solution.py:374
  77.0 7.4 %copy-start.14 = (f32[48,128]{1,0:T(8,128)S(1)}, f32[48,128]{1,0:T(8,128)}, u32[]{:S(2)}) copy-start(f32[48,128]{1,0:T(8,128)} %get-tuple-element.33) | copy-start | bytes 73732
  77.0 7.4 %copy-start.15 = (f32[48,128]{1,0:T(8,128)S(1)}, f32[48,128]{1,0:T(8,128)}, u32[]{:S(2)}) copy-start(f32[48,128]{1,0:T(8,128)} %get-tuple-element.37) | copy-start | bytes 73732
  77.0 7.4 %copy-start.16 = (f32[48,128]{1,0:T(8,128)S(1)}, f32[48,128]{1,0:T(8,128)}, u32[]{:S(2)}) copy-start(f32[48,128]{1,0:T(8,128)} %get-tuple-element.34) | copy-start | bytes 73732
  77.0 7.4 %copy-start.17 = (f32[48,128]{1,0:T(8,128)S(1)}, f32[48,128]{1,0:T(8,128)}, u32[]{:S(2)}) copy-start(f32[48,128]{1,0:T(8,128)} %get-tuple-element.38) | copy-start | bytes 73732
  77.0 7.4 %copy-start.18 = (f32[48,128]{1,0:T(8,128)S(1)}, f32[48,128]{1,0:T(8,128)}, u32[]{:S(2)}) copy-start(f32[48,128]{1,0:T(8,128)} %get-tuple-element.35) | copy-start | bytes 73732
  93.4 14.1 %all-to-all-start.4 = ((f32[32,8,192]{2,1,0:T(8,128)}), f32[32,8,192]{2,1,0:T(8,128)S(1)}, u32[]{:S(2)}, u32[]{:S(2)}) async-start(f32[32,8,192]{2,1,0:T(8,128)} %bitcast.71), calls=%async_computation.4 | async-start | bytes 524288 | tf_op jit(solution)/shard_map/all_to_all | solution.py:374
  97.2 19.8 %collective-permute-start.1 = (f32[3,1024]{1,0:T(4,128)S(1)}, f32[3,1024]{1,0:T(4,128)S(1)}, u32[]{:S(2)}, u32[]{:S(2)}) collective-permute-start(f32[3,1024]{1,0:T(4,128)S(1)} %bitcast.83), channel_id=1, source_target_pairs={{8,0},{16,8},{24,16},{9,1},{17,9},{25,17},{10,2},{18,10},{26,18},{... | collective-permute-start | bytes 36872 | tf_op jit(solution)/shard_map/ppermute | solution.py:320
  98.5 18.5 %collective-permute-start = (f32[3,1024]{1,0:T(4,128)S(1)}, f32[3,1024]{1,0:T(4,128)S(1)}, u32[]{:S(2)}, u32[]{:S(2)}) collective-permute-start(f32[3,1024]{1,0:T(4,128)S(1)} %bitcast.84), channel_id=1, source_target_pairs={{0,8},{8,16},{16,24},{1,9},{9,17},{17,25},{2,10},{10,18},{18,26},{... | collective-permute-start | bytes 36872 | tf_op jit(solution)/shard_map/ppermute | solution.py:320
  108.2 8.0 %copy-start.10 = (f32[3,4096]{1,0:T(4,128)S(1)}, f32[3,4096]{1,0:T(4,128)}, u32[]{:S(2)}) copy-start(f32[3,4096]{1,0:T(4,128)} %get-tuple-element.29) | copy-start | bytes 147460
  108.2 8.0 %copy-start.11 = (f32[3,4096]{1,0:T(4,128)S(1)}, f32[3,4096]{1,0:T(4,128)}, u32[]{:S(2)}) copy-start(f32[3,4096]{1,0:T(4,128)} %get-tuple-element.30) | copy-start | bytes 147460
  108.2 8.0 %copy-start.12 = (f32[3,4096]{1,0:T(4,128)S(1)}, f32[3,4096]{1,0:T(4,128)}, u32[]{:S(2)}) copy-start(f32[3,4096]{1,0:T(4,128)} %get-tuple-element.31) | copy-start | bytes 147460
  108.2 8.0 %copy-start.13 = (f32[3,4096]{1,0:T(4,128)S(1)}, f32[3,4096]{1,0:T(4,128)}, u32[]{:S(2)}) copy-start(f32[3,4096]{1,0:T(4,128)} %get-tuple-element.32) | copy-start | bytes 147460
  113.6 13.0 %all-to-all-start.5 = ((f32[32,8,192]{2,1,0:T(8,128)}), f32[32,8,192]{2,1,0:T(8,128)S(1)}, u32[]{:S(2)}, u32[]{:S(2)}) async-start(f32[32,8,192]{2,1,0:T(8,128)} %bitcast.69), calls=%async_computation.5 | async-start | bytes 524288 | tf_op jit(solution)/shard_map/all_to_all | solution.py:374
  (6 other events, 10.9 us)

commit v16 on v14

--- a/solution.py
+++ b/solution.py
@@ -187,30 +187,34 @@
     )(slab, q_state, element.reshape(1, -1), migration.reshape(1, -1))
 
 
-def first_kernel(pt_ref, ft_ref, vout_ref, send_ref):
+def first_kernel(pt_ref, dt_ref, g_ref, vout_ref, send_ref, ft_ref):
     own = vout_ref.shape[0]
-    rows = [
-        damping * jnp.sum(pt_ref[b] * ft_ref[:, b : b + 1], axis=0, keepdims=True)
-        for b in range(own)
-    ]
+    rows = []
+    for b in range(own):
+        column = jnp.sum(dt_ref[...] * g_ref[b : b + 1, :], axis=1, keepdims=True)
+        ft_ref[:, b : b + 1] = column
+        rows.append(damping * jnp.sum(pt_ref[b] * column, axis=0, keepdims=True))
     fresh = jnp.concatenate(rows, axis=0)
     vout_ref[...] = fresh
     for k in range(send_ref.shape[0] // own):
         send_ref[k * own : (k + 1) * own, :] = fresh
 
 
-def first_velocity(transposed, force_t, copies):
+def first_velocity(transposed, div_t, groups, copies):
     own, size = transposed.shape[0], transposed.shape[1]
     return pl.pallas_call(
         first_kernel,
         out_shape=(
             jax.ShapeDtypeStruct((own, size), jnp.float32),
             jax.ShapeDtypeStruct((copies * own, size), jnp.float32),
+            jax.ShapeDtypeStruct((size, own), jnp.float32),
         ),
         cost_estimate=pl.CostEstimate(
-            flops=2 * transposed.size, transcendentals=0, bytes_accessed=4 * transposed.size
-        ),
-    )(transposed, force_t)
+            flops=2 * (transposed.size + own * div_t.size),
+            transcendentals=0,
+            bytes_accessed=4 * (transposed.size + div_t.size),
+        ),
+    )(transposed, div_t, groups)
 
 
 def update_and_pack(q_state, increments, element, migration, table, capacity):
@@ -356,7 +360,6 @@
         .transpose(1, 0, 2)
         .reshape(own_blocks, BLOCK)
     )
-    force = jnp.dot(groups, div_map, precision=highest)
 
     def precondition(vector):
         return jnp.einsum("bij,bj->bi", preconditioner, vector, precision=highest)
@@ -365,8 +368,7 @@
     copies = n_slab * n_rad
     where_read = ((slab - 1) * slab_blocks + pattern).reshape(-1).astype(jnp.int32)
     transposed = jnp.swapaxes(preconditioner, 1, 2)
-    force_t = force.T
-    velocity, send = first_velocity(transposed, force_t, copies)
+    velocity, send, force_t = first_velocity(transposed, div_map.T, groups, copies)
     for sweep_index in range(1, ITERS):
         gathered = lax.all_to_all(send, ("slab", "rad"), 0, 0, tiled=True)
         velocity, send = sweep(

time: 133 us -> 133 us (level)
  local copies, waits for them, and re-layouts: 7.64 us -> 9.12 us
    unnamed x49 -> x50, local copies, waits for them, and re-layouts: 6.02 us -> 6.81 us
  transfers between devices with their start and end apart: 8 -> 8, of which waited for: 5 -> 5; matrix products, arithmetic and copies ran while one was open for 5% -> 6% of each run, Pallas kernels for 26% -> 26%
where the time goes in v16:
time: 133 us; the launch traced here: 132 us
  Pallas kernels  67.2 us (51%)
  starting transfers between devices  30.9 us (23%)
  waiting for transfers between devices  21 us (16%)
  local copies, waits for them, and re-layouts  9.12 us (7%)
  other arithmetic  3.24 us (2%)
    pallas_call x4, Pallas kernels, update_and_pack(): pl.pallas_call(functools.partial(update_kernel, groups16=groups16, slots1...  29.4 us
    pallas_call x5, Pallas kernels, sweep(): pl.pallas_call(sweep_kernel, out_shape=(jax.ShapeDtypeStruct(velocity.sha...  26.7 us
    all_to_all x5, waiting for transfers between devices, body(): gathered = lax.all_to_all(send, ('slab', 'rad'), 0, 0, tiled=True)  21 us
    all_to_all x5, starting transfers between devices, body(): gathered = lax.all_to_all(send, ('slab', 'rad'), 0, 0, tiled=True)  17.7 us
    pallas_call x1, Pallas kernels, stress_partials(): pl.pallas_call(functools.partial(stress_kernel, groups=groups, rows=rows)...  8.57 us
    all_to_all x1, starting transfers between devices, body(): received = lax.all_to_all(send, ('slab', 'rad'), 0, 0, tiled=True)  7.3 us
    unnamed x50, local copies, waits for them, and re-layouts  6.81 us
    ppermute x2, starting transfers between devices, passed_along(): return lax.ppermute(array, axis, pairs)  5.84 us
  transfers between devices with their start and end apart: 8, of which 5 were waited for; matrix products, arithmetic and copies ran while one was open for 6% of the time, Pallas kernels for 26%

profile of v16, /device:TPU:0, one launch (start us, length us, event | category | flops | bytes accessed | tf_op | source)
XLA Modules:
  0.0 132.4 jit_solution(14367184342338797079)
XLA Ops:
  0.7 8.6 %shard_map.133 = f32[32,12,128]{2,1,0:T(8,128)} custom-call(s32[1]{0:T(128)} %bitcast.12.slab_ref, f32[3,16384]{1,0:T(4,128)} %q_ref.9, s32[1,16384]{1,0:T(1,128)} %bitcast.82, s32[1,16384]{1,0:T(1,128)} %bitcast.71), custom_call_target="tpu_custom_call" | custom-call | flops 4026531840 | bytes 327680 | tf_op jit(solution)/shard_map/pallas_call | solution.py:178
  9.2 7.3 %all-to-all-start = ((f32[32,12,128]{2,1,0:T(8,128)}), f32[32,12,128]{2,1,0:T(8,128)S(1)}, u32[]{:S(2)}, u32[]{:S(2)}) async-start(f32[32,12,128]{2,1,0:T(8,128)} %shard_map.133), calls=%async_computation | async-start | bytes 524288 | tf_op jit(solution)/shard_map/all_to_all | solution.py:346
  16.7 1.8 %copy.44 = f32[8,192,192]{1,2,0:T(8,128)} copy(f32[8,192,192]{2,1,0:T(8,128)S(1)} %copy-done) | data formatting | bytes 2359296 | tf_op args[9]
  21.8 7.3 %shard_map.129 = (f32[3,4096]{1,0:T(4,128)}, f32[48,128]{1,0:T(8,128)}, f32[48,128]{1,0:T(8,128)}) custom-call(f32[3,16384]{1,0:T(4,128)} %q_ref.9, f32[3,16384]{1,0:T(4,128)} %inc_ref.7, s32[1,16384]{1,0:T(1,128)} %bitcast.83, s32[1,16384]{1,0:T(1,128)} %bitcast.72, bf16[160,384]{1,0:T(8,128)(2,1)} %pad_maximum_fusion.1.tab_ref, ...), custom_call_target="tpu_custom_call" | custom-call | flops 6442450944 | bytes 163840 | tf_op jit(solution)/shard_map/pallas_call | solution.py:242
  30.0 2.6 %shard_map.134 = (f32[8,192]{1,0:T(8,128)}, f32[256,192]{1,0:T(8,128)}, f32[192,8]{1,0:T(8,128)}) custom-call(f32[8,192,192]{2,1,0:T(8,128)} %bitcast.52, f32[192,192]{1,0:T(8,128)} %bitcast.63, f32[8,192]{1,0:T(8,128)} %reshape.96.g_ref), custom_call_target="tpu_custom_call" | custom-call | flops 1179648 | bytes 1327104 | tf_op jit(solution)/shard_map/pallas_call | solution.py:205
  32.5 5.8 %all-to-all-start.1 = ((f32[32,8,192]{2,1,0:T(8,128)}), f32[32,8,192]{2,1,0:T(8,128)S(1)}, u32[]{:S(2)}, u32[]{:S(2)}) async-start(f32[32,8,192]{2,1,0:T(8,128)} %bitcast.67), calls=%async_computation.1 | async-start | bytes 524288 | tf_op jit(solution)/shard_map/all_to_all | solution.py:373
  38.4 7.3 %shard_map.130 = (f32[3,4096]{1,0:T(4,128)}, f32[48,128]{1,0:T(8,128)}, f32[48,128]{1,0:T(8,128)}) custom-call(f32[3,16384]{1,0:T(4,128)} %q_ref.9, f32[3,16384]{1,0:T(4,128)} %inc_ref.7, s32[1,16384]{1,0:T(1,128)} %bitcast.84, s32[1,16384]{1,0:T(1,128)} %bitcast.73, bf16[160,384]{1,0:T(8,128)(2,1)} %pad_maximum_fusion.1.tab_ref, ...), custom_call_target="tpu_custom_call" | custom-call | flops 6442450944 | bytes 163840 | tf_op jit(solution)/shard_map/pallas_call | solution.py:242
  45.7 3.0 %all-to-all-done.1 = f32[32,8,192]{2,1,0:T(8,128)S(1)} async-done(((f32[32,8,192]{2,1,0:T(8,128)}), f32[32,8,192]{2,1,0:T(8,128)S(1)}, u32[]{:S(2)}, u32[]{:S(2)}) %all-to-all-start.1) | async-done | bytes 196640 | tf_op jit(solution)/shard_map/all_to_all | solution.py:373
  49.5 5.3 %shard_map.135 = (f32[8,192]{1,0:T(8,128)}, f32[256,192]{1,0:T(8,128)}) custom-call(s32[32]{0:T(128)} %reshape.94.idx_ref, f32[256,192]{1,0:T(8,128)} %bitcast.61, f32[8,4,192,192]{3,2,1,0:T(8,128)} %s_ref.9, f32[8,192,192]{2,1,0:T(8,128)} %bitcast.53, f32[192,8]{1,0:T(8,128)} %get-tuple-element.41.ft_ref, f32[8,192]{1,0:T(8,128)} %get-tuple-element.42.v_ref), custom_call_target="tpu_custom_call" | custom-call | flops 2949120 | bytes 6094848 | tf_op jit(solution)/shard_map/pallas_call | solution.py:303
  54.8 2.8 %all-to-all-start.2 = ((f32[32,8,192]{2,1,0:T(8,128)}), f32[32,8,192]{2,1,0:T(8,128)S(1)}, u32[]{:S(2)}, u32[]{:S(2)}) async-start(f32[32,8,192]{2,1,0:T(8,128)} %bitcast.68), calls=%async_computation.2 | async-start | bytes 524288 | tf_op jit(solution)/shard_map/all_to_all | solution.py:373
  57.6 7.3 %shard_map.131 = (f32[3,4096]{1,0:T(4,128)}, f32[48,128]{1,0:T(8,128)}, f32[48,128]{1,0:T(8,128)}) custom-call(f32[3,16384]{1,0:T(4,128)} %q_ref.9, f32[3,16384]{1,0:T(4,128)} %inc_ref.7, s32[1,16384]{1,0:T(1,128)} %bitcast.85, s32[1,16384]{1,0:T(1,128)} %bitcast.74, bf16[160,384]{1,0:T(8,128)(2,1)} %pad_maximum_fusion.1.tab_ref, ...), custom_call_target="tpu_custom_call" | custom-call | flops 6442450944 | bytes 163840 | tf_op jit(solution)/shard_map/pallas_call | solution.py:242
  64.9 3.0 %all-to-all-done.2 = f32[32,8,192]{2,1,0:T(8,128)S(1)} async-done(((f32[32,8,192]{2,1,0:T(8,128)}), f32[32,8,192]{2,1,0:T(8,128)S(1)}, u32[]{:S(2)}, u32[]{:S(2)}) %all-to-all-start.2) | async-done | bytes 196640 | tf_op jit(solution)/shard_map/all_to_all | solution.py:373
  68.7 5.3 %shard_map.136 = (f32[8,192]{1,0:T(8,128)}, f32[256,192]{1,0:T(8,128)}) custom-call(s32[32]{0:T(128)} %reshape.94.idx_ref, f32[256,192]{1,0:T(8,128)} %bitcast.62, f32[8,4,192,192]{3,2,1,0:T(8,128)} %s_ref.9, f32[8,192,192]{2,1,0:T(8,128)} %bitcast.54, f32[192,8]{1,0:T(8,128)} %get-tuple-element.41.ft_ref, f32[8,192]{1,0:T(8,128)} %get-tuple-element.44.v_ref), custom_call_target="tpu_custom_call" | custom-call | flops 2949120 | bytes 6094848 | tf_op jit(solution)/shard_map/pallas_call | solution.py:303
  74.0 2.8 %all-to-all-start.3 = ((f32[32,8,192]{2,1,0:T(8,128)}), f32[32,8,192]{2,1,0:T(8,128)S(1)}, u32[]{:S(2)}, u32[]{:S(2)}) async-start(f32[32,8,192]{2,1,0:T(8,128)} %bitcast.65), calls=%async_computation.3 | async-start | bytes 524288 | tf_op jit(solution)/shard_map/all_to_all | solution.py:373
  76.9 7.4 %shard_map.132 = (f32[3,4096]{1,0:T(4,128)}, f32[48,128]{1,0:T(8,128)}, f32[48,128]{1,0:T(8,128)}) custom-call(f32[3,16384]{1,0:T(4,128)} %q_ref.9, f32[3,16384]{1,0:T(4,128)} %inc_ref.7, s32[1,16384]{1,0:T(1,128)} %bitcast.86, s32[1,16384]{1,0:T(1,128)} %bitcast.75, bf16[160,384]{1,0:T(8,128)(2,1)} %pad_maximum_fusion.1.tab_ref, ...), custom_call_target="tpu_custom_call" | custom-call | flops 6442450944 | bytes 163840 | tf_op jit(solution)/shard_map/pallas_call | solution.py:242
  85.1 2.1 %all-to-all-done.3 = f32[32,8,192]{2,1,0:T(8,128)S(1)} async-done(((f32[32,8,192]{2,1,0:T(8,128)}), f32[32,8,192]{2,1,0:T(8,128)S(1)}, u32[]{:S(2)}, u32[]{:S(2)}) %all-to-all-start.3) | async-done | bytes 196640 | tf_op jit(solution)/shard_map/all_to_all | solution.py:373
  87.9 5.3 %shard_map.137 = (f32[8,192]{1,0:T(8,128)}, f32[256,192]{1,0:T(8,128)}) custom-call(s32[32]{0:T(128)} %reshape.94.idx_ref, f32[256,192]{1,0:T(8,128)} %bitcast.59, f32[8,4,192,192]{3,2,1,0:T(8,128)} %s_ref.9, f32[8,192,192]{2,1,0:T(8,128)} %bitcast.55, f32[192,8]{1,0:T(8,128)} %get-tuple-element.41.ft_ref, f32[8,192]{1,0:T(8,128)} %get-tuple-element.46.v_ref), custom_call_target="tpu_custom_call" | custom-call | flops 2949120 | bytes 6094848 | tf_op jit(solution)/shard_map/pallas_call | solution.py:303
  93.2 3.7 %all-to-all-start.4 = ((f32[32,8,192]{2,1,0:T(8,128)}), f32[32,8,192]{2,1,0:T(8,128)S(1)}, u32[]{:S(2)}, u32[]{:S(2)}) async-start(f32[32,8,192]{2,1,0:T(8,128)} %bitcast.66), calls=%async_computation.4 | async-start | bytes 524288 | tf_op jit(solution)/shard_map/all_to_all | solution.py:373
  98.3 4.5 %collective-permute-start = (f32[3,1024]{1,0:T(4,128)S(1)}, f32[3,1024]{1,0:T(4,128)S(1)}, u32[]{:S(2)}, u32[]{:S(2)}) collective-permute-start(f32[3,1024]{1,0:T(4,128)S(1)} %bitcast.79), channel_id=1, source_target_pairs={{0,8},{8,16},{16,24},{1,9},{9,17},{17,25},{2,10},{10,18},{18,26},{... | collective-permute-start | bytes 36872 | tf_op jit(solution)/shard_map/ppermute | solution.py:322
  102.9 4.5 %all-to-all-done.4 = f32[32,8,192]{2,1,0:T(8,128)S(1)} async-done(((f32[32,8,192]{2,1,0:T(8,128)}), f32[32,8,192]{2,1,0:T(8,128)S(1)}, u32[]{:S(2)}, u32[]{:S(2)}) %all-to-all-start.4) | async-done | bytes 196640 | tf_op jit(solution)/shard_map/all_to_all | solution.py:373
  108.1 5.4 %shard_map.138 = (f32[8,192]{1,0:T(8,128)}, f32[256,192]{1,0:T(8,128)}) custom-call(s32[32]{0:T(128)} %reshape.94.idx_ref, f32[256,192]{1,0:T(8,128)} %bitcast.60, f32[8,4,192,192]{3,2,1,0:T(8,128)} %s_ref.9, f32[8,192,192]{2,1,0:T(8,128)} %bitcast.56, f32[192,8]{1,0:T(8,128)} %get-tuple-element.41.ft_ref, f32[8,192]{1,0:T(8,128)} %get-tuple-element.48.v_ref), custom_call_target="tpu_custom_call" | custom-call | flops 2949120 | bytes 6094848 | tf_op jit(solution)/shard_map/pallas_call | solution.py:303
  113.4 2.6 %all-to-all-start.5 = ((f32[32,8,192]{2,1,0:T(8,128)}), f32[32,8,192]{2,1,0:T(8,128)S(1)}, u32[]{:S(2)}, u32[]{:S(2)}) async-start(f32[32,8,192]{2,1,0:T(8,128)} %bitcast.64), calls=%async_computation.5 | async-start | bytes 524288 | tf_op jit(solution)/shard_map/all_to_all | solution.py:373
  118.1 8.3 %all-to-all-done.5 = f32[32,8,192]{2,1,0:T(8,128)S(1)} async-done(((f32[32,8,192]{2,1,0:T(8,128)}), f32[32,8,192]{2,1,0:T(8,128)S(1)}, u32[]{:S(2)}, u32[]{:S(2)}) %all-to-all-start.5) | async-done | bytes 196640 | tf_op jit(solution)/shard_map/all_to_all | solution.py:373
  127.1 5.3 %shard_map.139 = (f32[8,192]{1,0:T(8,128)}, f32[256,192]{1,0:T(8,128)}) custom-call(s32[32]{0:T(128)} %reshape.94.idx_ref, f32[256,192]{1,0:T(8,128)} %bitcast.58, f32[8,4,192,192]{3,2,1,0:T(8,128)} %s_ref.9, f32[8,192,192]{2,1,0:T(8,128)} %bitcast.57, f32[192,8]{1,0:T(8,128)} %get-tuple-element.41.ft_ref, f32[8,192]{1,0:T(8,128)} %get-tuple-element.50.v_ref), custom_call_target="tpu_custom_call" | custom-call | flops 2949120 | bytes 6094848 | tf_op jit(solution)/shard_map/pallas_call | solution.py:303
  (77 shorter events, 11.9 us)
Async XLA Ops:
  0.6 15.9 %copy-start.8 = (s32[16384]{0:T(1024)S(1)}, s32[16384]{0:T(1024)}, u32[]{:S(2)}) copy-start(s32[16384]{0:T(1024)} %param.14) | copy-start | bytes 196612
  0.6 15.9 %copy-start.19 = (f32[384]{0:T(512)S(1)}, f32[384]{0:T(512)}, u32[]{:S(2)}) copy-start(f32[384]{0:T(512)} %param.15) | copy-start | bytes 4612
  0.7 16.0 %copy-start = (f32[8,192,192]{2,1,0:T(8,128)S(1)}, f32[8,192,192]{2,1,0:T(8,128)}, u32[]{:S(2)}) copy-start(f32[8,192,192]{2,1,0:T(8,128)} %param.19) | copy-start | bytes 3538948
  9.2 19.9 %all-to-all-start = ((f32[32,12,128]{2,1,0:T(8,128)}), f32[32,12,128]{2,1,0:T(8,128)S(1)}, u32[]{:S(2)}, u32[]{:S(2)}) async-start(f32[32,12,128]{2,1,0:T(8,128)} %shard_map.133), calls=%async_computation | async-start | bytes 524288 | tf_op jit(solution)/shard_map/all_to_all | solution.py:346
  16.7 1.8 %copy-start.6 = (f32[192,192]{1,0:T(8,128)S(1)}, f32[192,192]{1,0:T(8,128)}, u32[]{:S(2)}) copy-start(f32[192,192]{1,0:T(8,128)} %param.16) | copy-start | bytes 442372
  16.7 2.6 %copy-start.20 = (s32[8,4]{0,1:T(4,128)S(1)}, s32[8,4]{0,1:T(4,128)}, u32[]{:S(2)}) copy-start(s32[8,4]{0,1:T(4,128)} %param.18) | copy-start | bytes 388
  16.7 3.3 %copy-start.7 = (f32[5,3072]{1,0:T(8,128)S(1)}, f32[5,3072]{1,0:T(8,128)}, u32[]{:S(2)}) copy-start(f32[5,3072]{1,0:T(8,128)} %param.12) | copy-start | bytes 184324
  32.5 16.2 %all-to-all-start.1 = ((f32[32,8,192]{2,1,0:T(8,128)}), f32[32,8,192]{2,1,0:T(8,128)S(1)}, u32[]{:S(2)}, u32[]{:S(2)}) async-start(f32[32,8,192]{2,1,0:T(8,128)} %bitcast.67), calls=%async_computation.1 | async-start | bytes 524288 | tf_op jit(solution)/shard_map/all_to_all | solution.py:373
  54.8 13.2 %all-to-all-start.2 = ((f32[32,8,192]{2,1,0:T(8,128)}), f32[32,8,192]{2,1,0:T(8,128)S(1)}, u32[]{:S(2)}, u32[]{:S(2)}) async-start(f32[32,8,192]{2,1,0:T(8,128)} %bitcast.68), calls=%async_computation.2 | async-start | bytes 524288 | tf_op jit(solution)/shard_map/all_to_all | solution.py:373
  74.0 13.2 %all-to-all-start.3 = ((f32[32,8,192]{2,1,0:T(8,128)}), f32[32,8,192]{2,1,0:T(8,128)S(1)}, u32[]{:S(2)}, u32[]{:S(2)}) async-start(f32[32,8,192]{2,1,0:T(8,128)} %bitcast.65), calls=%async_computation.3 | async-start | bytes 524288 | tf_op jit(solution)/shard_map/all_to_all | solution.py:373
  76.8 7.4 %copy-start.13 = (f32[48,128]{1,0:T(8,128)S(1)}, f32[48,128]{1,0:T(8,128)}, u32[]{:S(2)}) copy-start(f32[48,128]{1,0:T(8,128)} %get-tuple-element.32) | copy-start | bytes 73732
  76.8 7.4 %copy-start.14 = (f32[48,128]{1,0:T(8,128)S(1)}, f32[48,128]{1,0:T(8,128)}, u32[]{:S(2)}) copy-start(f32[48,128]{1,0:T(8,128)} %get-tuple-element.36) | copy-start | bytes 73732
  76.8 7.4 %copy-start.15 = (f32[48,128]{1,0:T(8,128)S(1)}, f32[48,128]{1,0:T(8,128)}, u32[]{:S(2)}) copy-start(f32[48,128]{1,0:T(8,128)} %get-tuple-element.33) | copy-start | bytes 73732
  76.8 7.4 %copy-start.16 = (f32[48,128]{1,0:T(8,128)S(1)}, f32[48,128]{1,0:T(8,128)}, u32[]{:S(2)}) copy-start(f32[48,128]{1,0:T(8,128)} %get-tuple-element.37) | copy-start | bytes 73732
  76.9 7.4 %copy-start.17 = (f32[48,128]{1,0:T(8,128)S(1)}, f32[48,128]{1,0:T(8,128)}, u32[]{:S(2)}) copy-start(f32[48,128]{1,0:T(8,128)} %get-tuple-element.34) | copy-start | bytes 73732
  76.9 7.4 %copy-start.18 = (f32[48,128]{1,0:T(8,128)S(1)}, f32[48,128]{1,0:T(8,128)}, u32[]{:S(2)}) copy-start(f32[48,128]{1,0:T(8,128)} %get-tuple-element.38) | copy-start | bytes 73732
  93.2 14.1 %all-to-all-start.4 = ((f32[32,8,192]{2,1,0:T(8,128)}), f32[32,8,192]{2,1,0:T(8,128)S(1)}, u32[]{:S(2)}, u32[]{:S(2)}) async-start(f32[32,8,192]{2,1,0:T(8,128)} %bitcast.66), calls=%async_computation.4 | async-start | bytes 524288 | tf_op jit(solution)/shard_map/all_to_all | solution.py:373
  97.0 19.8 %collective-permute-start.1 = (f32[3,1024]{1,0:T(4,128)S(1)}, f32[3,1024]{1,0:T(4,128)S(1)}, u32[]{:S(2)}, u32[]{:S(2)}) collective-permute-start(f32[3,1024]{1,0:T(4,128)S(1)} %bitcast.78), channel_id=1, source_target_pairs={{8,0},{16,8},{24,16},{9,1},{17,9},{25,17},{10,2},{18,10},{26,18},{... | collective-permute-start | bytes 36872 | tf_op jit(solution)/shard_map/ppermute | solution.py:322
  98.3 18.5 %collective-permute-start = (f32[3,1024]{1,0:T(4,128)S(1)}, f32[3,1024]{1,0:T(4,128)S(1)}, u32[]{:S(2)}, u32[]{:S(2)}) collective-permute-start(f32[3,1024]{1,0:T(4,128)S(1)} %bitcast.79), channel_id=1, source_target_pairs={{0,8},{8,16},{16,24},{1,9},{9,17},{17,25},{2,10},{10,18},{18,26},{... | collective-permute-start | bytes 36872 | tf_op jit(solution)/shard_map/ppermute | solution.py:322
  108.0 8.0 %copy-start.9 = (f32[3,4096]{1,0:T(4,128)S(1)}, f32[3,4096]{1,0:T(4,128)}, u32[]{:S(2)}) copy-start(f32[3,4096]{1,0:T(4,128)} %get-tuple-element.28) | copy-start | bytes 147460
  108.1 8.0 %copy-start.10 = (f32[3,4096]{1,0:T(4,128)S(1)}, f32[3,4096]{1,0:T(4,128)}, u32[]{:S(2)}) copy-start(f32[3,4096]{1,0:T(4,128)} %get-tuple-element.29) | copy-start | bytes 147460
  108.1 8.0 %copy-start.11 = (f32[3,4096]{1,0:T(4,128)S(1)}, f32[3,4096]{1,0:T(4,128)}, u32[]{:S(2)}) copy-start(f32[3,4096]{1,0:T(4,128)} %get-tuple-element.30) | copy-start | bytes 147460
  108.1 8.0 %copy-start.12 = (f32[3,4096]{1,0:T(4,128)S(1)}, f32[3,4096]{1,0:T(4,128)}, u32[]{:S(2)}) copy-start(f32[3,4096]{1,0:T(4,128)} %get-tuple-element.31) | copy-start | bytes 147460
  113.4 13.0 %all-to-all-start.5 = ((f32[32,8,192]{2,1,0:T(8,128)}), f32[32,8,192]{2,1,0:T(8,128)S(1)}, u32[]{:S(2)}, u32[]{:S(2)}) async-start(f32[32,8,192]{2,1,0:T(8,128)} %bitcast.64), calls=%async_computation.5 | async-start | bytes 524288 | tf_op jit(solution)/shard_map/all_to_all | solution.py:373
  (5 other events, 3.5 us)

commit v17 on v10

--- a/solution.py
+++ b/solution.py
@@ -10,8 +10,8 @@
 BLOCK = 192
 ITERS = 6
 CHUNK = 512
-STRESS_CHUNK = 1024
-UPDATE_PARTS = 4
+STRESS_CHUNK = 4096
+UPDATE_PARTS = 8
 
 extensibility = 50.0
 time_step = 0.01
@@ -66,11 +66,13 @@
         kind = jnp.where(move == 0, 1, jnp.where(move == 1, 2, 0))
         key = kind * groups + (element >> 7)
         low = (low_iota == (element & 127)).astype(jnp.bfloat16)
-        low = jnp.concatenate([low, low, low], axis=1)
+        low = jnp.concatenate([low, low], axis=1)
         mask = row_iota == key
         spread = jnp.concatenate(
             [
-                jnp.concatenate([jnp.where(mask, piece, zero) for piece in bf16_pieces(term)], axis=1)
+                jnp.concatenate(
+                    [jnp.where(mask, piece, zero) for piece in bf16_pieces(term)[:2]], axis=1
+                )
                 for term in terms
             ],
             axis=0,
@@ -361,16 +363,19 @@
     where_read = ((slab - 1) * slab_blocks + pattern).reshape(-1).astype(jnp.int32)
     transposed = jnp.swapaxes(preconditioner, 1, 2)
     force_t = force.T
+    q_parts, upward, downward = [], 0.0, 0.0
+    q_part, upward, downward = update_part(0, prepared, element, q_state, increments, element, migration)
+    q_parts.append(q_part)
     velocity, send = first_velocity(transposed, force_t, copies)
-    q_parts, upward, downward = [], 0.0, 0.0
     for sweep_index in range(1, ITERS):
-        if len(q_parts) < UPDATE_PARTS:
-            q_part, up_part, down_part = update_part(
-                len(q_parts), prepared, velocity, q_state, increments, element, migration
-            )
-            q_parts.append(q_part)
-            upward = upward + up_part
-            downward = downward + down_part
+        for repeat in range(2):
+            if len(q_parts) < UPDATE_PARTS:
+                q_part, up_part, down_part = update_part(
+                    len(q_parts), prepared, velocity, q_state, increments, element, migration
+                )
+                q_parts.append(q_part)
+                upward = upward + up_part
+                downward = downward + down_part
         gathered = lax.all_to_all(send, ("slab", "rad"), 0, 0, tiled=True)
         velocity, send = sweep(
             where_read, gathered, stiffness, transposed, force_t, velocity, copies

time: 139 us -> 140 us (level)
  waiting for transfers between devices: 23.4 us -> 10.9 us
  starting transfers between devices: 30.6 us -> 37.7 us
  local copies, waits for them, and re-layouts: 7.72 us -> 10.8 us
  Pallas kernels: 71.4 us -> 74.2 us
    all_to_all x5, waiting for transfers between devices: 17.4 us -> 5.92 us  [body(): gathered = lax.all_to_all(send, ('slab', 'rad'), 0, 0, tiled=True)]
    pallas_call x4 -> x8, Pallas kernels: 29.4 us -> 36.6 us  [update_part(): pl.pallas_call(functools.partial(update_kernel, groups16=groups16, slots1...]
    all_to_all x5, starting transfers between devices: 18.3 us -> 25.4 us  [body(): gathered = lax.all_to_all(send, ('slab', 'rad'), 0, 0, tiled=True)]
    all_to_all x1, waiting for transfers between devices: 5.94 us -> 0.67 us  [body(): received = lax.all_to_all(send, ('slab', 'rad'), 0, 0, tiled=True)]
    pallas_call x1, Pallas kernels: 12.9 us -> 8.58 us  [stress_partials(): pl.pallas_call(functools.partial(stress_kernel, groups=groups, rows=rows)...]
    ppermute x2, waiting for transfers between devices: 0.01 us -> 4.34 us  [passed_along(): return lax.ppermute(array, axis, pairs)]
    unnamed x49 -> x74, local copies, waits for them, and re-layouts: 6.02 us -> 9.16 us
  transfers between devices with their start and end apart: 8 -> 8, of which waited for: 5 -> 6; matrix products, arithmetic and copies ran while one was open for 5% -> 7% of each run, Pallas kernels for 25% -> 30%
where the time goes in v17:
time: 140 us; the launch traced here: 139 us
  Pallas kernels  74.2 us (53%)
  starting transfers between devices  37.7 us (27%)
  waiting for transfers between devices  10.9 us (8%)
  local copies, waits for them, and re-layouts  10.8 us (8%)
  other arithmetic  2.46 us (2%)
    pallas_call x8, Pallas kernels, update_part(): pl.pallas_call(functools.partial(update_kernel, groups16=groups16, slots1...  36.6 us
    pallas_call x5, Pallas kernels, sweep(): pl.pallas_call(sweep_kernel, out_shape=(jax.ShapeDtypeStruct(velocity.sha...  26.6 us
    all_to_all x5, starting transfers between devices, body(): gathered = lax.all_to_all(send, ('slab', 'rad'), 0, 0, tiled=True)  25.4 us
    unnamed x74, local copies, waits for them, and re-layouts  9.16 us
    pallas_call x1, Pallas kernels, stress_partials(): pl.pallas_call(functools.partial(stress_kernel, groups=groups, rows=rows)...  8.58 us
    all_to_all x1, starting transfers between devices, body(): received = lax.all_to_all(send, ('slab', 'rad'), 0, 0, tiled=True)  7.3 us
    all_to_all x5, waiting for transfers between devices, body(): gathered = lax.all_to_all(send, ('slab', 'rad'), 0, 0, tiled=True)  5.92 us
    ppermute x2, starting transfers between devices, passed_along(): return lax.ppermute(array, axis, pairs)  4.97 us
  transfers between devices with their start and end apart: 8, of which 6 were waited for; matrix products, arithmetic and copies ran while one was open for 7% of the time, Pallas kernels for 30%

profile of v17, /device:TPU:0, one launch (start us, length us, event | category | flops | bytes accessed | tf_op | source)
XLA Modules:
  0.0 138.5 jit_solution(14925728139059313946)
XLA Ops:
  0.7 8.6 %shard_map.130 = f32[32,12,128]{2,1,0:T(8,128)} custom-call(s32[1]{0:T(128)} %bitcast.7.slab_ref, f32[3,16384]{1,0:T(4,128)} %q_ref.17, s32[1,16384]{1,0:T(1,128)} %bitcast.96, s32[1,16384]{1,0:T(1,128)} %bitcast.81), custom_call_target="tpu_custom_call" | custom-call | flops 4026531840 | bytes 327680 | tf_op jit(solution)/shard_map/pallas_call | solution.py:178
  9.3 7.3 %all-to-all-start = ((f32[32,12,128]{2,1,0:T(8,128)}), f32[32,12,128]{2,1,0:T(8,128)S(1)}, u32[]{:S(2)}, u32[]{:S(2)}) async-start(f32[32,12,128]{2,1,0:T(8,128)} %shard_map.130), calls=%async_computation | async-start | bytes 524288 | tf_op jit(solution)/shard_map/all_to_all | solution.py:344
  21.0 4.6 %shard_map.129 = (f32[3,2048]{1,0:T(4,128)}, f32[48,128]{1,0:T(8,128)}, f32[48,128]{1,0:T(8,128)}) custom-call(f32[3,16384]{1,0:T(4,128)} %q_ref.17, f32[3,16384]{1,0:T(4,128)} %inc_ref.15, s32[1,16384]{1,0:T(1,128)} %bitcast.97, s32[1,16384]{1,0:T(1,128)} %bitcast.82, bf16[160,384]{1,0:T(8,128)(2,1)} %pad_maximum_fusion.tab_ref, ...), custom_call_target="tpu_custom_call" | custom-call | flops 3221225472 | bytes 81920 | tf_op jit(solution)/shard_map/pallas_call | solution.py:241
  28.4 2.4 %shard_map.131 = (f32[8,192]{1,0:T(8,128)}, f32[256,192]{1,0:T(8,128)}) custom-call(f32[8,192,192]{2,1,0:T(8,128)} %bitcast.63, f32[192,8]{1,0:T(8,128)} %convolution_bitcast_fusion.ft_ref), custom_call_target="tpu_custom_call" | custom-call | flops 589824 | bytes 1179648 | tf_op jit(solution)/shard_map/pallas_call | solution.py:204
  30.8 5.2 %all-to-all-start.1 = ((f32[32,8,192]{2,1,0:T(8,128)}), f32[32,8,192]{2,1,0:T(8,128)S(1)}, u32[]{:S(2)}, u32[]{:S(2)}) async-start(f32[32,8,192]{2,1,0:T(8,128)} %bitcast.76), calls=%async_computation.1 | async-start | bytes 524288 | tf_op jit(solution)/shard_map/all_to_all | solution.py:379
  36.0 4.6 %shard_map.132 = (f32[3,2048]{1,0:T(4,128)}, f32[48,128]{1,0:T(8,128)}, f32[48,128]{1,0:T(8,128)}) custom-call(f32[3,16384]{1,0:T(4,128)} %q_ref.17, f32[3,16384]{1,0:T(4,128)} %inc_ref.15, s32[1,16384]{1,0:T(1,128)} %bitcast.98, s32[1,16384]{1,0:T(1,128)} %bitcast.83, bf16[160,384]{1,0:T(8,128)(2,1)} %pad_maximum_fusion.tab_ref, ...), custom_call_target="tpu_custom_call" | custom-call | flops 3221225472 | bytes 81920 | tf_op jit(solution)/shard_map/pallas_call | solution.py:241
  40.6 4.6 %shard_map.133 = (f32[3,2048]{1,0:T(4,128)}, f32[48,128]{1,0:T(8,128)}, f32[48,128]{1,0:T(8,128)}) custom-call(f32[3,16384]{1,0:T(4,128)} %q_ref.17, f32[3,16384]{1,0:T(4,128)} %inc_ref.15, s32[1,16384]{1,0:T(1,128)} %bitcast.99, s32[1,16384]{1,0:T(1,128)} %bitcast.84, bf16[160,384]{1,0:T(8,128)(2,1)} %pad_maximum_fusion.tab_ref, ...), custom_call_target="tpu_custom_call" | custom-call | flops 3221225472 | bytes 81920 | tf_op jit(solution)/shard_map/pallas_call | solution.py:241
  47.2 5.3 %shard_map.134 = (f32[8,192]{1,0:T(8,128)}, f32[256,192]{1,0:T(8,128)}) custom-call(s32[32]{0:T(128)} %reshape.108.idx_ref, f32[256,192]{1,0:T(8,128)} %bitcast.71, f32[8,4,192,192]{3,2,1,0:T(8,128)} %s_ref.9, f32[8,192,192]{2,1,0:T(8,128)} %bitcast.64, f32[192,8]{1,0:T(8,128)} %convolution_bitcast_fusion.ft_ref, f32[8,192]{1,0:T(8,128)} %get-tuple-element.40.after_ref.v_ref), custom_call_target="tpu_custom_call" | custom-call | flops 2949120 | bytes 6094848 | tf_op jit(solution)/shard_map/pallas_call | solution.py:301
  52.6 5.8 %all-to-all-start.2 = ((f32[32,8,192]{2,1,0:T(8,128)}), f32[32,8,192]{2,1,0:T(8,128)S(1)}, u32[]{:S(2)}, u32[]{:S(2)}) async-start(f32[32,8,192]{2,1,0:T(8,128)} %bitcast.77), calls=%async_computation.2 | async-start | bytes 524288 | tf_op jit(solution)/shard_map/all_to_all | solution.py:379
  58.4 4.6 %shard_map.136 = (f32[3,2048]{1,0:T(4,128)}, f32[48,128]{1,0:T(8,128)}, f32[48,128]{1,0:T(8,128)}) custom-call(f32[3,16384]{1,0:T(4,128)} %q_ref.17, f32[3,16384]{1,0:T(4,128)} %inc_ref.15, s32[1,16384]{1,0:T(1,128)} %bitcast.100, s32[1,16384]{1,0:T(1,128)} %bitcast.85, bf16[160,384]{1,0:T(8,128)(2,1)} %pad_maximum_fusion.tab_ref, ...), custom_call_target="tpu_custom_call" | custom-call | flops 3221225472 | bytes 81920 | tf_op jit(solution)/shard_map/pallas_call | solution.py:241
  63.0 4.6 %shard_map.135 = (f32[3,2048]{1,0:T(4,128)}, f32[48,128]{1,0:T(8,128)}, f32[48,128]{1,0:T(8,128)}) custom-call(f32[3,16384]{1,0:T(4,128)} %q_ref.17, f32[3,16384]{1,0:T(4,128)} %inc_ref.15, s32[1,16384]{1,0:T(1,128)} %bitcast.101, s32[1,16384]{1,0:T(1,128)} %bitcast.86, bf16[160,384]{1,0:T(8,128)(2,1)} %pad_maximum_fusion.tab_ref, ...), custom_call_target="tpu_custom_call" | custom-call | flops 3221225472 | bytes 81920 | tf_op jit(solution)/shard_map/pallas_call | solution.py:241
  69.5 5.3 %shard_map.137 = (f32[8,192]{1,0:T(8,128)}, f32[256,192]{1,0:T(8,128)}) custom-call(s32[32]{0:T(128)} %reshape.108.idx_ref, f32[256,192]{1,0:T(8,128)} %bitcast.72, f32[8,4,192,192]{3,2,1,0:T(8,128)} %s_ref.9, f32[8,192,192]{2,1,0:T(8,128)} %bitcast.65, f32[192,8]{1,0:T(8,128)} %convolution_bitcast_fusion.ft_ref, f32[8,192]{1,0:T(8,128)} %get-tuple-element.44.after_ref.v_ref), custom_call_target="tpu_custom_call" | custom-call | flops 2949120 | bytes 6094848 | tf_op jit(solution)/shard_map/pallas_call | solution.py:301
  74.8 5.4 %all-to-all-start.3 = ((f32[32,8,192]{2,1,0:T(8,128)}), f32[32,8,192]{2,1,0:T(8,128)S(1)}, u32[]{:S(2)}, u32[]{:S(2)}) async-start(f32[32,8,192]{2,1,0:T(8,128)} %bitcast.78), calls=%async_computation.3 | async-start | bytes 524288 | tf_op jit(solution)/shard_map/all_to_all | solution.py:379
  80.2 4.6 %shard_map.139 = (f32[3,2048]{1,0:T(4,128)}, f32[48,128]{1,0:T(8,128)}, f32[48,128]{1,0:T(8,128)}) custom-call(f32[3,16384]{1,0:T(4,128)} %q_ref.17, f32[3,16384]{1,0:T(4,128)} %inc_ref.15, s32[1,16384]{1,0:T(1,128)} %bitcast.102, s32[1,16384]{1,0:T(1,128)} %bitcast.87, bf16[160,384]{1,0:T(8,128)(2,1)} %pad_maximum_fusion.tab_ref, ...), custom_call_target="tpu_custom_call" | custom-call | flops 3221225472 | bytes 81920 | tf_op jit(solution)/shard_map/pallas_call | solution.py:241
  84.8 4.6 %shard_map.138 = (f32[3,2048]{1,0:T(4,128)}, f32[48,128]{1,0:T(8,128)}, f32[48,128]{1,0:T(8,128)}) custom-call(f32[3,16384]{1,0:T(4,128)} %q_ref.17, f32[3,16384]{1,0:T(4,128)} %inc_ref.15, s32[1,16384]{1,0:T(1,128)} %bitcast.103, s32[1,16384]{1,0:T(1,128)} %bitcast.88, bf16[160,384]{1,0:T(8,128)(2,1)} %pad_maximum_fusion.tab_ref, ...), custom_call_target="tpu_custom_call" | custom-call | flops 3221225472 | bytes 81920 | tf_op jit(solution)/shard_map/pallas_call | solution.py:241
  91.3 5.3 %shard_map.140 = (f32[8,192]{1,0:T(8,128)}, f32[256,192]{1,0:T(8,128)}) custom-call(s32[32]{0:T(128)} %reshape.108.idx_ref, f32[256,192]{1,0:T(8,128)} %bitcast.73, f32[8,4,192,192]{3,2,1,0:T(8,128)} %s_ref.9, f32[8,192,192]{2,1,0:T(8,128)} %bitcast.66, f32[192,8]{1,0:T(8,128)} %convolution_bitcast_fusion.ft_ref, f32[8,192]{1,0:T(8,128)} %get-tuple-element.48.after_ref.v_ref), custom_call_target="tpu_custom_call" | custom-call | flops 2949120 | bytes 6094848 | tf_op jit(solution)/shard_map/pallas_call | solution.py:301
  96.6 5.4 %all-to-all-start.4 = ((f32[32,8,192]{2,1,0:T(8,128)}), f32[32,8,192]{2,1,0:T(8,128)S(1)}, u32[]{:S(2)}, u32[]{:S(2)}) async-start(f32[32,8,192]{2,1,0:T(8,128)} %bitcast.74), calls=%async_computation.4 | async-start | bytes 524288 | tf_op jit(solution)/shard_map/all_to_all | solution.py:379
  102.2 4.6 %shard_map.141 = (f32[3,2048]{1,0:T(4,128)}, f32[48,128]{1,0:T(8,128)}, f32[48,128]{1,0:T(8,128)}) custom-call(f32[3,16384]{1,0:T(4,128)} %q_ref.17, f32[3,16384]{1,0:T(4,128)} %inc_ref.15, s32[1,16384]{1,0:T(1,128)} %bitcast.104, s32[1,16384]{1,0:T(1,128)} %bitcast.89, bf16[160,384]{1,0:T(8,128)(2,1)} %pad_maximum_fusion.tab_ref, ...), custom_call_target="tpu_custom_call" | custom-call | flops 3221225472 | bytes 81920 | tf_op jit(solution)/shard_map/pallas_call | solution.py:241
  107.7 3.7 %collective-permute-start = (f32[3,1024]{1,0:T(4,128)S(1)}, f32[3,1024]{1,0:T(4,128)S(1)}, u32[]{:S(2)}, u32[]{:S(2)}) collective-permute-start(f32[3,1024]{1,0:T(4,128)S(1)} %bitcast.92), channel_id=1, source_target_pairs={{0,8},{8,16},{16,24},{1,9},{9,17},{17,25},{2,10},{10,18},{18,26},{... | collective-permute-start | bytes 36872 | tf_op jit(solution)/shard_map/ppermute | solution.py:320
  113.1 5.3 %shard_map.142 = (f32[8,192]{1,0:T(8,128)}, f32[256,192]{1,0:T(8,128)}) custom-call(s32[32]{0:T(128)} %reshape.108.idx_ref, f32[256,192]{1,0:T(8,128)} %bitcast.69, f32[8,4,192,192]{3,2,1,0:T(8,128)} %s_ref.9, f32[8,192,192]{2,1,0:T(8,128)} %bitcast.67, f32[192,8]{1,0:T(8,128)} %convolution_bitcast_fusion.ft_ref, f32[8,192]{1,0:T(8,128)} %get-tuple-element.52.after_ref.v_ref), custom_call_target="tpu_custom_call" | custom-call | flops 2949120 | bytes 6094848 | tf_op jit(solution)/shard_map/pallas_call | solution.py:301
  118.5 3.6 %all-to-all-start.5 = ((f32[32,8,192]{2,1,0:T(8,128)}), f32[32,8,192]{2,1,0:T(8,128)S(1)}, u32[]{:S(2)}, u32[]{:S(2)}) async-start(f32[32,8,192]{2,1,0:T(8,128)} %bitcast.75), calls=%async_computation.5 | async-start | bytes 524288 | tf_op jit(solution)/shard_map/all_to_all | solution.py:379
  123.5 4.3 %collective-permute-done.1 = f32[3,1024]{1,0:T(4,128)S(1)} collective-permute-done((f32[3,1024]{1,0:T(4,128)S(1)}, f32[3,1024]{1,0:T(4,128)S(1)}, u32[]{:S(2)}, u32[]{:S(2)}) %collective-permute-start.1) | collective-permute-done | bytes 12320 | tf_op jit(solution)/shard_map/ppermute | solution.py:320
  128.5 4.0 %all-to-all-done.5 = f32[32,8,192]{2,1,0:T(8,128)S(1)} async-done(((f32[32,8,192]{2,1,0:T(8,128)}), f32[32,8,192]{2,1,0:T(8,128)S(1)}, u32[]{:S(2)}, u32[]{:S(2)}) %all-to-all-start.5) | async-done | bytes 196640 | tf_op jit(solution)/shard_map/all_to_all | solution.py:379
  133.2 5.3 %shard_map.143 = (f32[8,192]{1,0:T(8,128)}, f32[256,192]{1,0:T(8,128)}) custom-call(s32[32]{0:T(128)} %reshape.108.idx_ref, f32[256,192]{1,0:T(8,128)} %bitcast.70, f32[8,4,192,192]{3,2,1,0:T(8,128)} %s_ref.9, f32[8,192,192]{2,1,0:T(8,128)} %bitcast.68, f32[192,8]{1,0:T(8,128)} %convolution_bitcast_fusion.ft_ref, f32[8,192]{1,0:T(8,128)} %get-tuple-element.72.v_ref), custom_call_target="tpu_custom_call" | custom-call | flops 2949120 | bytes 6094848 | tf_op jit(solution)/shard_map/pallas_call | solution.py:301
  (106 shorter events, 18.4 us)
Async XLA Ops:
  0.6 26.6 %copy-start = (f32[192,192]{1,0:T(8,128)S(1)}, f32[192,192]{1,0:T(8,128)}, u32[]{:S(2)}) copy-start(f32[192,192]{1,0:T(8,128)} %param.16) | copy-start | bytes 442372
  0.7 15.9 %copy-start.8 = (s32[16384]{0:T(1024)S(1)}, s32[16384]{0:T(1024)}, u32[]{:S(2)}) copy-start(s32[16384]{0:T(1024)} %param.14) | copy-start | bytes 196612
  0.7 15.9 %copy-start.27 = (f32[384]{0:T(512)S(1)}, f32[384]{0:T(512)}, u32[]{:S(2)}) copy-start(f32[384]{0:T(512)} %param.15) | copy-start | bytes 4612
  0.7 16.0 %copy-start.1 = (f32[8,192,192]{2,1,0:T(8,128)S(1)}, f32[8,192,192]{2,1,0:T(8,128)}, u32[]{:S(2)}) copy-start(f32[8,192,192]{2,1,0:T(8,128)} %param.19) | copy-start | bytes 3538948
  9.3 17.7 %all-to-all-start = ((f32[32,12,128]{2,1,0:T(8,128)}), f32[32,12,128]{2,1,0:T(8,128)S(1)}, u32[]{:S(2)}, u32[]{:S(2)}) async-start(f32[32,12,128]{2,1,0:T(8,128)} %shard_map.130), calls=%async_computation | async-start | bytes 524288 | tf_op jit(solution)/shard_map/all_to_all | solution.py:344
  30.8 15.7 %all-to-all-start.1 = ((f32[32,8,192]{2,1,0:T(8,128)}), f32[32,8,192]{2,1,0:T(8,128)S(1)}, u32[]{:S(2)}, u32[]{:S(2)}) async-start(f32[32,8,192]{2,1,0:T(8,128)} %bitcast.76), calls=%async_computation.1 | async-start | bytes 524288 | tf_op jit(solution)/shard_map/all_to_all | solution.py:379
  52.6 16.2 %all-to-all-start.2 = ((f32[32,8,192]{2,1,0:T(8,128)}), f32[32,8,192]{2,1,0:T(8,128)S(1)}, u32[]{:S(2)}, u32[]{:S(2)}) async-start(f32[32,8,192]{2,1,0:T(8,128)} %bitcast.77), calls=%async_computation.2 | async-start | bytes 524288 | tf_op jit(solution)/shard_map/all_to_all | solution.py:379
  63.0 5.3 %copy-start.10 = (f32[3,2048]{1,0:T(4,128)S(1)}, f32[3,2048]{1,0:T(4,128)}, u32[]{:S(2)}) copy-start(f32[3,2048]{1,0:T(4,128)} %get-tuple-element.46) | copy-start | bytes 73732
  74.8 15.8 %all-to-all-start.3 = ((f32[32,8,192]{2,1,0:T(8,128)}), f32[32,8,192]{2,1,0:T(8,128)S(1)}, u32[]{:S(2)}, u32[]{:S(2)}) async-start(f32[32,8,192]{2,1,0:T(8,128)} %bitcast.78), calls=%async_computation.3 | async-start | bytes 524288 | tf_op jit(solution)/shard_map/all_to_all | solution.py:379
  84.8 5.3 %copy-start.11 = (f32[3,2048]{1,0:T(4,128)S(1)}, f32[3,2048]{1,0:T(4,128)}, u32[]{:S(2)}) copy-start(f32[3,2048]{1,0:T(4,128)} %get-tuple-element.50) | copy-start | bytes 73732
  96.6 15.8 %all-to-all-start.4 = ((f32[32,8,192]{2,1,0:T(8,128)}), f32[32,8,192]{2,1,0:T(8,128)S(1)}, u32[]{:S(2)}, u32[]{:S(2)}) async-start(f32[32,8,192]{2,1,0:T(8,128)} %bitcast.74), calls=%async_computation.4 | async-start | bytes 524288 | tf_op jit(solution)/shard_map/all_to_all | solution.py:379
  102.0 4.8 %copy-start.13 = (f32[48,128]{1,0:T(8,128)S(1)}, f32[48,128]{1,0:T(8,128)}, u32[]{:S(2)}) copy-start(f32[48,128]{1,0:T(8,128)} %get-tuple-element.54) | copy-start | bytes 73732
  102.0 4.8 %copy-start.14 = (f32[48,128]{1,0:T(8,128)S(1)}, f32[48,128]{1,0:T(8,128)}, u32[]{:S(2)}) copy-start(f32[48,128]{1,0:T(8,128)} %get-tuple-element.62) | copy-start | bytes 73732
  102.1 4.8 %copy-start.15 = (f32[48,128]{1,0:T(8,128)S(1)}, f32[48,128]{1,0:T(8,128)}, u32[]{:S(2)}) copy-start(f32[48,128]{1,0:T(8,128)} %get-tuple-element.55) | copy-start | bytes 73732
  102.1 4.7 %copy-start.16 = (f32[48,128]{1,0:T(8,128)S(1)}, f32[48,128]{1,0:T(8,128)}, u32[]{:S(2)}) copy-start(f32[48,128]{1,0:T(8,128)} %get-tuple-element.63) | copy-start | bytes 73732
  102.1 4.7 %copy-start.17 = (f32[48,128]{1,0:T(8,128)S(1)}, f32[48,128]{1,0:T(8,128)}, u32[]{:S(2)}) copy-start(f32[48,128]{1,0:T(8,128)} %get-tuple-element.56) | copy-start | bytes 73732
  102.1 4.7 %copy-start.18 = (f32[48,128]{1,0:T(8,128)S(1)}, f32[48,128]{1,0:T(8,128)}, u32[]{:S(2)}) copy-start(f32[48,128]{1,0:T(8,128)} %get-tuple-element.64) | copy-start | bytes 73732
  102.1 4.7 %copy-start.19 = (f32[48,128]{1,0:T(8,128)S(1)}, f32[48,128]{1,0:T(8,128)}, u32[]{:S(2)}) copy-start(f32[48,128]{1,0:T(8,128)} %get-tuple-element.58) | copy-start | bytes 73732
  102.1 4.7 %copy-start.20 = (f32[48,128]{1,0:T(8,128)S(1)}, f32[48,128]{1,0:T(8,128)}, u32[]{:S(2)}) copy-start(f32[48,128]{1,0:T(8,128)} %get-tuple-element.66) | copy-start | bytes 73732
  107.7 15.7 %collective-permute-start = (f32[3,1024]{1,0:T(4,128)S(1)}, f32[3,1024]{1,0:T(4,128)S(1)}, u32[]{:S(2)}, u32[]{:S(2)}) collective-permute-start(f32[3,1024]{1,0:T(4,128)S(1)} %bitcast.92), channel_id=1, source_target_pairs={{0,8},{8,16},{16,24},{1,9},{9,17},{17,25},{2,10},{10,18},{18,26},{... | collective-permute-start | bytes 36872 | tf_op jit(solution)/shard_map/ppermute | solution.py:320
  113.1 10.3 %copy-start.9 = (f32[3,2048]{1,0:T(4,128)S(1)}, f32[3,2048]{1,0:T(4,128)}, u32[]{:S(2)}) copy-start(f32[3,2048]{1,0:T(4,128)} %get-tuple-element.53) | copy-start | bytes 73732
  118.5 14.0 %all-to-all-start.5 = ((f32[32,8,192]{2,1,0:T(8,128)}), f32[32,8,192]{2,1,0:T(8,128)S(1)}, u32[]{:S(2)}, u32[]{:S(2)}) async-start(f32[32,8,192]{2,1,0:T(8,128)} %bitcast.75), calls=%async_computation.5 | async-start | bytes 524288 | tf_op jit(solution)/shard_map/all_to_all | solution.py:379
  122.1 5.7 %collective-permute-start.1 = (f32[3,1024]{1,0:T(4,128)S(1)}, f32[3,1024]{1,0:T(4,128)S(1)}, u32[]{:S(2)}, u32[]{:S(2)}) collective-permute-start(f32[3,1024]{1,0:T(4,128)S(1)} %bitcast.93), channel_id=1, source_target_pairs={{8,0},{16,8},{24,16},{9,1},{17,9},{25,17},{10,2},{18,10},{26,18},{... | collective-permute-start | bytes 36872 | tf_op jit(solution)/shard_map/ppermute | solution.py:320
  123.5 15.1 %copy-start.28 = (f32[3,16384]{1,0:T(4,128)}, f32[3,16384]{1,0:T(4,128)S(1)}, u32[]{:S(2)}) copy-start(f32[3,16384]{1,0:T(4,128)S(1)} %constant_dynamic-update-slice_fusion) | copy-start | bytes 589828
  (14 other events, 40.8 us)

commit v18 on v14

--- a/solution.py
+++ b/solution.py
@@ -10,7 +10,7 @@
 BLOCK = 192
 ITERS = 6
 CHUNK = 512
-STRESS_CHUNK = 4096
+STRESS_CHUNK = 8192
 UPDATE_PARTS = 4
 
 extensibility = 50.0

time: 133 us -> 132 us (level)
  no operation moved by 1% of the time
where the time goes in v18:
time: 132 us
  Pallas kernels  66.8 us (51%)
  starting transfers between devices  30.9 us (23%)
  waiting for transfers between devices  21 us (16%)
  local copies, waits for them, and re-layouts  7.64 us (6%)
  other arithmetic  3.24 us (2%)
    pallas_call x4, Pallas kernels, update_and_pack(): pl.pallas_call(functools.partial(update_kernel, groups16=groups16, slots1...  29.4 us
    pallas_call x5, Pallas kernels, sweep(): pl.pallas_call(sweep_kernel, out_shape=(jax.ShapeDtypeStruct(velocity.sha...  26.7 us
    all_to_all x5, waiting for transfers between devices, body(): gathered = lax.all_to_all(send, ('slab', 'rad'), 0, 0, tiled=True)  21 us
    all_to_all x5, starting transfers between devices, body(): gathered = lax.all_to_all(send, ('slab', 'rad'), 0, 0, tiled=True)  17.7 us
    pallas_call x1, Pallas kernels, stress_partials(): pl.pallas_call(functools.partial(stress_kernel, groups=groups, rows=rows)...  8.29 us
    all_to_all x1, starting transfers between devices, body(): received = lax.all_to_all(send, ('slab', 'rad'), 0, 0, tiled=True)  7.3 us
    unnamed x49, local copies, waits for them, and re-layouts  6.02 us
    ppermute x2, starting transfers between devices, passed_along(): return lax.ppermute(array, axis, pairs)  5.84 us
  transfers between devices with their start and end apart: 8, of which 5 were waited for; matrix products, arithmetic and copies ran while one was open for 5% of the time, Pallas kernels for 26%

profile of v18, /device:TPU:0, one launch (start us, length us, event | category | flops | bytes accessed | tf_op | source)
XLA Modules:
  0.0 131.7 jit_solution(7666533524526524827)
XLA Ops:
  0.7 8.3 %shard_map.133 = f32[32,12,128]{2,1,0:T(8,128)} custom-call(s32[1]{0:T(128)} %bitcast.12.slab_ref, f32[3,16384]{1,0:T(4,128)} %q_ref.9, s32[1,16384]{1,0:T(1,128)} %bitcast.84, s32[1,16384]{1,0:T(1,128)} %bitcast.73), custom_call_target="tpu_custom_call" | custom-call | flops 4026531840 | bytes 327680 | tf_op jit(solution)/shard_map/pallas_call | solution.py:178
  9.0 7.3 %all-to-all-start = ((f32[32,12,128]{2,1,0:T(8,128)}), f32[32,12,128]{2,1,0:T(8,128)S(1)}, u32[]{:S(2)}, u32[]{:S(2)}) async-start(f32[32,12,128]{2,1,0:T(8,128)} %shard_map.133), calls=%async_computation | async-start | bytes 524288 | tf_op jit(solution)/shard_map/all_to_all | solution.py:342
  16.4 1.8 %copy.52 = f32[8,192,192]{1,2,0:T(8,128)} copy(f32[8,192,192]{2,1,0:T(8,128)S(1)} %copy-done.1) | data formatting | bytes 2359296 | tf_op args[9]
  20.6 7.3 %shard_map.129 = (f32[3,4096]{1,0:T(4,128)}, f32[48,128]{1,0:T(8,128)}, f32[48,128]{1,0:T(8,128)}) custom-call(f32[3,16384]{1,0:T(4,128)} %q_ref.9, f32[3,16384]{1,0:T(4,128)} %inc_ref.7, s32[1,16384]{1,0:T(1,128)} %bitcast.85, s32[1,16384]{1,0:T(1,128)} %bitcast.74, bf16[160,384]{1,0:T(8,128)(2,1)} %pad_maximum_fusion.1.tab_ref, ...), custom_call_target="tpu_custom_call" | custom-call | flops 6442450944 | bytes 163840 | tf_op jit(solution)/shard_map/pallas_call | solution.py:238
  29.4 2.4 %shard_map.134 = (f32[8,192]{1,0:T(8,128)}, f32[256,192]{1,0:T(8,128)}) custom-call(f32[8,192,192]{2,1,0:T(8,128)} %bitcast.55, f32[192,8]{1,0:T(8,128)} %convolution_bitcast_fusion.ft_ref), custom_call_target="tpu_custom_call" | custom-call | flops 589824 | bytes 1179648 | tf_op jit(solution)/shard_map/pallas_call | solution.py:204
  31.9 5.8 %all-to-all-start.1 = ((f32[32,8,192]{2,1,0:T(8,128)}), f32[32,8,192]{2,1,0:T(8,128)S(1)}, u32[]{:S(2)}, u32[]{:S(2)}) async-start(f32[32,8,192]{2,1,0:T(8,128)} %bitcast.70), calls=%async_computation.1 | async-start | bytes 524288 | tf_op jit(solution)/shard_map/all_to_all | solution.py:371
  37.7 7.3 %shard_map.130 = (f32[3,4096]{1,0:T(4,128)}, f32[48,128]{1,0:T(8,128)}, f32[48,128]{1,0:T(8,128)}) custom-call(f32[3,16384]{1,0:T(4,128)} %q_ref.9, f32[3,16384]{1,0:T(4,128)} %inc_ref.7, s32[1,16384]{1,0:T(1,128)} %bitcast.86, s32[1,16384]{1,0:T(1,128)} %bitcast.75, bf16[160,384]{1,0:T(8,128)(2,1)} %pad_maximum_fusion.1.tab_ref, ...), custom_call_target="tpu_custom_call" | custom-call | flops 6442450944 | bytes 163840 | tf_op jit(solution)/shard_map/pallas_call | solution.py:238
  45.0 3.0 %all-to-all-done.1 = f32[32,8,192]{2,1,0:T(8,128)S(1)} async-done(((f32[32,8,192]{2,1,0:T(8,128)}), f32[32,8,192]{2,1,0:T(8,128)S(1)}, u32[]{:S(2)}, u32[]{:S(2)}) %all-to-all-start.1) | async-done | bytes 196640 | tf_op jit(solution)/shard_map/all_to_all | solution.py:371
  48.8 5.3 %shard_map.135 = (f32[8,192]{1,0:T(8,128)}, f32[256,192]{1,0:T(8,128)}) custom-call(s32[32]{0:T(128)} %reshape.94.idx_ref, f32[256,192]{1,0:T(8,128)} %bitcast.64, f32[8,4,192,192]{3,2,1,0:T(8,128)} %s_ref.9, f32[8,192,192]{2,1,0:T(8,128)} %bitcast.56, f32[192,8]{1,0:T(8,128)} %convolution_bitcast_fusion.ft_ref, f32[8,192]{1,0:T(8,128)} %get-tuple-element.40.v_ref), custom_call_target="tpu_custom_call" | custom-call | flops 2949120 | bytes 6094848 | tf_op jit(solution)/shard_map/pallas_call | solution.py:299
  54.1 2.8 %all-to-all-start.2 = ((f32[32,8,192]{2,1,0:T(8,128)}), f32[32,8,192]{2,1,0:T(8,128)S(1)}, u32[]{:S(2)}, u32[]{:S(2)}) async-start(f32[32,8,192]{2,1,0:T(8,128)} %bitcast.69), calls=%async_computation.2 | async-start | bytes 524288 | tf_op jit(solution)/shard_map/all_to_all | solution.py:371
  56.9 7.3 %shard_map.131 = (f32[3,4096]{1,0:T(4,128)}, f32[48,128]{1,0:T(8,128)}, f32[48,128]{1,0:T(8,128)}) custom-call(f32[3,16384]{1,0:T(4,128)} %q_ref.9, f32[3,16384]{1,0:T(4,128)} %inc_ref.7, s32[1,16384]{1,0:T(1,128)} %bitcast.87, s32[1,16384]{1,0:T(1,128)} %bitcast.76, bf16[160,384]{1,0:T(8,128)(2,1)} %pad_maximum_fusion.1.tab_ref, ...), custom_call_target="tpu_custom_call" | custom-call | flops 6442450944 | bytes 163840 | tf_op jit(solution)/shard_map/pallas_call | solution.py:238
  64.3 3.0 %all-to-all-done.2 = f32[32,8,192]{2,1,0:T(8,128)S(1)} async-done(((f32[32,8,192]{2,1,0:T(8,128)}), f32[32,8,192]{2,1,0:T(8,128)S(1)}, u32[]{:S(2)}, u32[]{:S(2)}) %all-to-all-start.2) | async-done | bytes 196640 | tf_op jit(solution)/shard_map/all_to_all | solution.py:371
  68.0 5.3 %shard_map.136 = (f32[8,192]{1,0:T(8,128)}, f32[256,192]{1,0:T(8,128)}) custom-call(s32[32]{0:T(128)} %reshape.94.idx_ref, f32[256,192]{1,0:T(8,128)} %bitcast.65, f32[8,4,192,192]{3,2,1,0:T(8,128)} %s_ref.9, f32[8,192,192]{2,1,0:T(8,128)} %bitcast.57, f32[192,8]{1,0:T(8,128)} %convolution_bitcast_fusion.ft_ref, f32[8,192]{1,0:T(8,128)} %get-tuple-element.42.v_ref), custom_call_target="tpu_custom_call" | custom-call | flops 2949120 | bytes 6094848 | tf_op jit(solution)/shard_map/pallas_call | solution.py:299
  73.3 2.8 %all-to-all-start.3 = ((f32[32,8,192]{2,1,0:T(8,128)}), f32[32,8,192]{2,1,0:T(8,128)S(1)}, u32[]{:S(2)}, u32[]{:S(2)}) async-start(f32[32,8,192]{2,1,0:T(8,128)} %bitcast.67), calls=%async_computation.3 | async-start | bytes 524288 | tf_op jit(solution)/shard_map/all_to_all | solution.py:371
  76.2 7.4 %shard_map.132 = (f32[3,4096]{1,0:T(4,128)}, f32[48,128]{1,0:T(8,128)}, f32[48,128]{1,0:T(8,128)}) custom-call(f32[3,16384]{1,0:T(4,128)} %q_ref.9, f32[3,16384]{1,0:T(4,128)} %inc_ref.7, s32[1,16384]{1,0:T(1,128)} %bitcast.88, s32[1,16384]{1,0:T(1,128)} %bitcast.77, bf16[160,384]{1,0:T(8,128)(2,1)} %pad_maximum_fusion.1.tab_ref, ...), custom_call_target="tpu_custom_call" | custom-call | flops 6442450944 | bytes 163840 | tf_op jit(solution)/shard_map/pallas_call | solution.py:238
  84.4 2.1 %all-to-all-done.3 = f32[32,8,192]{2,1,0:T(8,128)S(1)} async-done(((f32[32,8,192]{2,1,0:T(8,128)}), f32[32,8,192]{2,1,0:T(8,128)S(1)}, u32[]{:S(2)}, u32[]{:S(2)}) %all-to-all-start.3) | async-done | bytes 196640 | tf_op jit(solution)/shard_map/all_to_all | solution.py:371
  87.2 5.3 %shard_map.137 = (f32[8,192]{1,0:T(8,128)}, f32[256,192]{1,0:T(8,128)}) custom-call(s32[32]{0:T(128)} %reshape.94.idx_ref, f32[256,192]{1,0:T(8,128)} %bitcast.62, f32[8,4,192,192]{3,2,1,0:T(8,128)} %s_ref.9, f32[8,192,192]{2,1,0:T(8,128)} %bitcast.58, f32[192,8]{1,0:T(8,128)} %convolution_bitcast_fusion.ft_ref, f32[8,192]{1,0:T(8,128)} %get-tuple-element.44.v_ref), custom_call_target="tpu_custom_call" | custom-call | flops 2949120 | bytes 6094848 | tf_op jit(solution)/shard_map/pallas_call | solution.py:299
  92.6 3.7 %all-to-all-start.4 = ((f32[32,8,192]{2,1,0:T(8,128)}), f32[32,8,192]{2,1,0:T(8,128)S(1)}, u32[]{:S(2)}, u32[]{:S(2)}) async-start(f32[32,8,192]{2,1,0:T(8,128)} %bitcast.68), calls=%async_computation.4 | async-start | bytes 524288 | tf_op jit(solution)/shard_map/all_to_all | solution.py:371
  97.6 4.5 %collective-permute-start = (f32[3,1024]{1,0:T(4,128)S(1)}, f32[3,1024]{1,0:T(4,128)S(1)}, u32[]{:S(2)}, u32[]{:S(2)}) collective-permute-start(f32[3,1024]{1,0:T(4,128)S(1)} %bitcast.81), channel_id=1, source_target_pairs={{0,8},{8,16},{16,24},{1,9},{9,17},{17,25},{2,10},{10,18},{18,26},{... | collective-permute-start | bytes 36872 | tf_op jit(solution)/shard_map/ppermute | solution.py:318
  102.2 4.5 %all-to-all-done.4 = f32[32,8,192]{2,1,0:T(8,128)S(1)} async-done(((f32[32,8,192]{2,1,0:T(8,128)}), f32[32,8,192]{2,1,0:T(8,128)S(1)}, u32[]{:S(2)}, u32[]{:S(2)}) %all-to-all-start.4) | async-done | bytes 196640 | tf_op jit(solution)/shard_map/all_to_all | solution.py:371
  107.4 5.4 %shard_map.138 = (f32[8,192]{1,0:T(8,128)}, f32[256,192]{1,0:T(8,128)}) custom-call(s32[32]{0:T(128)} %reshape.94.idx_ref, f32[256,192]{1,0:T(8,128)} %bitcast.63, f32[8,4,192,192]{3,2,1,0:T(8,128)} %s_ref.9, f32[8,192,192]{2,1,0:T(8,128)} %bitcast.59, f32[192,8]{1,0:T(8,128)} %convolution_bitcast_fusion.ft_ref, f32[8,192]{1,0:T(8,128)} %get-tuple-element.46.v_ref), custom_call_target="tpu_custom_call" | custom-call | flops 2949120 | bytes 6094848 | tf_op jit(solution)/shard_map/pallas_call | solution.py:299
  112.7 2.6 %all-to-all-start.5 = ((f32[32,8,192]{2,1,0:T(8,128)}), f32[32,8,192]{2,1,0:T(8,128)S(1)}, u32[]{:S(2)}, u32[]{:S(2)}) async-start(f32[32,8,192]{2,1,0:T(8,128)} %bitcast.66), calls=%async_computation.5 | async-start | bytes 524288 | tf_op jit(solution)/shard_map/all_to_all | solution.py:371
  117.4 8.3 %all-to-all-done.5 = f32[32,8,192]{2,1,0:T(8,128)S(1)} async-done(((f32[32,8,192]{2,1,0:T(8,128)}), f32[32,8,192]{2,1,0:T(8,128)S(1)}, u32[]{:S(2)}, u32[]{:S(2)}) %all-to-all-start.5) | async-done | bytes 196640 | tf_op jit(solution)/shard_map/all_to_all | solution.py:371
  126.4 5.3 %shard_map.139 = (f32[8,192]{1,0:T(8,128)}, f32[256,192]{1,0:T(8,128)}) custom-call(s32[32]{0:T(128)} %reshape.94.idx_ref, f32[256,192]{1,0:T(8,128)} %bitcast.61, f32[8,4,192,192]{3,2,1,0:T(8,128)} %s_ref.9, f32[8,192,192]{2,1,0:T(8,128)} %bitcast.60, f32[192,8]{1,0:T(8,128)} %convolution_bitcast_fusion.ft_ref, f32[8,192]{1,0:T(8,128)} %get-tuple-element.48.v_ref), custom_call_target="tpu_custom_call" | custom-call | flops 2949120 | bytes 6094848 | tf_op jit(solution)/shard_map/pallas_call | solution.py:299
  (77 shorter events, 11.6 us)
Async XLA Ops:
  0.6 27.6 %copy-start = (f32[192,192]{1,0:T(8,128)S(1)}, f32[192,192]{1,0:T(8,128)}, u32[]{:S(2)}) copy-start(f32[192,192]{1,0:T(8,128)} %param.16) | copy-start | bytes 442372
  0.7 15.6 %copy-start.8 = (s32[16384]{0:T(1024)S(1)}, s32[16384]{0:T(1024)}, u32[]{:S(2)}) copy-start(s32[16384]{0:T(1024)} %param.14) | copy-start | bytes 196612
  0.7 15.7 %copy-start.19 = (f32[384]{0:T(512)S(1)}, f32[384]{0:T(512)}, u32[]{:S(2)}) copy-start(f32[384]{0:T(512)} %param.15) | copy-start | bytes 4612
  0.7 15.7 %copy-start.1 = (f32[8,192,192]{2,1,0:T(8,128)S(1)}, f32[8,192,192]{2,1,0:T(8,128)}, u32[]{:S(2)}) copy-start(f32[8,192,192]{2,1,0:T(8,128)} %param.19) | copy-start | bytes 3538948
  9.0 19.0 %all-to-all-start = ((f32[32,12,128]{2,1,0:T(8,128)}), f32[32,12,128]{2,1,0:T(8,128)S(1)}, u32[]{:S(2)}, u32[]{:S(2)}) async-start(f32[32,12,128]{2,1,0:T(8,128)} %shard_map.133), calls=%async_computation | async-start | bytes 524288 | tf_op jit(solution)/shard_map/all_to_all | solution.py:342
  16.4 1.8 %copy-start.20 = (s32[8,4]{0,1:T(4,128)S(1)}, s32[8,4]{0,1:T(4,128)}, u32[]{:S(2)}) copy-start(s32[8,4]{0,1:T(4,128)} %param.18) | copy-start | bytes 388
  16.4 2.4 %copy-start.7 = (f32[5,3072]{1,0:T(8,128)S(1)}, f32[5,3072]{1,0:T(8,128)}, u32[]{:S(2)}) copy-start(f32[5,3072]{1,0:T(8,128)} %param.12) | copy-start | bytes 184324
  31.9 16.2 %all-to-all-start.1 = ((f32[32,8,192]{2,1,0:T(8,128)}), f32[32,8,192]{2,1,0:T(8,128)S(1)}, u32[]{:S(2)}, u32[]{:S(2)}) async-start(f32[32,8,192]{2,1,0:T(8,128)} %bitcast.70), calls=%async_computation.1 | async-start | bytes 524288 | tf_op jit(solution)/shard_map/all_to_all | solution.py:371
  54.1 13.2 %all-to-all-start.2 = ((f32[32,8,192]{2,1,0:T(8,128)}), f32[32,8,192]{2,1,0:T(8,128)S(1)}, u32[]{:S(2)}, u32[]{:S(2)}) async-start(f32[32,8,192]{2,1,0:T(8,128)} %bitcast.69), calls=%async_computation.2 | async-start | bytes 524288 | tf_op jit(solution)/shard_map/all_to_all | solution.py:371
  73.3 13.2 %all-to-all-start.3 = ((f32[32,8,192]{2,1,0:T(8,128)}), f32[32,8,192]{2,1,0:T(8,128)S(1)}, u32[]{:S(2)}, u32[]{:S(2)}) async-start(f32[32,8,192]{2,1,0:T(8,128)} %bitcast.67), calls=%async_computation.3 | async-start | bytes 524288 | tf_op jit(solution)/shard_map/all_to_all | solution.py:371
  76.1 7.4 %copy-start.13 = (f32[48,128]{1,0:T(8,128)S(1)}, f32[48,128]{1,0:T(8,128)}, u32[]{:S(2)}) copy-start(f32[48,128]{1,0:T(8,128)} %get-tuple-element.31) | copy-start | bytes 73732
  76.1 7.4 %copy-start.14 = (f32[48,128]{1,0:T(8,128)S(1)}, f32[48,128]{1,0:T(8,128)}, u32[]{:S(2)}) copy-start(f32[48,128]{1,0:T(8,128)} %get-tuple-element.35) | copy-start | bytes 73732
  76.2 7.4 %copy-start.15 = (f32[48,128]{1,0:T(8,128)S(1)}, f32[48,128]{1,0:T(8,128)}, u32[]{:S(2)}) copy-start(f32[48,128]{1,0:T(8,128)} %get-tuple-element.32) | copy-start | bytes 73732
  76.2 7.4 %copy-start.16 = (f32[48,128]{1,0:T(8,128)S(1)}, f32[48,128]{1,0:T(8,128)}, u32[]{:S(2)}) copy-start(f32[48,128]{1,0:T(8,128)} %get-tuple-element.36) | copy-start | bytes 73732
  76.2 7.4 %copy-start.17 = (f32[48,128]{1,0:T(8,128)S(1)}, f32[48,128]{1,0:T(8,128)}, u32[]{:S(2)}) copy-start(f32[48,128]{1,0:T(8,128)} %get-tuple-element.33) | copy-start | bytes 73732
  76.2 7.4 %copy-start.18 = (f32[48,128]{1,0:T(8,128)S(1)}, f32[48,128]{1,0:T(8,128)}, u32[]{:S(2)}) copy-start(f32[48,128]{1,0:T(8,128)} %get-tuple-element.37) | copy-start | bytes 73732
  92.6 14.1 %all-to-all-start.4 = ((f32[32,8,192]{2,1,0:T(8,128)}), f32[32,8,192]{2,1,0:T(8,128)S(1)}, u32[]{:S(2)}, u32[]{:S(2)}) async-start(f32[32,8,192]{2,1,0:T(8,128)} %bitcast.68), calls=%async_computation.4 | async-start | bytes 524288 | tf_op jit(solution)/shard_map/all_to_all | solution.py:371
  96.3 19.8 %collective-permute-start.1 = (f32[3,1024]{1,0:T(4,128)S(1)}, f32[3,1024]{1,0:T(4,128)S(1)}, u32[]{:S(2)}, u32[]{:S(2)}) collective-permute-start(f32[3,1024]{1,0:T(4,128)S(1)} %bitcast.80), channel_id=1, source_target_pairs={{8,0},{16,8},{24,16},{9,1},{17,9},{25,17},{10,2},{18,10},{26,18},{... | collective-permute-start | bytes 36872 | tf_op jit(solution)/shard_map/ppermute | solution.py:318
  97.6 18.5 %collective-permute-start = (f32[3,1024]{1,0:T(4,128)S(1)}, f32[3,1024]{1,0:T(4,128)S(1)}, u32[]{:S(2)}, u32[]{:S(2)}) collective-permute-start(f32[3,1024]{1,0:T(4,128)S(1)} %bitcast.81), channel_id=1, source_target_pairs={{0,8},{8,16},{16,24},{1,9},{9,17},{17,25},{2,10},{10,18},{18,26},{... | collective-permute-start | bytes 36872 | tf_op jit(solution)/shard_map/ppermute | solution.py:318
  107.4 8.0 %copy-start.9 = (f32[3,4096]{1,0:T(4,128)S(1)}, f32[3,4096]{1,0:T(4,128)}, u32[]{:S(2)}) copy-start(f32[3,4096]{1,0:T(4,128)} %get-tuple-element.27) | copy-start | bytes 147460
  107.4 8.0 %copy-start.10 = (f32[3,4096]{1,0:T(4,128)S(1)}, f32[3,4096]{1,0:T(4,128)}, u32[]{:S(2)}) copy-start(f32[3,4096]{1,0:T(4,128)} %get-tuple-element.28) | copy-start | bytes 147460
  107.4 8.0 %copy-start.11 = (f32[3,4096]{1,0:T(4,128)S(1)}, f32[3,4096]{1,0:T(4,128)}, u32[]{:S(2)}) copy-start(f32[3,4096]{1,0:T(4,128)} %get-tuple-element.29) | copy-start | bytes 147460
  107.4 8.0 %copy-start.12 = (f32[3,4096]{1,0:T(4,128)S(1)}, f32[3,4096]{1,0:T(4,128)}, u32[]{:S(2)}) copy-start(f32[3,4096]{1,0:T(4,128)} %get-tuple-element.30) | copy-start | bytes 147460
  112.7 13.0 %all-to-all-start.5 = ((f32[32,8,192]{2,1,0:T(8,128)}), f32[32,8,192]{2,1,0:T(8,128)S(1)}, u32[]{:S(2)}, u32[]{:S(2)}) async-start(f32[32,8,192]{2,1,0:T(8,128)} %bitcast.66), calls=%async_computation.5 | async-start | bytes 524288 | tf_op jit(solution)/shard_map/all_to_all | solution.py:371
  (5 other events, 3.5 us)

commit v19 on v18

--- a/solution.py
+++ b/solution.py
@@ -9,7 +9,7 @@
 
 BLOCK = 192
 ITERS = 6
-CHUNK = 512
+CHUNK = 1024
 STRESS_CHUNK = 8192
 UPDATE_PARTS = 4
 

time: 132 us -> 131 us (level)
  Pallas kernels: 66.8 us -> 64.6 us
  waiting for transfers between devices: 21 us -> 22.5 us
    pallas_call x4, Pallas kernels: 29.4 us -> 27.2 us  [update_and_pack(): pl.pallas_call(functools.partial(update_kernel, groups16=groups16, slots1...]
    all_to_all x5, waiting for transfers between devices: 21 us -> 22.5 us  [body(): gathered = lax.all_to_all(send, ('slab', 'rad'), 0, 0, tiled=True)]
  transfers between devices with their start and end apart: 8 -> 8, of which waited for: 5 -> 5; matrix products, arithmetic and copies ran while one was open for 5% -> 5% of each run, Pallas kernels for 26% -> 25%
where the time goes in v19:
time: 131 us; the launch traced here: 130 us
  Pallas kernels  64.6 us (49%)
  starting transfers between devices  30.1 us (23%)
  waiting for transfers between devices  22.5 us (17%)
  local copies, waits for them, and re-layouts  7.64 us (6%)
  other arithmetic  3.24 us (2%)
    pallas_call x4, Pallas kernels, update_and_pack(): pl.pallas_call(functools.partial(update_kernel, groups16=groups16, slots1...  27.2 us
    pallas_call x5, Pallas kernels, sweep(): pl.pallas_call(sweep_kernel, out_shape=(jax.ShapeDtypeStruct(velocity.sha...  26.7 us
    all_to_all x5, waiting for transfers between devices, body(): gathered = lax.all_to_all(send, ('slab', 'rad'), 0, 0, tiled=True)  22.5 us
    all_to_all x5, starting transfers between devices, body(): gathered = lax.all_to_all(send, ('slab', 'rad'), 0, 0, tiled=True)  16.9 us
    pallas_call x1, Pallas kernels, stress_partials(): pl.pallas_call(functools.partial(stress_kernel, groups=groups, rows=rows)...  8.29 us
    all_to_all x1, starting transfers between devices, body(): received = lax.all_to_all(send, ('slab', 'rad'), 0, 0, tiled=True)  7.3 us
    unnamed x49, local copies, waits for them, and re-layouts  6.02 us
    ppermute x2, starting transfers between devices, passed_along(): return lax.ppermute(array, axis, pairs)  5.84 us
  transfers between devices with their start and end apart: 8, of which 5 were waited for; matrix products, arithmetic and copies ran while one was open for 5% of the time, Pallas kernels for 25%

profile of v19, /device:TPU:0, one launch (start us, length us, event | category | flops | bytes accessed | tf_op | source)
XLA Modules:
  0.0 130.2 jit_solution(11469442530130661042)
XLA Ops:
  0.7 8.3 %shard_map.133 = f32[32,12,128]{2,1,0:T(8,128)} custom-call(s32[1]{0:T(128)} %bitcast.12.slab_ref, f32[3,16384]{1,0:T(4,128)} %q_ref.9, s32[1,16384]{1,0:T(1,128)} %bitcast.84, s32[1,16384]{1,0:T(1,128)} %bitcast.73), custom_call_target="tpu_custom_call" | custom-call | flops 4026531840 | bytes 327680 | tf_op jit(solution)/shard_map/pallas_call | solution.py:178
  9.0 7.3 %all-to-all-start = ((f32[32,12,128]{2,1,0:T(8,128)}), f32[32,12,128]{2,1,0:T(8,128)S(1)}, u32[]{:S(2)}, u32[]{:S(2)}) async-start(f32[32,12,128]{2,1,0:T(8,128)} %shard_map.133), calls=%async_computation | async-start | bytes 524288 | tf_op jit(solution)/shard_map/all_to_all | solution.py:342
  16.4 1.8 %copy.52 = f32[8,192,192]{1,2,0:T(8,128)} copy(f32[8,192,192]{2,1,0:T(8,128)S(1)} %copy-done.1) | data formatting | bytes 2359296 | tf_op args[9]
  20.6 6.8 %shard_map.129 = (f32[3,4096]{1,0:T(4,128)}, f32[48,128]{1,0:T(8,128)}, f32[48,128]{1,0:T(8,128)}) custom-call(f32[3,16384]{1,0:T(4,128)} %q_ref.9, f32[3,16384]{1,0:T(4,128)} %inc_ref.7, s32[1,16384]{1,0:T(1,128)} %bitcast.85, s32[1,16384]{1,0:T(1,128)} %bitcast.74, bf16[160,384]{1,0:T(8,128)(2,1)} %pad_maximum_fusion.1.tab_ref, ...), custom_call_target="tpu_custom_call" | custom-call | flops 6442450944 | bytes 163840 | tf_op jit(solution)/shard_map/pallas_call | solution.py:238
  28.9 2.4 %shard_map.134 = (f32[8,192]{1,0:T(8,128)}, f32[256,192]{1,0:T(8,128)}) custom-call(f32[8,192,192]{2,1,0:T(8,128)} %bitcast.55, f32[192,8]{1,0:T(8,128)} %convolution_bitcast_fusion.ft_ref), custom_call_target="tpu_custom_call" | custom-call | flops 589824 | bytes 1179648 | tf_op jit(solution)/shard_map/pallas_call | solution.py:204
  31.3 5.8 %all-to-all-start.1 = ((f32[32,8,192]{2,1,0:T(8,128)}), f32[32,8,192]{2,1,0:T(8,128)S(1)}, u32[]{:S(2)}, u32[]{:S(2)}) async-start(f32[32,8,192]{2,1,0:T(8,128)} %bitcast.70), calls=%async_computation.1 | async-start | bytes 524288 | tf_op jit(solution)/shard_map/all_to_all | solution.py:371
  37.1 6.8 %shard_map.130 = (f32[3,4096]{1,0:T(4,128)}, f32[48,128]{1,0:T(8,128)}, f32[48,128]{1,0:T(8,128)}) custom-call(f32[3,16384]{1,0:T(4,128)} %q_ref.9, f32[3,16384]{1,0:T(4,128)} %inc_ref.7, s32[1,16384]{1,0:T(1,128)} %bitcast.86, s32[1,16384]{1,0:T(1,128)} %bitcast.75, bf16[160,384]{1,0:T(8,128)(2,1)} %pad_maximum_fusion.1.tab_ref, ...), custom_call_target="tpu_custom_call" | custom-call | flops 6442450944 | bytes 163840 | tf_op jit(solution)/shard_map/pallas_call | solution.py:238
  43.9 3.6 %all-to-all-done.1 = f32[32,8,192]{2,1,0:T(8,128)S(1)} async-done(((f32[32,8,192]{2,1,0:T(8,128)}), f32[32,8,192]{2,1,0:T(8,128)S(1)}, u32[]{:S(2)}, u32[]{:S(2)}) %all-to-all-start.1) | async-done | bytes 196640 | tf_op jit(solution)/shard_map/all_to_all | solution.py:371
  48.2 5.3 %shard_map.135 = (f32[8,192]{1,0:T(8,128)}, f32[256,192]{1,0:T(8,128)}) custom-call(s32[32]{0:T(128)} %reshape.94.idx_ref, f32[256,192]{1,0:T(8,128)} %bitcast.64, f32[8,4,192,192]{3,2,1,0:T(8,128)} %s_ref.9, f32[8,192,192]{2,1,0:T(8,128)} %bitcast.56, f32[192,8]{1,0:T(8,128)} %convolution_bitcast_fusion.ft_ref, f32[8,192]{1,0:T(8,128)} %get-tuple-element.40.v_ref), custom_call_target="tpu_custom_call" | custom-call | flops 2949120 | bytes 6094848 | tf_op jit(solution)/shard_map/pallas_call | solution.py:299
  53.6 2.6 %all-to-all-start.2 = ((f32[32,8,192]{2,1,0:T(8,128)}), f32[32,8,192]{2,1,0:T(8,128)S(1)}, u32[]{:S(2)}, u32[]{:S(2)}) async-start(f32[32,8,192]{2,1,0:T(8,128)} %bitcast.69), calls=%async_computation.2 | async-start | bytes 524288 | tf_op jit(solution)/shard_map/all_to_all | solution.py:371
  56.1 6.8 %shard_map.131 = (f32[3,4096]{1,0:T(4,128)}, f32[48,128]{1,0:T(8,128)}, f32[48,128]{1,0:T(8,128)}) custom-call(f32[3,16384]{1,0:T(4,128)} %q_ref.9, f32[3,16384]{1,0:T(4,128)} %inc_ref.7, s32[1,16384]{1,0:T(1,128)} %bitcast.87, s32[1,16384]{1,0:T(1,128)} %bitcast.76, bf16[160,384]{1,0:T(8,128)(2,1)} %pad_maximum_fusion.1.tab_ref, ...), custom_call_target="tpu_custom_call" | custom-call | flops 6442450944 | bytes 163840 | tf_op jit(solution)/shard_map/pallas_call | solution.py:238
  62.9 3.6 %all-to-all-done.2 = f32[32,8,192]{2,1,0:T(8,128)S(1)} async-done(((f32[32,8,192]{2,1,0:T(8,128)}), f32[32,8,192]{2,1,0:T(8,128)S(1)}, u32[]{:S(2)}, u32[]{:S(2)}) %all-to-all-start.2) | async-done | bytes 196640 | tf_op jit(solution)/shard_map/all_to_all | solution.py:371
  67.2 5.3 %shard_map.136 = (f32[8,192]{1,0:T(8,128)}, f32[256,192]{1,0:T(8,128)}) custom-call(s32[32]{0:T(128)} %reshape.94.idx_ref, f32[256,192]{1,0:T(8,128)} %bitcast.65, f32[8,4,192,192]{3,2,1,0:T(8,128)} %s_ref.9, f32[8,192,192]{2,1,0:T(8,128)} %bitcast.57, f32[192,8]{1,0:T(8,128)} %convolution_bitcast_fusion.ft_ref, f32[8,192]{1,0:T(8,128)} %get-tuple-element.42.v_ref), custom_call_target="tpu_custom_call" | custom-call | flops 2949120 | bytes 6094848 | tf_op jit(solution)/shard_map/pallas_call | solution.py:299
  72.6 2.8 %all-to-all-start.3 = ((f32[32,8,192]{2,1,0:T(8,128)}), f32[32,8,192]{2,1,0:T(8,128)S(1)}, u32[]{:S(2)}, u32[]{:S(2)}) async-start(f32[32,8,192]{2,1,0:T(8,128)} %bitcast.67), calls=%async_computation.3 | async-start | bytes 524288 | tf_op jit(solution)/shard_map/all_to_all | solution.py:371
  75.4 6.8 %shard_map.132 = (f32[3,4096]{1,0:T(4,128)}, f32[48,128]{1,0:T(8,128)}, f32[48,128]{1,0:T(8,128)}) custom-call(f32[3,16384]{1,0:T(4,128)} %q_ref.9, f32[3,16384]{1,0:T(4,128)} %inc_ref.7, s32[1,16384]{1,0:T(1,128)} %bitcast.88, s32[1,16384]{1,0:T(1,128)} %bitcast.77, bf16[160,384]{1,0:T(8,128)(2,1)} %pad_maximum_fusion.1.tab_ref, ...), custom_call_target="tpu_custom_call" | custom-call | flops 6442450944 | bytes 163840 | tf_op jit(solution)/shard_map/pallas_call | solution.py:238
  83.0 2.5 %all-to-all-done.3 = f32[32,8,192]{2,1,0:T(8,128)S(1)} async-done(((f32[32,8,192]{2,1,0:T(8,128)}), f32[32,8,192]{2,1,0:T(8,128)S(1)}, u32[]{:S(2)}, u32[]{:S(2)}) %all-to-all-start.3) | async-done | bytes 196640 | tf_op jit(solution)/shard_map/all_to_all | solution.py:371
  86.2 5.3 %shard_map.137 = (f32[8,192]{1,0:T(8,128)}, f32[256,192]{1,0:T(8,128)}) custom-call(s32[32]{0:T(128)} %reshape.94.idx_ref, f32[256,192]{1,0:T(8,128)} %bitcast.62, f32[8,4,192,192]{3,2,1,0:T(8,128)} %s_ref.9, f32[8,192,192]{2,1,0:T(8,128)} %bitcast.58, f32[192,8]{1,0:T(8,128)} %convolution_bitcast_fusion.ft_ref, f32[8,192]{1,0:T(8,128)} %get-tuple-element.44.v_ref), custom_call_target="tpu_custom_call" | custom-call | flops 2949120 | bytes 6094848 | tf_op jit(solution)/shard_map/pallas_call | solution.py:299
  91.6 3.2 %all-to-all-start.4 = ((f32[32,8,192]{2,1,0:T(8,128)}), f32[32,8,192]{2,1,0:T(8,128)S(1)}, u32[]{:S(2)}, u32[]{:S(2)}) async-start(f32[32,8,192]{2,1,0:T(8,128)} %bitcast.68), calls=%async_computation.4 | async-start | bytes 524288 | tf_op jit(solution)/shard_map/all_to_all | solution.py:371
  96.1 4.5 %collective-permute-start = (f32[3,1024]{1,0:T(4,128)S(1)}, f32[3,1024]{1,0:T(4,128)S(1)}, u32[]{:S(2)}, u32[]{:S(2)}) collective-permute-start(f32[3,1024]{1,0:T(4,128)S(1)} %bitcast.81), channel_id=1, source_target_pairs={{0,8},{8,16},{16,24},{1,9},{9,17},{17,25},{2,10},{10,18},{18,26},{... | collective-permute-start | bytes 36872 | tf_op jit(solution)/shard_map/ppermute | solution.py:318
  100.7 4.5 %all-to-all-done.4 = f32[32,8,192]{2,1,0:T(8,128)S(1)} async-done(((f32[32,8,192]{2,1,0:T(8,128)}), f32[32,8,192]{2,1,0:T(8,128)S(1)}, u32[]{:S(2)}, u32[]{:S(2)}) %all-to-all-start.4) | async-done | bytes 196640 | tf_op jit(solution)/shard_map/all_to_all | solution.py:371
  105.9 5.4 %shard_map.138 = (f32[8,192]{1,0:T(8,128)}, f32[256,192]{1,0:T(8,128)}) custom-call(s32[32]{0:T(128)} %reshape.94.idx_ref, f32[256,192]{1,0:T(8,128)} %bitcast.63, f32[8,4,192,192]{3,2,1,0:T(8,128)} %s_ref.9, f32[8,192,192]{2,1,0:T(8,128)} %bitcast.59, f32[192,8]{1,0:T(8,128)} %convolution_bitcast_fusion.ft_ref, f32[8,192]{1,0:T(8,128)} %get-tuple-element.46.v_ref), custom_call_target="tpu_custom_call" | custom-call | flops 2949120 | bytes 6094848 | tf_op jit(solution)/shard_map/pallas_call | solution.py:299
  111.2 2.6 %all-to-all-start.5 = ((f32[32,8,192]{2,1,0:T(8,128)}), f32[32,8,192]{2,1,0:T(8,128)S(1)}, u32[]{:S(2)}, u32[]{:S(2)}) async-start(f32[32,8,192]{2,1,0:T(8,128)} %bitcast.66), calls=%async_computation.5 | async-start | bytes 524288 | tf_op jit(solution)/shard_map/all_to_all | solution.py:371
  115.9 8.3 %all-to-all-done.5 = f32[32,8,192]{2,1,0:T(8,128)S(1)} async-done(((f32[32,8,192]{2,1,0:T(8,128)}), f32[32,8,192]{2,1,0:T(8,128)S(1)}, u32[]{:S(2)}, u32[]{:S(2)}) %all-to-all-start.5) | async-done | bytes 196640 | tf_op jit(solution)/shard_map/all_to_all | solution.py:371
  124.9 5.3 %shard_map.139 = (f32[8,192]{1,0:T(8,128)}, f32[256,192]{1,0:T(8,128)}) custom-call(s32[32]{0:T(128)} %reshape.94.idx_ref, f32[256,192]{1,0:T(8,128)} %bitcast.61, f32[8,4,192,192]{3,2,1,0:T(8,128)} %s_ref.9, f32[8,192,192]{2,1,0:T(8,128)} %bitcast.60, f32[192,8]{1,0:T(8,128)} %convolution_bitcast_fusion.ft_ref, f32[8,192]{1,0:T(8,128)} %get-tuple-element.48.v_ref), custom_call_target="tpu_custom_call" | custom-call | flops 2949120 | bytes 6094848 | tf_op jit(solution)/shard_map/pallas_call | solution.py:299
  (77 shorter events, 11.6 us)
Async XLA Ops:
  0.6 27.0 %copy-start = (f32[192,192]{1,0:T(8,128)S(1)}, f32[192,192]{1,0:T(8,128)}, u32[]{:S(2)}) copy-start(f32[192,192]{1,0:T(8,128)} %param.16) | copy-start | bytes 442372
  0.7 15.6 %copy-start.8 = (s32[16384]{0:T(1024)S(1)}, s32[16384]{0:T(1024)}, u32[]{:S(2)}) copy-start(s32[16384]{0:T(1024)} %param.14) | copy-start | bytes 196612
  0.7 15.7 %copy-start.19 = (f32[384]{0:T(512)S(1)}, f32[384]{0:T(512)}, u32[]{:S(2)}) copy-start(f32[384]{0:T(512)} %param.15) | copy-start | bytes 4612
  0.7 15.7 %copy-start.1 = (f32[8,192,192]{2,1,0:T(8,128)S(1)}, f32[8,192,192]{2,1,0:T(8,128)}, u32[]{:S(2)}) copy-start(f32[8,192,192]{2,1,0:T(8,128)} %param.19) | copy-start | bytes 3538948
  9.0 18.5 %all-to-all-start = ((f32[32,12,128]{2,1,0:T(8,128)}), f32[32,12,128]{2,1,0:T(8,128)S(1)}, u32[]{:S(2)}, u32[]{:S(2)}) async-start(f32[32,12,128]{2,1,0:T(8,128)} %shard_map.133), calls=%async_computation | async-start | bytes 524288 | tf_op jit(solution)/shard_map/all_to_all | solution.py:342
  16.4 1.8 %copy-start.20 = (s32[8,4]{0,1:T(4,128)S(1)}, s32[8,4]{0,1:T(4,128)}, u32[]{:S(2)}) copy-start(s32[8,4]{0,1:T(4,128)} %param.18) | copy-start | bytes 388
  16.4 2.4 %copy-start.7 = (f32[5,3072]{1,0:T(8,128)S(1)}, f32[5,3072]{1,0:T(8,128)}, u32[]{:S(2)}) copy-start(f32[5,3072]{1,0:T(8,128)} %param.12) | copy-start | bytes 184324
  31.3 16.2 %all-to-all-start.1 = ((f32[32,8,192]{2,1,0:T(8,128)}), f32[32,8,192]{2,1,0:T(8,128)S(1)}, u32[]{:S(2)}, u32[]{:S(2)}) async-start(f32[32,8,192]{2,1,0:T(8,128)} %bitcast.70), calls=%async_computation.1 | async-start | bytes 524288 | tf_op jit(solution)/shard_map/all_to_all | solution.py:371
  53.6 13.0 %all-to-all-start.2 = ((f32[32,8,192]{2,1,0:T(8,128)}), f32[32,8,192]{2,1,0:T(8,128)S(1)}, u32[]{:S(2)}, u32[]{:S(2)}) async-start(f32[32,8,192]{2,1,0:T(8,128)} %bitcast.69), calls=%async_computation.2 | async-start | bytes 524288 | tf_op jit(solution)/shard_map/all_to_all | solution.py:371
  72.6 13.0 %all-to-all-start.3 = ((f32[32,8,192]{2,1,0:T(8,128)}), f32[32,8,192]{2,1,0:T(8,128)S(1)}, u32[]{:S(2)}, u32[]{:S(2)}) async-start(f32[32,8,192]{2,1,0:T(8,128)} %bitcast.67), calls=%async_computation.3 | async-start | bytes 524288 | tf_op jit(solution)/shard_map/all_to_all | solution.py:371
  75.3 6.9 %copy-start.13 = (f32[48,128]{1,0:T(8,128)S(1)}, f32[48,128]{1,0:T(8,128)}, u32[]{:S(2)}) copy-start(f32[48,128]{1,0:T(8,128)} %get-tuple-element.31) | copy-start | bytes 73732
  75.3 6.9 %copy-start.14 = (f32[48,128]{1,0:T(8,128)S(1)}, f32[48,128]{1,0:T(8,128)}, u32[]{:S(2)}) copy-start(f32[48,128]{1,0:T(8,128)} %get-tuple-element.35) | copy-start | bytes 73732
  75.4 6.9 %copy-start.15 = (f32[48,128]{1,0:T(8,128)S(1)}, f32[48,128]{1,0:T(8,128)}, u32[]{:S(2)}) copy-start(f32[48,128]{1,0:T(8,128)} %get-tuple-element.32) | copy-start | bytes 73732
  75.4 6.9 %copy-start.16 = (f32[48,128]{1,0:T(8,128)S(1)}, f32[48,128]{1,0:T(8,128)}, u32[]{:S(2)}) copy-start(f32[48,128]{1,0:T(8,128)} %get-tuple-element.36) | copy-start | bytes 73732
  75.4 6.9 %copy-start.17 = (f32[48,128]{1,0:T(8,128)S(1)}, f32[48,128]{1,0:T(8,128)}, u32[]{:S(2)}) copy-start(f32[48,128]{1,0:T(8,128)} %get-tuple-element.33) | copy-start | bytes 73732
  75.4 6.9 %copy-start.18 = (f32[48,128]{1,0:T(8,128)S(1)}, f32[48,128]{1,0:T(8,128)}, u32[]{:S(2)}) copy-start(f32[48,128]{1,0:T(8,128)} %get-tuple-element.37) | copy-start | bytes 73732
  91.6 13.6 %all-to-all-start.4 = ((f32[32,8,192]{2,1,0:T(8,128)}), f32[32,8,192]{2,1,0:T(8,128)S(1)}, u32[]{:S(2)}, u32[]{:S(2)}) async-start(f32[32,8,192]{2,1,0:T(8,128)} %bitcast.68), calls=%async_computation.4 | async-start | bytes 524288 | tf_op jit(solution)/shard_map/all_to_all | solution.py:371
  94.8 19.8 %collective-permute-start.1 = (f32[3,1024]{1,0:T(4,128)S(1)}, f32[3,1024]{1,0:T(4,128)S(1)}, u32[]{:S(2)}, u32[]{:S(2)}) collective-permute-start(f32[3,1024]{1,0:T(4,128)S(1)} %bitcast.80), channel_id=1, source_target_pairs={{8,0},{16,8},{24,16},{9,1},{17,9},{25,17},{10,2},{18,10},{26,18},{... | collective-permute-start | bytes 36872 | tf_op jit(solution)/shard_map/ppermute | solution.py:318
  96.1 18.5 %collective-permute-start = (f32[3,1024]{1,0:T(4,128)S(1)}, f32[3,1024]{1,0:T(4,128)S(1)}, u32[]{:S(2)}, u32[]{:S(2)}) collective-permute-start(f32[3,1024]{1,0:T(4,128)S(1)} %bitcast.81), channel_id=1, source_target_pairs={{0,8},{8,16},{16,24},{1,9},{9,17},{17,25},{2,10},{10,18},{18,26},{... | collective-permute-start | bytes 36872 | tf_op jit(solution)/shard_map/ppermute | solution.py:318
  105.8 8.0 %copy-start.9 = (f32[3,4096]{1,0:T(4,128)S(1)}, f32[3,4096]{1,0:T(4,128)}, u32[]{:S(2)}) copy-start(f32[3,4096]{1,0:T(4,128)} %get-tuple-element.27) | copy-start | bytes 147460
  105.8 8.0 %copy-start.10 = (f32[3,4096]{1,0:T(4,128)S(1)}, f32[3,4096]{1,0:T(4,128)}, u32[]{:S(2)}) copy-start(f32[3,4096]{1,0:T(4,128)} %get-tuple-element.28) | copy-start | bytes 147460
  105.8 8.0 %copy-start.11 = (f32[3,4096]{1,0:T(4,128)S(1)}, f32[3,4096]{1,0:T(4,128)}, u32[]{:S(2)}) copy-start(f32[3,4096]{1,0:T(4,128)} %get-tuple-element.29) | copy-start | bytes 147460
  105.8 8.0 %copy-start.12 = (f32[3,4096]{1,0:T(4,128)S(1)}, f32[3,4096]{1,0:T(4,128)}, u32[]{:S(2)}) copy-start(f32[3,4096]{1,0:T(4,128)} %get-tuple-element.30) | copy-start | bytes 147460
  111.2 13.0 %all-to-all-start.5 = ((f32[32,8,192]{2,1,0:T(8,128)}), f32[32,8,192]{2,1,0:T(8,128)S(1)}, u32[]{:S(2)}, u32[]{:S(2)}) async-start(f32[32,8,192]{2,1,0:T(8,128)} %bitcast.66), calls=%async_computation.5 | async-start | bytes 524288 | tf_op jit(solution)/shard_map/all_to_all | solution.py:371
  (5 other events, 3.5 us)

commit v20 on v19

--- a/solution.py
+++ b/solution.py
@@ -9,7 +9,7 @@
 
 BLOCK = 192
 ITERS = 6
-CHUNK = 1024
+CHUNK = 2048
 STRESS_CHUNK = 8192
 UPDATE_PARTS = 4
 

time: 131 us -> 134 us (1.023)
  Pallas kernels: 64.6 us -> 68.6 us
  waiting for transfers between devices: 22.5 us -> 19.2 us
  starting transfers between devices: 30.1 us -> 32.7 us
    pallas_call x4, Pallas kernels: 27.2 us -> 31.3 us  [update_and_pack(): pl.pallas_call(functools.partial(update_kernel, groups16=groups16, slots1...]
    all_to_all x5, waiting for transfers between devices: 22.5 us -> 19.2 us  [body(): gathered = lax.all_to_all(send, ('slab', 'rad'), 0, 0, tiled=True)]
    all_to_all x5, starting transfers between devices: 16.9 us -> 19.5 us  [body(): gathered = lax.all_to_all(send, ('slab', 'rad'), 0, 0, tiled=True)]
  transfers between devices with their start and end apart: 8 -> 8, of which waited for: 5 -> 5; matrix products, arithmetic and copies ran while one was open for 5% -> 5% of each run, Pallas kernels for 25% -> 27%
where the time goes in v20:
time: 134 us
  Pallas kernels  68.6 us (51%)
  starting transfers between devices  32.7 us (24%)
  waiting for transfers between devices  19.2 us (14%)
  local copies, waits for them, and re-layouts  7.64 us (6%)
  other arithmetic  3.24 us (2%)
    pallas_call x4, Pallas kernels, update_and_pack(): pl.pallas_call(functools.partial(update_kernel, groups16=groups16, slots1...  31.3 us
    pallas_call x5, Pallas kernels, sweep(): pl.pallas_call(sweep_kernel, out_shape=(jax.ShapeDtypeStruct(velocity.sha...  26.7 us
    all_to_all x5, starting transfers between devices, body(): gathered = lax.all_to_all(send, ('slab', 'rad'), 0, 0, tiled=True)  19.5 us
    all_to_all x5, waiting for transfers between devices, body(): gathered = lax.all_to_all(send, ('slab', 'rad'), 0, 0, tiled=True)  19.2 us
    pallas_call x1, Pallas kernels, stress_partials(): pl.pallas_call(functools.partial(stress_kernel, groups=groups, rows=rows)...  8.29 us
    all_to_all x1, starting transfers between devices, body(): received = lax.all_to_all(send, ('slab', 'rad'), 0, 0, tiled=True)  7.3 us
    unnamed x49, local copies, waits for them, and re-layouts  6.02 us
    ppermute x2, starting transfers between devices, passed_along(): return lax.ppermute(array, axis, pairs)  5.84 us
  transfers between devices with their start and end apart: 8, of which 5 were waited for; matrix products, arithmetic and copies ran while one was open for 5% of the time, Pallas kernels for 27%

profile of v20, /device:TPU:0, one launch (start us, length us, event | category | flops | bytes accessed | tf_op | source)
XLA Modules:
  0.0 133.6 jit_solution(18115302177626789275)
XLA Ops:
  0.7 8.3 %shard_map.133 = f32[32,12,128]{2,1,0:T(8,128)} custom-call(s32[1]{0:T(128)} %bitcast.12.slab_ref, f32[3,16384]{1,0:T(4,128)} %q_ref.9, s32[1,16384]{1,0:T(1,128)} %bitcast.84, s32[1,16384]{1,0:T(1,128)} %bitcast.73), custom_call_target="tpu_custom_call" | custom-call | flops 4026531840 | bytes 327680 | tf_op jit(solution)/shard_map/pallas_call | solution.py:178
  9.0 7.3 %all-to-all-start = ((f32[32,12,128]{2,1,0:T(8,128)}), f32[32,12,128]{2,1,0:T(8,128)S(1)}, u32[]{:S(2)}, u32[]{:S(2)}) async-start(f32[32,12,128]{2,1,0:T(8,128)} %shard_map.133), calls=%async_computation | async-start | bytes 524288 | tf_op jit(solution)/shard_map/all_to_all | solution.py:342
  16.4 1.8 %copy.52 = f32[8,192,192]{1,2,0:T(8,128)} copy(f32[8,192,192]{2,1,0:T(8,128)S(1)} %copy-done.1) | data formatting | bytes 2359296 | tf_op args[9]
  20.6 7.8 %shard_map.129 = (f32[3,4096]{1,0:T(4,128)}, f32[48,128]{1,0:T(8,128)}, f32[48,128]{1,0:T(8,128)}) custom-call(f32[3,16384]{1,0:T(4,128)} %q_ref.9, f32[3,16384]{1,0:T(4,128)} %inc_ref.7, s32[1,16384]{1,0:T(1,128)} %bitcast.85, s32[1,16384]{1,0:T(1,128)} %bitcast.74, bf16[160,384]{1,0:T(8,128)(2,1)} %pad_maximum_fusion.1.tab_ref, ...), custom_call_target="tpu_custom_call" | custom-call | flops 6442450944 | bytes 163840 | tf_op jit(solution)/shard_map/pallas_call | solution.py:238
  29.9 2.4 %shard_map.134 = (f32[8,192]{1,0:T(8,128)}, f32[256,192]{1,0:T(8,128)}) custom-call(f32[8,192,192]{2,1,0:T(8,128)} %bitcast.55, f32[192,8]{1,0:T(8,128)} %convolution_bitcast_fusion.ft_ref), custom_call_target="tpu_custom_call" | custom-call | flops 589824 | bytes 1179648 | tf_op jit(solution)/shard_map/pallas_call | solution.py:204
  32.3 6.0 %all-to-all-start.1 = ((f32[32,8,192]{2,1,0:T(8,128)}), f32[32,8,192]{2,1,0:T(8,128)S(1)}, u32[]{:S(2)}, u32[]{:S(2)}) async-start(f32[32,8,192]{2,1,0:T(8,128)} %bitcast.70), calls=%async_computation.1 | async-start | bytes 524288 | tf_op jit(solution)/shard_map/all_to_all | solution.py:371
  38.3 7.8 %shard_map.130 = (f32[3,4096]{1,0:T(4,128)}, f32[48,128]{1,0:T(8,128)}, f32[48,128]{1,0:T(8,128)}) custom-call(f32[3,16384]{1,0:T(4,128)} %q_ref.9, f32[3,16384]{1,0:T(4,128)} %inc_ref.7, s32[1,16384]{1,0:T(1,128)} %bitcast.86, s32[1,16384]{1,0:T(1,128)} %bitcast.75, bf16[160,384]{1,0:T(8,128)(2,1)} %pad_maximum_fusion.1.tab_ref, ...), custom_call_target="tpu_custom_call" | custom-call | flops 6442450944 | bytes 163840 | tf_op jit(solution)/shard_map/pallas_call | solution.py:238
  46.1 2.4 %all-to-all-done.1 = f32[32,8,192]{2,1,0:T(8,128)S(1)} async-done(((f32[32,8,192]{2,1,0:T(8,128)}), f32[32,8,192]{2,1,0:T(8,128)S(1)}, u32[]{:S(2)}, u32[]{:S(2)}) %all-to-all-start.1) | async-done | bytes 196640 | tf_op jit(solution)/shard_map/all_to_all | solution.py:371
  49.2 5.3 %shard_map.135 = (f32[8,192]{1,0:T(8,128)}, f32[256,192]{1,0:T(8,128)}) custom-call(s32[32]{0:T(128)} %reshape.94.idx_ref, f32[256,192]{1,0:T(8,128)} %bitcast.64, f32[8,4,192,192]{3,2,1,0:T(8,128)} %s_ref.9, f32[8,192,192]{2,1,0:T(8,128)} %bitcast.56, f32[192,8]{1,0:T(8,128)} %convolution_bitcast_fusion.ft_ref, f32[8,192]{1,0:T(8,128)} %get-tuple-element.40.v_ref), custom_call_target="tpu_custom_call" | custom-call | flops 2949120 | bytes 6094848 | tf_op jit(solution)/shard_map/pallas_call | solution.py:299
  54.6 3.3 %all-to-all-start.2 = ((f32[32,8,192]{2,1,0:T(8,128)}), f32[32,8,192]{2,1,0:T(8,128)S(1)}, u32[]{:S(2)}, u32[]{:S(2)}) async-start(f32[32,8,192]{2,1,0:T(8,128)} %bitcast.69), calls=%async_computation.2 | async-start | bytes 524288 | tf_op jit(solution)/shard_map/all_to_all | solution.py:371
  57.8 7.8 %shard_map.131 = (f32[3,4096]{1,0:T(4,128)}, f32[48,128]{1,0:T(8,128)}, f32[48,128]{1,0:T(8,128)}) custom-call(f32[3,16384]{1,0:T(4,128)} %q_ref.9, f32[3,16384]{1,0:T(4,128)} %inc_ref.7, s32[1,16384]{1,0:T(1,128)} %bitcast.87, s32[1,16384]{1,0:T(1,128)} %bitcast.76, bf16[160,384]{1,0:T(8,128)(2,1)} %pad_maximum_fusion.1.tab_ref, ...), custom_call_target="tpu_custom_call" | custom-call | flops 6442450944 | bytes 163840 | tf_op jit(solution)/shard_map/pallas_call | solution.py:238
  65.7 2.6 %all-to-all-done.2 = f32[32,8,192]{2,1,0:T(8,128)S(1)} async-done(((f32[32,8,192]{2,1,0:T(8,128)}), f32[32,8,192]{2,1,0:T(8,128)S(1)}, u32[]{:S(2)}, u32[]{:S(2)}) %all-to-all-start.2) | async-done | bytes 196640 | tf_op jit(solution)/shard_map/all_to_all | solution.py:371
  68.9 5.3 %shard_map.136 = (f32[8,192]{1,0:T(8,128)}, f32[256,192]{1,0:T(8,128)}) custom-call(s32[32]{0:T(128)} %reshape.94.idx_ref, f32[256,192]{1,0:T(8,128)} %bitcast.65, f32[8,4,192,192]{3,2,1,0:T(8,128)} %s_ref.9, f32[8,192,192]{2,1,0:T(8,128)} %bitcast.57, f32[192,8]{1,0:T(8,128)} %convolution_bitcast_fusion.ft_ref, f32[8,192]{1,0:T(8,128)} %get-tuple-element.42.v_ref), custom_call_target="tpu_custom_call" | custom-call | flops 2949120 | bytes 6094848 | tf_op jit(solution)/shard_map/pallas_call | solution.py:299
  74.3 3.5 %all-to-all-start.3 = ((f32[32,8,192]{2,1,0:T(8,128)}), f32[32,8,192]{2,1,0:T(8,128)S(1)}, u32[]{:S(2)}, u32[]{:S(2)}) async-start(f32[32,8,192]{2,1,0:T(8,128)} %bitcast.67), calls=%async_computation.3 | async-start | bytes 524288 | tf_op jit(solution)/shard_map/all_to_all | solution.py:371
  77.8 7.9 %shard_map.132 = (f32[3,4096]{1,0:T(4,128)}, f32[48,128]{1,0:T(8,128)}, f32[48,128]{1,0:T(8,128)}) custom-call(f32[3,16384]{1,0:T(4,128)} %q_ref.9, f32[3,16384]{1,0:T(4,128)} %inc_ref.7, s32[1,16384]{1,0:T(1,128)} %bitcast.88, s32[1,16384]{1,0:T(1,128)} %bitcast.77, bf16[160,384]{1,0:T(8,128)(2,1)} %pad_maximum_fusion.1.tab_ref, ...), custom_call_target="tpu_custom_call" | custom-call | flops 6442450944 | bytes 163840 | tf_op jit(solution)/shard_map/pallas_call | solution.py:238
  86.5 1.4 %all-to-all-done.3 = f32[32,8,192]{2,1,0:T(8,128)S(1)} async-done(((f32[32,8,192]{2,1,0:T(8,128)}), f32[32,8,192]{2,1,0:T(8,128)S(1)}, u32[]{:S(2)}, u32[]{:S(2)}) %all-to-all-start.3) | async-done | bytes 196640 | tf_op jit(solution)/shard_map/all_to_all | solution.py:371
  88.6 5.3 %shard_map.137 = (f32[8,192]{1,0:T(8,128)}, f32[256,192]{1,0:T(8,128)}) custom-call(s32[32]{0:T(128)} %reshape.94.idx_ref, f32[256,192]{1,0:T(8,128)} %bitcast.62, f32[8,4,192,192]{3,2,1,0:T(8,128)} %s_ref.9, f32[8,192,192]{2,1,0:T(8,128)} %bitcast.58, f32[192,8]{1,0:T(8,128)} %convolution_bitcast_fusion.ft_ref, f32[8,192]{1,0:T(8,128)} %get-tuple-element.44.v_ref), custom_call_target="tpu_custom_call" | custom-call | flops 2949120 | bytes 6094848 | tf_op jit(solution)/shard_map/pallas_call | solution.py:299
  93.9 4.2 %all-to-all-start.4 = ((f32[32,8,192]{2,1,0:T(8,128)}), f32[32,8,192]{2,1,0:T(8,128)S(1)}, u32[]{:S(2)}, u32[]{:S(2)}) async-start(f32[32,8,192]{2,1,0:T(8,128)} %bitcast.68), calls=%async_computation.4 | async-start | bytes 524288 | tf_op jit(solution)/shard_map/all_to_all | solution.py:371
  99.5 4.5 %collective-permute-start = (f32[3,1024]{1,0:T(4,128)S(1)}, f32[3,1024]{1,0:T(4,128)S(1)}, u32[]{:S(2)}, u32[]{:S(2)}) collective-permute-start(f32[3,1024]{1,0:T(4,128)S(1)} %bitcast.81), channel_id=1, source_target_pairs={{0,8},{8,16},{16,24},{1,9},{9,17},{17,25},{2,10},{10,18},{18,26},{... | collective-permute-start | bytes 36872 | tf_op jit(solution)/shard_map/ppermute | solution.py:318
  104.0 4.5 %all-to-all-done.4 = f32[32,8,192]{2,1,0:T(8,128)S(1)} async-done(((f32[32,8,192]{2,1,0:T(8,128)}), f32[32,8,192]{2,1,0:T(8,128)S(1)}, u32[]{:S(2)}, u32[]{:S(2)}) %all-to-all-start.4) | async-done | bytes 196640 | tf_op jit(solution)/shard_map/all_to_all | solution.py:371
  109.2 5.4 %shard_map.138 = (f32[8,192]{1,0:T(8,128)}, f32[256,192]{1,0:T(8,128)}) custom-call(s32[32]{0:T(128)} %reshape.94.idx_ref, f32[256,192]{1,0:T(8,128)} %bitcast.63, f32[8,4,192,192]{3,2,1,0:T(8,128)} %s_ref.9, f32[8,192,192]{2,1,0:T(8,128)} %bitcast.59, f32[192,8]{1,0:T(8,128)} %convolution_bitcast_fusion.ft_ref, f32[8,192]{1,0:T(8,128)} %get-tuple-element.46.v_ref), custom_call_target="tpu_custom_call" | custom-call | flops 2949120 | bytes 6094848 | tf_op jit(solution)/shard_map/pallas_call | solution.py:299
  114.6 2.6 %all-to-all-start.5 = ((f32[32,8,192]{2,1,0:T(8,128)}), f32[32,8,192]{2,1,0:T(8,128)S(1)}, u32[]{:S(2)}, u32[]{:S(2)}) async-start(f32[32,8,192]{2,1,0:T(8,128)} %bitcast.66), calls=%async_computation.5 | async-start | bytes 524288 | tf_op jit(solution)/shard_map/all_to_all | solution.py:371
  119.3 8.3 %all-to-all-done.5 = f32[32,8,192]{2,1,0:T(8,128)S(1)} async-done(((f32[32,8,192]{2,1,0:T(8,128)}), f32[32,8,192]{2,1,0:T(8,128)S(1)}, u32[]{:S(2)}, u32[]{:S(2)}) %all-to-all-start.5) | async-done | bytes 196640 | tf_op jit(solution)/shard_map/all_to_all | solution.py:371
  128.3 5.3 %shard_map.139 = (f32[8,192]{1,0:T(8,128)}, f32[256,192]{1,0:T(8,128)}) custom-call(s32[32]{0:T(128)} %reshape.94.idx_ref, f32[256,192]{1,0:T(8,128)} %bitcast.61, f32[8,4,192,192]{3,2,1,0:T(8,128)} %s_ref.9, f32[8,192,192]{2,1,0:T(8,128)} %bitcast.60, f32[192,8]{1,0:T(8,128)} %convolution_bitcast_fusion.ft_ref, f32[8,192]{1,0:T(8,128)} %get-tuple-element.48.v_ref), custom_call_target="tpu_custom_call" | custom-call | flops 2949120 | bytes 6094848 | tf_op jit(solution)/shard_map/pallas_call | solution.py:299
  (77 shorter events, 11.6 us)
Async XLA Ops:
  0.6 28.0 %copy-start = (f32[192,192]{1,0:T(8,128)S(1)}, f32[192,192]{1,0:T(8,128)}, u32[]{:S(2)}) copy-start(f32[192,192]{1,0:T(8,128)} %param.16) | copy-start | bytes 442372
  0.7 15.6 %copy-start.8 = (s32[16384]{0:T(1024)S(1)}, s32[16384]{0:T(1024)}, u32[]{:S(2)}) copy-start(s32[16384]{0:T(1024)} %param.14) | copy-start | bytes 196612
  0.7 15.7 %copy-start.19 = (f32[384]{0:T(512)S(1)}, f32[384]{0:T(512)}, u32[]{:S(2)}) copy-start(f32[384]{0:T(512)} %param.15) | copy-start | bytes 4612
  0.7 15.7 %copy-start.1 = (f32[8,192,192]{2,1,0:T(8,128)S(1)}, f32[8,192,192]{2,1,0:T(8,128)}, u32[]{:S(2)}) copy-start(f32[8,192,192]{2,1,0:T(8,128)} %param.19) | copy-start | bytes 3538948
  9.0 19.5 %all-to-all-start = ((f32[32,12,128]{2,1,0:T(8,128)}), f32[32,12,128]{2,1,0:T(8,128)S(1)}, u32[]{:S(2)}, u32[]{:S(2)}) async-start(f32[32,12,128]{2,1,0:T(8,128)} %shard_map.133), calls=%async_computation | async-start | bytes 524288 | tf_op jit(solution)/shard_map/all_to_all | solution.py:342
  16.4 1.8 %copy-start.20 = (s32[8,4]{0,1:T(4,128)S(1)}, s32[8,4]{0,1:T(4,128)}, u32[]{:S(2)}) copy-start(s32[8,4]{0,1:T(4,128)} %param.18) | copy-start | bytes 388
  16.4 2.4 %copy-start.7 = (f32[5,3072]{1,0:T(8,128)S(1)}, f32[5,3072]{1,0:T(8,128)}, u32[]{:S(2)}) copy-start(f32[5,3072]{1,0:T(8,128)} %param.12) | copy-start | bytes 184324
  32.3 16.2 %all-to-all-start.1 = ((f32[32,8,192]{2,1,0:T(8,128)}), f32[32,8,192]{2,1,0:T(8,128)S(1)}, u32[]{:S(2)}, u32[]{:S(2)}) async-start(f32[32,8,192]{2,1,0:T(8,128)} %bitcast.70), calls=%async_computation.1 | async-start | bytes 524288 | tf_op jit(solution)/shard_map/all_to_all | solution.py:371
  54.6 13.7 %all-to-all-start.2 = ((f32[32,8,192]{2,1,0:T(8,128)}), f32[32,8,192]{2,1,0:T(8,128)S(1)}, u32[]{:S(2)}, u32[]{:S(2)}) async-start(f32[32,8,192]{2,1,0:T(8,128)} %bitcast.69), calls=%async_computation.2 | async-start | bytes 524288 | tf_op jit(solution)/shard_map/all_to_all | solution.py:371
  74.3 13.6 %all-to-all-start.3 = ((f32[32,8,192]{2,1,0:T(8,128)}), f32[32,8,192]{2,1,0:T(8,128)S(1)}, u32[]{:S(2)}, u32[]{:S(2)}) async-start(f32[32,8,192]{2,1,0:T(8,128)} %bitcast.67), calls=%async_computation.3 | async-start | bytes 524288 | tf_op jit(solution)/shard_map/all_to_all | solution.py:371
  77.7 7.9 %copy-start.13 = (f32[48,128]{1,0:T(8,128)S(1)}, f32[48,128]{1,0:T(8,128)}, u32[]{:S(2)}) copy-start(f32[48,128]{1,0:T(8,128)} %get-tuple-element.31) | copy-start | bytes 73732
  77.8 7.9 %copy-start.14 = (f32[48,128]{1,0:T(8,128)S(1)}, f32[48,128]{1,0:T(8,128)}, u32[]{:S(2)}) copy-start(f32[48,128]{1,0:T(8,128)} %get-tuple-element.35) | copy-start | bytes 73732
  77.8 7.9 %copy-start.15 = (f32[48,128]{1,0:T(8,128)S(1)}, f32[48,128]{1,0:T(8,128)}, u32[]{:S(2)}) copy-start(f32[48,128]{1,0:T(8,128)} %get-tuple-element.32) | copy-start | bytes 73732
  77.8 7.9 %copy-start.16 = (f32[48,128]{1,0:T(8,128)S(1)}, f32[48,128]{1,0:T(8,128)}, u32[]{:S(2)}) copy-start(f32[48,128]{1,0:T(8,128)} %get-tuple-element.36) | copy-start | bytes 73732
  77.8 7.9 %copy-start.17 = (f32[48,128]{1,0:T(8,128)S(1)}, f32[48,128]{1,0:T(8,128)}, u32[]{:S(2)}) copy-start(f32[48,128]{1,0:T(8,128)} %get-tuple-element.33) | copy-start | bytes 73732
  77.8 7.9 %copy-start.18 = (f32[48,128]{1,0:T(8,128)S(1)}, f32[48,128]{1,0:T(8,128)}, u32[]{:S(2)}) copy-start(f32[48,128]{1,0:T(8,128)} %get-tuple-element.37) | copy-start | bytes 73732
  93.9 14.6 %all-to-all-start.4 = ((f32[32,8,192]{2,1,0:T(8,128)}), f32[32,8,192]{2,1,0:T(8,128)S(1)}, u32[]{:S(2)}, u32[]{:S(2)}) async-start(f32[32,8,192]{2,1,0:T(8,128)} %bitcast.68), calls=%async_computation.4 | async-start | bytes 524288 | tf_op jit(solution)/shard_map/all_to_all | solution.py:371
  98.2 19.8 %collective-permute-start.1 = (f32[3,1024]{1,0:T(4,128)S(1)}, f32[3,1024]{1,0:T(4,128)S(1)}, u32[]{:S(2)}, u32[]{:S(2)}) collective-permute-start(f32[3,1024]{1,0:T(4,128)S(1)} %bitcast.80), channel_id=1, source_target_pairs={{8,0},{16,8},{24,16},{9,1},{17,9},{25,17},{10,2},{18,10},{26,18},{... | collective-permute-start | bytes 36872 | tf_op jit(solution)/shard_map/ppermute | solution.py:318
  99.5 18.5 %collective-permute-start = (f32[3,1024]{1,0:T(4,128)S(1)}, f32[3,1024]{1,0:T(4,128)S(1)}, u32[]{:S(2)}, u32[]{:S(2)}) collective-permute-start(f32[3,1024]{1,0:T(4,128)S(1)} %bitcast.81), channel_id=1, source_target_pairs={{0,8},{8,16},{16,24},{1,9},{9,17},{17,25},{2,10},{10,18},{18,26},{... | collective-permute-start | bytes 36872 | tf_op jit(solution)/shard_map/ppermute | solution.py:318
  109.2 8.0 %copy-start.9 = (f32[3,4096]{1,0:T(4,128)S(1)}, f32[3,4096]{1,0:T(4,128)}, u32[]{:S(2)}) copy-start(f32[3,4096]{1,0:T(4,128)} %get-tuple-element.27) | copy-start | bytes 147460
  109.2 8.0 %copy-start.10 = (f32[3,4096]{1,0:T(4,128)S(1)}, f32[3,4096]{1,0:T(4,128)}, u32[]{:S(2)}) copy-start(f32[3,4096]{1,0:T(4,128)} %get-tuple-element.28) | copy-start | bytes 147460
  109.2 8.0 %copy-start.11 = (f32[3,4096]{1,0:T(4,128)S(1)}, f32[3,4096]{1,0:T(4,128)}, u32[]{:S(2)}) copy-start(f32[3,4096]{1,0:T(4,128)} %get-tuple-element.29) | copy-start | bytes 147460
  109.2 8.0 %copy-start.12 = (f32[3,4096]{1,0:T(4,128)S(1)}, f32[3,4096]{1,0:T(4,128)}, u32[]{:S(2)}) copy-start(f32[3,4096]{1,0:T(4,128)} %get-tuple-element.30) | copy-start | bytes 147460
  114.6 13.0 %all-to-all-start.5 = ((f32[32,8,192]{2,1,0:T(8,128)}), f32[32,8,192]{2,1,0:T(8,128)S(1)}, u32[]{:S(2)}, u32[]{:S(2)}) async-start(f32[32,8,192]{2,1,0:T(8,128)} %bitcast.66), calls=%async_computation.5 | async-start | bytes 524288 | tf_op jit(solution)/shard_map/all_to_all | solution.py:371
  (5 other events, 3.5 us)
